TPU v7x, 512 devices: a whole 4x4x16 slice. The times are simulated.
512 devices in a mesh: grp: 16 (over z), lat: 32 (over y, x, core).
Axes of the slice: x: 4, y: 4, z: 16, core: 2. Of those that a mesh axis runs over, the one named last changes fastest.
Arguments:
- stream: bfloat16 [256, 8192], P('lat'), may hold values from -26 to 26
- batch_index: int32 [256], replicated, may hold values from 0 to 255
- weight: bfloat16 [8192, 65536], P(None, ('grp', 'lat')), may hold values from -0.26516504 to 0.26516504
- enc_bias: float32 [65536], P(('grp', 'lat')), may hold values from -1.5 to 0.5
- dec_bias: float32 [8192], replicated, may hold values from -3 to 3
Outputs:
- weight_grad: bfloat16 [8192, 65536], P(None, ('grp', 'lat'))
- bias_grad: float32 [65536], P(('grp', 'lat'))
- recon_error: bfloat16 [256, 8192], P('lat')
All inputs are finite; a program needn't handle non-finite values.
Results may differ from a plain program's by a relative error of at most 0.025.
Values may be sent and summed in bfloat16 or wider, within the bound.
No kernel may reach another device: no remote copies, remote signals or barrier semaphores. Data moves between devices by JAX's collectives and lax.ppermute only.
A program may use at most 64 MiB of HBM per device.

v0:
```python
import jax
import jax.numpy as jnp
from jax import lax
from jax.sharding import PartitionSpec as P

sharpness = 8.0
penalty = 0.25
epsilon = 1e-06


def body(stream, batch_index, weight, enc_bias, dec_bias):
    own_rows = stream.shape[0]
    rank_lat = lax.axis_index("lat")
    gathered = lax.all_gather(stream, "lat", axis=0, tiled=True)
    batch = jnp.take(gathered, batch_index, axis=0)
    centered = (batch.astype(jnp.float32) - dec_bias).astype(jnp.bfloat16)
    preact = jnp.dot(centered, weight, preferred_element_type=jnp.float32) + enc_bias
    active = (jax.nn.softplus(sharpness * preact) / sharpness).astype(jnp.bfloat16)
    first_row = rank_lat * own_rows
    own_batch = lax.dynamic_slice_in_dim(batch, first_row, own_rows, 0)
    block_recon = lax.psum_scatter(
        lax.dot_general(
            active, weight, (((1,), (1,)), ((), ())), preferred_element_type=jnp.float32
        ).astype(jnp.bfloat16),
        "lat",
        scatter_dimension=0,
        tiled=True,
    )
    recon = lax.psum(block_recon, "grp").astype(jnp.float32)
    error_own = recon + dec_bias - own_batch.astype(jnp.float32)
    grad_own = (2.0 * error_own).astype(jnp.bfloat16)
    grad_rows = lax.all_gather(grad_own, "lat", axis=0, tiled=True)
    grad_active = jnp.dot(grad_rows, weight, preferred_element_type=jnp.float32)
    decoder_grad = lax.dot_general(
        grad_rows, active, (((0,), (0,)), ((), ())), preferred_element_type=jnp.float32
    )
    grad_pre = (grad_active + penalty) * jax.nn.sigmoid(sharpness * preact)
    encoder_grad = lax.dot_general(
        centered,
        grad_pre.astype(jnp.bfloat16),
        (((0,), (0,)), ((), ())),
        preferred_element_type=jnp.float32,
    )
    grad_raw = encoder_grad + decoder_grad
    bias_raw = jnp.sum(grad_pre, axis=0)
    local_squares = jnp.sum(grad_raw * grad_raw) + jnp.sum(bias_raw * bias_raw)
    total_squares = lax.psum(local_squares, ("grp", "lat"))
    entries = (weight.shape[0] + 1) * weight.shape[1] * lax.axis_size("lat") * lax.axis_size("grp")
    factor = jnp.minimum(1.0, 1.0 / jnp.sqrt(total_squares / entries + epsilon))
    return (
        (grad_raw * factor).astype(jnp.bfloat16),
        bias_raw * factor,
        error_own.astype(jnp.bfloat16),
    )


def solution(mesh):
    return jax.shard_map(
        body,
        mesh=mesh,
        in_specs=(P("lat", None), P(), P(None, ("grp", "lat")), P(("grp", "lat")), P()),
        out_specs=(P(None, ("grp", "lat")), P(("grp", "lat")), P("lat", None)),
        check_vma=False,
    )
```

profile of v0, /device:TPU:6, one launch (start us, length us, event | category | flops | bytes accessed | tf_op | source)
XLA Modules:
  0.0 527.5 jit_solution(4097323418237096294)
XLA Ops:
  7.2 0.7 all-gather.3.cloned.1.call-update
  7.9 0.0 reduce-scatter.2.cloned.1.call-start
  8.0 0.7 compare_select_fusion.1
  8.7 0.7 compare_and_fusion
  9.3 67.3 %all-gather.3.cloned.1.call-done = bf16[256,8192]{1,0:T(8,128)(2,1)} async-done(((bf16[8,8192]{1,0:T(8,128)(2,1)}), bf16[256,8192]{1,0:T(8,128)(2,1)}) %all-gather.3.cloned.1.call-update) | async-done | bytes 4194320 | tf_op jit(solution)/shard_map/all_gather | solution.py:14
  76.6 11.7 %gather_fusion = bf16[256,8192]{1,0:T(8,128)(2,1)} fusion(bf16[256,8192]{1,0:T(8,128)(2,1)} %all-gather.3.cloned.1.call-done, s32[1024]{0:T(1024)S(1)} %pad_clamp_fusion), kind=kCustom, calls=%fused_computation | custom fusion | bytes 8389632 | tf_op jit(solution)/shard_map/jit(_take)/gather | solution.py:15
  88.3 2.7 broadcast_select_fusion
  91.0 1.9 copy-done.1
  92.9 1.3 fusion.4
  94.2 3.2 convolution_convert_fusion
  97.5 0.0 all-reduce.2.cloned.1.call-start
  97.6 104.7 %reduce-scatter.2.cloned.1.call-done = bf16[8,8192]{1,0:T(8,128)(2,1)} async-done(((bf16[256,8192]{1,0:T(8,128)(2,1)}), bf16[8,8192]{1,0:T(8,128)(2,1)}) %reduce-scatter.2.cloned.1.call-update) | async-done | bytes 131088 | tf_op jit(solution)/shard_map/reduce_scatter | solution.py:21
  202.3 0.2 all-gather.5.cloned.1.call-start
  202.5 136.4 %all-reduce.2.cloned.1.call-done = bf16[8,8192]{1,0:T(8,128)(2,1)} async-done(((bf16[8,8192]{1,0:T(8,128)(2,1)}), bf16[8,8192]{1,0:T(8,128)(2,1)}) %all-reduce.2.cloned.1.call-update) | async-done | bytes 131088 | tf_op jit(solution)/shard_map/psum | solution.py:29
  338.9 1.7 fusion.5
  340.6 59.9 %all-gather.5.cloned.1.call-done = bf16[256,8192]{1,0:T(8,128)(2,1)} async-done(((bf16[8,8192]{1,0:T(8,128)(2,1)}), bf16[256,8192]{1,0:T(8,128)(2,1)}) %all-gather.5.cloned.1.call-update) | async-done | bytes 4194320 | tf_op jit(solution)/shard_map/all_gather | solution.py:32
  400.5 3.6 fusion.11
  404.1 1.5 fusion
  405.7 0.6 multiply_reduce_fusion.1
  406.3 0.1 copy-done.3
  406.3 4.4 multiply_reduce_fusion
  412.0 104.1 %psum.15 = f32[]{:T(128)} all-reduce(f32[]{:T(128)S(6)} %add.67), channel_id=1, replica_groups=mesh['grp'=16,'lat'=32] {'grp','lat'}, use_global_device_ids=true, to_apply=%region_5.6 | all-reduce | flops 1 | bytes 8 | tf_op jit(solution)/shard_map/psum | solution.py:47
  516.7 0.5 broadcast_multiply_fusion
  517.2 3.7 multiply_convert_fusion
  (15 shorter events, 0.1 us)
Async XLA Ops:
  7.2 85.8 %copy-start = (bf16[8192,128]{1,0:T(8,128)(2,1)S(1)}, bf16[8192,128]{1,0:T(8,128)(2,1)}, u32[]{:S(2)}) copy-start(bf16[8192,128]{1,0:T(8,128)(2,1)} %param.7) | copy-start | bytes 6291460
  7.2 69.4 %all-gather.3.cloned.1.call-start = ((), (), s32[]{:S(2)}) async-start(), calls=%async_computation.1 | async-start | bytes 4325376 | tf_op jit(solution)/shard_map/all_gather | solution.py:14
  7.9 194.3 %reduce-scatter.2.cloned.1.call-start = ((), (), s32[]{:S(2)}) async-start(), calls=%async_computation.2 | async-start | bytes 4325376 | tf_op jit(solution)/shard_map/reduce_scatter | solution.py:21
  88.3 4.6 copy-start.4
  88.3 4.6 copy-start.5
  91.0 1.9 copy-start.1
  97.5 241.4 %all-reduce.2.cloned.1.call-start = ((), (), s32[]{:S(2)}) async-start(), calls=%async_computation.3 | async-start | bytes 262144 | tf_op jit(solution)/shard_map/psum | solution.py:29
  202.3 198.3 %all-gather.5.cloned.1.call-start = ((), (), s32[]{:S(2)}) async-start(), calls=%async_computation.4 | async-start | bytes 4325376 | tf_op jit(solution)/shard_map/all_gather | solution.py:32
  400.5 3.6 copy-start.2
  404.1 2.2 copy-start.3
Sparse Core Ops, SparseCore 0:
  11.1 65.4 all-gather.2
  97.6 104.5 reduce-scatter.1
  204.7 134.1 all-reduce.1
  342.4 58.0 all-gather.4
where the time goes:
time: 529 us; the launch traced here: 527 us
  waiting for transfers between devices  369 us (70%)
  blocking collectives  104 us (20%)
  between operations  15.8 us (3%)
  matrix products  14 us (3%)
  local copies, waits for them, and re-layouts  13.7 us (3%)
  other arithmetic  10.6 us (2%)
    psum x1, waiting for transfers between devices, body(): recon = lax.psum(block_recon, 'grp').astype(jnp.float32)  136 us
    reduce_scatter x1, waiting for transfers between devices, body(): lax.psum_scatter(lax.dot_general(active, weight, (((1,), (1,)), ((), ()))...  105 us
    psum x1, blocking collectives, body(): total_squares = lax.psum(local_squares, ('grp', 'lat'))  104 us
    all_gather x1, waiting for transfers between devices, body(): gathered = lax.all_gather(stream, 'lat', axis=0, tiled=True)  67.3 us
    all_gather x1, waiting for transfers between devices, body(): grad_rows = lax.all_gather(grad_own, 'lat', axis=0, tiled=True)  59.9 us
    gather x1, local copies, waits for them, and re-layouts, body(): batch = jnp.take(gathered, batch_index, axis=0)  11.7 us
  transfers between devices with their start and end apart: 4, of which 4 were waited for; matrix products, arithmetic and copies ran while one was open for 0% of the time, Pallas kernels for 0%

commit v1 on v0

--- a/solution.py
+++ b/solution.py
@@ -8,11 +8,29 @@
 epsilon = 1e-06
 
 
+def xor_pairs(n, bit):
+    return [(i, i ^ (1 << bit)) for i in range(n)]
+
+
+def butterfly_sum(x, axis, n, send_dtype):
+    acc = x
+    for bit in range(n.bit_length() - 1):
+        sent = acc.astype(send_dtype)
+        acc = sent.astype(jnp.float32) + lax.ppermute(sent, axis, xor_pairs(n, bit)).astype(jnp.float32)
+    return acc
+
+
 def body(stream, batch_index, weight, enc_bias, dec_bias):
     own_rows = stream.shape[0]
+    n_lat = lax.axis_size("lat")
+    n_grp = lax.axis_size("grp")
     rank_lat = lax.axis_index("lat")
     gathered = lax.all_gather(stream, "lat", axis=0, tiled=True)
-    batch = jnp.take(gathered, batch_index, axis=0)
+    n_rows = gathered.shape[0]
+    onehot = (batch_index[:, None] == lax.broadcasted_iota(jnp.int32, (batch_index.shape[0], n_rows), 1)).astype(
+        gathered.dtype
+    )
+    batch = jnp.dot(onehot, gathered, preferred_element_type=jnp.float32).astype(jnp.bfloat16)
     centered = (batch.astype(jnp.float32) - dec_bias).astype(jnp.bfloat16)
     preact = jnp.dot(centered, weight, preferred_element_type=jnp.float32) + enc_bias
     active = (jax.nn.softplus(sharpness * preact) / sharpness).astype(jnp.bfloat16)
@@ -26,7 +44,7 @@
         scatter_dimension=0,
         tiled=True,
     )
-    recon = lax.psum(block_recon, "grp").astype(jnp.float32)
+    recon = butterfly_sum(block_recon.astype(jnp.float32), "grp", n_grp, jnp.bfloat16)
     error_own = recon + dec_bias - own_batch.astype(jnp.float32)
     grad_own = (2.0 * error_own).astype(jnp.bfloat16)
     grad_rows = lax.all_gather(grad_own, "lat", axis=0, tiled=True)
@@ -44,8 +62,10 @@
     grad_raw = encoder_grad + decoder_grad
     bias_raw = jnp.sum(grad_pre, axis=0)
     local_squares = jnp.sum(grad_raw * grad_raw) + jnp.sum(bias_raw * bias_raw)
-    total_squares = lax.psum(local_squares, ("grp", "lat"))
-    entries = (weight.shape[0] + 1) * weight.shape[1] * lax.axis_size("lat") * lax.axis_size("grp")
+    squares = jnp.broadcast_to(local_squares, (1, 128))
+    squares = butterfly_sum(squares, "lat", n_lat, jnp.float32)
+    total_squares = butterfly_sum(squares, "grp", n_grp, jnp.float32)[0, 0]
+    entries = (weight.shape[0] + 1) * weight.shape[1] * n_lat * n_grp
     factor = jnp.minimum(1.0, 1.0 / jnp.sqrt(total_squares / entries + epsilon))
     return (
         (grad_raw * factor).astype(jnp.bfloat16),

time: 529 us -> 390 us (0.74)
  blocking collectives: 104 us -> 0 us
  waiting for transfers between devices: 369 us -> 278 us
  starting transfers between devices: 0.34 us -> 69.2 us
  local copies, waits for them, and re-layouts: 13.7 us -> 2.03 us
    psum x1 -> x0, waiting for transfers between devices: 136 us -> none  [body(): recon = lax.psum(block_recon, 'grp').astype(jnp.float32)]
    psum x1 -> x0, blocking collectives: 104 us -> none  [body(): total_squares = lax.psum(local_squares, ('grp', 'lat'))]
    ppermute x0 -> x13, starting transfers between devices: none -> 69 us  [butterfly_sum(): lax.ppermute(sent, axis, xor_pairs(n, bit)).astype(jnp.float32)]
    ppermute x0 -> x13, waiting for transfers between devices: none -> 42.6 us  [butterfly_sum(): lax.ppermute(sent, axis, xor_pairs(n, bit)).astype(jnp.float32)]
    gather x1 -> x0, local copies, waits for them, and re-layouts: 11.7 us -> none  [body(): batch = jnp.take(gathered, batch_index, axis=0)]
  transfers between devices with their start and end apart: 4 -> 16, of which waited for: 4 -> 16; matrix products, arithmetic and copies ran while one was open for 0% -> 0% of each run, Pallas kernels for 0% -> 0%
where the time goes in v1:
time: 390 us; the launch traced here: 389 us
  waiting for transfers between devices  278 us (71%)
  starting transfers between devices  69.2 us (18%)
  matrix products  17.5 us (4%)
  between operations  15.3 us (4%)
  other arithmetic  7.54 us (2%)
    reduce_scatter x1, waiting for transfers between devices, body(): lax.psum_scatter(lax.dot_general(active, weight, (((1,), (1,)), ((), ()))...  105 us
    ppermute x13, starting transfers between devices, butterfly_sum(): lax.ppermute(sent, axis, xor_pairs(n, bit)).astype(jnp.float32)  69 us
    all_gather x1, waiting for transfers between devices, body(): gathered = lax.all_gather(stream, 'lat', axis=0, tiled=True)  68.6 us
    all_gather x1, waiting for transfers between devices, body(): grad_rows = lax.all_gather(grad_own, 'lat', axis=0, tiled=True)  61.2 us
    ppermute x13, waiting for transfers between devices, butterfly_sum(): lax.ppermute(sent, axis, xor_pairs(n, bit)).astype(jnp.float32)  42.6 us
  transfers between devices with their start and end apart: 16, of which 16 were waited for; matrix products, arithmetic and copies ran while one was open for 0% of the time, Pallas kernels for 0%

profile of v1, /device:TPU:6, one launch (start us, length us, event | category | flops | bytes accessed | tf_op | source)
XLA Modules:
  0.0 389.3 jit_solution(13155373175371023812)
XLA Ops:
  8.0 68.6 %all-gather.3.cloned.1.call-done = bf16[256,8192]{1,0:T(8,128)(2,1)} async-done(((bf16[8,8192]{1,0:T(8,128)(2,1)}), bf16[256,8192]{1,0:T(8,128)(2,1)}) %all-gather.3.cloned.1.call-update) | async-done | bytes 4194320 | tf_op jit(solution)/shard_map/all_gather | solution.py:28
  76.6 3.5 convolution_convert_fusion.1
  86.7 104.6 %reduce-scatter.2.cloned.1.call-done = bf16[8,8192]{1,0:T(8,128)(2,1)} async-done(((bf16[256,8192]{1,0:T(8,128)(2,1)}), bf16[8,8192]{1,0:T(8,128)(2,1)}) %reduce-scatter.2.cloned.1.call-update) | async-done | bytes 131088 | tf_op jit(solution)/shard_map/reduce_scatter | solution.py:39
  191.3 3.5 collective-permute-start
  194.8 3.6 collective-permute-done
  199.3 4.5 %collective-permute-start.1 = (bf16[8,8192]{1,0:T(8,128)(2,1)S(1)}, bf16[8,8192]{1,0:T(8,128)(2,1)S(1)}, u32[]{:S(2)}, u32[]{:S(2)}) collective-permute-start(bf16[8,8192]{1,0:T(8,128)(2,1)S(1)} %add_convert_fusion.2), channel_id=1, source_target_pairs={{0,64},{32,96},{64,0},{96,32},{128,192},{160,224},{192,128},{224,1... | collective-permute-start | bytes 393224 | tf_op jit(solution)/shard_map/ppermute | solution.py:19
  203.8 4.7 %collective-permute-done.1 = bf16[8,8192]{1,0:T(8,128)(2,1)S(1)} collective-permute-done((bf16[8,8192]{1,0:T(8,128)(2,1)S(1)}, bf16[8,8192]{1,0:T(8,128)(2,1)S(1)}, u32[]{:S(2)}, u32[]{:S(2)}) %collective-permute-start.1) | collective-permute-done | bytes 131104 | tf_op jit(solution)/shard_map/ppermute | solution.py:19
  208.5 8.0 %collective-permute-start.2 = (bf16[8,8192]{1,0:T(8,128)(2,1)S(1)}, bf16[8,8192]{1,0:T(8,128)(2,1)S(1)}, u32[]{:S(2)}, u32[]{:S(2)}) collective-permute-start(bf16[8,8192]{1,0:T(8,128)(2,1)S(1)} %add_convert_fusion.1), channel_id=1, source_target_pairs={{0,128},{32,160},{64,192},{96,224},{128,0},{160,32},{192,64},{224,... | collective-permute-start | bytes 393224 | tf_op jit(solution)/shard_map/ppermute | solution.py:19
  216.5 7.0 %collective-permute-done.2 = bf16[8,8192]{1,0:T(8,128)(2,1)S(1)} collective-permute-done((bf16[8,8192]{1,0:T(8,128)(2,1)S(1)}, bf16[8,8192]{1,0:T(8,128)(2,1)S(1)}, u32[]{:S(2)}, u32[]{:S(2)}) %collective-permute-start.2) | collective-permute-done | bytes 131104 | tf_op jit(solution)/shard_map/ppermute | solution.py:19
  223.6 11.7 %collective-permute-start.3 = (bf16[8,8192]{1,0:T(8,128)(2,1)S(1)}, bf16[8,8192]{1,0:T(8,128)(2,1)S(1)}, u32[]{:S(2)}, u32[]{:S(2)}) collective-permute-start(bf16[8,8192]{1,0:T(8,128)(2,1)S(1)} %add_convert_fusion), channel_id=1, source_target_pairs={{0,256},{32,288},{64,320},{96,352},{128,384},{160,416},{192,448},{... | collective-permute-start | bytes 393224 | tf_op jit(solution)/shard_map/ppermute | solution.py:19
  235.3 5.7 %collective-permute-done.3 = bf16[8,8192]{1,0:T(8,128)(2,1)S(1)} collective-permute-done((bf16[8,8192]{1,0:T(8,128)(2,1)S(1)}, bf16[8,8192]{1,0:T(8,128)(2,1)S(1)}, u32[]{:S(2)}, u32[]{:S(2)}) %collective-permute-start.3) | collective-permute-done | bytes 131104 | tf_op jit(solution)/shard_map/ppermute | solution.py:19
  242.7 61.2 %all-gather.5.cloned.1.call-done = bf16[256,8192]{1,0:T(8,128)(2,1)} async-done(((bf16[8,8192]{1,0:T(8,128)(2,1)}), bf16[256,8192]{1,0:T(8,128)(2,1)}) %all-gather.5.cloned.1.call-update) | async-done | bytes 4194320 | tf_op jit(solution)/shard_map/all_gather | solution.py:50
  303.9 3.6 fusion.12
  309.6 4.4 %multiply_reduce_fusion = (f32[]{:T(128)}, f32[8192,128]{1,0:T(8,128)}) fusion(f32[8192,128]{1,0:T(8,128)S(1)} %fusion, bf16[256,8192]{1,0:T(8,128)(2,1)S(1)} %copy-done.3, f32[256,128]{1,0:T(8,128)S(1)} %fusion.4), kind=kOutput, calls=%fused_computation.5 | convolution fusion | flops 540278784 | bytes 12713988 | tf_op jit(solution)/shard_map/dot_general | solution.py:52
  323.8 3.4 collective-permute-start.6
  327.1 3.5 collective-permute-done.6
  332.6 3.5 collective-permute-done.7
  336.1 3.4 collective-permute-start.8
  339.5 3.5 collective-permute-done.8
  343.1 3.5 collective-permute-start.9
  348.5 4.4 %collective-permute-start.10 = (f32[1,128]{1,0:T(1,128)S(1)}, f32[1,128]{1,0:T(1,128)S(1)}, u32[]{:S(2)}, u32[]{:S(2)}) collective-permute-start(f32[1,128]{1,0:T(1,128)S(1)} %add.103), channel_id=1, source_target_pairs={{0,64},{32,96},{64,0},{96,32},{128,192},{160,224},{192,128},{224,1... | collective-permute-start | bytes 1544 | tf_op jit(solution)/shard_map/ppermute | solution.py:19
  354.8 7.6 %collective-permute-start.11 = (f32[1,128]{1,0:T(1,128)S(1)}, f32[1,128]{1,0:T(1,128)S(1)}, u32[]{:S(2)}, u32[]{:S(2)}) collective-permute-start(f32[1,128]{1,0:T(1,128)S(1)} %add.104), channel_id=1, source_target_pairs={{0,128},{32,160},{64,192},{96,224},{128,0},{160,32},{192,64},{224,... | collective-permute-start | bytes 1544 | tf_op jit(solution)/shard_map/ppermute | solution.py:19
  364.1 12.8 %collective-permute-start.12 = (f32[1,128]{1,0:T(1,128)S(1)}, f32[1,128]{1,0:T(1,128)S(1)}, u32[]{:S(2)}, u32[]{:S(2)}) collective-permute-start(f32[1,128]{1,0:T(1,128)S(1)} %add.105), channel_id=1, source_target_pairs={{0,256},{32,288},{64,320},{96,352},{128,384},{160,416},{192,448},{... | collective-permute-start | bytes 1544 | tf_op jit(solution)/shard_map/ppermute | solution.py:19
  379.1 3.7 multiply_convert_fusion
  (46 shorter events, 30.1 us)
Async XLA Ops:
  7.2 74.9 %copy-start = (bf16[8192,128]{1,0:T(8,128)(2,1)S(1)}, bf16[8192,128]{1,0:T(8,128)(2,1)}, u32[]{:S(2)}) copy-start(bf16[8192,128]{1,0:T(8,128)(2,1)} %param.7) | copy-start | bytes 6291460
  7.2 69.4 %all-gather.3.cloned.1.call-start = ((), (), s32[]{:S(2)}) async-start(), calls=%async_computation.1 | async-start | bytes 4325376 | tf_op jit(solution)/shard_map/all_gather | solution.py:28
  7.9 74.2 %copy-start.4 = (f32[8192]{0:T(1024)S(1)}, f32[8192]{0:T(1024)}, u32[]{:S(2)}) copy-start(f32[8192]{0:T(1024)} %param.9) | copy-start | bytes 98308
  7.9 74.2 %copy-start.5 = (f32[128]{0:T(128)S(1)}, f32[128]{0:T(128)}, u32[]{:S(2)}) copy-start(f32[128]{0:T(128)} %param.8) | copy-start | bytes 1540
  7.9 183.4 %reduce-scatter.2.cloned.1.call-start = ((), (), s32[]{:S(2)}) async-start(), calls=%async_computation.2 | async-start | bytes 4325376 | tf_op jit(solution)/shard_map/reduce_scatter | solution.py:39
  80.1 2.0 copy-start.1
  86.6 217.2 %all-gather.5.cloned.1.call-start = ((), (), s32[]{:S(2)}) async-start(), calls=%async_computation.3 | async-start | bytes 4325376 | tf_op jit(solution)/shard_map/all_gather | solution.py:50
  191.3 7.1 %collective-permute-start = (bf16[8,8192]{1,0:T(8,128)(2,1)}, bf16[8,8192]{1,0:T(8,128)(2,1)S(1)}, u32[]{:S(2)}, u32[]{:S(2)}) collective-permute-start(bf16[8,8192]{1,0:T(8,128)(2,1)} %reduce-scatter.2.cloned.1.call-done), channel_id=1, source_target_pairs={{0,32},{32,0},{64,96},{96,64},{128,160},{160,128},{192,224},{224,1... | collective-permute-start | bytes 393224 | tf_op jit(solution)/shard_map/ppermute | solution.py:19
  199.3 9.2 %collective-permute-start.1 = (bf16[8,8192]{1,0:T(8,128)(2,1)S(1)}, bf16[8,8192]{1,0:T(8,128)(2,1)S(1)}, u32[]{:S(2)}, u32[]{:S(2)}) collective-permute-start(bf16[8,8192]{1,0:T(8,128)(2,1)S(1)} %add_convert_fusion.2), channel_id=1, source_target_pairs={{0,64},{32,96},{64,0},{96,32},{128,192},{160,224},{192,128},{224,1... | collective-permute-start | bytes 393224 | tf_op jit(solution)/shard_map/ppermute | solution.py:19
  208.5 15.0 %collective-permute-start.2 = (bf16[8,8192]{1,0:T(8,128)(2,1)S(1)}, bf16[8,8192]{1,0:T(8,128)(2,1)S(1)}, u32[]{:S(2)}, u32[]{:S(2)}) collective-permute-start(bf16[8,8192]{1,0:T(8,128)(2,1)S(1)} %add_convert_fusion.1), channel_id=1, source_target_pairs={{0,128},{32,160},{64,192},{96,224},{128,0},{160,32},{192,64},{224,... | collective-permute-start | bytes 393224 | tf_op jit(solution)/shard_map/ppermute | solution.py:19
  223.6 17.4 %collective-permute-start.3 = (bf16[8,8192]{1,0:T(8,128)(2,1)S(1)}, bf16[8,8192]{1,0:T(8,128)(2,1)S(1)}, u32[]{:S(2)}, u32[]{:S(2)}) collective-permute-start(bf16[8,8192]{1,0:T(8,128)(2,1)S(1)} %add_convert_fusion), channel_id=1, source_target_pairs={{0,256},{32,288},{64,320},{96,352},{128,384},{160,416},{192,448},{... | collective-permute-start | bytes 393224 | tf_op jit(solution)/shard_map/ppermute | solution.py:19
  303.9 3.6 copy-start.2
  307.5 2.2 copy-start.3
  315.3 3.0 collective-permute-start.4
  318.3 5.4 %collective-permute-start.5 = (f32[1,128]{1,0:T(1,128)S(1)}, f32[1,128]{1,0:T(1,128)S(1)}, u32[]{:S(2)}, u32[]{:S(2)}) collective-permute-start(f32[1,128]{1,0:T(1,128)S(1)} %broadcast_add_fusion), channel_id=1, source_target_pairs={{0,2},{1,3},{2,0},{3,1},{4,6},{5,7},{6,4},{7,5},{8,10},{9,11},{10,... | collective-permute-start | bytes 1544 | tf_op jit(solution)/shard_map/ppermute | solution.py:19
  323.8 6.9 %collective-permute-start.6 = (f32[1,128]{1,0:T(1,128)S(1)}, f32[1,128]{1,0:T(1,128)S(1)}, u32[]{:S(2)}, u32[]{:S(2)}) collective-permute-start(f32[1,128]{1,0:T(1,128)S(1)} %fusion.20), channel_id=1, source_target_pairs={{0,4},{1,5},{2,6},{3,7},{4,0},{5,1},{6,2},{7,3},{8,12},{9,13},{10,... | collective-permute-start | bytes 1544 | tf_op jit(solution)/shard_map/ppermute | solution.py:19
  330.7 5.4 %collective-permute-start.7 = (f32[1,128]{1,0:T(1,128)S(1)}, f32[1,128]{1,0:T(1,128)S(1)}, u32[]{:S(2)}, u32[]{:S(2)}) collective-permute-start(f32[1,128]{1,0:T(1,128)S(1)} %add.100), channel_id=1, source_target_pairs={{0,8},{1,9},{2,10},{3,11},{4,12},{5,13},{6,14},{7,15},{8,0},{9,1},... | collective-permute-start | bytes 1544 | tf_op jit(solution)/shard_map/ppermute | solution.py:19
  336.1 6.9 %collective-permute-start.8 = (f32[1,128]{1,0:T(1,128)S(1)}, f32[1,128]{1,0:T(1,128)S(1)}, u32[]{:S(2)}, u32[]{:S(2)}) collective-permute-start(f32[1,128]{1,0:T(1,128)S(1)} %add.101), channel_id=1, source_target_pairs={{0,16},{1,17},{2,18},{3,19},{4,20},{5,21},{6,22},{7,23},{8,24},{9,... | collective-permute-start | bytes 1544 | tf_op jit(solution)/shard_map/ppermute | solution.py:19
  343.1 5.4 %collective-permute-start.9 = (f32[1,128]{1,0:T(1,128)S(1)}, f32[1,128]{1,0:T(1,128)S(1)}, u32[]{:S(2)}, u32[]{:S(2)}) collective-permute-start(f32[1,128]{1,0:T(1,128)S(1)} %add.102), channel_id=1, source_target_pairs={{0,32},{32,0},{64,96},{96,64},{128,160},{160,128},{192,224},{224,1... | collective-permute-start | bytes 1544 | tf_op jit(solution)/shard_map/ppermute | solution.py:19
  348.5 6.3 %collective-permute-start.10 = (f32[1,128]{1,0:T(1,128)S(1)}, f32[1,128]{1,0:T(1,128)S(1)}, u32[]{:S(2)}, u32[]{:S(2)}) collective-permute-start(f32[1,128]{1,0:T(1,128)S(1)} %add.103), channel_id=1, source_target_pairs={{0,64},{32,96},{64,0},{96,32},{128,192},{160,224},{192,128},{224,1... | collective-permute-start | bytes 1544 | tf_op jit(solution)/shard_map/ppermute | solution.py:19
  354.8 9.3 %collective-permute-start.11 = (f32[1,128]{1,0:T(1,128)S(1)}, f32[1,128]{1,0:T(1,128)S(1)}, u32[]{:S(2)}, u32[]{:S(2)}) collective-permute-start(f32[1,128]{1,0:T(1,128)S(1)} %add.104), channel_id=1, source_target_pairs={{0,128},{32,160},{64,192},{96,224},{128,0},{160,32},{192,64},{224,... | collective-permute-start | bytes 1544 | tf_op jit(solution)/shard_map/ppermute | solution.py:19
  364.1 14.3 %collective-permute-start.12 = (f32[1,128]{1,0:T(1,128)S(1)}, f32[1,128]{1,0:T(1,128)S(1)}, u32[]{:S(2)}, u32[]{:S(2)}) collective-permute-start(f32[1,128]{1,0:T(1,128)S(1)} %add.105), channel_id=1, source_target_pairs={{0,256},{32,288},{64,320},{96,352},{128,384},{160,416},{192,448},{... | collective-permute-start | bytes 1544 | tf_op jit(solution)/shard_map/ppermute | solution.py:19
Sparse Core Ops, SparseCore 0:
  11.2 65.4 all-gather.2
  86.7 104.5 reduce-scatter.1
  242.8 60.9 all-gather.4

commit v2 on v1

v2 whole, which is shorter than its diff:
```python
import jax
import jax.numpy as jnp
import numpy as np
from jax import lax
from jax.sharding import Mesh
from jax.sharding import PartitionSpec as P

sharpness = 8.0
penalty = 0.25
epsilon = 1e-06

LAT = ("chip", "core")
ALL = ("grp", "chip", "core")


def xor_pairs(n, bit):
    return [(i, i ^ (1 << bit)) for i in range(n)]


def butterfly_sum(x, axis, n, send_dtype):
    acc = x
    for bit in range(n.bit_length() - 1):
        sent = acc.astype(send_dtype)
        acc = sent.astype(jnp.float32) + lax.ppermute(sent, axis, xor_pairs(n, bit)).astype(jnp.float32)
    return acc


def swap_cores(x):
    return lax.ppermute(x, "core", [(0, 1), (1, 0)])


def body(stream, batch_index, weight, enc_bias, dec_bias):
    own_rows = stream.shape[0]
    n_chip = lax.axis_size("chip")
    n_grp = lax.axis_size("grp")
    chip = lax.axis_index("chip")
    core = lax.axis_index("core")
    half = n_chip * own_rows
    n_tok = batch_index.shape[0]

    mine = lax.all_gather(stream, "chip", axis=0, tiled=True)
    gathered = jnp.concatenate([mine, swap_cores(mine)], axis=0)

    q = jnp.arange(n_tok, dtype=jnp.int32)
    side = q // half
    q_chip = (q % half) // own_rows
    q_row = q % own_rows
    q_core = jnp.where(side == 0, core, 1 - core)
    token = (q_chip * 2 + q_core) * own_rows + q_row
    src = jnp.take(batch_index, token)
    s_chip = src // (2 * own_rows)
    s_core = (src // own_rows) % 2
    place = jnp.where(s_core == core, 0, half) + s_chip * own_rows + src % own_rows
    onehot = (place[:, None] == lax.broadcasted_iota(jnp.int32, (n_tok, gathered.shape[0]), 1)).astype(
        gathered.dtype
    )
    batch = jnp.dot(onehot, gathered, preferred_element_type=jnp.float32).astype(jnp.bfloat16)
    centered = (batch.astype(jnp.float32) - dec_bias).astype(jnp.bfloat16)
    preact = jnp.dot(centered, weight, preferred_element_type=jnp.float32) + enc_bias
    active = (jax.nn.softplus(sharpness * preact) / sharpness).astype(jnp.bfloat16)
    own_batch = lax.dynamic_slice_in_dim(batch, chip * own_rows, own_rows, 0)

    partial = lax.dot_general(
        active, weight, (((1,), (1,)), ((), ())), preferred_element_type=jnp.float32
    ).astype(jnp.bfloat16)
    halves = partial.reshape(2, n_chip, own_rows, partial.shape[1])
    by_core = jnp.where(core == 0, halves, halves[::-1])
    lat_order = jnp.swapaxes(by_core, 0, 1).reshape(partial.shape)
    block_recon = lax.psum_scatter(lat_order, LAT, scatter_dimension=0, tiled=True)
    recon = butterfly_sum(block_recon.astype(jnp.float32), "grp", n_grp, jnp.bfloat16)
    error_own = recon + dec_bias - own_batch.astype(jnp.float32)
    grad_own = (2.0 * error_own).astype(jnp.bfloat16)
    grad_mine = lax.all_gather(grad_own, "chip", axis=0, tiled=True)
    grad_rows = jnp.concatenate([grad_mine, swap_cores(grad_mine)], axis=0)

    grad_active = jnp.dot(grad_rows, weight, preferred_element_type=jnp.float32)
    decoder_grad = lax.dot_general(
        grad_rows, active, (((0,), (0,)), ((), ())), preferred_element_type=jnp.float32
    )
    grad_pre = (grad_active + penalty) * jax.nn.sigmoid(sharpness * preact)
    encoder_grad = lax.dot_general(
        centered,
        grad_pre.astype(jnp.bfloat16),
        (((0,), (0,)), ((), ())),
        preferred_element_type=jnp.float32,
    )
    grad_raw = encoder_grad + decoder_grad
    bias_raw = jnp.sum(grad_pre, axis=0)
    local_squares = jnp.sum(grad_raw * grad_raw) + jnp.sum(bias_raw * bias_raw)
    squares = jnp.broadcast_to(local_squares, (1, 128))
    squares = butterfly_sum(squares, "core", 2, jnp.float32)
    squares = butterfly_sum(squares, "chip", n_chip, jnp.float32)
    total_squares = butterfly_sum(squares, "grp", n_grp, jnp.float32)[0, 0]
    entries = (weight.shape[0] + 1) * weight.shape[1] * 2 * n_chip * n_grp
    factor = jnp.minimum(1.0, 1.0 / jnp.sqrt(total_squares / entries + epsilon))
    return (
        (grad_raw * factor).astype(jnp.bfloat16),
        bias_raw * factor,
        error_own.astype(jnp.bfloat16),
    )


def solution(mesh):
    devices = np.asarray(mesh.devices)
    n_grp, n_lat = devices.shape
    split = Mesh(devices.reshape(n_grp, n_lat // 2, 2), ALL)
    return jax.shard_map(
        body,
        mesh=split,
        in_specs=(P(LAT, None), P(), P(None, ALL), P(ALL), P()),
        out_specs=(P(None, ALL), P(ALL), P(LAT, None)),
        check_vma=False,
    )
```

time: 390 us -> 400 us (1.026)
  local copies, waits for them, and re-layouts: 2.03 us -> 6.56 us
  matrix products: 17.5 us -> 13.3 us
    ppermute x0 -> x2, waiting for transfers between devices: none -> 4.98 us  [swap_cores(): return lax.ppermute(x, 'core', [(0, 1), (1, 0)])]
  transfers between devices with their start and end apart: 16 -> 18, of which waited for: 16 -> 18; matrix products, arithmetic and copies ran while one was open for 0% -> 1% of each run, Pallas kernels for 0% -> 0%
where the time goes in v2:
time: 400 us; the launch traced here: 399 us
  waiting for transfers between devices  281 us (70%)
  starting transfers between devices  72.7 us (18%)
  between operations  15.4 us (4%)
  matrix products  13.3 us (3%)
  other arithmetic  10.7 us (3%)
  local copies, waits for them, and re-layouts  6.56 us (2%)
    reduce_scatter x1, waiting for transfers between devices, body(): lax.psum_scatter(lat_order, LAT, scatter_dimension=0, tiled=True)  105 us
    ppermute x13, starting transfers between devices, butterfly_sum(): lax.ppermute(sent, axis, xor_pairs(n, bit)).astype(jnp.float32)  68.7 us
    all_gather x1, waiting for transfers between devices, body(): mine = lax.all_gather(stream, 'chip', axis=0, tiled=True)  67.4 us
    all_gather x1, waiting for transfers between devices, body(): grad_mine = lax.all_gather(grad_own, 'chip', axis=0, tiled=True)  60 us
    ppermute x13, waiting for transfers between devices, butterfly_sum(): lax.ppermute(sent, axis, xor_pairs(n, bit)).astype(jnp.float32)  42.9 us
  transfers between devices with their start and end apart: 18, of which 18 were waited for; matrix products, arithmetic and copies ran while one was open for 1% of the time, Pallas kernels for 0%

profile of v2, /device:TPU:6, one launch (start us, length us, event | category | flops | bytes accessed | tf_op | source)
XLA Modules:
  0.0 399.3 jit_solution(17982487750044333137)
XLA Ops:
  8.0 67.4 %all-gather.3.cloned.1.call-done = bf16[128,8192]{1,0:T(8,128)(2,1)} async-done(((bf16[8,8192]{1,0:T(8,128)(2,1)}), bf16[128,8192]{1,0:T(8,128)(2,1)}) %all-gather.3.cloned.1.call-update) | async-done | bytes 2097168 | tf_op jit(solution)/shard_map/all_gather | solution.py:41
  81.8 3.5 convolution_convert_fusion.1
  93.4 104.6 %reduce-scatter.2.cloned.1.call-done = bf16[8,8192]{1,0:T(8,128)(2,1)} async-done(((bf16[256,8192]{1,0:T(8,128)(2,1)}), bf16[8,8192]{1,0:T(8,128)(2,1)}) %reduce-scatter.2.cloned.1.call-update) | async-done | bytes 131088 | tf_op jit(solution)/shard_map/reduce_scatter | solution.py:69
  198.0 3.5 collective-permute-start.1
  201.5 3.6 collective-permute-done.1
  206.0 4.4 %collective-permute-start.2 = (bf16[8,8192]{1,0:T(8,128)(2,1)S(1)}, bf16[8,8192]{1,0:T(8,128)(2,1)S(1)}, u32[]{:S(2)}, u32[]{:S(2)}) collective-permute-start(bf16[8,8192]{1,0:T(8,128)(2,1)S(1)} %add_convert_fusion.2), channel_id=1, source_target_pairs={{0,64},{32,96},{64,0},{96,32},{128,192},{160,224},{192,128},{224,1... | collective-permute-start | bytes 393224 | tf_op jit(solution)/shard_map/ppermute | solution.py:24
  210.4 4.7 %collective-permute-done.2 = bf16[8,8192]{1,0:T(8,128)(2,1)S(1)} collective-permute-done((bf16[8,8192]{1,0:T(8,128)(2,1)S(1)}, bf16[8,8192]{1,0:T(8,128)(2,1)S(1)}, u32[]{:S(2)}, u32[]{:S(2)}) %collective-permute-start.2) | collective-permute-done | bytes 131104 | tf_op jit(solution)/shard_map/ppermute | solution.py:24
  215.2 7.9 %collective-permute-start.3 = (bf16[8,8192]{1,0:T(8,128)(2,1)S(1)}, bf16[8,8192]{1,0:T(8,128)(2,1)S(1)}, u32[]{:S(2)}, u32[]{:S(2)}) collective-permute-start(bf16[8,8192]{1,0:T(8,128)(2,1)S(1)} %add_convert_fusion.1), channel_id=1, source_target_pairs={{0,128},{32,160},{64,192},{96,224},{128,0},{160,32},{192,64},{224,... | collective-permute-start | bytes 393224 | tf_op jit(solution)/shard_map/ppermute | solution.py:24
  223.2 7.1 %collective-permute-done.3 = bf16[8,8192]{1,0:T(8,128)(2,1)S(1)} collective-permute-done((bf16[8,8192]{1,0:T(8,128)(2,1)S(1)}, bf16[8,8192]{1,0:T(8,128)(2,1)S(1)}, u32[]{:S(2)}, u32[]{:S(2)}) %collective-permute-start.3) | collective-permute-done | bytes 131104 | tf_op jit(solution)/shard_map/ppermute | solution.py:24
  230.3 11.7 %collective-permute-start.4 = (bf16[8,8192]{1,0:T(8,128)(2,1)S(1)}, bf16[8,8192]{1,0:T(8,128)(2,1)S(1)}, u32[]{:S(2)}, u32[]{:S(2)}) collective-permute-start(bf16[8,8192]{1,0:T(8,128)(2,1)S(1)} %add_convert_fusion), channel_id=1, source_target_pairs={{0,256},{32,288},{64,320},{96,352},{128,384},{160,416},{192,448},{... | collective-permute-start | bytes 393224 | tf_op jit(solution)/shard_map/ppermute | solution.py:24
  242.0 5.7 %collective-permute-done.4 = bf16[8,8192]{1,0:T(8,128)(2,1)S(1)} collective-permute-done((bf16[8,8192]{1,0:T(8,128)(2,1)S(1)}, bf16[8,8192]{1,0:T(8,128)(2,1)S(1)}, u32[]{:S(2)}, u32[]{:S(2)}) %collective-permute-start.4) | collective-permute-done | bytes 131104 | tf_op jit(solution)/shard_map/ppermute | solution.py:24
  249.4 60.0 %all-gather.5.cloned.1.call-done = bf16[128,8192]{1,0:T(8,128)(2,1)} async-done(((bf16[8,8192]{1,0:T(8,128)(2,1)}), bf16[128,8192]{1,0:T(8,128)(2,1)}) %all-gather.5.cloned.1.call-update) | async-done | bytes 2097168 | tf_op jit(solution)/shard_map/all_gather | solution.py:73
  319.6 4.4 %multiply_reduce_fusion = (f32[]{:T(128)}, f32[8192,128]{1,0:T(8,128)}) fusion(f32[8192,128]{1,0:T(8,128)S(1)} %fusion.3, bf16[256,8192]{1,0:T(8,128)(2,1)S(1)} %constant_dynamic-update-slice_fusion, f32[256,128]{1,0:T(8,128)S(1)} %fusion.7), kind=kOutput, calls=%fused_computation.10 | convolution fusion | flops 540278784 | bytes 12713988 | tf_op jit(solution)/shard_map/dot_general | solution.py:77
  330.5 3.2 collective-permute-done.7
  333.7 3.3 collective-permute-start.8
  337.1 3.6 collective-permute-done.8
  342.5 3.5 collective-permute-done.9
  346.1 3.4 collective-permute-start.10
  349.4 3.6 collective-permute-done.10
  353.0 3.4 collective-permute-start.11
  358.4 4.4 %collective-permute-start.12 = (f32[1,128]{1,0:T(1,128)S(1)}, f32[1,128]{1,0:T(1,128)S(1)}, u32[]{:S(2)}, u32[]{:S(2)}) collective-permute-start(f32[1,128]{1,0:T(1,128)S(1)} %add.281), channel_id=1, source_target_pairs={{0,64},{32,96},{64,0},{96,32},{128,192},{160,224},{192,128},{224,1... | collective-permute-start | bytes 1544 | tf_op jit(solution)/shard_map/ppermute | solution.py:24
  364.7 7.6 %collective-permute-start.13 = (f32[1,128]{1,0:T(1,128)S(1)}, f32[1,128]{1,0:T(1,128)S(1)}, u32[]{:S(2)}, u32[]{:S(2)}) collective-permute-start(f32[1,128]{1,0:T(1,128)S(1)} %add.282), channel_id=1, source_target_pairs={{0,128},{32,160},{64,192},{96,224},{128,0},{160,32},{192,64},{224,... | collective-permute-start | bytes 1544 | tf_op jit(solution)/shard_map/ppermute | solution.py:24
  374.1 12.8 %collective-permute-start.14 = (f32[1,128]{1,0:T(1,128)S(1)}, f32[1,128]{1,0:T(1,128)S(1)}, u32[]{:S(2)}, u32[]{:S(2)}) collective-permute-start(f32[1,128]{1,0:T(1,128)S(1)} %add.283), channel_id=1, source_target_pairs={{0,256},{32,288},{64,320},{96,352},{128,384},{160,416},{192,448},{... | collective-permute-start | bytes 1544 | tf_op jit(solution)/shard_map/ppermute | solution.py:24
  389.0 3.7 multiply_convert_fusion
  (56 shorter events, 42.6 us)
Async XLA Ops:
  7.2 80.1 %copy-start = (bf16[8192,128]{1,0:T(8,128)(2,1)S(1)}, bf16[8192,128]{1,0:T(8,128)(2,1)}, u32[]{:S(2)}) copy-start(bf16[8192,128]{1,0:T(8,128)(2,1)} %param.7) | copy-start | bytes 6291460
  7.2 68.2 %all-gather.3.cloned.1.call-start = ((), (), s32[]{:S(2)}) async-start(), calls=%async_computation.1 | async-start | bytes 2228224 | tf_op jit(solution)/shard_map/all_gather | solution.py:41
  7.9 190.1 %reduce-scatter.2.cloned.1.call-start = ((), (), s32[]{:S(2)}) async-start(), calls=%async_computation.2 | async-start | bytes 4325376 | tf_op jit(solution)/shard_map/reduce_scatter | solution.py:69
  75.4 6.4 %collective-permute-start = (bf16[128,8192]{1,0:T(8,128)(2,1)}, bf16[128,8192]{1,0:T(8,128)(2,1)}, u32[]{:S(2)}, u32[]{:S(2)}) collective-permute-start(bf16[128,8192]{1,0:T(8,128)(2,1)} %all-gather.3.cloned.1.call-done), channel_id=1, source_target_pairs={{0,1},{1,0},{2,3},{3,2},{4,5},{5,4},{6,7},{7,6},{8,9},{9,8},{10,11... | collective-permute-start | bytes 6291464 | tf_op jit(solution)/shard_map/ppermute | solution.py:29
  79.4 7.9 %copy-start.3 = (f32[8192]{0:T(1024)S(1)}, f32[8192]{0:T(1024)}, u32[]{:S(2)}) copy-start(f32[8192]{0:T(1024)} %param.9) | copy-start | bytes 98308
  79.4 7.9 %copy-start.4 = (f32[128]{0:T(128)S(1)}, f32[128]{0:T(128)}, u32[]{:S(2)}) copy-start(f32[128]{0:T(128)} %param.8) | copy-start | bytes 1540
  85.3 1.9 copy-start.1
  93.3 216.1 %all-gather.5.cloned.1.call-start = ((), (), s32[]{:S(2)}) async-start(), calls=%async_computation.3 | async-start | bytes 2228224 | tf_op jit(solution)/shard_map/all_gather | solution.py:73
  198.0 7.1 %collective-permute-start.1 = (bf16[8,8192]{1,0:T(8,128)(2,1)}, bf16[8,8192]{1,0:T(8,128)(2,1)S(1)}, u32[]{:S(2)}, u32[]{:S(2)}) collective-permute-start(bf16[8,8192]{1,0:T(8,128)(2,1)} %reduce-scatter.2.cloned.1.call-done), channel_id=1, source_target_pairs={{0,32},{32,0},{64,96},{96,64},{128,160},{160,128},{192,224},{224,1... | collective-permute-start | bytes 393224 | tf_op jit(solution)/shard_map/ppermute | solution.py:24
  206.0 9.2 %collective-permute-start.2 = (bf16[8,8192]{1,0:T(8,128)(2,1)S(1)}, bf16[8,8192]{1,0:T(8,128)(2,1)S(1)}, u32[]{:S(2)}, u32[]{:S(2)}) collective-permute-start(bf16[8,8192]{1,0:T(8,128)(2,1)S(1)} %add_convert_fusion.2), channel_id=1, source_target_pairs={{0,64},{32,96},{64,0},{96,32},{128,192},{160,224},{192,128},{224,1... | collective-permute-start | bytes 393224 | tf_op jit(solution)/shard_map/ppermute | solution.py:24
  215.2 15.0 %collective-permute-start.3 = (bf16[8,8192]{1,0:T(8,128)(2,1)S(1)}, bf16[8,8192]{1,0:T(8,128)(2,1)S(1)}, u32[]{:S(2)}, u32[]{:S(2)}) collective-permute-start(bf16[8,8192]{1,0:T(8,128)(2,1)S(1)} %add_convert_fusion.1), channel_id=1, source_target_pairs={{0,128},{32,160},{64,192},{96,224},{128,0},{160,32},{192,64},{224,... | collective-permute-start | bytes 393224 | tf_op jit(solution)/shard_map/ppermute | solution.py:24
  230.3 17.4 %collective-permute-start.4 = (bf16[8,8192]{1,0:T(8,128)(2,1)S(1)}, bf16[8,8192]{1,0:T(8,128)(2,1)S(1)}, u32[]{:S(2)}, u32[]{:S(2)}) collective-permute-start(bf16[8,8192]{1,0:T(8,128)(2,1)S(1)} %add_convert_fusion), channel_id=1, source_target_pairs={{0,256},{32,288},{64,320},{96,352},{128,384},{160,416},{192,448},{... | collective-permute-start | bytes 393224 | tf_op jit(solution)/shard_map/ppermute | solution.py:24
  309.4 6.3 %collective-permute-start.5 = (bf16[128,8192]{1,0:T(8,128)(2,1)}, bf16[128,8192]{1,0:T(8,128)(2,1)S(1)}, u32[]{:S(2)}, u32[]{:S(2)}) collective-permute-start(bf16[128,8192]{1,0:T(8,128)(2,1)} %all-gather.5.cloned.1.call-done), channel_id=1, source_target_pairs={{0,1},{1,0},{2,3},{3,2},{4,5},{5,4},{6,7},{7,6},{8,9},{9,8},{10,11... | collective-permute-start | bytes 6291464 | tf_op jit(solution)/shard_map/ppermute | solution.py:29
  315.9 2.2 copy-start.2
  325.3 3.0 collective-permute-start.6
  328.3 5.4 %collective-permute-start.7 = (f32[1,128]{1,0:T(1,128)S(1)}, f32[1,128]{1,0:T(1,128)S(1)}, u32[]{:S(2)}, u32[]{:S(2)}) collective-permute-start(f32[1,128]{1,0:T(1,128)S(1)} %broadcast_add_fusion), channel_id=1, source_target_pairs={{0,2},{2,0},{4,6},{6,4},{8,10},{10,8},{12,14},{14,12},{16,18},{18,... | collective-permute-start | bytes 1544 | tf_op jit(solution)/shard_map/ppermute | solution.py:24
  333.7 6.9 %collective-permute-start.8 = (f32[1,128]{1,0:T(1,128)S(1)}, f32[1,128]{1,0:T(1,128)S(1)}, u32[]{:S(2)}, u32[]{:S(2)}) collective-permute-start(f32[1,128]{1,0:T(1,128)S(1)} %fusion.30), channel_id=1, source_target_pairs={{0,4},{2,6},{4,0},{6,2},{8,12},{10,14},{12,8},{14,10},{16,20},{18,... | collective-permute-start | bytes 1544 | tf_op jit(solution)/shard_map/ppermute | solution.py:24
  340.6 5.4 %collective-permute-start.9 = (f32[1,128]{1,0:T(1,128)S(1)}, f32[1,128]{1,0:T(1,128)S(1)}, u32[]{:S(2)}, u32[]{:S(2)}) collective-permute-start(f32[1,128]{1,0:T(1,128)S(1)} %add.278), channel_id=1, source_target_pairs={{0,8},{2,10},{4,12},{6,14},{8,0},{10,2},{12,4},{14,6},{16,24},{18,... | collective-permute-start | bytes 1544 | tf_op jit(solution)/shard_map/ppermute | solution.py:24
  346.1 6.9 %collective-permute-start.10 = (f32[1,128]{1,0:T(1,128)S(1)}, f32[1,128]{1,0:T(1,128)S(1)}, u32[]{:S(2)}, u32[]{:S(2)}) collective-permute-start(f32[1,128]{1,0:T(1,128)S(1)} %add.279), channel_id=1, source_target_pairs={{0,16},{2,18},{4,20},{6,22},{8,24},{10,26},{12,28},{14,30},{16,0},... | collective-permute-start | bytes 1544 | tf_op jit(solution)/shard_map/ppermute | solution.py:24
  353.0 5.4 %collective-permute-start.11 = (f32[1,128]{1,0:T(1,128)S(1)}, f32[1,128]{1,0:T(1,128)S(1)}, u32[]{:S(2)}, u32[]{:S(2)}) collective-permute-start(f32[1,128]{1,0:T(1,128)S(1)} %add.280), channel_id=1, source_target_pairs={{0,32},{32,0},{64,96},{96,64},{128,160},{160,128},{192,224},{224,1... | collective-permute-start | bytes 1544 | tf_op jit(solution)/shard_map/ppermute | solution.py:24
  358.4 6.3 %collective-permute-start.12 = (f32[1,128]{1,0:T(1,128)S(1)}, f32[1,128]{1,0:T(1,128)S(1)}, u32[]{:S(2)}, u32[]{:S(2)}) collective-permute-start(f32[1,128]{1,0:T(1,128)S(1)} %add.281), channel_id=1, source_target_pairs={{0,64},{32,96},{64,0},{96,32},{128,192},{160,224},{192,128},{224,1... | collective-permute-start | bytes 1544 | tf_op jit(solution)/shard_map/ppermute | solution.py:24
  364.7 9.3 %collective-permute-start.13 = (f32[1,128]{1,0:T(1,128)S(1)}, f32[1,128]{1,0:T(1,128)S(1)}, u32[]{:S(2)}, u32[]{:S(2)}) collective-permute-start(f32[1,128]{1,0:T(1,128)S(1)} %add.282), channel_id=1, source_target_pairs={{0,128},{32,160},{64,192},{96,224},{128,0},{160,32},{192,64},{224,... | collective-permute-start | bytes 1544 | tf_op jit(solution)/shard_map/ppermute | solution.py:24
  374.1 14.3 %collective-permute-start.14 = (f32[1,128]{1,0:T(1,128)S(1)}, f32[1,128]{1,0:T(1,128)S(1)}, u32[]{:S(2)}, u32[]{:S(2)}) collective-permute-start(f32[1,128]{1,0:T(1,128)S(1)} %add.283), channel_id=1, source_target_pairs={{0,256},{32,288},{64,320},{96,352},{128,384},{160,416},{192,448},{... | collective-permute-start | bytes 1544 | tf_op jit(solution)/shard_map/ppermute | solution.py:24
Sparse Core Ops, SparseCore 0:
  11.0 64.3 all-gather.2
  93.4 104.5 reduce-scatter.1
  249.5 59.8 all-gather.4

commit v3 on v1

--- a/solution.py
+++ b/solution.py
@@ -1,5 +1,6 @@
 import jax
 import jax.numpy as jnp
+import numpy as np
 from jax import lax
 from jax.sharding import PartitionSpec as P
 
@@ -20,6 +21,35 @@
     return acc
 
 
+LAT_MASKS = (1, 2, 6, 8, 24)
+
+
+def logical_rank(r):
+    b = [(r >> i) & 1 for i in range(5)]
+    return (b[0] << 4) | ((b[1] ^ b[2]) << 3) | (b[2] << 2) | ((b[3] ^ b[4]) << 1) | b[4]
+
+
+def lat_rank_of(p):
+    l0, l1, l2, l3, l4 = [(p >> i) & 1 for i in range(5)]
+    return l4 | ((l3 ^ l2) << 1) | (l2 << 2) | ((l1 ^ l0) << 3) | (l0 << 4)
+
+
+def masked_pairs(n, mask):
+    return [(i, i ^ mask) for i in range(n)]
+
+
+def halving_scatter(x, rank, n):
+    me = logical_rank(rank)
+    acc = x.reshape((n,) + x.shape[1:])
+    for j, mask in enumerate(LAT_MASKS):
+        bit = (me >> (4 - j)) & 1
+        acc = acc.reshape((2, acc.shape[0] // 2) + acc.shape[1:])
+        kept = lax.dynamic_index_in_dim(acc, bit, 0, keepdims=False)
+        sent = lax.dynamic_index_in_dim(acc, 1 - bit, 0, keepdims=False).astype(jnp.bfloat16)
+        acc = kept.astype(jnp.float32) + lax.ppermute(sent, "lat", masked_pairs(n, mask)).astype(jnp.float32)
+    return acc[0]
+
+
 def body(stream, batch_index, weight, enc_bias, dec_bias):
     own_rows = stream.shape[0]
     n_lat = lax.axis_size("lat")
@@ -36,14 +66,12 @@
     active = (jax.nn.softplus(sharpness * preact) / sharpness).astype(jnp.bfloat16)
     first_row = rank_lat * own_rows
     own_batch = lax.dynamic_slice_in_dim(batch, first_row, own_rows, 0)
-    block_recon = lax.psum_scatter(
-        lax.dot_general(
-            active, weight, (((1,), (1,)), ((), ())), preferred_element_type=jnp.float32
-        ).astype(jnp.bfloat16),
-        "lat",
-        scatter_dimension=0,
-        tiled=True,
-    )
+    order = np.array([lat_rank_of(p) for p in range(n_lat)], dtype=np.int32)
+    active_log = jnp.take(active.reshape(n_lat, own_rows, -1), order, axis=0).reshape(active.shape)
+    partial = lax.dot_general(
+        active_log, weight, (((1,), (1,)), ((), ())), preferred_element_type=jnp.float32
+    ).astype(jnp.bfloat16)
+    block_recon = halving_scatter(partial.reshape(n_lat, own_rows, -1), rank_lat, n_lat)
     recon = butterfly_sum(block_recon.astype(jnp.float32), "grp", n_grp, jnp.bfloat16)
     error_own = recon + dec_bias - own_batch.astype(jnp.float32)
     grad_own = (2.0 * error_own).astype(jnp.bfloat16)
@@ -63,7 +91,8 @@
     bias_raw = jnp.sum(grad_pre, axis=0)
     local_squares = jnp.sum(grad_raw * grad_raw) + jnp.sum(bias_raw * bias_raw)
     squares = jnp.broadcast_to(local_squares, (1, 128))
-    squares = butterfly_sum(squares, "lat", n_lat, jnp.float32)
+    for mask in LAT_MASKS:
+        squares = squares + lax.ppermute(squares, "lat", masked_pairs(n_lat, mask))
     total_squares = butterfly_sum(squares, "grp", n_grp, jnp.float32)[0, 0]
     entries = (weight.shape[0] + 1) * weight.shape[1] * n_lat * n_grp
     factor = jnp.minimum(1.0, 1.0 / jnp.sqrt(total_squares / entries + epsilon))

time: 390 us -> 364 us (0.933)
  waiting for transfers between devices: 278 us -> 224 us
  starting transfers between devices: 69.2 us -> 81.5 us
  local copies, waits for them, and re-layouts: 2.03 us -> 11.2 us
  other arithmetic: 7.54 us -> 14.7 us
    reduce_scatter x1 -> x0, waiting for transfers between devices: 105 us -> none  [body(): lax.psum_scatter(lax.dot_general(active, weight, (((1,), (1,)), ((), ()))...]
    ppermute x0 -> x10, waiting for transfers between devices: none -> 70.1 us  [the longest x5 54.9 us: halving_scatter(): lax.ppermute(sent, 'lat', masked_pairs(n, mask)).astype(jnp.float32)]
    ppermute x0 -> x10, starting transfers between devices: none -> 23.9 us  [the longest x5 12 us: halving_scatter(): lax.ppermute(sent, 'lat', masked_pairs(n, mask)).astype(jnp.float32)]
    ppermute x13 -> x8, waiting for transfers between devices: 42.6 us -> 26.1 us  [butterfly_sum(): lax.ppermute(sent, axis, xor_pairs(n, bit)).astype(jnp.float32)]
    ppermute x13 -> x8, starting transfers between devices: 69 us -> 57.6 us  [butterfly_sum(): lax.ppermute(sent, axis, xor_pairs(n, bit)).astype(jnp.float32)]
    add x0 -> x9, other arithmetic: none -> 6.37 us  [the longest x4 6.35 us: halving_scatter(): kept.astype(jnp.float32)]
    unnamed x12 -> x22, local copies, waits for them, and re-layouts: 2.03 us -> 8.18 us
  transfers between devices with their start and end apart: 16 -> 20, of which waited for: 16 -> 20; matrix products, arithmetic and copies ran while one was open for 0% -> 0% of each run, Pallas kernels for 0% -> 0%
where the time goes in v3:
time: 364 us; the launch traced here: 363 us
  waiting for transfers between devices  224 us (62%)
  starting transfers between devices  81.5 us (22%)
  between operations  15.8 us (4%)
  matrix products  15.5 us (4%)
  other arithmetic  14.7 us (4%)
  local copies, waits for them, and re-layouts  11.2 us (3%)
    all_gather x1, waiting for transfers between devices, body(): gathered = lax.all_gather(stream, 'lat', axis=0, tiled=True)  68 us
    all_gather x1, waiting for transfers between devices, body(): grad_rows = lax.all_gather(grad_own, 'lat', axis=0, tiled=True)  59.2 us
    ppermute x8, starting transfers between devices, butterfly_sum(): lax.ppermute(sent, axis, xor_pairs(n, bit)).astype(jnp.float32)  57.6 us
    ppermute x5, waiting for transfers between devices, halving_scatter(): lax.ppermute(sent, 'lat', masked_pairs(n, mask)).astype(jnp.float32)  54.9 us
    ppermute x8, waiting for transfers between devices, butterfly_sum(): lax.ppermute(sent, axis, xor_pairs(n, bit)).astype(jnp.float32)  26.1 us
    ppermute x5, waiting for transfers between devices, body(): squares = squares + lax.ppermute(squares, 'lat', masked_pairs(n_lat, mask))  15.2 us
    ppermute x5, starting transfers between devices, halving_scatter(): lax.ppermute(sent, 'lat', masked_pairs(n, mask)).astype(jnp.float32)  12 us
    ppermute x5, starting transfers between devices, body(): squares = squares + lax.ppermute(squares, 'lat', masked_pairs(n_lat, mask))  11.9 us
  transfers between devices with their start and end apart: 20, of which 20 were waited for; matrix products, arithmetic and copies ran while one was open for 0% of the time, Pallas kernels for 0%

profile of v3, /device:TPU:6, one launch (start us, length us, event | category | flops | bytes accessed | tf_op | source)
XLA Modules:
  0.0 362.9 jit_solution(13006634283891032807)
XLA Ops:
  8.6 68.0 %all-gather.3.cloned.1.call-done = bf16[256,8192]{1,0:T(8,128)(2,1)} async-done(((bf16[8,8192]{1,0:T(8,128)(2,1)}), bf16[256,8192]{1,0:T(8,128)(2,1)}) %all-gather.3.cloned.1.call-update) | async-done | bytes 4194320 | tf_op jit(solution)/shard_map/all_gather | solution.py:58
  76.6 3.5 convolution_convert_fusion.1
  91.0 4.2 %collective-permute-done = bf16[16,8,8192]{2,1,0:T(8,128)(2,1)} collective-permute-done((bf16[16,8,8192]{2,1,0:T(8,128)(2,1)}, bf16[16,8,8192]{2,1,0:T(8,128)(2,1)}, u32[]{:S(2)}, u32[]{:S(2)}) %collective-permute-start) | collective-permute-done | bytes 2097184 | tf_op jit(solution)/shard_map/ppermute | solution.py:49
  102.4 25.0 %collective-permute-done.1 = bf16[8,8,8192]{2,1,0:T(8,128)(2,1)} collective-permute-done((bf16[8,8,8192]{2,1,0:T(8,128)(2,1)S(1)}, bf16[8,8,8192]{2,1,0:T(8,128)(2,1)}, u32[]{:S(2)}, u32[]{:S(2)}) %collective-permute-start.1) | collective-permute-done | bytes 1048608 | tf_op jit(solution)/shard_map/ppermute | solution.py:49
  133.7 13.6 %collective-permute-done.2 = bf16[4,8,8192]{2,1,0:T(8,128)(2,1)} collective-permute-done((bf16[4,8,8192]{2,1,0:T(8,128)(2,1)S(1)}, bf16[4,8,8192]{2,1,0:T(8,128)(2,1)}, u32[]{:S(2)}, u32[]{:S(2)}) %collective-permute-start.2) | collective-permute-done | bytes 524320 | tf_op jit(solution)/shard_map/ppermute | solution.py:49
  151.5 6.9 %collective-permute-done.3 = bf16[2,8,8192]{2,1,0:T(8,128)(2,1)S(1)} collective-permute-done((bf16[2,8,8192]{2,1,0:T(8,128)(2,1)}, bf16[2,8,8192]{2,1,0:T(8,128)(2,1)S(1)}, u32[]{:S(2)}, u32[]{:S(2)}) %collective-permute-start.3) | collective-permute-done | bytes 262176 | tf_op jit(solution)/shard_map/ppermute | solution.py:49
  162.1 5.2 %collective-permute-done.4 = bf16[1,8,8192]{2,1,0:T(8,128)(2,1)S(1)} collective-permute-done((bf16[1,8,8192]{2,1,0:T(8,128)(2,1)S(1)}, bf16[1,8,8192]{2,1,0:T(8,128)(2,1)S(1)}, u32[]{:S(2)}, u32[]{:S(2)}) %collective-permute-start.4) | collective-permute-done | bytes 131104 | tf_op jit(solution)/shard_map/ppermute | solution.py:49
  168.3 3.5 collective-permute-start.5
  175.2 4.7 %collective-permute-start.6 = (bf16[8,8192]{1,0:T(8,128)(2,1)S(1)}, bf16[8,8192]{1,0:T(8,128)(2,1)S(1)}, u32[]{:S(2)}, u32[]{:S(2)}) collective-permute-start(bf16[8,8192]{1,0:T(8,128)(2,1)S(1)} %add_convert_fusion.2), channel_id=1, source_target_pairs={{0,64},{32,96},{64,0},{96,32},{128,192},{160,224},{192,128},{224,1... | collective-permute-start | bytes 393224 | tf_op jit(solution)/shard_map/ppermute | solution.py:20
  179.9 4.4 %collective-permute-done.6 = bf16[8,8192]{1,0:T(8,128)(2,1)S(1)} collective-permute-done((bf16[8,8192]{1,0:T(8,128)(2,1)S(1)}, bf16[8,8192]{1,0:T(8,128)(2,1)S(1)}, u32[]{:S(2)}, u32[]{:S(2)}) %collective-permute-start.6) | collective-permute-done | bytes 131104 | tf_op jit(solution)/shard_map/ppermute | solution.py:20
  184.4 8.1 %collective-permute-start.7 = (bf16[8,8192]{1,0:T(8,128)(2,1)S(1)}, bf16[8,8192]{1,0:T(8,128)(2,1)S(1)}, u32[]{:S(2)}, u32[]{:S(2)}) collective-permute-start(bf16[8,8192]{1,0:T(8,128)(2,1)S(1)} %add_convert_fusion.1), channel_id=1, source_target_pairs={{0,128},{32,160},{64,192},{96,224},{128,0},{160,32},{192,64},{224,... | collective-permute-start | bytes 393224 | tf_op jit(solution)/shard_map/ppermute | solution.py:20
  192.4 7.1 %collective-permute-done.7 = bf16[8,8192]{1,0:T(8,128)(2,1)S(1)} collective-permute-done((bf16[8,8192]{1,0:T(8,128)(2,1)S(1)}, bf16[8,8192]{1,0:T(8,128)(2,1)S(1)}, u32[]{:S(2)}, u32[]{:S(2)}) %collective-permute-start.7) | collective-permute-done | bytes 131104 | tf_op jit(solution)/shard_map/ppermute | solution.py:20
  199.5 13.0 %collective-permute-start.8 = (bf16[8,8192]{1,0:T(8,128)(2,1)S(1)}, bf16[8,8192]{1,0:T(8,128)(2,1)S(1)}, u32[]{:S(2)}, u32[]{:S(2)}) collective-permute-start(bf16[8,8192]{1,0:T(8,128)(2,1)S(1)} %add_convert_fusion), channel_id=1, source_target_pairs={{0,256},{32,288},{64,320},{96,352},{128,384},{160,416},{192,448},{... | collective-permute-start | bytes 393224 | tf_op jit(solution)/shard_map/ppermute | solution.py:20
  212.5 4.2 %collective-permute-done.8 = bf16[8,8192]{1,0:T(8,128)(2,1)S(1)} collective-permute-done((bf16[8,8192]{1,0:T(8,128)(2,1)S(1)}, bf16[8,8192]{1,0:T(8,128)(2,1)S(1)}, u32[]{:S(2)}, u32[]{:S(2)}) %collective-permute-start.8) | collective-permute-done | bytes 131104 | tf_op jit(solution)/shard_map/ppermute | solution.py:20
  218.5 59.2 %all-gather.5.cloned.1.call-done = bf16[256,8192]{1,0:T(8,128)(2,1)} async-done(((bf16[8,8192]{1,0:T(8,128)(2,1)}), bf16[256,8192]{1,0:T(8,128)(2,1)}) %all-gather.5.cloned.1.call-update) | async-done | bytes 4194320 | tf_op jit(solution)/shard_map/all_gather | solution.py:78
  277.7 3.6 fusion.17
  283.5 4.4 %multiply_reduce_fusion = (f32[]{:T(128)}, f32[8192,128]{1,0:T(8,128)}) fusion(f32[8192,128]{1,0:T(8,128)S(1)} %fusion, bf16[256,8192]{1,0:T(8,128)(2,1)S(1)} %copy-done.5, f32[256,128]{1,0:T(8,128)S(1)} %fusion.4), kind=kOutput, calls=%fused_computation.7 | convolution fusion | flops 540278784 | bytes 12713988 | tf_op jit(solution)/shard_map/dot_general | solution.py:80
  300.4 3.8 %collective-permute-done.11 = f32[1,128]{1,0:T(1,128)S(1)} collective-permute-done((f32[1,128]{1,0:T(1,128)S(1)}, f32[1,128]{1,0:T(1,128)S(1)}, u32[]{:S(2)}, u32[]{:S(2)}) %collective-permute-start.11) | collective-permute-done | bytes 544 | tf_op jit(solution)/shard_map/ppermute | solution.py:95
  306.2 3.5 collective-permute-done.12
  312.5 3.8 %collective-permute-done.13 = f32[1,128]{1,0:T(1,128)S(1)} collective-permute-done((f32[1,128]{1,0:T(1,128)S(1)}, f32[1,128]{1,0:T(1,128)S(1)}, u32[]{:S(2)}, u32[]{:S(2)}) %collective-permute-start.13) | collective-permute-done | bytes 544 | tf_op jit(solution)/shard_map/ppermute | solution.py:95
  321.7 4.4 %collective-permute-start.15 = (f32[1,128]{1,0:T(1,128)S(1)}, f32[1,128]{1,0:T(1,128)S(1)}, u32[]{:S(2)}, u32[]{:S(2)}) collective-permute-start(f32[1,128]{1,0:T(1,128)S(1)} %add.181), channel_id=1, source_target_pairs={{0,64},{32,96},{64,0},{96,32},{128,192},{160,224},{192,128},{224,1... | collective-permute-start | bytes 1544 | tf_op jit(solution)/shard_map/ppermute | solution.py:20
  328.1 7.6 %collective-permute-start.16 = (f32[1,128]{1,0:T(1,128)S(1)}, f32[1,128]{1,0:T(1,128)S(1)}, u32[]{:S(2)}, u32[]{:S(2)}) collective-permute-start(f32[1,128]{1,0:T(1,128)S(1)} %add.182), channel_id=1, source_target_pairs={{0,128},{32,160},{64,192},{96,224},{128,0},{160,32},{192,64},{224,... | collective-permute-start | bytes 1544 | tf_op jit(solution)/shard_map/ppermute | solution.py:20
  337.4 12.8 %collective-permute-start.17 = (f32[1,128]{1,0:T(1,128)S(1)}, f32[1,128]{1,0:T(1,128)S(1)}, u32[]{:S(2)}, u32[]{:S(2)}) collective-permute-start(f32[1,128]{1,0:T(1,128)S(1)} %add.183), channel_id=1, source_target_pairs={{0,256},{32,288},{64,320},{96,352},{128,384},{160,416},{192,448},{... | collective-permute-start | bytes 1544 | tf_op jit(solution)/shard_map/ppermute | solution.py:20
  352.3 3.7 %multiply_convert_fusion = bf16[8192,128]{1,0:T(8,128)(2,1)} fusion(f32[8192,128]{1,0:T(8,128)} %get-tuple-element.6, f32[]{:T(128)} %bitcast.15), kind=kLoop, calls=%fused_computation.6 | loop fusion | flops 2097152 | bytes 6291460 | tf_op jit(solution)/shard_map/convert_element_type | solution.py:100
  (76 shorter events, 68.8 us)
Async XLA Ops:
  7.2 74.9 %copy-start = (bf16[8192,128]{1,0:T(8,128)(2,1)S(1)}, bf16[8192,128]{1,0:T(8,128)(2,1)}, u32[]{:S(2)}) copy-start(bf16[8192,128]{1,0:T(8,128)(2,1)} %param.8) | copy-start | bytes 6291460
  7.2 69.4 %all-gather.3.cloned.1.call-start = ((), (), s32[]{:S(2)}) async-start(), calls=%async_computation | async-start | bytes 4325376 | tf_op jit(solution)/shard_map/all_gather | solution.py:58
  7.9 269.8 %all-gather.5.cloned.1.call-start = ((), (), s32[]{:S(2)}) async-start(), calls=%async_computation.1 | async-start | bytes 4325376 | tf_op jit(solution)/shard_map/all_gather | solution.py:78
  8.6 73.5 %copy-start.8 = (f32[8192]{0:T(1024)S(1)}, f32[8192]{0:T(1024)}, u32[]{:S(2)}) copy-start(f32[8192]{0:T(1024)} %param.10) | copy-start | bytes 98308
  8.6 73.5 %copy-start.10 = (f32[128]{0:T(128)S(1)}, f32[128]{0:T(128)}, u32[]{:S(2)}) copy-start(f32[128]{0:T(128)} %param.9) | copy-start | bytes 1540
  88.8 6.4 %collective-permute-start = (bf16[16,8,8192]{2,1,0:T(8,128)(2,1)}, bf16[16,8,8192]{2,1,0:T(8,128)(2,1)}, u32[]{:S(2)}, u32[]{:S(2)}) collective-permute-start(bf16[16,8,8192]{2,1,0:T(8,128)(2,1)} %dynamic-slice_bitcast_fusion), channel_id=1, source_target_pairs={{0,1},{1,0},{2,3},{3,2},{4,5},{5,4},{6,7},{7,6},{8,9},{9,8},{10,11... | collective-permute-start | bytes 6291464 | tf_op jit(solution)/shard_map/ppermute | solution.py:49
  100.1 27.3 %collective-permute-start.1 = (bf16[8,8,8192]{2,1,0:T(8,128)(2,1)S(1)}, bf16[8,8,8192]{2,1,0:T(8,128)(2,1)}, u32[]{:S(2)}, u32[]{:S(2)}) collective-permute-start(bf16[8,8,8192]{2,1,0:T(8,128)(2,1)S(1)} %fusion.5), channel_id=1, source_target_pairs={{0,2},{1,3},{2,0},{3,1},{4,6},{5,7},{6,4},{7,5},{8,10},{9,11},{10,... | collective-permute-start | bytes 3145736 | tf_op jit(solution)/shard_map/ppermute | solution.py:49
  130.9 16.5 %collective-permute-start.2 = (bf16[4,8,8192]{2,1,0:T(8,128)(2,1)S(1)}, bf16[4,8,8192]{2,1,0:T(8,128)(2,1)}, u32[]{:S(2)}, u32[]{:S(2)}) collective-permute-start(bf16[4,8,8192]{2,1,0:T(8,128)(2,1)S(1)} %fusion.6), channel_id=1, source_target_pairs={{0,6},{1,7},{2,4},{3,5},{4,2},{5,3},{6,0},{7,1},{8,14},{9,15},{10,... | collective-permute-start | bytes 1572872 | tf_op jit(solution)/shard_map/ppermute | solution.py:49
  149.5 8.8 %collective-permute-start.3 = (bf16[2,8,8192]{2,1,0:T(8,128)(2,1)}, bf16[2,8,8192]{2,1,0:T(8,128)(2,1)S(1)}, u32[]{:S(2)}, u32[]{:S(2)}) collective-permute-start(bf16[2,8,8192]{2,1,0:T(8,128)(2,1)} %fusion.7), channel_id=1, source_target_pairs={{0,8},{1,9},{2,10},{3,11},{4,12},{5,13},{6,14},{7,15},{8,0},{9,1},... | collective-permute-start | bytes 786440 | tf_op jit(solution)/shard_map/ppermute | solution.py:49
  159.2 8.1 %collective-permute-start.4 = (bf16[1,8,8192]{2,1,0:T(8,128)(2,1)S(1)}, bf16[1,8,8192]{2,1,0:T(8,128)(2,1)S(1)}, u32[]{:S(2)}, u32[]{:S(2)}) collective-permute-start(bf16[1,8,8192]{2,1,0:T(8,128)(2,1)S(1)} %dynamic-slice_convert_fusion.3), channel_id=1, source_target_pairs={{0,24},{1,25},{2,26},{3,27},{4,28},{5,29},{6,30},{7,31},{8,16},{9,... | collective-permute-start | bytes 393224 | tf_op jit(solution)/shard_map/ppermute | solution.py:49
  168.3 113.0 %copy-start.9 = (f32[8192]{0:T(1024)S(1)}, f32[8192]{0:T(1024)}, u32[]{:S(2)}) copy-start(f32[8192]{0:T(1024)} %param.10) | copy-start | bytes 98308
  168.3 6.9 %collective-permute-start.5 = (bf16[8,8192]{1,0:T(8,128)(2,1)S(1)}, bf16[8,8192]{1,0:T(8,128)(2,1)S(1)}, u32[]{:S(2)}, u32[]{:S(2)}) collective-permute-start(bf16[8,8192]{1,0:T(8,128)(2,1)S(1)} %fusion.9), channel_id=1, source_target_pairs={{0,32},{32,0},{64,96},{96,64},{128,160},{160,128},{192,224},{224,1... | collective-permute-start | bytes 393224 | tf_op jit(solution)/shard_map/ppermute | solution.py:20
  175.2 9.2 %collective-permute-start.6 = (bf16[8,8192]{1,0:T(8,128)(2,1)S(1)}, bf16[8,8192]{1,0:T(8,128)(2,1)S(1)}, u32[]{:S(2)}, u32[]{:S(2)}) collective-permute-start(bf16[8,8192]{1,0:T(8,128)(2,1)S(1)} %add_convert_fusion.2), channel_id=1, source_target_pairs={{0,64},{32,96},{64,0},{96,32},{128,192},{160,224},{192,128},{224,1... | collective-permute-start | bytes 393224 | tf_op jit(solution)/shard_map/ppermute | solution.py:20
  184.4 15.1 %collective-permute-start.7 = (bf16[8,8192]{1,0:T(8,128)(2,1)S(1)}, bf16[8,8192]{1,0:T(8,128)(2,1)S(1)}, u32[]{:S(2)}, u32[]{:S(2)}) collective-permute-start(bf16[8,8192]{1,0:T(8,128)(2,1)S(1)} %add_convert_fusion.1), channel_id=1, source_target_pairs={{0,128},{32,160},{64,192},{96,224},{128,0},{160,32},{192,64},{224,... | collective-permute-start | bytes 393224 | tf_op jit(solution)/shard_map/ppermute | solution.py:20
  199.5 17.2 %collective-permute-start.8 = (bf16[8,8192]{1,0:T(8,128)(2,1)S(1)}, bf16[8,8192]{1,0:T(8,128)(2,1)S(1)}, u32[]{:S(2)}, u32[]{:S(2)}) collective-permute-start(bf16[8,8192]{1,0:T(8,128)(2,1)S(1)} %add_convert_fusion), channel_id=1, source_target_pairs={{0,256},{32,288},{64,320},{96,352},{128,384},{160,416},{192,448},{... | collective-permute-start | bytes 393224 | tf_op jit(solution)/shard_map/ppermute | solution.py:20
  289.2 3.0 collective-permute-start.9
  292.2 5.4 %collective-permute-start.10 = (f32[1,128]{1,0:T(1,128)S(1)}, f32[1,128]{1,0:T(1,128)S(1)}, u32[]{:S(2)}, u32[]{:S(2)}) collective-permute-start(f32[1,128]{1,0:T(1,128)S(1)} %broadcast_add_fusion), channel_id=1, source_target_pairs={{0,2},{1,3},{2,0},{3,1},{4,6},{5,7},{6,4},{7,5},{8,10},{9,11},{10,... | collective-permute-start | bytes 1544 | tf_op jit(solution)/shard_map/ppermute | solution.py:95
  297.6 6.6 %collective-permute-start.11 = (f32[1,128]{1,0:T(1,128)S(1)}, f32[1,128]{1,0:T(1,128)S(1)}, u32[]{:S(2)}, u32[]{:S(2)}) collective-permute-start(f32[1,128]{1,0:T(1,128)S(1)} %fusion.25), channel_id=1, source_target_pairs={{0,6},{1,7},{2,4},{3,5},{4,2},{5,3},{6,0},{7,1},{8,14},{9,15},{10,... | collective-permute-start | bytes 1544 | tf_op jit(solution)/shard_map/ppermute | solution.py:95
  304.3 5.4 %collective-permute-start.12 = (f32[1,128]{1,0:T(1,128)S(1)}, f32[1,128]{1,0:T(1,128)S(1)}, u32[]{:S(2)}, u32[]{:S(2)}) collective-permute-start(f32[1,128]{1,0:T(1,128)S(1)} %add.178), channel_id=1, source_target_pairs={{0,8},{1,9},{2,10},{3,11},{4,12},{5,13},{6,14},{7,15},{8,0},{9,1},... | collective-permute-start | bytes 1544 | tf_op jit(solution)/shard_map/ppermute | solution.py:95
  309.7 6.6 %collective-permute-start.13 = (f32[1,128]{1,0:T(1,128)S(1)}, f32[1,128]{1,0:T(1,128)S(1)}, u32[]{:S(2)}, u32[]{:S(2)}) collective-permute-start(f32[1,128]{1,0:T(1,128)S(1)} %add.179), channel_id=1, source_target_pairs={{0,24},{1,25},{2,26},{3,27},{4,28},{5,29},{6,30},{7,31},{8,16},{9,... | collective-permute-start | bytes 1544 | tf_op jit(solution)/shard_map/ppermute | solution.py:95
  316.3 5.4 %collective-permute-start.14 = (f32[1,128]{1,0:T(1,128)S(1)}, f32[1,128]{1,0:T(1,128)S(1)}, u32[]{:S(2)}, u32[]{:S(2)}) collective-permute-start(f32[1,128]{1,0:T(1,128)S(1)} %add.180), channel_id=1, source_target_pairs={{0,32},{32,0},{64,96},{96,64},{128,160},{160,128},{192,224},{224,1... | collective-permute-start | bytes 1544 | tf_op jit(solution)/shard_map/ppermute | solution.py:20
  321.7 6.3 %collective-permute-start.15 = (f32[1,128]{1,0:T(1,128)S(1)}, f32[1,128]{1,0:T(1,128)S(1)}, u32[]{:S(2)}, u32[]{:S(2)}) collective-permute-start(f32[1,128]{1,0:T(1,128)S(1)} %add.181), channel_id=1, source_target_pairs={{0,64},{32,96},{64,0},{96,32},{128,192},{160,224},{192,128},{224,1... | collective-permute-start | bytes 1544 | tf_op jit(solution)/shard_map/ppermute | solution.py:20
  328.1 9.3 %collective-permute-start.16 = (f32[1,128]{1,0:T(1,128)S(1)}, f32[1,128]{1,0:T(1,128)S(1)}, u32[]{:S(2)}, u32[]{:S(2)}) collective-permute-start(f32[1,128]{1,0:T(1,128)S(1)} %add.182), channel_id=1, source_target_pairs={{0,128},{32,160},{64,192},{96,224},{128,0},{160,32},{192,64},{224,... | collective-permute-start | bytes 1544 | tf_op jit(solution)/shard_map/ppermute | solution.py:20
  337.4 14.3 %collective-permute-start.17 = (f32[1,128]{1,0:T(1,128)S(1)}, f32[1,128]{1,0:T(1,128)S(1)}, u32[]{:S(2)}, u32[]{:S(2)}) collective-permute-start(f32[1,128]{1,0:T(1,128)S(1)} %add.183), channel_id=1, source_target_pairs={{0,256},{32,288},{64,320},{96,352},{128,384},{160,416},{192,448},{... | collective-permute-start | bytes 1544 | tf_op jit(solution)/shard_map/ppermute | solution.py:20
  (7 other events, 13.9 us)
Sparse Core Ops, SparseCore 0:
  11.1 65.4 all-gather.2
  218.6 59.0 all-gather.4

commit v4 on v3

--- a/solution.py
+++ b/solution.py
@@ -21,27 +21,57 @@
     return acc
 
 
-LAT_MASKS = (1, 2, 6, 8, 24)
+CORE, X1, X3, Y1, Y3 = 1, 2, 6, 8, 24
+LAT_MASKS = (CORE, X1, X3, Y1, Y3)
+ORDER_X_FIRST = (CORE, X1, X3, Y1, Y3)
+ORDER_Y_FIRST = (CORE, Y1, Y3, X1, X3)
 
 
-def logical_rank(r):
-    b = [(r >> i) & 1 for i in range(5)]
-    return (b[0] << 4) | ((b[1] ^ b[2]) << 3) | (b[2] << 2) | ((b[3] ^ b[4]) << 1) | b[4]
+def logical_rank(r, masks):
+    coeffs = basis_coefficients(masks)
+    out = 0
+    for bit in range(5):
+        rb = (r >> bit) & 1
+        for j in range(5):
+            if (coeffs[bit] >> j) & 1:
+                out = out ^ (rb << (4 - j))
+    return out
 
 
-def lat_rank_of(p):
-    l0, l1, l2, l3, l4 = [(p >> i) & 1 for i in range(5)]
-    return l4 | ((l3 ^ l2) << 1) | (l2 << 2) | ((l1 ^ l0) << 3) | (l0 << 4)
+def basis_coefficients(masks):
+    rows = [(m, 1 << j) for j, m in enumerate(masks)]
+    result = []
+    for bit in range(5):
+        target = 1 << bit
+        found = None
+        for combo in range(1, 32):
+            v = 0
+            for j in range(5):
+                if (combo >> j) & 1:
+                    v ^= rows[j][0]
+            if v == target:
+                found = combo
+                break
+        result.append(found)
+    return result
+
+
+def lat_rank_of(p, masks):
+    r = 0
+    for j, m in enumerate(masks):
+        if (p >> (4 - j)) & 1:
+            r ^= m
+    return r
 
 
 def masked_pairs(n, mask):
     return [(i, i ^ mask) for i in range(n)]
 
 
-def halving_scatter(x, rank, n):
-    me = logical_rank(rank)
-    acc = x.reshape((n,) + x.shape[1:])
-    for j, mask in enumerate(LAT_MASKS):
+def halving_scatter(x, rank, n, masks):
+    me = logical_rank(rank, masks)
+    acc = x
+    for j, mask in enumerate(masks):
         bit = (me >> (4 - j)) & 1
         acc = acc.reshape((2, acc.shape[0] // 2) + acc.shape[1:])
         kept = lax.dynamic_index_in_dim(acc, bit, 0, keepdims=False)
@@ -66,12 +96,17 @@
     active = (jax.nn.softplus(sharpness * preact) / sharpness).astype(jnp.bfloat16)
     first_row = rank_lat * own_rows
     own_batch = lax.dynamic_slice_in_dim(batch, first_row, own_rows, 0)
-    order = np.array([lat_rank_of(p) for p in range(n_lat)], dtype=np.int32)
-    active_log = jnp.take(active.reshape(n_lat, own_rows, -1), order, axis=0).reshape(active.shape)
-    partial = lax.dot_general(
-        active_log, weight, (((1,), (1,)), ((), ())), preferred_element_type=jnp.float32
-    ).astype(jnp.bfloat16)
-    block_recon = halving_scatter(partial.reshape(n_lat, own_rows, -1), rank_lat, n_lat)
+    blocks = active.reshape(n_lat, own_rows, -1)
+    cols = weight.shape[0] // 2
+    halves = []
+    for k, masks in enumerate((ORDER_X_FIRST, ORDER_Y_FIRST)):
+        order = np.array([lat_rank_of(p, masks) for p in range(n_lat)], dtype=np.int32)
+        rows = jnp.take(blocks, order, axis=0).reshape(active.shape)
+        part = lax.dot_general(
+            rows, weight[k * cols:(k + 1) * cols], (((1,), (1,)), ((), ())), preferred_element_type=jnp.float32
+        ).astype(jnp.bfloat16)
+        halves.append(halving_scatter(part.reshape(n_lat, own_rows, cols), rank_lat, n_lat, masks))
+    block_recon = jnp.concatenate(halves, axis=1)
     recon = butterfly_sum(block_recon.astype(jnp.float32), "grp", n_grp, jnp.bfloat16)
     error_own = recon + dec_bias - own_batch.astype(jnp.float32)
     grad_own = (2.0 * error_own).astype(jnp.bfloat16)

time: 364 us -> 336 us (0.923)
  waiting for transfers between devices: 224 us -> 192 us
  starting transfers between devices: 81.5 us -> 96.2 us
  local copies, waits for them, and re-layouts: 11.2 us -> 4.72 us
  other arithmetic: 14.7 us -> 8.3 us
    ppermute x5 -> x10, waiting for transfers between devices: 54.9 us -> 19.3 us  [halving_scatter(): lax.ppermute(sent, 'lat', masked_pairs(n, mask)).astype(jnp.float32)]
    ppermute x5 -> x10, starting transfers between devices: 12 us -> 28.1 us  [halving_scatter(): lax.ppermute(sent, 'lat', masked_pairs(n, mask)).astype(jnp.float32)]
    unnamed x22 -> x16, local copies, waits for them, and re-layouts: 8.18 us -> 2.1 us
    add x4 -> x8, other arithmetic: 6.35 us -> 0.86 us  [halving_scatter(): kept.astype(jnp.float32)]
  transfers between devices with their start and end apart: 20 -> 25, of which waited for: 20 -> 21; matrix products, arithmetic and copies ran while one was open for 0% -> 1% of each run, Pallas kernels for 0% -> 0%
where the time goes in v4:
time: 336 us; the launch traced here: 335 us
  waiting for transfers between devices  192 us (57%)
  starting transfers between devices  96.2 us (29%)
  matrix products  18.1 us (5%)
  between operations  16 us (5%)
  other arithmetic  8.3 us (2%)
  local copies, waits for them, and re-layouts  4.72 us (1%)
    all_gather x1, waiting for transfers between devices, body(): gathered = lax.all_gather(stream, 'lat', axis=0, tiled=True)  68 us
    all_gather x1, waiting for transfers between devices, body(): grad_rows = lax.all_gather(grad_own, 'lat', axis=0, tiled=True)  61.5 us
    ppermute x8, starting transfers between devices, butterfly_sum(): lax.ppermute(sent, axis, xor_pairs(n, bit)).astype(jnp.float32)  56.1 us
    ppermute x10, starting transfers between devices, halving_scatter(): lax.ppermute(sent, 'lat', masked_pairs(n, mask)).astype(jnp.float32)  28.1 us
    ppermute x8, waiting for transfers between devices, butterfly_sum(): lax.ppermute(sent, axis, xor_pairs(n, bit)).astype(jnp.float32)  27.4 us
    ppermute x10, waiting for transfers between devices, halving_scatter(): lax.ppermute(sent, 'lat', masked_pairs(n, mask)).astype(jnp.float32)  19.3 us
    ppermute x5, waiting for transfers between devices, body(): squares = squares + lax.ppermute(squares, 'lat', masked_pairs(n_lat, mask))  15.2 us
    ppermute x5, starting transfers between devices, body(): squares = squares + lax.ppermute(squares, 'lat', masked_pairs(n_lat, mask))  11.9 us
  transfers between devices with their start and end apart: 25, of which 21 were waited for; matrix products, arithmetic and copies ran while one was open for 1% of the time, Pallas kernels for 0%

profile of v4, /device:TPU:6, one launch (start us, length us, event | category | flops | bytes accessed | tf_op | source)
XLA Modules:
  0.0 335.3 jit_solution(7007581744680739737)
XLA Ops:
  8.6 68.0 %all-gather.3.cloned.1.call-done = bf16[256,8192]{1,0:T(8,128)(2,1)} async-done(((bf16[8,8192]{1,0:T(8,128)(2,1)}), bf16[256,8192]{1,0:T(8,128)(2,1)}) %all-gather.3.cloned.1.call-update) | async-done | bytes 4194320 | tf_op jit(solution)/shard_map/all_gather | solution.py:88
  76.6 3.5 %convolution_convert_fusion = bf16[256,8192]{1,0:T(8,128)(2,1)S(1)} fusion(bf16[256,8192]{1,0:T(8,128)(2,1)} %all-gather.3.cloned.1.call-done, s32[256]{0:T(256)} %param.10), kind=kOutput, calls=%fused_computation.2 | convolution fusion | flops 1075904512 | bytes 8389632 | tf_op jit(solution)/shard_map/dot_general | solution.py:93
  99.5 10.9 %collective-permute-done.1 = bf16[8,8,4096]{2,1,0:T(8,128)(2,1)S(1)} collective-permute-done((bf16[8,8,4096]{2,1,0:T(8,128)(2,1)S(1)}, bf16[8,8,4096]{2,1,0:T(8,128)(2,1)S(1)}, u32[]{:S(2)}, u32[]{:S(2)}) %collective-permute-start.1) | collective-permute-done | bytes 524320 | tf_op jit(solution)/shard_map/ppermute | solution.py:79
  113.6 4.4 %collective-permute-start.7 = (bf16[4,8,4096]{2,1,0:T(8,128)(2,1)S(1)}, bf16[4,8,4096]{2,1,0:T(8,128)(2,1)S(1)}, u32[]{:S(2)}, u32[]{:S(2)}) collective-permute-start(bf16[4,8,4096]{2,1,0:T(8,128)(2,1)S(1)} %fusion.10), channel_id=1, source_target_pairs={{0,24},{1,25},{2,26},{3,27},{4,28},{5,29},{6,30},{7,31},{8,16},{9,... | collective-permute-start | bytes 786440 | tf_op jit(solution)/shard_map/ppermute | solution.py:79
  131.2 4.3 %collective-permute-start.9 = (bf16[1,8,4096]{2,1,0:T(8,128)(2,1)S(1)}, bf16[1,8,4096]{2,1,0:T(8,128)(2,1)S(1)}, u32[]{:S(2)}, u32[]{:S(2)}) collective-permute-start(bf16[1,8,4096]{2,1,0:T(8,128)(2,1)S(1)} %dynamic-slice_convert_fusion.6), channel_id=1, source_target_pairs={{0,6},{1,7},{2,4},{3,5},{4,2},{5,3},{6,0},{7,1},{8,14},{9,15},{10,... | collective-permute-start | bytes 196616 | tf_op jit(solution)/shard_map/ppermute | solution.py:79
  138.6 3.5 %collective-permute-start.10 = (bf16[8,8192]{1,0:T(8,128)(2,1)S(1)}, bf16[8,8192]{1,0:T(8,128)(2,1)S(1)}, u32[]{:S(2)}, u32[]{:S(2)}) collective-permute-start(bf16[8,8192]{1,0:T(8,128)(2,1)S(1)} %pad_maximum_fusion), channel_id=1, source_target_pairs={{0,32},{32,0},{64,96},{96,64},{128,160},{160,128},{192,224},{224,1... | collective-permute-start | bytes 393224 | tf_op jit(solution)/shard_map/ppermute | solution.py:20
  142.1 3.4 %collective-permute-done.10 = bf16[8,8192]{1,0:T(8,128)(2,1)S(1)} collective-permute-done((bf16[8,8192]{1,0:T(8,128)(2,1)S(1)}, bf16[8,8192]{1,0:T(8,128)(2,1)S(1)}, u32[]{:S(2)}, u32[]{:S(2)}) %collective-permute-start.10) | collective-permute-done | bytes 131104 | tf_op jit(solution)/shard_map/ppermute | solution.py:20
  145.5 4.7 %collective-permute-start.11 = (bf16[8,8192]{1,0:T(8,128)(2,1)S(1)}, bf16[8,8192]{1,0:T(8,128)(2,1)S(1)}, u32[]{:S(2)}, u32[]{:S(2)}) collective-permute-start(bf16[8,8192]{1,0:T(8,128)(2,1)S(1)} %add_convert_fusion.2), channel_id=1, source_target_pairs={{0,64},{32,96},{64,0},{96,32},{128,192},{160,224},{192,128},{224,1... | collective-permute-start | bytes 393224 | tf_op jit(solution)/shard_map/ppermute | solution.py:20
  150.2 4.5 %collective-permute-done.11 = bf16[8,8192]{1,0:T(8,128)(2,1)S(1)} collective-permute-done((bf16[8,8192]{1,0:T(8,128)(2,1)S(1)}, bf16[8,8192]{1,0:T(8,128)(2,1)S(1)}, u32[]{:S(2)}, u32[]{:S(2)}) %collective-permute-start.11) | collective-permute-done | bytes 131104 | tf_op jit(solution)/shard_map/ppermute | solution.py:20
  154.7 8.1 %collective-permute-start.12 = (bf16[8,8192]{1,0:T(8,128)(2,1)S(1)}, bf16[8,8192]{1,0:T(8,128)(2,1)S(1)}, u32[]{:S(2)}, u32[]{:S(2)}) collective-permute-start(bf16[8,8192]{1,0:T(8,128)(2,1)S(1)} %add_convert_fusion.1), channel_id=1, source_target_pairs={{0,128},{32,160},{64,192},{96,224},{128,0},{160,32},{192,64},{224,... | collective-permute-start | bytes 393224 | tf_op jit(solution)/shard_map/ppermute | solution.py:20
  162.8 7.1 %collective-permute-done.12 = bf16[8,8192]{1,0:T(8,128)(2,1)S(1)} collective-permute-done((bf16[8,8192]{1,0:T(8,128)(2,1)S(1)}, bf16[8,8192]{1,0:T(8,128)(2,1)S(1)}, u32[]{:S(2)}, u32[]{:S(2)}) %collective-permute-start.12) | collective-permute-done | bytes 131104 | tf_op jit(solution)/shard_map/ppermute | solution.py:20
  169.9 11.5 %collective-permute-start.13 = (bf16[8,8192]{1,0:T(8,128)(2,1)S(1)}, bf16[8,8192]{1,0:T(8,128)(2,1)S(1)}, u32[]{:S(2)}, u32[]{:S(2)}) collective-permute-start(bf16[8,8192]{1,0:T(8,128)(2,1)S(1)} %add_convert_fusion), channel_id=1, source_target_pairs={{0,256},{32,288},{64,320},{96,352},{128,384},{160,416},{192,448},{... | collective-permute-start | bytes 393224 | tf_op jit(solution)/shard_map/ppermute | solution.py:20
  181.5 5.4 %collective-permute-done.13 = bf16[8,8192]{1,0:T(8,128)(2,1)S(1)} collective-permute-done((bf16[8,8192]{1,0:T(8,128)(2,1)S(1)}, bf16[8,8192]{1,0:T(8,128)(2,1)S(1)}, u32[]{:S(2)}, u32[]{:S(2)}) %collective-permute-start.13) | collective-permute-done | bytes 131104 | tf_op jit(solution)/shard_map/ppermute | solution.py:20
  188.6 61.5 %all-gather.5.cloned.1.call-done = bf16[256,8192]{1,0:T(8,128)(2,1)} async-done(((bf16[8,8192]{1,0:T(8,128)(2,1)}), bf16[256,8192]{1,0:T(8,128)(2,1)}) %all-gather.5.cloned.1.call-update) | async-done | bytes 4194320 | tf_op jit(solution)/shard_map/all_gather | solution.py:113
  250.1 3.6 %fusion.24 = (f32[128]{0:T(128)S(1)}, bf16[256,128]{1,0:T(8,128)(2,1)S(1)}) fusion(f32[256,128]{1,0:T(8,128)S(1)} %fusion.4, bf16[256,8192]{1,0:T(8,128)(2,1)} %all-gather.5.cloned.1.call-done, bf16[8192,128]{1,0:T(8,128)(2,1)S(1)} %copy-done.4), kind=kOutput, calls=%fused_computation.66 | convolution fusion | flops 537100160 | bytes 6488576 | tf_op jit(solution)/shard_map/dot_general | solution.py:114
  255.9 4.4 %multiply_reduce_fusion = (f32[]{:T(128)}, f32[8192,128]{1,0:T(8,128)}) fusion(f32[8192,128]{1,0:T(8,128)S(1)} %fusion, bf16[256,8192]{1,0:T(8,128)(2,1)S(1)} %copy-done.2, f32[256,128]{1,0:T(8,128)S(1)} %fusion.4), kind=kOutput, calls=%fused_computation.8 | convolution fusion | flops 540278784 | bytes 12713988 | tf_op jit(solution)/shard_map/dot_general | solution.py:115
  272.8 3.8 %collective-permute-done.16 = f32[1,128]{1,0:T(1,128)S(1)} collective-permute-done((f32[1,128]{1,0:T(1,128)S(1)}, f32[1,128]{1,0:T(1,128)S(1)}, u32[]{:S(2)}, u32[]{:S(2)}) %collective-permute-start.16) | collective-permute-done | bytes 544 | tf_op jit(solution)/shard_map/ppermute | solution.py:130
  278.6 3.5 %collective-permute-done.17 = f32[1,128]{1,0:T(1,128)S(1)} collective-permute-done((f32[1,128]{1,0:T(1,128)S(1)}, f32[1,128]{1,0:T(1,128)S(1)}, u32[]{:S(2)}, u32[]{:S(2)}) %collective-permute-start.17) | collective-permute-done | bytes 544 | tf_op jit(solution)/shard_map/ppermute | solution.py:130
  284.9 3.8 %collective-permute-done.18 = f32[1,128]{1,0:T(1,128)S(1)} collective-permute-done((f32[1,128]{1,0:T(1,128)S(1)}, f32[1,128]{1,0:T(1,128)S(1)}, u32[]{:S(2)}, u32[]{:S(2)}) %collective-permute-start.18) | collective-permute-done | bytes 544 | tf_op jit(solution)/shard_map/ppermute | solution.py:130
  288.7 3.5 %collective-permute-start.19 = (f32[1,128]{1,0:T(1,128)S(1)}, f32[1,128]{1,0:T(1,128)S(1)}, u32[]{:S(2)}, u32[]{:S(2)}) collective-permute-start(f32[1,128]{1,0:T(1,128)S(1)} %add.241), channel_id=1, source_target_pairs={{0,32},{32,0},{64,96},{96,64},{128,160},{160,128},{192,224},{224,1... | collective-permute-start | bytes 1544 | tf_op jit(solution)/shard_map/ppermute | solution.py:20
  294.1 4.4 %collective-permute-start.20 = (f32[1,128]{1,0:T(1,128)S(1)}, f32[1,128]{1,0:T(1,128)S(1)}, u32[]{:S(2)}, u32[]{:S(2)}) collective-permute-start(f32[1,128]{1,0:T(1,128)S(1)} %add.242), channel_id=1, source_target_pairs={{0,64},{32,96},{64,0},{96,32},{128,192},{160,224},{192,128},{224,1... | collective-permute-start | bytes 1544 | tf_op jit(solution)/shard_map/ppermute | solution.py:20
  300.5 7.6 %collective-permute-start.21 = (f32[1,128]{1,0:T(1,128)S(1)}, f32[1,128]{1,0:T(1,128)S(1)}, u32[]{:S(2)}, u32[]{:S(2)}) collective-permute-start(f32[1,128]{1,0:T(1,128)S(1)} %add.243), channel_id=1, source_target_pairs={{0,128},{32,160},{64,192},{96,224},{128,0},{160,32},{192,64},{224,... | collective-permute-start | bytes 1544 | tf_op jit(solution)/shard_map/ppermute | solution.py:20
  309.8 12.8 %collective-permute-start.22 = (f32[1,128]{1,0:T(1,128)S(1)}, f32[1,128]{1,0:T(1,128)S(1)}, u32[]{:S(2)}, u32[]{:S(2)}) collective-permute-start(f32[1,128]{1,0:T(1,128)S(1)} %add.244), channel_id=1, source_target_pairs={{0,256},{32,288},{64,320},{96,352},{128,384},{160,416},{192,448},{... | collective-permute-start | bytes 1544 | tf_op jit(solution)/shard_map/ppermute | solution.py:20
  324.7 3.7 %multiply_convert_fusion = bf16[8192,128]{1,0:T(8,128)(2,1)} fusion(f32[8192,128]{1,0:T(8,128)} %get-tuple-element.7, f32[]{:T(128)} %bitcast.29), kind=kLoop, calls=%fused_computation.7 | loop fusion | flops 2097152 | bytes 6291460 | tf_op jit(solution)/shard_map/convert_element_type | solution.py:135
  (94 shorter events, 67.4 us)
Async XLA Ops:
  7.2 69.4 %all-gather.3.cloned.1.call-start = ((), (), s32[]{:S(2)}) async-start(), calls=%async_computation | async-start | bytes 4325376 | tf_op jit(solution)/shard_map/all_gather | solution.py:88
  7.9 242.2 %all-gather.5.cloned.1.call-start = ((), (), s32[]{:S(2)}) async-start(), calls=%async_computation.1 | async-start | bytes 4325376 | tf_op jit(solution)/shard_map/all_gather | solution.py:113
  87.1 7.0 %collective-permute-start = (bf16[16,8,4096]{2,1,0:T(8,128)(2,1)}, bf16[16,8,4096]{2,1,0:T(8,128)(2,1)S(1)}, u32[]{:S(2)}, u32[]{:S(2)}) collective-permute-start(bf16[16,8,4096]{2,1,0:T(8,128)(2,1)} %dynamic-slice_bitcast_fusion.1), channel_id=1, source_target_pairs={{0,1},{1,0},{2,3},{3,2},{4,5},{5,4},{6,7},{7,6},{8,9},{9,8},{10,11... | collective-permute-start | bytes 3145736 | tf_op jit(solution)/shard_map/ppermute | solution.py:79
  91.9 4.8 %collective-permute-start.5 = (bf16[16,8,4096]{2,1,0:T(8,128)(2,1)S(1)}, bf16[16,8,4096]{2,1,0:T(8,128)(2,1)S(1)}, u32[]{:S(2)}, u32[]{:S(2)}) collective-permute-start(bf16[16,8,4096]{2,1,0:T(8,128)(2,1)S(1)} %dynamic-slice_bitcast_fusion), channel_id=1, source_target_pairs={{0,1},{1,0},{2,3},{3,2},{4,5},{5,4},{6,7},{7,6},{8,9},{9,8},{10,11... | collective-permute-start | bytes 3145736 | tf_op jit(solution)/shard_map/ppermute | solution.py:79
  94.5 16.0 %collective-permute-start.1 = (bf16[8,8,4096]{2,1,0:T(8,128)(2,1)S(1)}, bf16[8,8,4096]{2,1,0:T(8,128)(2,1)S(1)}, u32[]{:S(2)}, u32[]{:S(2)}) collective-permute-start(bf16[8,8,4096]{2,1,0:T(8,128)(2,1)S(1)} %fusion.7), channel_id=1, source_target_pairs={{0,2},{1,3},{2,0},{3,1},{4,6},{5,7},{6,4},{7,5},{8,10},{9,11},{10,... | collective-permute-start | bytes 1572872 | tf_op jit(solution)/shard_map/ppermute | solution.py:79
  97.1 16.3 %collective-permute-start.6 = (bf16[8,8,4096]{2,1,0:T(8,128)(2,1)S(1)}, bf16[8,8,4096]{2,1,0:T(8,128)(2,1)S(1)}, u32[]{:S(2)}, u32[]{:S(2)}) collective-permute-start(bf16[8,8,4096]{2,1,0:T(8,128)(2,1)S(1)} %fusion.8), channel_id=1, source_target_pairs={{0,8},{1,9},{2,10},{3,11},{4,12},{5,13},{6,14},{7,15},{8,0},{9,1},... | collective-permute-start | bytes 1572872 | tf_op jit(solution)/shard_map/ppermute | solution.py:79
  110.6 10.7 %collective-permute-start.2 = (bf16[4,8,4096]{2,1,0:T(8,128)(2,1)S(1)}, bf16[4,8,4096]{2,1,0:T(8,128)(2,1)S(1)}, u32[]{:S(2)}, u32[]{:S(2)}) collective-permute-start(bf16[4,8,4096]{2,1,0:T(8,128)(2,1)S(1)} %fusion.9), channel_id=1, source_target_pairs={{0,6},{1,7},{2,4},{3,5},{4,2},{5,3},{6,0},{7,1},{8,14},{9,15},{10,... | collective-permute-start | bytes 786440 | tf_op jit(solution)/shard_map/ppermute | solution.py:79
  113.6 10.6 %collective-permute-start.7 = (bf16[4,8,4096]{2,1,0:T(8,128)(2,1)S(1)}, bf16[4,8,4096]{2,1,0:T(8,128)(2,1)S(1)}, u32[]{:S(2)}, u32[]{:S(2)}) collective-permute-start(bf16[4,8,4096]{2,1,0:T(8,128)(2,1)S(1)} %fusion.10), channel_id=1, source_target_pairs={{0,24},{1,25},{2,26},{3,27},{4,28},{5,29},{6,30},{7,31},{8,16},{9,... | collective-permute-start | bytes 786440 | tf_op jit(solution)/shard_map/ppermute | solution.py:79
  121.4 6.9 %collective-permute-start.3 = (bf16[2,8,4096]{2,1,0:T(8,128)(2,1)S(1)}, bf16[2,8,4096]{2,1,0:T(8,128)(2,1)S(1)}, u32[]{:S(2)}, u32[]{:S(2)}) collective-permute-start(bf16[2,8,4096]{2,1,0:T(8,128)(2,1)S(1)} %fusion.12), channel_id=1, source_target_pairs={{0,8},{1,9},{2,10},{3,11},{4,12},{5,13},{6,14},{7,15},{8,0},{9,1},... | collective-permute-start | bytes 393224 | tf_op jit(solution)/shard_map/ppermute | solution.py:79
  124.2 6.9 %collective-permute-start.8 = (bf16[2,8,4096]{2,1,0:T(8,128)(2,1)S(1)}, bf16[2,8,4096]{2,1,0:T(8,128)(2,1)S(1)}, u32[]{:S(2)}, u32[]{:S(2)}) collective-permute-start(bf16[2,8,4096]{2,1,0:T(8,128)(2,1)S(1)} %fusion.13), channel_id=1, source_target_pairs={{0,2},{1,3},{2,0},{3,1},{4,6},{5,7},{6,4},{7,5},{8,10},{9,11},{10,... | collective-permute-start | bytes 393224 | tf_op jit(solution)/shard_map/ppermute | solution.py:79
  128.3 7.4 %collective-permute-start.4 = (bf16[1,8,4096]{2,1,0:T(8,128)(2,1)S(1)}, bf16[1,8,4096]{2,1,0:T(8,128)(2,1)S(1)}, u32[]{:S(2)}, u32[]{:S(2)}) collective-permute-start(bf16[1,8,4096]{2,1,0:T(8,128)(2,1)S(1)} %dynamic-slice_convert_fusion.7), channel_id=1, source_target_pairs={{0,24},{1,25},{2,26},{3,27},{4,28},{5,29},{6,30},{7,31},{8,16},{9,... | collective-permute-start | bytes 196616 | tf_op jit(solution)/shard_map/ppermute | solution.py:79
  131.2 7.4 %collective-permute-start.9 = (bf16[1,8,4096]{2,1,0:T(8,128)(2,1)S(1)}, bf16[1,8,4096]{2,1,0:T(8,128)(2,1)S(1)}, u32[]{:S(2)}, u32[]{:S(2)}) collective-permute-start(bf16[1,8,4096]{2,1,0:T(8,128)(2,1)S(1)} %dynamic-slice_convert_fusion.6), channel_id=1, source_target_pairs={{0,6},{1,7},{2,4},{3,5},{4,2},{5,3},{6,0},{7,1},{8,14},{9,15},{10,... | collective-permute-start | bytes 196616 | tf_op jit(solution)/shard_map/ppermute | solution.py:79
  138.6 6.9 %collective-permute-start.10 = (bf16[8,8192]{1,0:T(8,128)(2,1)S(1)}, bf16[8,8192]{1,0:T(8,128)(2,1)S(1)}, u32[]{:S(2)}, u32[]{:S(2)}) collective-permute-start(bf16[8,8192]{1,0:T(8,128)(2,1)S(1)} %pad_maximum_fusion), channel_id=1, source_target_pairs={{0,32},{32,0},{64,96},{96,64},{128,160},{160,128},{192,224},{224,1... | collective-permute-start | bytes 393224 | tf_op jit(solution)/shard_map/ppermute | solution.py:20
  145.5 9.2 %collective-permute-start.11 = (bf16[8,8192]{1,0:T(8,128)(2,1)S(1)}, bf16[8,8192]{1,0:T(8,128)(2,1)S(1)}, u32[]{:S(2)}, u32[]{:S(2)}) collective-permute-start(bf16[8,8192]{1,0:T(8,128)(2,1)S(1)} %add_convert_fusion.2), channel_id=1, source_target_pairs={{0,64},{32,96},{64,0},{96,32},{128,192},{160,224},{192,128},{224,1... | collective-permute-start | bytes 393224 | tf_op jit(solution)/shard_map/ppermute | solution.py:20
  154.7 15.1 %collective-permute-start.12 = (bf16[8,8192]{1,0:T(8,128)(2,1)S(1)}, bf16[8,8192]{1,0:T(8,128)(2,1)S(1)}, u32[]{:S(2)}, u32[]{:S(2)}) collective-permute-start(bf16[8,8192]{1,0:T(8,128)(2,1)S(1)} %add_convert_fusion.1), channel_id=1, source_target_pairs={{0,128},{32,160},{64,192},{96,224},{128,0},{160,32},{192,64},{224,... | collective-permute-start | bytes 393224 | tf_op jit(solution)/shard_map/ppermute | solution.py:20
  169.9 17.0 %collective-permute-start.13 = (bf16[8,8192]{1,0:T(8,128)(2,1)S(1)}, bf16[8,8192]{1,0:T(8,128)(2,1)S(1)}, u32[]{:S(2)}, u32[]{:S(2)}) collective-permute-start(bf16[8,8192]{1,0:T(8,128)(2,1)S(1)} %add_convert_fusion), channel_id=1, source_target_pairs={{0,256},{32,288},{64,320},{96,352},{128,384},{160,416},{192,448},{... | collective-permute-start | bytes 393224 | tf_op jit(solution)/shard_map/ppermute | solution.py:20
  264.6 5.4 %collective-permute-start.15 = (f32[1,128]{1,0:T(1,128)S(1)}, f32[1,128]{1,0:T(1,128)S(1)}, u32[]{:S(2)}, u32[]{:S(2)}) collective-permute-start(f32[1,128]{1,0:T(1,128)S(1)} %broadcast_add_fusion), channel_id=1, source_target_pairs={{0,2},{1,3},{2,0},{3,1},{4,6},{5,7},{6,4},{7,5},{8,10},{9,11},{10,... | collective-permute-start | bytes 1544 | tf_op jit(solution)/shard_map/ppermute | solution.py:130
  270.0 6.6 %collective-permute-start.16 = (f32[1,128]{1,0:T(1,128)S(1)}, f32[1,128]{1,0:T(1,128)S(1)}, u32[]{:S(2)}, u32[]{:S(2)}) collective-permute-start(f32[1,128]{1,0:T(1,128)S(1)} %fusion.31), channel_id=1, source_target_pairs={{0,6},{1,7},{2,4},{3,5},{4,2},{5,3},{6,0},{7,1},{8,14},{9,15},{10,... | collective-permute-start | bytes 1544 | tf_op jit(solution)/shard_map/ppermute | solution.py:130
  276.7 5.4 %collective-permute-start.17 = (f32[1,128]{1,0:T(1,128)S(1)}, f32[1,128]{1,0:T(1,128)S(1)}, u32[]{:S(2)}, u32[]{:S(2)}) collective-permute-start(f32[1,128]{1,0:T(1,128)S(1)} %add.239), channel_id=1, source_target_pairs={{0,8},{1,9},{2,10},{3,11},{4,12},{5,13},{6,14},{7,15},{8,0},{9,1},... | collective-permute-start | bytes 1544 | tf_op jit(solution)/shard_map/ppermute | solution.py:130
  282.1 6.6 %collective-permute-start.18 = (f32[1,128]{1,0:T(1,128)S(1)}, f32[1,128]{1,0:T(1,128)S(1)}, u32[]{:S(2)}, u32[]{:S(2)}) collective-permute-start(f32[1,128]{1,0:T(1,128)S(1)} %add.240), channel_id=1, source_target_pairs={{0,24},{1,25},{2,26},{3,27},{4,28},{5,29},{6,30},{7,31},{8,16},{9,... | collective-permute-start | bytes 1544 | tf_op jit(solution)/shard_map/ppermute | solution.py:130
  288.7 5.4 %collective-permute-start.19 = (f32[1,128]{1,0:T(1,128)S(1)}, f32[1,128]{1,0:T(1,128)S(1)}, u32[]{:S(2)}, u32[]{:S(2)}) collective-permute-start(f32[1,128]{1,0:T(1,128)S(1)} %add.241), channel_id=1, source_target_pairs={{0,32},{32,0},{64,96},{96,64},{128,160},{160,128},{192,224},{224,1... | collective-permute-start | bytes 1544 | tf_op jit(solution)/shard_map/ppermute | solution.py:20
  294.1 6.3 %collective-permute-start.20 = (f32[1,128]{1,0:T(1,128)S(1)}, f32[1,128]{1,0:T(1,128)S(1)}, u32[]{:S(2)}, u32[]{:S(2)}) collective-permute-start(f32[1,128]{1,0:T(1,128)S(1)} %add.242), channel_id=1, source_target_pairs={{0,64},{32,96},{64,0},{96,32},{128,192},{160,224},{192,128},{224,1... | collective-permute-start | bytes 1544 | tf_op jit(solution)/shard_map/ppermute | solution.py:20
  300.5 9.3 %collective-permute-start.21 = (f32[1,128]{1,0:T(1,128)S(1)}, f32[1,128]{1,0:T(1,128)S(1)}, u32[]{:S(2)}, u32[]{:S(2)}) collective-permute-start(f32[1,128]{1,0:T(1,128)S(1)} %add.243), channel_id=1, source_target_pairs={{0,128},{32,160},{64,192},{96,224},{128,0},{160,32},{192,64},{224,... | collective-permute-start | bytes 1544 | tf_op jit(solution)/shard_map/ppermute | solution.py:20
  309.8 14.3 %collective-permute-start.22 = (f32[1,128]{1,0:T(1,128)S(1)}, f32[1,128]{1,0:T(1,128)S(1)}, u32[]{:S(2)}, u32[]{:S(2)}) collective-permute-start(f32[1,128]{1,0:T(1,128)S(1)} %add.244), channel_id=1, source_target_pairs={{0,256},{32,288},{64,320},{96,352},{128,384},{160,416},{192,448},{... | collective-permute-start | bytes 1544 | tf_op jit(solution)/shard_map/ppermute | solution.py:20
  (9 other events, 373.8 us)
Sparse Core Ops, SparseCore 0:
  11.1 65.4 all-gather.2
  188.7 61.3 all-gather.4

commit v5 on v4

--- a/solution.py
+++ b/solution.py
@@ -80,12 +80,33 @@
     return acc[0]
 
 
+def doubling_gather(x, rank, n, masks):
+    me = logical_rank(rank, masks)
+    acc = x[None]
+    for j in reversed(range(len(masks))):
+        bit = (me >> (4 - j)) & 1
+        got = lax.ppermute(acc, "lat", masked_pairs(n, masks[j]))
+        pair = jnp.stack([acc, got])
+        acc = jnp.where(bit == 0, pair, pair[::-1]).reshape((2 * acc.shape[0],) + acc.shape[1:])
+    order = np.array([logical_rank(r, masks) for r in range(n)], dtype=np.int32)
+    return jnp.take(acc, order, axis=0)
+
+
+def lat_gather(x, rank, n):
+    cols = x.shape[1] // 2
+    parts = [
+        doubling_gather(x[:, k * cols:(k + 1) * cols], rank, n, masks)
+        for k, masks in enumerate((ORDER_X_FIRST, ORDER_Y_FIRST))
+    ]
+    return jnp.concatenate(parts, axis=2).reshape(n * x.shape[0], x.shape[1])
+
+
 def body(stream, batch_index, weight, enc_bias, dec_bias):
     own_rows = stream.shape[0]
     n_lat = lax.axis_size("lat")
     n_grp = lax.axis_size("grp")
     rank_lat = lax.axis_index("lat")
-    gathered = lax.all_gather(stream, "lat", axis=0, tiled=True)
+    gathered = lat_gather(stream, rank_lat, n_lat)
     n_rows = gathered.shape[0]
     onehot = (batch_index[:, None] == lax.broadcasted_iota(jnp.int32, (batch_index.shape[0], n_rows), 1)).astype(
         gathered.dtype
@@ -110,7 +131,7 @@
     recon = butterfly_sum(block_recon.astype(jnp.float32), "grp", n_grp, jnp.bfloat16)
     error_own = recon + dec_bias - own_batch.astype(jnp.float32)
     grad_own = (2.0 * error_own).astype(jnp.bfloat16)
-    grad_rows = lax.all_gather(grad_own, "lat", axis=0, tiled=True)
+    grad_rows = lat_gather(grad_own, rank_lat, n_lat)
     grad_active = jnp.dot(grad_rows, weight, preferred_element_type=jnp.float32)
     decoder_grad = lax.dot_general(
         grad_rows, active, (((0,), (0,)), ((), ())), preferred_element_type=jnp.float32

time: 336 us -> 300 us (0.89)
  waiting for transfers between devices: 192 us -> 91.4 us
  starting transfers between devices: 96.2 us -> 154 us
  between operations: 16 us -> 3.02 us
  other arithmetic: 8.3 us -> 16.8 us
  local copies, waits for them, and re-layouts: 4.72 us -> 13 us
    all_gather x2 -> x0, waiting for transfers between devices: 129 us -> none  [the longest x1 68 us: body(): gathered = lax.all_gather(stream, 'lat', axis=0, tiled=True)]
    ppermute x0 -> x20, starting transfers between devices: none -> 55.4 us  [doubling_gather(): got = lax.ppermute(acc, 'lat', masked_pairs(n, masks[j]))]
    ppermute x0 -> x20, waiting for transfers between devices: none -> 27.9 us  [doubling_gather(): got = lax.ppermute(acc, 'lat', masked_pairs(n, masks[j]))]
    gather x0 -> x4, local copies, waits for them, and re-layouts: none -> 8.06 us  [doubling_gather(): return jnp.take(acc, order, axis=0)]
    another operation x0 -> x24, other arithmetic: none -> 4.1 us  [doubling_gather(): pair = jnp.stack([acc, got])]
  transfers between devices with their start and end apart: 25 -> 43, of which waited for: 21 -> 33; matrix products, arithmetic and copies ran while one was open for 1% -> 4% of each run, Pallas kernels for 0% -> 0%
where the time goes in v5:
time: 300 us; the launch traced here: 298 us
  starting transfers between devices  154 us (51%)
  waiting for transfers between devices  91.4 us (30%)
  matrix products  19.6 us (7%)
  other arithmetic  16.8 us (6%)
  local copies, waits for them, and re-layouts  13 us (4%)
  between operations  3.02 us (1%)
    ppermute x8, starting transfers between devices, butterfly_sum(): lax.ppermute(sent, axis, xor_pairs(n, bit)).astype(jnp.float32)  58.2 us
    ppermute x20, starting transfers between devices, doubling_gather(): got = lax.ppermute(acc, 'lat', masked_pairs(n, masks[j]))  55.4 us
    ppermute x10, starting transfers between devices, halving_scatter(): lax.ppermute(sent, 'lat', masked_pairs(n, mask)).astype(jnp.float32)  29.5 us
    ppermute x8, waiting for transfers between devices, butterfly_sum(): lax.ppermute(sent, axis, xor_pairs(n, bit)).astype(jnp.float32)  28.4 us
    ppermute x20, waiting for transfers between devices, doubling_gather(): got = lax.ppermute(acc, 'lat', masked_pairs(n, masks[j]))  27.9 us
    ppermute x10, waiting for transfers between devices, halving_scatter(): lax.ppermute(sent, 'lat', masked_pairs(n, mask)).astype(jnp.float32)  18.9 us
    ppermute x5, waiting for transfers between devices, body(): squares = squares + lax.ppermute(squares, 'lat', masked_pairs(n_lat, mask))  16.2 us
    ppermute x5, starting transfers between devices, body(): squares = squares + lax.ppermute(squares, 'lat', masked_pairs(n_lat, mask))  11.1 us
  transfers between devices with their start and end apart: 43, of which 33 were waited for; matrix products, arithmetic and copies ran while one was open for 4% of the time, Pallas kernels for 0%

profile of v5, /device:TPU:6, one launch (start us, length us, event | category | flops | bytes accessed | tf_op | source)
XLA Modules:
  0.0 298.0 jit_solution(7495631433578688240)
XLA Ops:
  1.5 4.9 %collective-permute-start = (bf16[1,8,4096]{2,1,0:T(8,128)(2,1)S(1)}, bf16[1,8,4096]{2,1,0:T(8,128)(2,1)S(1)}, u32[]{:S(2)}, u32[]{:S(2)}) collective-permute-start(bf16[1,8,4096]{2,1,0:T(8,128)(2,1)S(1)} %get-tuple-element.18), channel_id=1, source_target_pairs={{0,24},{1,25},{2,26},{3,27},{4,28},{5,29},{6,30},{7,31},{8,16},{9,... | collective-permute-start | bytes 196616 | tf_op jit(solution)/shard_map/ppermute | solution.py:88
  6.5 4.8 %collective-permute-start.5 = (bf16[1,8,4096]{2,1,0:T(8,128)(2,1)S(1)}, bf16[1,8,4096]{2,1,0:T(8,128)(2,1)S(1)}, u32[]{:S(2)}, u32[]{:S(2)}) collective-permute-start(bf16[1,8,4096]{2,1,0:T(8,128)(2,1)S(1)} %get-tuple-element.19), channel_id=1, source_target_pairs={{0,6},{1,7},{2,4},{3,5},{4,2},{5,3},{6,0},{7,1},{8,14},{9,15},{10,... | collective-permute-start | bytes 196616 | tf_op jit(solution)/shard_map/ppermute | solution.py:88
  35.3 5.6 %collective-permute-done.3 = bf16[8,8,4096]{2,1,0:T(8,128)(2,1)S(1)} collective-permute-done((bf16[8,8,4096]{2,1,0:T(8,128)(2,1)S(1)}, bf16[8,8,4096]{2,1,0:T(8,128)(2,1)S(1)}, u32[]{:S(2)}, u32[]{:S(2)}) %collective-permute-start.3) | collective-permute-done | bytes 524320 | tf_op jit(solution)/shard_map/ppermute | solution.py:88
  53.9 3.7 %convolution_convert_fusion = bf16[256,8192]{1,0:T(8,128)(2,1)S(1)} fusion(bf16[32,8,4096]{2,1,0:T(8,128)(2,1)} %gather_fusion.1, bf16[32,8,4096]{2,1,0:T(8,128)(2,1)} %gather_fusion, s32[256]{0:T(256)S(1)} %copy-done.7), kind=kOutput, calls=%fused_computation.6 | convolution fusion | flops 1084293120 | bytes 8389632 | tf_op jit(solution)/shard_map/dot_general | solution.py:114
  75.4 11.4 %collective-permute-done.11 = bf16[8,8,4096]{2,1,0:T(8,128)(2,1)S(1)} collective-permute-done((bf16[8,8,4096]{2,1,0:T(8,128)(2,1)S(1)}, bf16[8,8,4096]{2,1,0:T(8,128)(2,1)S(1)}, u32[]{:S(2)}, u32[]{:S(2)}) %collective-permute-start.11) | collective-permute-done | bytes 524320 | tf_op jit(solution)/shard_map/ppermute | solution.py:79
  90.2 5.1 %collective-permute-start.17 = (bf16[4,8,4096]{2,1,0:T(8,128)(2,1)S(1)}, bf16[4,8,4096]{2,1,0:T(8,128)(2,1)S(1)}, u32[]{:S(2)}, u32[]{:S(2)}) collective-permute-start(bf16[4,8,4096]{2,1,0:T(8,128)(2,1)S(1)} %fusion.14), channel_id=1, source_target_pairs={{0,24},{1,25},{2,26},{3,27},{4,28},{5,29},{6,30},{7,31},{8,16},{9,... | collective-permute-start | bytes 786440 | tf_op jit(solution)/shard_map/ppermute | solution.py:79
  108.3 4.9 %collective-permute-start.19 = (bf16[1,8,4096]{2,1,0:T(8,128)(2,1)S(1)}, bf16[1,8,4096]{2,1,0:T(8,128)(2,1)S(1)}, u32[]{:S(2)}, u32[]{:S(2)}) collective-permute-start(bf16[1,8,4096]{2,1,0:T(8,128)(2,1)S(1)} %dynamic-slice_convert_fusion.6), channel_id=1, source_target_pairs={{0,6},{1,7},{2,4},{3,5},{4,2},{5,3},{6,0},{7,1},{8,14},{9,15},{10,... | collective-permute-start | bytes 196616 | tf_op jit(solution)/shard_map/ppermute | solution.py:79
  118.2 4.4 %collective-permute-done.20 = bf16[8,8192]{1,0:T(8,128)(2,1)S(1)} collective-permute-done((bf16[8,8192]{1,0:T(8,128)(2,1)S(1)}, bf16[8,8192]{1,0:T(8,128)(2,1)S(1)}, u32[]{:S(2)}, u32[]{:S(2)}) %collective-permute-start.20) | collective-permute-done | bytes 131104 | tf_op jit(solution)/shard_map/ppermute | solution.py:20
  122.6 3.8 %collective-permute-start.21 = (bf16[8,8192]{1,0:T(8,128)(2,1)S(1)}, bf16[8,8192]{1,0:T(8,128)(2,1)S(1)}, u32[]{:S(2)}, u32[]{:S(2)}) collective-permute-start(bf16[8,8192]{1,0:T(8,128)(2,1)S(1)} %add_convert_fusion.2), channel_id=1, source_target_pairs={{0,64},{32,96},{64,0},{96,32},{128,192},{160,224},{192,128},{224,1... | collective-permute-start | bytes 393224 | tf_op jit(solution)/shard_map/ppermute | solution.py:20
  126.4 5.4 %collective-permute-done.21 = bf16[8,8192]{1,0:T(8,128)(2,1)S(1)} collective-permute-done((bf16[8,8192]{1,0:T(8,128)(2,1)S(1)}, bf16[8,8192]{1,0:T(8,128)(2,1)S(1)}, u32[]{:S(2)}, u32[]{:S(2)}) %collective-permute-start.21) | collective-permute-done | bytes 131104 | tf_op jit(solution)/shard_map/ppermute | solution.py:20
  131.8 6.7 %collective-permute-start.22 = (bf16[8,8192]{1,0:T(8,128)(2,1)S(1)}, bf16[8,8192]{1,0:T(8,128)(2,1)S(1)}, u32[]{:S(2)}, u32[]{:S(2)}) collective-permute-start(bf16[8,8192]{1,0:T(8,128)(2,1)S(1)} %add_convert_fusion.1), channel_id=1, source_target_pairs={{0,128},{32,160},{64,192},{96,224},{128,0},{160,32},{192,64},{224,... | collective-permute-start | bytes 393224 | tf_op jit(solution)/shard_map/ppermute | solution.py:20
  138.5 8.3 %collective-permute-done.22 = bf16[8,8192]{1,0:T(8,128)(2,1)S(1)} collective-permute-done((bf16[8,8192]{1,0:T(8,128)(2,1)S(1)}, bf16[8,8192]{1,0:T(8,128)(2,1)S(1)}, u32[]{:S(2)}, u32[]{:S(2)}) %collective-permute-start.22) | collective-permute-done | bytes 131104 | tf_op jit(solution)/shard_map/ppermute | solution.py:20
  146.9 15.1 %collective-permute-start.23 = (bf16[8,8192]{1,0:T(8,128)(2,1)S(1)}, bf16[8,8192]{1,0:T(8,128)(2,1)S(1)}, u32[]{:S(2)}, u32[]{:S(2)}) collective-permute-start(bf16[8,8192]{1,0:T(8,128)(2,1)S(1)} %add_convert_fusion), channel_id=1, source_target_pairs={{0,256},{32,288},{64,320},{96,352},{128,384},{160,416},{192,448},{... | collective-permute-start | bytes 393224 | tf_op jit(solution)/shard_map/ppermute | solution.py:20
  166.6 4.8 %collective-permute-start.24 = (bf16[1,8,4096]{2,1,0:T(8,128)(2,1)S(1)}, bf16[1,8,4096]{2,1,0:T(8,128)(2,1)S(1)}, u32[]{:S(2)}, u32[]{:S(2)}) collective-permute-start(bf16[1,8,4096]{2,1,0:T(8,128)(2,1)S(1)} %get-tuple-element.10), channel_id=1, source_target_pairs={{0,24},{1,25},{2,26},{3,27},{4,28},{5,29},{6,30},{7,31},{8,16},{9,... | collective-permute-start | bytes 196616 | tf_op jit(solution)/shard_map/ppermute | solution.py:88
  180.9 4.6 %collective-permute-start.26 = (bf16[4,8,4096]{2,1,0:T(8,128)(2,1)S(1)}, bf16[4,8,4096]{2,1,0:T(8,128)(2,1)S(1)}, u32[]{:S(2)}, u32[]{:S(2)}) collective-permute-start(bf16[4,8,4096]{2,1,0:T(8,128)(2,1)S(1)} %bitcast.206), channel_id=1, source_target_pairs={{0,6},{1,7},{2,4},{3,5},{4,2},{5,3},{6,0},{7,1},{8,14},{9,15},{10,... | collective-permute-start | bytes 786440 | tf_op jit(solution)/shard_map/ppermute | solution.py:88
  197.3 4.3 %collective-permute-done.27 = bf16[8,8,4096]{2,1,0:T(8,128)(2,1)S(1)} collective-permute-done((bf16[8,8,4096]{2,1,0:T(8,128)(2,1)S(1)}, bf16[8,8,4096]{2,1,0:T(8,128)(2,1)S(1)}, u32[]{:S(2)}, u32[]{:S(2)}) %collective-permute-start.27) | collective-permute-done | bytes 524320 | tf_op jit(solution)/shard_map/ppermute | solution.py:88
  215.3 4.3 %fusion.39 = (f32[128]{0:T(128)S(1)}, bf16[256,128]{1,0:T(8,128)(2,1)S(1)}) fusion(f32[256,128]{1,0:T(8,128)S(1)} %fusion.8, bf16[8192,128]{1,0:T(8,128)(2,1)} %param.17, bf16[32,8,4096]{2,1,0:T(8,128)(2,1)} %gather_fusion.5, bf16[32,8,4096]{2,1,0:T(8,128)(2,1)} %gather_fusion.4), kind=kOutput, calls=%fused_computation.136 | convolution fusion | flops 545488768 | bytes 6488576 | tf_op jit(solution)/shard_map/dot_general | solution.py:135
  221.8 5.0 %multiply_reduce_fusion = (f32[]{:T(128)}, f32[8192,128]{1,0:T(8,128)}) fusion(f32[8192,128]{1,0:T(8,128)S(1)} %fusion.2, f32[256,128]{1,0:T(8,128)S(1)} %fusion.8, bf16[32,8,4096]{2,1,0:T(8,128)(2,1)S(1)} %copy-done.4, bf16[32,8,4096]{2,1,0:T(8,128)(2,1)S(1)} %copy-done.3), kind=kOutput, calls=%fused_computation.16 | convolution fusion | flops 548667392 | bytes 12713988 | tf_op jit(solution)/shard_map/dot_general | solution.py:136
  239.7 4.2 %collective-permute-done.36 = f32[1,128]{1,0:T(1,128)S(1)} collective-permute-done((f32[1,128]{1,0:T(1,128)S(1)}, f32[1,128]{1,0:T(1,128)S(1)}, u32[]{:S(2)}, u32[]{:S(2)}) %collective-permute-start.36) | collective-permute-done | bytes 544 | tf_op jit(solution)/shard_map/ppermute | solution.py:151
  251.9 4.1 %collective-permute-done.38 = f32[1,128]{1,0:T(1,128)S(1)} collective-permute-done((f32[1,128]{1,0:T(1,128)S(1)}, f32[1,128]{1,0:T(1,128)S(1)}, u32[]{:S(2)}, u32[]{:S(2)}) %collective-permute-start.38) | collective-permute-done | bytes 544 | tf_op jit(solution)/shard_map/ppermute | solution.py:151
  261.4 5.0 %collective-permute-start.40 = (f32[1,128]{1,0:T(1,128)S(1)}, f32[1,128]{1,0:T(1,128)S(1)}, u32[]{:S(2)}, u32[]{:S(2)}) collective-permute-start(f32[1,128]{1,0:T(1,128)S(1)} %add.248), channel_id=1, source_target_pairs={{0,64},{32,96},{64,0},{96,32},{128,192},{160,224},{192,128},{224,1... | collective-permute-start | bytes 1544 | tf_op jit(solution)/shard_map/ppermute | solution.py:20
  267.9 10.1 %collective-permute-start.41 = (f32[1,128]{1,0:T(1,128)S(1)}, f32[1,128]{1,0:T(1,128)S(1)}, u32[]{:S(2)}, u32[]{:S(2)}) collective-permute-start(f32[1,128]{1,0:T(1,128)S(1)} %add.249), channel_id=1, source_target_pairs={{0,128},{32,160},{64,192},{96,224},{128,0},{160,32},{192,64},{224,... | collective-permute-start | bytes 1544 | tf_op jit(solution)/shard_map/ppermute | solution.py:20
  279.5 12.1 %collective-permute-start.42 = (f32[1,128]{1,0:T(1,128)S(1)}, f32[1,128]{1,0:T(1,128)S(1)}, u32[]{:S(2)}, u32[]{:S(2)}) collective-permute-start(f32[1,128]{1,0:T(1,128)S(1)} %add.250), channel_id=1, source_target_pairs={{0,256},{32,288},{64,320},{96,352},{128,384},{160,416},{192,448},{... | collective-permute-start | bytes 1544 | tf_op jit(solution)/shard_map/ppermute | solution.py:20
  294.3 3.7 %multiply_convert_fusion = bf16[8192,128]{1,0:T(8,128)(2,1)} fusion(f32[8192,128]{1,0:T(8,128)} %get-tuple-element.24, f32[]{:T(128)} %bitcast.99), kind=kLoop, calls=%fused_computation.15 | loop fusion | flops 2097152 | bytes 6291460 | tf_op jit(solution)/shard_map/convert_element_type | solution.py:156
  (178 shorter events, 148.8 us)
Async XLA Ops:
  1.5 11.7 %collective-permute-start = (bf16[1,8,4096]{2,1,0:T(8,128)(2,1)S(1)}, bf16[1,8,4096]{2,1,0:T(8,128)(2,1)S(1)}, u32[]{:S(2)}, u32[]{:S(2)}) collective-permute-start(bf16[1,8,4096]{2,1,0:T(8,128)(2,1)S(1)} %get-tuple-element.18), channel_id=1, source_target_pairs={{0,24},{1,25},{2,26},{3,27},{4,28},{5,29},{6,30},{7,31},{8,16},{9,... | collective-permute-start | bytes 196616 | tf_op jit(solution)/shard_map/ppermute | solution.py:88
  6.5 8.8 %collective-permute-start.5 = (bf16[1,8,4096]{2,1,0:T(8,128)(2,1)S(1)}, bf16[1,8,4096]{2,1,0:T(8,128)(2,1)S(1)}, u32[]{:S(2)}, u32[]{:S(2)}) collective-permute-start(bf16[1,8,4096]{2,1,0:T(8,128)(2,1)S(1)} %get-tuple-element.19), channel_id=1, source_target_pairs={{0,6},{1,7},{2,4},{3,5},{4,2},{5,3},{6,0},{7,1},{8,14},{9,15},{10,... | collective-permute-start | bytes 196616 | tf_op jit(solution)/shard_map/ppermute | solution.py:88
  15.3 8.4 %collective-permute-start.6 = (bf16[2,8,4096]{2,1,0:T(8,128)(2,1)S(1)}, bf16[2,8,4096]{2,1,0:T(8,128)(2,1)S(1)}, u32[]{:S(2)}, u32[]{:S(2)}) collective-permute-start(bf16[2,8,4096]{2,1,0:T(8,128)(2,1)S(1)} %get-tuple-element.22), channel_id=1, source_target_pairs={{0,2},{1,3},{2,0},{3,1},{4,6},{5,7},{6,4},{7,5},{8,10},{9,11},{10,... | collective-permute-start | bytes 393224 | tf_op jit(solution)/shard_map/ppermute | solution.py:88
  20.3 9.5 %collective-permute-start.2 = (bf16[4,8,4096]{2,1,0:T(8,128)(2,1)S(1)}, bf16[4,8,4096]{2,1,0:T(8,128)(2,1)S(1)}, u32[]{:S(2)}, u32[]{:S(2)}) collective-permute-start(bf16[4,8,4096]{2,1,0:T(8,128)(2,1)S(1)} %bitcast.208), channel_id=1, source_target_pairs={{0,6},{1,7},{2,4},{3,5},{4,2},{5,3},{6,0},{7,1},{8,14},{9,15},{10,... | collective-permute-start | bytes 786440 | tf_op jit(solution)/shard_map/ppermute | solution.py:88
  23.8 9.5 %collective-permute-start.7 = (bf16[4,8,4096]{2,1,0:T(8,128)(2,1)S(1)}, bf16[4,8,4096]{2,1,0:T(8,128)(2,1)S(1)}, u32[]{:S(2)}, u32[]{:S(2)}) collective-permute-start(bf16[4,8,4096]{2,1,0:T(8,128)(2,1)S(1)} %bitcast.212), channel_id=1, source_target_pairs={{0,24},{1,25},{2,26},{3,27},{4,28},{5,29},{6,30},{7,31},{8,16},{9,... | collective-permute-start | bytes 786440 | tf_op jit(solution)/shard_map/ppermute | solution.py:88
  29.9 11.1 %collective-permute-start.3 = (bf16[8,8,4096]{2,1,0:T(8,128)(2,1)S(1)}, bf16[8,8,4096]{2,1,0:T(8,128)(2,1)S(1)}, u32[]{:S(2)}, u32[]{:S(2)}) collective-permute-start(bf16[8,8,4096]{2,1,0:T(8,128)(2,1)S(1)} %bitcast.198), channel_id=1, source_target_pairs={{0,2},{1,3},{2,0},{3,1},{4,6},{5,7},{6,4},{7,5},{8,10},{9,11},{10,... | collective-permute-start | bytes 1572872 | tf_op jit(solution)/shard_map/ppermute | solution.py:88
  33.4 11.6 %collective-permute-start.8 = (bf16[8,8,4096]{2,1,0:T(8,128)(2,1)S(1)}, bf16[8,8,4096]{2,1,0:T(8,128)(2,1)S(1)}, u32[]{:S(2)}, u32[]{:S(2)}) collective-permute-start(bf16[8,8,4096]{2,1,0:T(8,128)(2,1)S(1)} %bitcast.200), channel_id=1, source_target_pairs={{0,8},{1,9},{2,10},{3,11},{4,12},{5,13},{6,14},{7,15},{8,0},{9,1},... | collective-permute-start | bytes 1572872 | tf_op jit(solution)/shard_map/ppermute | solution.py:88
  70.6 16.2 %collective-permute-start.11 = (bf16[8,8,4096]{2,1,0:T(8,128)(2,1)S(1)}, bf16[8,8,4096]{2,1,0:T(8,128)(2,1)S(1)}, u32[]{:S(2)}, u32[]{:S(2)}) collective-permute-start(bf16[8,8,4096]{2,1,0:T(8,128)(2,1)S(1)} %fusion.11), channel_id=1, source_target_pairs={{0,2},{1,3},{2,0},{3,1},{4,6},{5,7},{6,4},{7,5},{8,10},{9,11},{10,... | collective-permute-start | bytes 1572872 | tf_op jit(solution)/shard_map/ppermute | solution.py:79
  73.1 16.9 %collective-permute-start.16 = (bf16[8,8,4096]{2,1,0:T(8,128)(2,1)S(1)}, bf16[8,8,4096]{2,1,0:T(8,128)(2,1)S(1)}, u32[]{:S(2)}, u32[]{:S(2)}) collective-permute-start(bf16[8,8,4096]{2,1,0:T(8,128)(2,1)S(1)} %fusion.12), channel_id=1, source_target_pairs={{0,8},{1,9},{2,10},{3,11},{4,12},{5,13},{6,14},{7,15},{8,0},{9,1},... | collective-permute-start | bytes 1572872 | tf_op jit(solution)/shard_map/ppermute | solution.py:79
  86.9 11.0 %collective-permute-start.12 = (bf16[4,8,4096]{2,1,0:T(8,128)(2,1)S(1)}, bf16[4,8,4096]{2,1,0:T(8,128)(2,1)S(1)}, u32[]{:S(2)}, u32[]{:S(2)}) collective-permute-start(bf16[4,8,4096]{2,1,0:T(8,128)(2,1)S(1)} %fusion.13), channel_id=1, source_target_pairs={{0,6},{1,7},{2,4},{3,5},{4,2},{5,3},{6,0},{7,1},{8,14},{9,15},{10,... | collective-permute-start | bytes 786440 | tf_op jit(solution)/shard_map/ppermute | solution.py:79
  90.2 11.0 %collective-permute-start.17 = (bf16[4,8,4096]{2,1,0:T(8,128)(2,1)S(1)}, bf16[4,8,4096]{2,1,0:T(8,128)(2,1)S(1)}, u32[]{:S(2)}, u32[]{:S(2)}) collective-permute-start(bf16[4,8,4096]{2,1,0:T(8,128)(2,1)S(1)} %fusion.14), channel_id=1, source_target_pairs={{0,24},{1,25},{2,26},{3,27},{4,28},{5,29},{6,30},{7,31},{8,16},{9,... | collective-permute-start | bytes 786440 | tf_op jit(solution)/shard_map/ppermute | solution.py:79
  104.9 8.3 %collective-permute-start.14 = (bf16[1,8,4096]{2,1,0:T(8,128)(2,1)S(1)}, bf16[1,8,4096]{2,1,0:T(8,128)(2,1)S(1)}, u32[]{:S(2)}, u32[]{:S(2)}) collective-permute-start(bf16[1,8,4096]{2,1,0:T(8,128)(2,1)S(1)} %dynamic-slice_convert_fusion.7), channel_id=1, source_target_pairs={{0,24},{1,25},{2,26},{3,27},{4,28},{5,29},{6,30},{7,31},{8,16},{9,... | collective-permute-start | bytes 196616 | tf_op jit(solution)/shard_map/ppermute | solution.py:79
  108.3 7.4 %collective-permute-start.19 = (bf16[1,8,4096]{2,1,0:T(8,128)(2,1)S(1)}, bf16[1,8,4096]{2,1,0:T(8,128)(2,1)S(1)}, u32[]{:S(2)}, u32[]{:S(2)}) collective-permute-start(bf16[1,8,4096]{2,1,0:T(8,128)(2,1)S(1)} %dynamic-slice_convert_fusion.6), channel_id=1, source_target_pairs={{0,6},{1,7},{2,4},{3,5},{4,2},{5,3},{6,0},{7,1},{8,14},{9,15},{10,... | collective-permute-start | bytes 196616 | tf_op jit(solution)/shard_map/ppermute | solution.py:79
  122.6 9.2 %collective-permute-start.21 = (bf16[8,8192]{1,0:T(8,128)(2,1)S(1)}, bf16[8,8192]{1,0:T(8,128)(2,1)S(1)}, u32[]{:S(2)}, u32[]{:S(2)}) collective-permute-start(bf16[8,8192]{1,0:T(8,128)(2,1)S(1)} %add_convert_fusion.2), channel_id=1, source_target_pairs={{0,64},{32,96},{64,0},{96,32},{128,192},{160,224},{192,128},{224,1... | collective-permute-start | bytes 393224 | tf_op jit(solution)/shard_map/ppermute | solution.py:20
  131.8 15.0 %collective-permute-start.22 = (bf16[8,8192]{1,0:T(8,128)(2,1)S(1)}, bf16[8,8192]{1,0:T(8,128)(2,1)S(1)}, u32[]{:S(2)}, u32[]{:S(2)}) collective-permute-start(bf16[8,8192]{1,0:T(8,128)(2,1)S(1)} %add_convert_fusion.1), channel_id=1, source_target_pairs={{0,128},{32,160},{64,192},{96,224},{128,0},{160,32},{192,64},{224,... | collective-permute-start | bytes 393224 | tf_op jit(solution)/shard_map/ppermute | solution.py:20
  146.9 18.1 %collective-permute-start.23 = (bf16[8,8192]{1,0:T(8,128)(2,1)S(1)}, bf16[8,8192]{1,0:T(8,128)(2,1)S(1)}, u32[]{:S(2)}, u32[]{:S(2)}) collective-permute-start(bf16[8,8192]{1,0:T(8,128)(2,1)S(1)} %add_convert_fusion), channel_id=1, source_target_pairs={{0,256},{32,288},{64,320},{96,352},{128,384},{160,416},{192,448},{... | collective-permute-start | bytes 393224 | tf_op jit(solution)/shard_map/ppermute | solution.py:20
  166.6 7.4 %collective-permute-start.24 = (bf16[1,8,4096]{2,1,0:T(8,128)(2,1)S(1)}, bf16[1,8,4096]{2,1,0:T(8,128)(2,1)S(1)}, u32[]{:S(2)}, u32[]{:S(2)}) collective-permute-start(bf16[1,8,4096]{2,1,0:T(8,128)(2,1)S(1)} %get-tuple-element.10), channel_id=1, source_target_pairs={{0,24},{1,25},{2,26},{3,27},{4,28},{5,29},{6,30},{7,31},{8,16},{9,... | collective-permute-start | bytes 196616 | tf_op jit(solution)/shard_map/ppermute | solution.py:88
  171.4 7.4 %collective-permute-start.29 = (bf16[1,8,4096]{2,1,0:T(8,128)(2,1)S(1)}, bf16[1,8,4096]{2,1,0:T(8,128)(2,1)S(1)}, u32[]{:S(2)}, u32[]{:S(2)}) collective-permute-start(bf16[1,8,4096]{2,1,0:T(8,128)(2,1)S(1)} %get-tuple-element.11), channel_id=1, source_target_pairs={{0,6},{1,7},{2,4},{3,5},{4,2},{5,3},{6,0},{7,1},{8,14},{9,15},{10,... | collective-permute-start | bytes 196616 | tf_op jit(solution)/shard_map/ppermute | solution.py:88
  180.9 9.5 %collective-permute-start.26 = (bf16[4,8,4096]{2,1,0:T(8,128)(2,1)S(1)}, bf16[4,8,4096]{2,1,0:T(8,128)(2,1)S(1)}, u32[]{:S(2)}, u32[]{:S(2)}) collective-permute-start(bf16[4,8,4096]{2,1,0:T(8,128)(2,1)S(1)} %bitcast.206), channel_id=1, source_target_pairs={{0,6},{1,7},{2,4},{3,5},{4,2},{5,3},{6,0},{7,1},{8,14},{9,15},{10,... | collective-permute-start | bytes 786440 | tf_op jit(solution)/shard_map/ppermute | solution.py:88
  185.8 9.5 %collective-permute-start.31 = (bf16[4,8,4096]{2,1,0:T(8,128)(2,1)S(1)}, bf16[4,8,4096]{2,1,0:T(8,128)(2,1)S(1)}, u32[]{:S(2)}, u32[]{:S(2)}) collective-permute-start(bf16[4,8,4096]{2,1,0:T(8,128)(2,1)S(1)} %bitcast.210), channel_id=1, source_target_pairs={{0,24},{1,25},{2,26},{3,27},{4,28},{5,29},{6,30},{7,31},{8,16},{9,... | collective-permute-start | bytes 786440 | tf_op jit(solution)/shard_map/ppermute | solution.py:88
  190.6 11.1 %collective-permute-start.27 = (bf16[8,8,4096]{2,1,0:T(8,128)(2,1)S(1)}, bf16[8,8,4096]{2,1,0:T(8,128)(2,1)S(1)}, u32[]{:S(2)}, u32[]{:S(2)}) collective-permute-start(bf16[8,8,4096]{2,1,0:T(8,128)(2,1)S(1)} %bitcast.194), channel_id=1, source_target_pairs={{0,2},{1,3},{2,0},{3,1},{4,6},{5,7},{6,4},{7,5},{8,10},{9,11},{10,... | collective-permute-start | bytes 1572872 | tf_op jit(solution)/shard_map/ppermute | solution.py:88
  195.4 11.1 %collective-permute-start.32 = (bf16[8,8,4096]{2,1,0:T(8,128)(2,1)S(1)}, bf16[8,8,4096]{2,1,0:T(8,128)(2,1)S(1)}, u32[]{:S(2)}, u32[]{:S(2)}) collective-permute-start(bf16[8,8,4096]{2,1,0:T(8,128)(2,1)S(1)} %bitcast.196), channel_id=1, source_target_pairs={{0,8},{1,9},{2,10},{3,11},{4,12},{5,13},{6,14},{7,15},{8,0},{9,1},... | collective-permute-start | bytes 1572872 | tf_op jit(solution)/shard_map/ppermute | solution.py:88
  267.9 11.6 %collective-permute-start.41 = (f32[1,128]{1,0:T(1,128)S(1)}, f32[1,128]{1,0:T(1,128)S(1)}, u32[]{:S(2)}, u32[]{:S(2)}) collective-permute-start(f32[1,128]{1,0:T(1,128)S(1)} %add.249), channel_id=1, source_target_pairs={{0,128},{32,160},{64,192},{96,224},{128,0},{160,32},{192,64},{224,... | collective-permute-start | bytes 1544 | tf_op jit(solution)/shard_map/ppermute | solution.py:20
  279.5 14.1 %collective-permute-start.42 = (f32[1,128]{1,0:T(1,128)S(1)}, f32[1,128]{1,0:T(1,128)S(1)}, u32[]{:S(2)}, u32[]{:S(2)}) collective-permute-start(f32[1,128]{1,0:T(1,128)S(1)} %add.250), channel_id=1, source_target_pairs={{0,256},{32,288},{64,320},{96,352},{128,384},{160,416},{192,448},{... | collective-permute-start | bytes 1544 | tf_op jit(solution)/shard_map/ppermute | solution.py:20
  (28 other events, 142.6 us)

commit v6 on v5

--- a/solution.py
+++ b/solution.py
@@ -9,15 +9,11 @@
 epsilon = 1e-06
 
 
-def xor_pairs(n, bit):
-    return [(i, i ^ (1 << bit)) for i in range(n)]
-
-
-def butterfly_sum(x, axis, n, send_dtype):
+def butterfly_sum(x, axis, n, send_dtype, masks):
     acc = x
-    for bit in range(n.bit_length() - 1):
+    for mask in masks:
         sent = acc.astype(send_dtype)
-        acc = sent.astype(jnp.float32) + lax.ppermute(sent, axis, xor_pairs(n, bit)).astype(jnp.float32)
+        acc = sent.astype(jnp.float32) + lax.ppermute(sent, axis, masked_pairs(n, mask)).astype(jnp.float32)
     return acc
 
 
@@ -25,6 +21,8 @@
 LAT_MASKS = (CORE, X1, X3, Y1, Y3)
 ORDER_X_FIRST = (CORE, X1, X3, Y1, Y3)
 ORDER_Y_FIRST = (CORE, Y1, Y3, X1, X3)
+ORDERS = (ORDER_X_FIRST, ORDER_Y_FIRST)
+GRP_MASKS = (1, 2, 4, 12)
 
 
 def logical_rank(r, masks):
@@ -88,17 +86,20 @@
         got = lax.ppermute(acc, "lat", masked_pairs(n, masks[j]))
         pair = jnp.stack([acc, got])
         acc = jnp.where(bit == 0, pair, pair[::-1]).reshape((2 * acc.shape[0],) + acc.shape[1:])
-    order = np.array([logical_rank(r, masks) for r in range(n)], dtype=np.int32)
-    return jnp.take(acc, order, axis=0)
+    return acc
 
 
-def lat_gather(x, rank, n):
+def column_halves(x, rank, n):
     cols = x.shape[1] // 2
-    parts = [
-        doubling_gather(x[:, k * cols:(k + 1) * cols], rank, n, masks)
-        for k, masks in enumerate((ORDER_X_FIRST, ORDER_Y_FIRST))
-    ]
-    return jnp.concatenate(parts, axis=2).reshape(n * x.shape[0], x.shape[1])
+    return [doubling_gather(x[:, k * cols:(k + 1) * cols], rank, n, masks) for k, masks in enumerate(ORDERS)]
+
+
+def block_perm(src_masks, dst_masks, n):
+    return np.array([logical_rank(lat_rank_of(p, dst_masks), src_masks) for p in range(n)], dtype=np.int32)
+
+
+def take_blocks(x, perm, rows):
+    return jnp.take(x.reshape((len(perm), rows) + x.shape[1:]), perm, axis=0).reshape(x.shape)
 
 
 def body(stream, batch_index, weight, enc_bias, dec_bias):
@@ -106,35 +107,49 @@
     n_lat = lax.axis_size("lat")
     n_grp = lax.axis_size("grp")
     rank_lat = lax.axis_index("lat")
-    gathered = lat_gather(stream, rank_lat, n_lat)
-    n_rows = gathered.shape[0]
-    onehot = (batch_index[:, None] == lax.broadcasted_iota(jnp.int32, (batch_index.shape[0], n_rows), 1)).astype(
-        gathered.dtype
+    n_tok = batch_index.shape[0]
+    cols = weight.shape[0] // 2
+    order_a, order_b = ORDERS
+    token_of_row = np.array(
+        [lat_rank_of(i // own_rows, order_a) * own_rows + i % own_rows for i in range(n_tok)], dtype=np.int32
     )
-    batch = jnp.dot(onehot, gathered, preferred_element_type=jnp.float32).astype(jnp.bfloat16)
+    src = jnp.take(batch_index, token_of_row)
+    stream_halves = column_halves(stream, rank_lat, n_lat)
+    batch_halves = []
+    for masks, rows in zip(ORDERS, stream_halves):
+        place = logical_rank(src // own_rows, masks) * own_rows + src % own_rows
+        onehot = (place[:, None] == lax.broadcasted_iota(jnp.int32, (n_tok, n_tok), 1)).astype(rows.dtype)
+        batch_halves.append(
+            jnp.dot(onehot, rows.reshape(n_tok, cols), preferred_element_type=jnp.float32).astype(jnp.bfloat16)
+        )
+    batch = jnp.concatenate(batch_halves, axis=1)
     centered = (batch.astype(jnp.float32) - dec_bias).astype(jnp.bfloat16)
     preact = jnp.dot(centered, weight, preferred_element_type=jnp.float32) + enc_bias
     active = (jax.nn.softplus(sharpness * preact) / sharpness).astype(jnp.bfloat16)
-    first_row = rank_lat * own_rows
-    own_batch = lax.dynamic_slice_in_dim(batch, first_row, own_rows, 0)
-    blocks = active.reshape(n_lat, own_rows, -1)
-    cols = weight.shape[0] // 2
+    own_block = logical_rank(rank_lat, order_a)
+    own_batch = lax.dynamic_slice_in_dim(batch, own_block * own_rows, own_rows, 0)
+    active_b = take_blocks(active, block_perm(order_a, order_b, n_lat), own_rows)
     halves = []
-    for k, masks in enumerate((ORDER_X_FIRST, ORDER_Y_FIRST)):
-        order = np.array([lat_rank_of(p, masks) for p in range(n_lat)], dtype=np.int32)
-        rows = jnp.take(blocks, order, axis=0).reshape(active.shape)
+    for k, (masks, rows) in enumerate(zip(ORDERS, (active, active_b))):
         part = lax.dot_general(
             rows, weight[k * cols:(k + 1) * cols], (((1,), (1,)), ((), ())), preferred_element_type=jnp.float32
         ).astype(jnp.bfloat16)
         halves.append(halving_scatter(part.reshape(n_lat, own_rows, cols), rank_lat, n_lat, masks))
     block_recon = jnp.concatenate(halves, axis=1)
-    recon = butterfly_sum(block_recon.astype(jnp.float32), "grp", n_grp, jnp.bfloat16)
+    recon = butterfly_sum(block_recon.astype(jnp.float32), "grp", n_grp, jnp.bfloat16, GRP_MASKS)
     error_own = recon + dec_bias - own_batch.astype(jnp.float32)
     grad_own = (2.0 * error_own).astype(jnp.bfloat16)
-    grad_rows = lat_gather(grad_own, rank_lat, n_lat)
-    grad_active = jnp.dot(grad_rows, weight, preferred_element_type=jnp.float32)
-    decoder_grad = lax.dot_general(
-        grad_rows, active, (((0,), (0,)), ((), ())), preferred_element_type=jnp.float32
+    grad_a, grad_b = [g.reshape(n_tok, cols) for g in column_halves(grad_own, rank_lat, n_lat)]
+    active_part_b = jnp.dot(grad_b, weight[cols:], preferred_element_type=jnp.float32)
+    grad_active = jnp.dot(grad_a, weight[:cols], preferred_element_type=jnp.float32) + take_blocks(
+        active_part_b, block_perm(order_b, order_a, n_lat), own_rows
+    )
+    decoder_grad = jnp.concatenate(
+        [
+            lax.dot_general(g, a, (((0,), (0,)), ((), ())), preferred_element_type=jnp.float32)
+            for g, a in ((grad_a, active), (grad_b, active_b))
+        ],
+        axis=0,
     )
     grad_pre = (grad_active + penalty) * jax.nn.sigmoid(sharpness * preact)
     encoder_grad = lax.dot_general(
@@ -149,7 +164,7 @@
     squares = jnp.broadcast_to(local_squares, (1, 128))
     for mask in LAT_MASKS:
         squares = squares + lax.ppermute(squares, "lat", masked_pairs(n_lat, mask))
-    total_squares = butterfly_sum(squares, "grp", n_grp, jnp.float32)[0, 0]
+    total_squares = butterfly_sum(squares, "grp", n_grp, jnp.float32, GRP_MASKS)[0, 0]
     entries = (weight.shape[0] + 1) * weight.shape[1] * n_lat * n_grp
     factor = jnp.minimum(1.0, 1.0 / jnp.sqrt(total_squares / entries + epsilon))
     return (

time: 300 us -> 281 us (0.937)
  starting transfers between devices: 154 us -> 140 us
  waiting for transfers between devices: 91.4 us -> 94.9 us
  matrix products: 19.6 us -> 16.6 us
    ppermute x8, starting transfers between devices: 58.2 us -> 42.9 us  [butterfly_sum(): lax.ppermute(sent, axis, masked_pairs(n, mask)).astype(jnp.float32)]
    dot_general x3 -> x6, matrix products: 12.9 us -> 6.07 us  [the longest x2 3.12 us: body(): lax.dot_general(g, a, (((0,), (0,)), ((), ())), preferred_element_type=jn...]
    gather x6 -> x3, local copies, waits for them, and re-layouts: 9.25 us -> 3.13 us  [the longest x1 1.95 us: body(): src = jnp.take(batch_index, token_of_row)]
    dot_general x1, matrix products: 1.51 us -> 6.4 us  [body(): lax.dot_general(centered, grad_pre.astype(jnp.bfloat16), (((0,), (0,)), (...]
    unnamed x18 -> x30, local copies, waits for them, and re-layouts: 1.37 us -> 4.84 us
    ppermute x8, waiting for transfers between devices: 28.4 us -> 31.6 us  [butterfly_sum(): lax.ppermute(sent, axis, masked_pairs(n, mask)).astype(jnp.float32)]
  transfers between devices with their start and end apart: 43 -> 43, of which waited for: 33 -> 32; matrix products, arithmetic and copies ran while one was open for 4% -> 4% of each run, Pallas kernels for 0% -> 0%
where the time goes in v6:
time: 281 us; the launch traced here: 279 us
  starting transfers between devices  140 us (50%)
  waiting for transfers between devices  94.9 us (34%)
  matrix products  16.6 us (6%)
  other arithmetic  14.4 us (5%)
  local copies, waits for them, and re-layouts  10.4 us (4%)
  between operations  3.14 us (1%)
    ppermute x20, starting transfers between devices, doubling_gather(): got = lax.ppermute(acc, 'lat', masked_pairs(n, masks[j]))  55.7 us
    ppermute x8, starting transfers between devices, butterfly_sum(): lax.ppermute(sent, axis, masked_pairs(n, mask)).astype(jnp.float32)  42.9 us
    ppermute x8, waiting for transfers between devices, butterfly_sum(): lax.ppermute(sent, axis, masked_pairs(n, mask)).astype(jnp.float32)  31.6 us
    ppermute x10, starting transfers between devices, halving_scatter(): lax.ppermute(sent, 'lat', masked_pairs(n, mask)).astype(jnp.float32)  29.4 us
    ppermute x20, waiting for transfers between devices, doubling_gather(): got = lax.ppermute(acc, 'lat', masked_pairs(n, masks[j]))  29.1 us
    ppermute x10, waiting for transfers between devices, halving_scatter(): lax.ppermute(sent, 'lat', masked_pairs(n, mask)).astype(jnp.float32)  18.9 us
    ppermute x5, waiting for transfers between devices, body(): squares = squares + lax.ppermute(squares, 'lat', masked_pairs(n_lat, mask))  15.3 us
    ppermute x5, starting transfers between devices, body(): squares = squares + lax.ppermute(squares, 'lat', masked_pairs(n_lat, mask))  11.8 us
  transfers between devices with their start and end apart: 43, of which 32 were waited for; matrix products, arithmetic and copies ran while one was open for 4% of the time, Pallas kernels for 0%

profile of v6, /device:TPU:6, one launch (start us, length us, event | category | flops | bytes accessed | tf_op | source)
XLA Modules:
  0.0 279.3 jit_solution(16909149450828491135)
XLA Ops:
  1.5 4.9 %collective-permute-start = (bf16[1,8,4096]{2,1,0:T(8,128)(2,1)S(1)}, bf16[1,8,4096]{2,1,0:T(8,128)(2,1)S(1)}, u32[]{:S(2)}, u32[]{:S(2)}) collective-permute-start(bf16[1,8,4096]{2,1,0:T(8,128)(2,1)S(1)} %get-tuple-element.18), channel_id=1, source_target_pairs={{0,24},{1,25},{2,26},{3,27},{4,28},{5,29},{6,30},{7,31},{8,16},{9,... | collective-permute-start | bytes 196616 | tf_op jit(solution)/shard_map/ppermute | solution.py:86
  6.5 4.8 %collective-permute-start.5 = (bf16[1,8,4096]{2,1,0:T(8,128)(2,1)S(1)}, bf16[1,8,4096]{2,1,0:T(8,128)(2,1)S(1)}, u32[]{:S(2)}, u32[]{:S(2)}) collective-permute-start(bf16[1,8,4096]{2,1,0:T(8,128)(2,1)S(1)} %get-tuple-element.19), channel_id=1, source_target_pairs={{0,6},{1,7},{2,4},{3,5},{4,2},{5,3},{6,0},{7,1},{8,14},{9,15},{10,... | collective-permute-start | bytes 196616 | tf_op jit(solution)/shard_map/ppermute | solution.py:86
  23.8 4.4 %collective-permute-start.7 = (bf16[4,8,4096]{2,1,0:T(8,128)(2,1)S(1)}, bf16[4,8,4096]{2,1,0:T(8,128)(2,1)S(1)}, u32[]{:S(2)}, u32[]{:S(2)}) collective-permute-start(bf16[4,8,4096]{2,1,0:T(8,128)(2,1)S(1)} %bitcast.210), channel_id=1, source_target_pairs={{0,24},{1,25},{2,26},{3,27},{4,28},{5,29},{6,30},{7,31},{8,16},{9,... | collective-permute-start | bytes 786440 | tf_op jit(solution)/shard_map/ppermute | solution.py:86
  36.0 5.7 %collective-permute-done.3 = bf16[8,8,4096]{2,1,0:T(8,128)(2,1)S(1)} collective-permute-done((bf16[8,8,4096]{2,1,0:T(8,128)(2,1)S(1)}, bf16[8,8,4096]{2,1,0:T(8,128)(2,1)S(1)}, u32[]{:S(2)}, u32[]{:S(2)}) %collective-permute-start.3) | collective-permute-done | bytes 524320 | tf_op jit(solution)/shard_map/ppermute | solution.py:86
  69.4 11.4 %collective-permute-done.11 = bf16[8,8,4096]{2,1,0:T(8,128)(2,1)S(1)} collective-permute-done((bf16[8,8,4096]{2,1,0:T(8,128)(2,1)S(1)}, bf16[8,8,4096]{2,1,0:T(8,128)(2,1)S(1)}, u32[]{:S(2)}, u32[]{:S(2)}) %collective-permute-start.11) | collective-permute-done | bytes 524320 | tf_op jit(solution)/shard_map/ppermute | solution.py:77
  84.2 5.1 %collective-permute-start.17 = (bf16[4,8,4096]{2,1,0:T(8,128)(2,1)S(1)}, bf16[4,8,4096]{2,1,0:T(8,128)(2,1)S(1)}, u32[]{:S(2)}, u32[]{:S(2)}) collective-permute-start(bf16[4,8,4096]{2,1,0:T(8,128)(2,1)S(1)} %fusion.14), channel_id=1, source_target_pairs={{0,24},{1,25},{2,26},{3,27},{4,28},{5,29},{6,30},{7,31},{8,16},{9,... | collective-permute-start | bytes 786440 | tf_op jit(solution)/shard_map/ppermute | solution.py:77
  98.5 3.9 %collective-permute-start.14 = (bf16[1,8,4096]{2,1,0:T(8,128)(2,1)S(1)}, bf16[1,8,4096]{2,1,0:T(8,128)(2,1)S(1)}, u32[]{:S(2)}, u32[]{:S(2)}) collective-permute-start(bf16[1,8,4096]{2,1,0:T(8,128)(2,1)S(1)} %dynamic-slice_convert_fusion.7), channel_id=1, source_target_pairs={{0,24},{1,25},{2,26},{3,27},{4,28},{5,29},{6,30},{7,31},{8,16},{9,... | collective-permute-start | bytes 196616 | tf_op jit(solution)/shard_map/ppermute | solution.py:77
  102.6 4.3 %collective-permute-start.19 = (bf16[1,8,4096]{2,1,0:T(8,128)(2,1)S(1)}, bf16[1,8,4096]{2,1,0:T(8,128)(2,1)S(1)}, u32[]{:S(2)}, u32[]{:S(2)}) collective-permute-start(bf16[1,8,4096]{2,1,0:T(8,128)(2,1)S(1)} %dynamic-slice_convert_fusion.6), channel_id=1, source_target_pairs={{0,6},{1,7},{2,4},{3,5},{4,2},{5,3},{6,0},{7,1},{8,14},{9,15},{10,... | collective-permute-start | bytes 196616 | tf_op jit(solution)/shard_map/ppermute | solution.py:77
  112.2 4.6 %collective-permute-done.20 = bf16[8,8192]{1,0:T(8,128)(2,1)S(1)} collective-permute-done((bf16[8,8192]{1,0:T(8,128)(2,1)S(1)}, bf16[8,8192]{1,0:T(8,128)(2,1)S(1)}, u32[]{:S(2)}, u32[]{:S(2)}) %collective-permute-start.20) | collective-permute-done | bytes 131104 | tf_op jit(solution)/shard_map/ppermute | solution.py:16
  116.9 3.8 %collective-permute-start.21 = (bf16[8,8192]{1,0:T(8,128)(2,1)S(1)}, bf16[8,8192]{1,0:T(8,128)(2,1)S(1)}, u32[]{:S(2)}, u32[]{:S(2)}) collective-permute-start(bf16[8,8192]{1,0:T(8,128)(2,1)S(1)} %add_convert_fusion.2), channel_id=1, source_target_pairs={{0,64},{32,96},{64,0},{96,32},{128,192},{160,224},{192,128},{224,1... | collective-permute-start | bytes 393224 | tf_op jit(solution)/shard_map/ppermute | solution.py:16
  120.7 5.3 %collective-permute-done.21 = bf16[8,8192]{1,0:T(8,128)(2,1)S(1)} collective-permute-done((bf16[8,8192]{1,0:T(8,128)(2,1)S(1)}, bf16[8,8192]{1,0:T(8,128)(2,1)S(1)}, u32[]{:S(2)}, u32[]{:S(2)}) %collective-permute-start.21) | collective-permute-done | bytes 131104 | tf_op jit(solution)/shard_map/ppermute | solution.py:16
  126.1 8.5 %collective-permute-start.22 = (bf16[8,8192]{1,0:T(8,128)(2,1)S(1)}, bf16[8,8192]{1,0:T(8,128)(2,1)S(1)}, u32[]{:S(2)}, u32[]{:S(2)}) collective-permute-start(bf16[8,8192]{1,0:T(8,128)(2,1)S(1)} %add_convert_fusion.1), channel_id=1, source_target_pairs={{0,128},{32,160},{64,192},{96,224},{128,0},{160,32},{192,64},{224,... | collective-permute-start | bytes 393224 | tf_op jit(solution)/shard_map/ppermute | solution.py:16
  134.6 7.1 %collective-permute-done.22 = bf16[8,8192]{1,0:T(8,128)(2,1)S(1)} collective-permute-done((bf16[8,8192]{1,0:T(8,128)(2,1)S(1)}, bf16[8,8192]{1,0:T(8,128)(2,1)S(1)}, u32[]{:S(2)}, u32[]{:S(2)}) %collective-permute-start.22) | collective-permute-done | bytes 131104 | tf_op jit(solution)/shard_map/ppermute | solution.py:16
  141.8 6.4 %collective-permute-start.23 = (bf16[8,8192]{1,0:T(8,128)(2,1)S(1)}, bf16[8,8192]{1,0:T(8,128)(2,1)S(1)}, u32[]{:S(2)}, u32[]{:S(2)}) collective-permute-start(bf16[8,8192]{1,0:T(8,128)(2,1)S(1)} %add_convert_fusion), channel_id=1, source_target_pairs={{0,384},{32,416},{64,448},{96,480},{128,256},{160,288},{192,320},{... | collective-permute-start | bytes 393224 | tf_op jit(solution)/shard_map/ppermute | solution.py:16
  148.2 4.5 %collective-permute-done.23 = bf16[8,8192]{1,0:T(8,128)(2,1)S(1)} collective-permute-done((bf16[8,8192]{1,0:T(8,128)(2,1)S(1)}, bf16[8,8192]{1,0:T(8,128)(2,1)S(1)}, u32[]{:S(2)}, u32[]{:S(2)}) %collective-permute-start.23) | collective-permute-done | bytes 131104 | tf_op jit(solution)/shard_map/ppermute | solution.py:16
  154.4 4.6 %collective-permute-start.24 = (bf16[1,8,4096]{2,1,0:T(8,128)(2,1)S(1)}, bf16[1,8,4096]{2,1,0:T(8,128)(2,1)S(1)}, u32[]{:S(2)}, u32[]{:S(2)}) collective-permute-start(bf16[1,8,4096]{2,1,0:T(8,128)(2,1)S(1)} %get-tuple-element.10), channel_id=1, source_target_pairs={{0,24},{1,25},{2,26},{3,27},{4,28},{5,29},{6,30},{7,31},{8,16},{9,... | collective-permute-start | bytes 196616 | tf_op jit(solution)/shard_map/ppermute | solution.py:86
  168.9 4.2 %collective-permute-start.26 = (bf16[4,8,4096]{2,1,0:T(8,128)(2,1)S(1)}, bf16[4,8,4096]{2,1,0:T(8,128)(2,1)S(1)}, u32[]{:S(2)}, u32[]{:S(2)}) collective-permute-start(bf16[4,8,4096]{2,1,0:T(8,128)(2,1)S(1)} %bitcast.204), channel_id=1, source_target_pairs={{0,6},{1,7},{2,4},{3,5},{4,2},{5,3},{6,0},{7,1},{8,14},{9,15},{10,... | collective-permute-start | bytes 786440 | tf_op jit(solution)/shard_map/ppermute | solution.py:86
  184.9 4.7 %collective-permute-done.27 = bf16[8,8,4096]{2,1,0:T(8,128)(2,1)S(1)} collective-permute-done((bf16[8,8,4096]{2,1,0:T(8,128)(2,1)S(1)}, bf16[8,8,4096]{2,1,0:T(8,128)(2,1)S(1)}, u32[]{:S(2)}, u32[]{:S(2)}) %collective-permute-start.27) | collective-permute-done | bytes 524320 | tf_op jit(solution)/shard_map/ppermute | solution.py:86
  208.0 6.4 %multiply_reduce_fusion = (f32[]{:T(128)}, f32[8192,128]{1,0:T(8,128)}) fusion(f32[4096,128]{1,0:T(8,128)S(1)} %fusion.33, f32[4096,128]{1,0:T(8,128)S(1)} %fusion.41, bf16[256,128]{1,0:T(8,128)(2,1)S(1)} %get-tuple-element.28, bf16[256,4096]{1,0:T(8,128)(2,1)S(1)} %copy-done.6, bf16[256,4096]{1,0:T(8,128)(2,1)S(1)} %copy-done.4, f32[8192]{0:T(1024)S(1)} %copy-done.12), kind=kOutput, calls=%fused_computation.13 | convolution fusion | flops 553648128 | bytes 12681220 | tf_op jit(solution)/shard_map/dot_general | solution.py:155
  227.1 3.7 %collective-permute-done.36 = f32[1,128]{1,0:T(1,128)S(1)} collective-permute-done((f32[1,128]{1,0:T(1,128)S(1)}, f32[1,128]{1,0:T(1,128)S(1)}, u32[]{:S(2)}, u32[]{:S(2)}) %collective-permute-start.36) | collective-permute-done | bytes 544 | tf_op jit(solution)/shard_map/ppermute | solution.py:166
  248.3 6.4 %collective-permute-start.40 = (f32[1,128]{1,0:T(1,128)S(1)}, f32[1,128]{1,0:T(1,128)S(1)}, u32[]{:S(2)}, u32[]{:S(2)}) collective-permute-start(f32[1,128]{1,0:T(1,128)S(1)} %add.295), channel_id=1, source_target_pairs={{0,64},{32,96},{64,0},{96,32},{128,192},{160,224},{192,128},{224,1... | collective-permute-start | bytes 1544 | tf_op jit(solution)/shard_map/ppermute | solution.py:16
  256.2 5.7 %collective-permute-start.41 = (f32[1,128]{1,0:T(1,128)S(1)}, f32[1,128]{1,0:T(1,128)S(1)}, u32[]{:S(2)}, u32[]{:S(2)}) collective-permute-start(f32[1,128]{1,0:T(1,128)S(1)} %add.296), channel_id=1, source_target_pairs={{0,128},{32,160},{64,192},{96,224},{128,0},{160,32},{192,64},{224,... | collective-permute-start | bytes 1544 | tf_op jit(solution)/shard_map/ppermute | solution.py:16
  265.6 7.8 %collective-permute-start.42 = (f32[1,128]{1,0:T(1,128)S(1)}, f32[1,128]{1,0:T(1,128)S(1)}, u32[]{:S(2)}, u32[]{:S(2)}) collective-permute-start(f32[1,128]{1,0:T(1,128)S(1)} %add.297), channel_id=1, source_target_pairs={{0,384},{32,416},{64,448},{96,480},{128,256},{160,288},{192,320},{... | collective-permute-start | bytes 1544 | tf_op jit(solution)/shard_map/ppermute | solution.py:16
  275.5 3.7 %multiply_convert_fusion = bf16[8192,128]{1,0:T(8,128)(2,1)} fusion(f32[8192,128]{1,0:T(8,128)} %get-tuple-element.26, f32[]{:T(128)} %bitcast.99), kind=kLoop, calls=%fused_computation.12 | loop fusion | flops 2097152 | bytes 6291460 | tf_op jit(solution)/shard_map/convert_element_type | solution.py:171
  (190 shorter events, 143.9 us)
Async XLA Ops:
  1.5 12.5 %collective-permute-start = (bf16[1,8,4096]{2,1,0:T(8,128)(2,1)S(1)}, bf16[1,8,4096]{2,1,0:T(8,128)(2,1)S(1)}, u32[]{:S(2)}, u32[]{:S(2)}) collective-permute-start(bf16[1,8,4096]{2,1,0:T(8,128)(2,1)S(1)} %get-tuple-element.18), channel_id=1, source_target_pairs={{0,24},{1,25},{2,26},{3,27},{4,28},{5,29},{6,30},{7,31},{8,16},{9,... | collective-permute-start | bytes 196616 | tf_op jit(solution)/shard_map/ppermute | solution.py:86
  6.5 9.5 %collective-permute-start.5 = (bf16[1,8,4096]{2,1,0:T(8,128)(2,1)S(1)}, bf16[1,8,4096]{2,1,0:T(8,128)(2,1)S(1)}, u32[]{:S(2)}, u32[]{:S(2)}) collective-permute-start(bf16[1,8,4096]{2,1,0:T(8,128)(2,1)S(1)} %get-tuple-element.19), channel_id=1, source_target_pairs={{0,6},{1,7},{2,4},{3,5},{4,2},{5,3},{6,0},{7,1},{8,14},{9,15},{10,... | collective-permute-start | bytes 196616 | tf_op jit(solution)/shard_map/ppermute | solution.py:86
  16.1 7.6 %collective-permute-start.6 = (bf16[2,8,4096]{2,1,0:T(8,128)(2,1)S(1)}, bf16[2,8,4096]{2,1,0:T(8,128)(2,1)S(1)}, u32[]{:S(2)}, u32[]{:S(2)}) collective-permute-start(bf16[2,8,4096]{2,1,0:T(8,128)(2,1)S(1)} %get-tuple-element.22), channel_id=1, source_target_pairs={{0,2},{1,3},{2,0},{3,1},{4,6},{5,7},{6,4},{7,5},{8,10},{9,11},{10,... | collective-permute-start | bytes 393224 | tf_op jit(solution)/shard_map/ppermute | solution.py:86
  21.0 9.5 %collective-permute-start.2 = (bf16[4,8,4096]{2,1,0:T(8,128)(2,1)S(1)}, bf16[4,8,4096]{2,1,0:T(8,128)(2,1)S(1)}, u32[]{:S(2)}, u32[]{:S(2)}) collective-permute-start(bf16[4,8,4096]{2,1,0:T(8,128)(2,1)S(1)} %bitcast.206), channel_id=1, source_target_pairs={{0,6},{1,7},{2,4},{3,5},{4,2},{5,3},{6,0},{7,1},{8,14},{9,15},{10,... | collective-permute-start | bytes 786440 | tf_op jit(solution)/shard_map/ppermute | solution.py:86
  23.8 9.5 %collective-permute-start.7 = (bf16[4,8,4096]{2,1,0:T(8,128)(2,1)S(1)}, bf16[4,8,4096]{2,1,0:T(8,128)(2,1)S(1)}, u32[]{:S(2)}, u32[]{:S(2)}) collective-permute-start(bf16[4,8,4096]{2,1,0:T(8,128)(2,1)S(1)} %bitcast.210), channel_id=1, source_target_pairs={{0,24},{1,25},{2,26},{3,27},{4,28},{5,29},{6,30},{7,31},{8,16},{9,... | collective-permute-start | bytes 786440 | tf_op jit(solution)/shard_map/ppermute | solution.py:86
  30.6 11.1 %collective-permute-start.3 = (bf16[8,8,4096]{2,1,0:T(8,128)(2,1)S(1)}, bf16[8,8,4096]{2,1,0:T(8,128)(2,1)S(1)}, u32[]{:S(2)}, u32[]{:S(2)}) collective-permute-start(bf16[8,8,4096]{2,1,0:T(8,128)(2,1)S(1)} %bitcast.196), channel_id=1, source_target_pairs={{0,2},{1,3},{2,0},{3,1},{4,6},{5,7},{6,4},{7,5},{8,10},{9,11},{10,... | collective-permute-start | bytes 1572872 | tf_op jit(solution)/shard_map/ppermute | solution.py:86
  33.4 12.3 %collective-permute-start.8 = (bf16[8,8,4096]{2,1,0:T(8,128)(2,1)S(1)}, bf16[8,8,4096]{2,1,0:T(8,128)(2,1)S(1)}, u32[]{:S(2)}, u32[]{:S(2)}) collective-permute-start(bf16[8,8,4096]{2,1,0:T(8,128)(2,1)S(1)} %bitcast.198), channel_id=1, source_target_pairs={{0,8},{1,9},{2,10},{3,11},{4,12},{5,13},{6,14},{7,15},{8,0},{9,1},... | collective-permute-start | bytes 1572872 | tf_op jit(solution)/shard_map/ppermute | solution.py:86
  64.9 15.9 %collective-permute-start.11 = (bf16[8,8,4096]{2,1,0:T(8,128)(2,1)S(1)}, bf16[8,8,4096]{2,1,0:T(8,128)(2,1)S(1)}, u32[]{:S(2)}, u32[]{:S(2)}) collective-permute-start(bf16[8,8,4096]{2,1,0:T(8,128)(2,1)S(1)} %fusion.11), channel_id=1, source_target_pairs={{0,2},{1,3},{2,0},{3,1},{4,6},{5,7},{6,4},{7,5},{8,10},{9,11},{10,... | collective-permute-start | bytes 1572872 | tf_op jit(solution)/shard_map/ppermute | solution.py:77
  67.2 16.8 %collective-permute-start.16 = (bf16[8,8,4096]{2,1,0:T(8,128)(2,1)S(1)}, bf16[8,8,4096]{2,1,0:T(8,128)(2,1)S(1)}, u32[]{:S(2)}, u32[]{:S(2)}) collective-permute-start(bf16[8,8,4096]{2,1,0:T(8,128)(2,1)S(1)} %fusion.12), channel_id=1, source_target_pairs={{0,8},{1,9},{2,10},{3,11},{4,12},{5,13},{6,14},{7,15},{8,0},{9,1},... | collective-permute-start | bytes 1572872 | tf_op jit(solution)/shard_map/ppermute | solution.py:77
  80.9 10.6 %collective-permute-start.12 = (bf16[4,8,4096]{2,1,0:T(8,128)(2,1)S(1)}, bf16[4,8,4096]{2,1,0:T(8,128)(2,1)S(1)}, u32[]{:S(2)}, u32[]{:S(2)}) collective-permute-start(bf16[4,8,4096]{2,1,0:T(8,128)(2,1)S(1)} %fusion.13), channel_id=1, source_target_pairs={{0,6},{1,7},{2,4},{3,5},{4,2},{5,3},{6,0},{7,1},{8,14},{9,15},{10,... | collective-permute-start | bytes 786440 | tf_op jit(solution)/shard_map/ppermute | solution.py:77
  84.2 10.6 %collective-permute-start.17 = (bf16[4,8,4096]{2,1,0:T(8,128)(2,1)S(1)}, bf16[4,8,4096]{2,1,0:T(8,128)(2,1)S(1)}, u32[]{:S(2)}, u32[]{:S(2)}) collective-permute-start(bf16[4,8,4096]{2,1,0:T(8,128)(2,1)S(1)} %fusion.14), channel_id=1, source_target_pairs={{0,24},{1,25},{2,26},{3,27},{4,28},{5,29},{6,30},{7,31},{8,16},{9,... | collective-permute-start | bytes 786440 | tf_op jit(solution)/shard_map/ppermute | solution.py:77
  94.9 7.6 %collective-permute-start.18 = (bf16[2,8,4096]{2,1,0:T(8,128)(2,1)S(1)}, bf16[2,8,4096]{2,1,0:T(8,128)(2,1)S(1)}, u32[]{:S(2)}, u32[]{:S(2)}) collective-permute-start(bf16[2,8,4096]{2,1,0:T(8,128)(2,1)S(1)} %fusion.18), channel_id=1, source_target_pairs={{0,2},{1,3},{2,0},{3,1},{4,6},{5,7},{6,4},{7,5},{8,10},{9,11},{10,... | collective-permute-start | bytes 393224 | tf_op jit(solution)/shard_map/ppermute | solution.py:77
  98.5 8.3 %collective-permute-start.14 = (bf16[1,8,4096]{2,1,0:T(8,128)(2,1)S(1)}, bf16[1,8,4096]{2,1,0:T(8,128)(2,1)S(1)}, u32[]{:S(2)}, u32[]{:S(2)}) collective-permute-start(bf16[1,8,4096]{2,1,0:T(8,128)(2,1)S(1)} %dynamic-slice_convert_fusion.7), channel_id=1, source_target_pairs={{0,24},{1,25},{2,26},{3,27},{4,28},{5,29},{6,30},{7,31},{8,16},{9,... | collective-permute-start | bytes 196616 | tf_op jit(solution)/shard_map/ppermute | solution.py:77
  116.9 9.2 %collective-permute-start.21 = (bf16[8,8192]{1,0:T(8,128)(2,1)S(1)}, bf16[8,8192]{1,0:T(8,128)(2,1)S(1)}, u32[]{:S(2)}, u32[]{:S(2)}) collective-permute-start(bf16[8,8192]{1,0:T(8,128)(2,1)S(1)} %add_convert_fusion.2), channel_id=1, source_target_pairs={{0,64},{32,96},{64,0},{96,32},{128,192},{160,224},{192,128},{224,1... | collective-permute-start | bytes 393224 | tf_op jit(solution)/shard_map/ppermute | solution.py:16
  126.1 15.7 %collective-permute-start.22 = (bf16[8,8192]{1,0:T(8,128)(2,1)S(1)}, bf16[8,8192]{1,0:T(8,128)(2,1)S(1)}, u32[]{:S(2)}, u32[]{:S(2)}) collective-permute-start(bf16[8,8192]{1,0:T(8,128)(2,1)S(1)} %add_convert_fusion.1), channel_id=1, source_target_pairs={{0,128},{32,160},{64,192},{96,224},{128,0},{160,32},{192,64},{224,... | collective-permute-start | bytes 393224 | tf_op jit(solution)/shard_map/ppermute | solution.py:16
  141.8 10.9 %collective-permute-start.23 = (bf16[8,8192]{1,0:T(8,128)(2,1)S(1)}, bf16[8,8192]{1,0:T(8,128)(2,1)S(1)}, u32[]{:S(2)}, u32[]{:S(2)}) collective-permute-start(bf16[8,8192]{1,0:T(8,128)(2,1)S(1)} %add_convert_fusion), channel_id=1, source_target_pairs={{0,384},{32,416},{64,448},{96,480},{128,256},{160,288},{192,320},{... | collective-permute-start | bytes 393224 | tf_op jit(solution)/shard_map/ppermute | solution.py:16
  154.4 7.5 %collective-permute-start.24 = (bf16[1,8,4096]{2,1,0:T(8,128)(2,1)S(1)}, bf16[1,8,4096]{2,1,0:T(8,128)(2,1)S(1)}, u32[]{:S(2)}, u32[]{:S(2)}) collective-permute-start(bf16[1,8,4096]{2,1,0:T(8,128)(2,1)S(1)} %get-tuple-element.10), channel_id=1, source_target_pairs={{0,24},{1,25},{2,26},{3,27},{4,28},{5,29},{6,30},{7,31},{8,16},{9,... | collective-permute-start | bytes 196616 | tf_op jit(solution)/shard_map/ppermute | solution.py:86
  168.9 9.5 %collective-permute-start.26 = (bf16[4,8,4096]{2,1,0:T(8,128)(2,1)S(1)}, bf16[4,8,4096]{2,1,0:T(8,128)(2,1)S(1)}, u32[]{:S(2)}, u32[]{:S(2)}) collective-permute-start(bf16[4,8,4096]{2,1,0:T(8,128)(2,1)S(1)} %bitcast.204), channel_id=1, source_target_pairs={{0,6},{1,7},{2,4},{3,5},{4,2},{5,3},{6,0},{7,1},{8,14},{9,15},{10,... | collective-permute-start | bytes 786440 | tf_op jit(solution)/shard_map/ppermute | solution.py:86
  173.3 9.5 %collective-permute-start.31 = (bf16[4,8,4096]{2,1,0:T(8,128)(2,1)S(1)}, bf16[4,8,4096]{2,1,0:T(8,128)(2,1)S(1)}, u32[]{:S(2)}, u32[]{:S(2)}) collective-permute-start(bf16[4,8,4096]{2,1,0:T(8,128)(2,1)S(1)} %bitcast.208), channel_id=1, source_target_pairs={{0,24},{1,25},{2,26},{3,27},{4,28},{5,29},{6,30},{7,31},{8,16},{9,... | collective-permute-start | bytes 786440 | tf_op jit(solution)/shard_map/ppermute | solution.py:86
  178.5 11.1 %collective-permute-start.27 = (bf16[8,8,4096]{2,1,0:T(8,128)(2,1)S(1)}, bf16[8,8,4096]{2,1,0:T(8,128)(2,1)S(1)}, u32[]{:S(2)}, u32[]{:S(2)}) collective-permute-start(bf16[8,8,4096]{2,1,0:T(8,128)(2,1)S(1)} %bitcast.192), channel_id=1, source_target_pairs={{0,2},{1,3},{2,0},{3,1},{4,6},{5,7},{6,4},{7,5},{8,10},{9,11},{10,... | collective-permute-start | bytes 1572872 | tf_op jit(solution)/shard_map/ppermute | solution.py:86
  183.0 11.1 %collective-permute-start.32 = (bf16[8,8,4096]{2,1,0:T(8,128)(2,1)S(1)}, bf16[8,8,4096]{2,1,0:T(8,128)(2,1)S(1)}, u32[]{:S(2)}, u32[]{:S(2)}) collective-permute-start(bf16[8,8,4096]{2,1,0:T(8,128)(2,1)S(1)} %bitcast.194), channel_id=1, source_target_pairs={{0,8},{1,9},{2,10},{3,11},{4,12},{5,13},{6,14},{7,15},{8,0},{9,1},... | collective-permute-start | bytes 1572872 | tf_op jit(solution)/shard_map/ppermute | solution.py:86
  248.3 7.9 %collective-permute-start.40 = (f32[1,128]{1,0:T(1,128)S(1)}, f32[1,128]{1,0:T(1,128)S(1)}, u32[]{:S(2)}, u32[]{:S(2)}) collective-permute-start(f32[1,128]{1,0:T(1,128)S(1)} %add.295), channel_id=1, source_target_pairs={{0,64},{32,96},{64,0},{96,32},{128,192},{160,224},{192,128},{224,1... | collective-permute-start | bytes 1544 | tf_op jit(solution)/shard_map/ppermute | solution.py:16
  256.2 9.3 %collective-permute-start.41 = (f32[1,128]{1,0:T(1,128)S(1)}, f32[1,128]{1,0:T(1,128)S(1)}, u32[]{:S(2)}, u32[]{:S(2)}) collective-permute-start(f32[1,128]{1,0:T(1,128)S(1)} %add.296), channel_id=1, source_target_pairs={{0,128},{32,160},{64,192},{96,224},{128,0},{160,32},{192,64},{224,... | collective-permute-start | bytes 1544 | tf_op jit(solution)/shard_map/ppermute | solution.py:16
  265.6 9.3 %collective-permute-start.42 = (f32[1,128]{1,0:T(1,128)S(1)}, f32[1,128]{1,0:T(1,128)S(1)}, u32[]{:S(2)}, u32[]{:S(2)}) collective-permute-start(f32[1,128]{1,0:T(1,128)S(1)} %add.297), channel_id=1, source_target_pairs={{0,384},{32,416},{64,448},{96,480},{128,256},{160,288},{192,320},{... | collective-permute-start | bytes 1544 | tf_op jit(solution)/shard_map/ppermute | solution.py:16
  (34 other events, 262.1 us)

commit v7 on v6

--- a/solution.py
+++ b/solution.py
@@ -17,12 +17,27 @@
     return acc
 
 
+def quad_sum(x, axis, n, send_dtype, pairs):
+    acc = x
+    for masks in pairs:
+        sent = acc.astype(send_dtype)
+        if len(masks) == 1:
+            acc = sent.astype(jnp.float32) + lax.ppermute(sent, axis, masked_pairs(n, masks[0])).astype(jnp.float32)
+            continue
+        m1, m2 = masks
+        a, b, c = [lax.ppermute(sent, axis, masked_pairs(n, m)).astype(jnp.float32) for m in (m1, m2, m1 ^ m2)]
+        acc = (sent.astype(jnp.float32) + a) + (b + c)
+    return acc
+
+
 CORE, X1, X3, Y1, Y3 = 1, 2, 6, 8, 24
 LAT_MASKS = (CORE, X1, X3, Y1, Y3)
 ORDER_X_FIRST = (CORE, X1, X3, Y1, Y3)
 ORDER_Y_FIRST = (CORE, Y1, Y3, X1, X3)
 ORDERS = (ORDER_X_FIRST, ORDER_Y_FIRST)
 GRP_MASKS = (1, 2, 4, 12)
+GRP_QUADS = ((1, 2), (4, 12))
+LAT_QUADS = ((CORE, X1), (X3, Y1), (Y3,))
 
 
 def logical_rank(r, masks):
@@ -136,7 +151,7 @@
         ).astype(jnp.bfloat16)
         halves.append(halving_scatter(part.reshape(n_lat, own_rows, cols), rank_lat, n_lat, masks))
     block_recon = jnp.concatenate(halves, axis=1)
-    recon = butterfly_sum(block_recon.astype(jnp.float32), "grp", n_grp, jnp.bfloat16, GRP_MASKS)
+    recon = quad_sum(block_recon.astype(jnp.float32), "grp", n_grp, jnp.bfloat16, GRP_QUADS)
     error_own = recon + dec_bias - own_batch.astype(jnp.float32)
     grad_own = (2.0 * error_own).astype(jnp.bfloat16)
     grad_a, grad_b = [g.reshape(n_tok, cols) for g in column_halves(grad_own, rank_lat, n_lat)]
@@ -162,9 +177,8 @@
     bias_raw = jnp.sum(grad_pre, axis=0)
     local_squares = jnp.sum(grad_raw * grad_raw) + jnp.sum(bias_raw * bias_raw)
     squares = jnp.broadcast_to(local_squares, (1, 128))
-    for mask in LAT_MASKS:
-        squares = squares + lax.ppermute(squares, "lat", masked_pairs(n_lat, mask))
-    total_squares = butterfly_sum(squares, "grp", n_grp, jnp.float32, GRP_MASKS)[0, 0]
+    squares = quad_sum(squares, "lat", n_lat, jnp.float32, LAT_QUADS)
+    total_squares = quad_sum(squares, "grp", n_grp, jnp.float32, GRP_QUADS)[0, 0]
     entries = (weight.shape[0] + 1) * weight.shape[1] * n_lat * n_grp
     factor = jnp.minimum(1.0, 1.0 / jnp.sqrt(total_squares / entries + epsilon))
     return (

time: 281 us -> 297 us (1.057)
  starting transfers between devices: 140 us -> 163 us
  waiting for transfers between devices: 94.9 us -> 89.1 us
    ppermute x13 -> x19, starting transfers between devices: 54.7 us -> 78.7 us  [the longest x18 75 us: quad_sum(): lax.ppermute(sent, axis, masked_pairs(n, m)).astype(jnp.float32)]
    ppermute x13 -> x19, waiting for transfers between devices: 47 us -> 38.1 us  [the longest x18 35.2 us: quad_sum(): lax.ppermute(sent, axis, masked_pairs(n, m)).astype(jnp.float32)]
    ppermute x20, waiting for transfers between devices: 29.1 us -> 32.1 us  [doubling_gather(): got = lax.ppermute(acc, 'lat', masked_pairs(n, masks[j]))]
  transfers between devices with their start and end apart: 43 -> 49, of which waited for: 32 -> 27; matrix products, arithmetic and copies ran while one was open for 4% -> 4% of each run, Pallas kernels for 0% -> 0%
where the time goes in v7:
time: 297 us; the launch traced here: 296 us
  starting transfers between devices  163 us (55%)
  waiting for transfers between devices  89.1 us (30%)
  matrix products  16.5 us (6%)
  other arithmetic  14.5 us (5%)
  local copies, waits for them, and re-layouts  8.9 us (3%)
  between operations  3.31 us (1%)
    ppermute x18, starting transfers between devices, quad_sum(): lax.ppermute(sent, axis, masked_pairs(n, m)).astype(jnp.float32)  75 us
    ppermute x20, starting transfers between devices, doubling_gather(): got = lax.ppermute(acc, 'lat', masked_pairs(n, masks[j]))  55.1 us
    ppermute x18, waiting for transfers between devices, quad_sum(): lax.ppermute(sent, axis, masked_pairs(n, m)).astype(jnp.float32)  35.2 us
    ppermute x20, waiting for transfers between devices, doubling_gather(): got = lax.ppermute(acc, 'lat', masked_pairs(n, masks[j]))  32.1 us
    ppermute x10, starting transfers between devices, halving_scatter(): lax.ppermute(sent, 'lat', masked_pairs(n, mask)).astype(jnp.float32)  29.6 us
    ppermute x10, waiting for transfers between devices, halving_scatter(): lax.ppermute(sent, 'lat', masked_pairs(n, mask)).astype(jnp.float32)  18.8 us
    dot_general x1, matrix products, body(): lax.dot_general(centered, grad_pre.astype(jnp.bfloat16), (((0,), (0,)), (...  6.39 us
  transfers between devices with their start and end apart: 49, of which 27 were waited for; matrix products, arithmetic and copies ran while one was open for 4% of the time, Pallas kernels for 0%

profile of v7, /device:TPU:6, one launch (start us, length us, event | category | flops | bytes accessed | tf_op | source)
XLA Modules:
  0.0 295.5 jit_solution(564775613763528125)
XLA Ops:
  1.5 4.9 %collective-permute-start = (bf16[1,8,4096]{2,1,0:T(8,128)(2,1)S(1)}, bf16[1,8,4096]{2,1,0:T(8,128)(2,1)S(1)}, u32[]{:S(2)}, u32[]{:S(2)}) collective-permute-start(bf16[1,8,4096]{2,1,0:T(8,128)(2,1)S(1)} %get-tuple-element.18), channel_id=1, source_target_pairs={{0,24},{1,25},{2,26},{3,27},{4,28},{5,29},{6,30},{7,31},{8,16},{9,... | collective-permute-start | bytes 196616 | tf_op jit(solution)/shard_map/ppermute | solution.py:101
  6.5 4.8 %collective-permute-start.5 = (bf16[1,8,4096]{2,1,0:T(8,128)(2,1)S(1)}, bf16[1,8,4096]{2,1,0:T(8,128)(2,1)S(1)}, u32[]{:S(2)}, u32[]{:S(2)}) collective-permute-start(bf16[1,8,4096]{2,1,0:T(8,128)(2,1)S(1)} %get-tuple-element.19), channel_id=1, source_target_pairs={{0,6},{1,7},{2,4},{3,5},{4,2},{5,3},{6,0},{7,1},{8,14},{9,15},{10,... | collective-permute-start | bytes 196616 | tf_op jit(solution)/shard_map/ppermute | solution.py:101
  23.8 4.4 %collective-permute-start.7 = (bf16[4,8,4096]{2,1,0:T(8,128)(2,1)S(1)}, bf16[4,8,4096]{2,1,0:T(8,128)(2,1)S(1)}, u32[]{:S(2)}, u32[]{:S(2)}) collective-permute-start(bf16[4,8,4096]{2,1,0:T(8,128)(2,1)S(1)} %bitcast.210), channel_id=1, source_target_pairs={{0,24},{1,25},{2,26},{3,27},{4,28},{5,29},{6,30},{7,31},{8,16},{9,... | collective-permute-start | bytes 786440 | tf_op jit(solution)/shard_map/ppermute | solution.py:101
  36.0 5.7 %collective-permute-done.3 = bf16[8,8,4096]{2,1,0:T(8,128)(2,1)S(1)} collective-permute-done((bf16[8,8,4096]{2,1,0:T(8,128)(2,1)S(1)}, bf16[8,8,4096]{2,1,0:T(8,128)(2,1)S(1)}, u32[]{:S(2)}, u32[]{:S(2)}) %collective-permute-start.3) | collective-permute-done | bytes 524320 | tf_op jit(solution)/shard_map/ppermute | solution.py:101
  67.9 11.4 %collective-permute-done.11 = bf16[8,8,4096]{2,1,0:T(8,128)(2,1)S(1)} collective-permute-done((bf16[8,8,4096]{2,1,0:T(8,128)(2,1)S(1)}, bf16[8,8,4096]{2,1,0:T(8,128)(2,1)S(1)}, u32[]{:S(2)}, u32[]{:S(2)}) %collective-permute-start.11) | collective-permute-done | bytes 524320 | tf_op jit(solution)/shard_map/ppermute | solution.py:92
  82.7 5.1 %collective-permute-start.17 = (bf16[4,8,4096]{2,1,0:T(8,128)(2,1)S(1)}, bf16[4,8,4096]{2,1,0:T(8,128)(2,1)S(1)}, u32[]{:S(2)}, u32[]{:S(2)}) collective-permute-start(bf16[4,8,4096]{2,1,0:T(8,128)(2,1)S(1)} %fusion.14), channel_id=1, source_target_pairs={{0,24},{1,25},{2,26},{3,27},{4,28},{5,29},{6,30},{7,31},{8,16},{9,... | collective-permute-start | bytes 786440 | tf_op jit(solution)/shard_map/ppermute | solution.py:92
  97.2 4.0 %collective-permute-start.14 = (bf16[1,8,4096]{2,1,0:T(8,128)(2,1)S(1)}, bf16[1,8,4096]{2,1,0:T(8,128)(2,1)S(1)}, u32[]{:S(2)}, u32[]{:S(2)}) collective-permute-start(bf16[1,8,4096]{2,1,0:T(8,128)(2,1)S(1)} %dynamic-slice_convert_fusion.7), channel_id=1, source_target_pairs={{0,24},{1,25},{2,26},{3,27},{4,28},{5,29},{6,30},{7,31},{8,16},{9,... | collective-permute-start | bytes 196616 | tf_op jit(solution)/shard_map/ppermute | solution.py:92
  101.2 4.3 %collective-permute-start.19 = (bf16[1,8,4096]{2,1,0:T(8,128)(2,1)S(1)}, bf16[1,8,4096]{2,1,0:T(8,128)(2,1)S(1)}, u32[]{:S(2)}, u32[]{:S(2)}) collective-permute-start(bf16[1,8,4096]{2,1,0:T(8,128)(2,1)S(1)} %dynamic-slice_convert_fusion.6), channel_id=1, source_target_pairs={{0,6},{1,7},{2,4},{3,5},{4,2},{5,3},{6,0},{7,1},{8,14},{9,15},{10,... | collective-permute-start | bytes 196616 | tf_op jit(solution)/shard_map/ppermute | solution.py:92
  110.7 5.2 %collective-permute-start.21 = (bf16[8,8192]{1,0:T(8,128)(2,1)S(1)}, bf16[8,8192]{1,0:T(8,128)(2,1)S(1)}, u32[]{:S(2)}, u32[]{:S(2)}) collective-permute-start(bf16[8,8192]{1,0:T(8,128)(2,1)S(1)} %pad_maximum_fusion.19), channel_id=1, source_target_pairs={{0,64},{32,96},{64,0},{96,32},{128,192},{160,224},{192,128},{224,1... | collective-permute-start | bytes 393224 | tf_op jit(solution)/shard_map/ppermute | solution.py:28
  124.7 10.6 %collective-permute-start.23 = (bf16[8,8192]{1,0:T(8,128)(2,1)S(1)}, bf16[8,8192]{1,0:T(8,128)(2,1)S(1)}, u32[]{:S(2)}, u32[]{:S(2)}) collective-permute-start(bf16[8,8192]{1,0:T(8,128)(2,1)S(1)} %add_convert_fusion), channel_id=1, source_target_pairs={{0,128},{32,160},{64,192},{96,224},{128,0},{160,32},{192,64},{224,... | collective-permute-start | bytes 393224 | tf_op jit(solution)/shard_map/ppermute | solution.py:28
  135.2 5.0 %collective-permute-start.24 = (bf16[8,8192]{1,0:T(8,128)(2,1)S(1)}, bf16[8,8192]{1,0:T(8,128)(2,1)S(1)}, u32[]{:S(2)}, u32[]{:S(2)}) collective-permute-start(bf16[8,8192]{1,0:T(8,128)(2,1)S(1)} %add_convert_fusion), channel_id=1, source_target_pairs={{0,384},{32,416},{64,448},{96,480},{128,256},{160,288},{192,320},{... | collective-permute-start | bytes 393224 | tf_op jit(solution)/shard_map/ppermute | solution.py:28
  140.3 4.1 %collective-permute-start.25 = (bf16[8,8192]{1,0:T(8,128)(2,1)S(1)}, bf16[8,8192]{1,0:T(8,128)(2,1)S(1)}, u32[]{:S(2)}, u32[]{:S(2)}) collective-permute-start(bf16[8,8192]{1,0:T(8,128)(2,1)S(1)} %add_convert_fusion), channel_id=1, source_target_pairs={{0,256},{32,288},{64,320},{96,352},{128,384},{160,416},{192,448},{... | collective-permute-start | bytes 393224 | tf_op jit(solution)/shard_map/ppermute | solution.py:28
  145.7 12.8 %collective-permute-done.24 = bf16[8,8192]{1,0:T(8,128)(2,1)S(1)} collective-permute-done((bf16[8,8192]{1,0:T(8,128)(2,1)S(1)}, bf16[8,8192]{1,0:T(8,128)(2,1)S(1)}, u32[]{:S(2)}, u32[]{:S(2)}) %collective-permute-start.24) | collective-permute-done | bytes 131104 | tf_op jit(solution)/shard_map/ppermute | solution.py:28
  160.1 4.9 %collective-permute-start.26 = (bf16[1,8,4096]{2,1,0:T(8,128)(2,1)S(1)}, bf16[1,8,4096]{2,1,0:T(8,128)(2,1)S(1)}, u32[]{:S(2)}, u32[]{:S(2)}) collective-permute-start(bf16[1,8,4096]{2,1,0:T(8,128)(2,1)S(1)} %get-tuple-element.10), channel_id=1, source_target_pairs={{0,24},{1,25},{2,26},{3,27},{4,28},{5,29},{6,30},{7,31},{8,16},{9,... | collective-permute-start | bytes 196616 | tf_op jit(solution)/shard_map/ppermute | solution.py:101
  175.2 3.9 %collective-permute-start.28 = (bf16[4,8,4096]{2,1,0:T(8,128)(2,1)S(1)}, bf16[4,8,4096]{2,1,0:T(8,128)(2,1)S(1)}, u32[]{:S(2)}, u32[]{:S(2)}) collective-permute-start(bf16[4,8,4096]{2,1,0:T(8,128)(2,1)S(1)} %bitcast.204), channel_id=1, source_target_pairs={{0,6},{1,7},{2,4},{3,5},{4,2},{5,3},{6,0},{7,1},{8,14},{9,15},{10,... | collective-permute-start | bytes 786440 | tf_op jit(solution)/shard_map/ppermute | solution.py:101
  198.2 4.1 %collective-permute-done.34 = bf16[8,8,4096]{2,1,0:T(8,128)(2,1)S(1)} collective-permute-done((bf16[8,8,4096]{2,1,0:T(8,128)(2,1)S(1)}, bf16[8,8,4096]{2,1,0:T(8,128)(2,1)S(1)}, u32[]{:S(2)}, u32[]{:S(2)}) %collective-permute-start.34) | collective-permute-done | bytes 524320 | tf_op jit(solution)/shard_map/ppermute | solution.py:101
  216.2 6.4 %multiply_reduce_fusion = (f32[]{:T(128)}, f32[8192,128]{1,0:T(8,128)}) fusion(f32[4096,128]{1,0:T(8,128)S(1)} %fusion.32, f32[4096,128]{1,0:T(8,128)S(1)} %fusion.40, bf16[256,128]{1,0:T(8,128)(2,1)S(1)} %get-tuple-element.28, bf16[256,4096]{1,0:T(8,128)(2,1)S(1)} %copy-done.7, bf16[256,4096]{1,0:T(8,128)(2,1)S(1)} %copy-done.5, f32[8192]{0:T(1024)S(1)} %copy-done.11), kind=kOutput, calls=%fused_computation.13 | convolution fusion | flops 553648128 | bytes 12681220 | tf_op jit(solution)/shard_map/dot_general | solution.py:170
  237.2 6.0 %collective-permute-start.41 = (f32[1,128]{1,0:T(1,128)S(1)}, f32[1,128]{1,0:T(1,128)S(1)}, u32[]{:S(2)}, u32[]{:S(2)}) collective-permute-start(f32[1,128]{1,0:T(1,128)S(1)} %add_add_fusion.3), channel_id=1, source_target_pairs={{0,14},{1,15},{2,12},{3,13},{4,10},{5,11},{6,8},{7,9},{8,6},{9,7},... | collective-permute-start | bytes 1544 | tf_op jit(solution)/shard_map/ppermute | solution.py:28
  256.6 4.9 %collective-permute-start.45 = (f32[1,128]{1,0:T(1,128)S(1)}, f32[1,128]{1,0:T(1,128)S(1)}, u32[]{:S(2)}, u32[]{:S(2)}) collective-permute-start(f32[1,128]{1,0:T(1,128)S(1)} %add.316), channel_id=1, source_target_pairs={{0,96},{32,64},{64,32},{96,0},{128,224},{160,192},{192,160},{224,1... | collective-permute-start | bytes 1544 | tf_op jit(solution)/shard_map/ppermute | solution.py:28
  263.9 7.1 %collective-permute-start.46 = (f32[1,128]{1,0:T(1,128)S(1)}, f32[1,128]{1,0:T(1,128)S(1)}, u32[]{:S(2)}, u32[]{:S(2)}) collective-permute-start(f32[1,128]{1,0:T(1,128)S(1)} %add_add_fusion.1), channel_id=1, source_target_pairs={{0,128},{32,160},{64,192},{96,224},{128,0},{160,32},{192,64},{224,... | collective-permute-start | bytes 1544 | tf_op jit(solution)/shard_map/ppermute | solution.py:28
  271.0 6.0 %collective-permute-start.47 = (f32[1,128]{1,0:T(1,128)S(1)}, f32[1,128]{1,0:T(1,128)S(1)}, u32[]{:S(2)}, u32[]{:S(2)}) collective-permute-start(f32[1,128]{1,0:T(1,128)S(1)} %add_add_fusion.1), channel_id=1, source_target_pairs={{0,384},{32,416},{64,448},{96,480},{128,256},{160,288},{192,320},{... | collective-permute-start | bytes 1544 | tf_op jit(solution)/shard_map/ppermute | solution.py:28
  277.0 3.8 %collective-permute-start.48 = (f32[1,128]{1,0:T(1,128)S(1)}, f32[1,128]{1,0:T(1,128)S(1)}, u32[]{:S(2)}, u32[]{:S(2)}) collective-permute-start(f32[1,128]{1,0:T(1,128)S(1)} %add_add_fusion.1), channel_id=1, source_target_pairs={{0,256},{32,288},{64,320},{96,352},{128,384},{160,416},{192,448},{... | collective-permute-start | bytes 1544 | tf_op jit(solution)/shard_map/ppermute | solution.py:28
  280.9 10.3 %collective-permute-done.48 = f32[1,128]{1,0:T(1,128)S(1)} collective-permute-done((f32[1,128]{1,0:T(1,128)S(1)}, f32[1,128]{1,0:T(1,128)S(1)}, u32[]{:S(2)}, u32[]{:S(2)}) %collective-permute-start.48) | collective-permute-done | bytes 544 | tf_op jit(solution)/shard_map/ppermute | solution.py:28
  291.8 3.7 %multiply_convert_fusion = bf16[8192,128]{1,0:T(8,128)(2,1)} fusion(f32[8192,128]{1,0:T(8,128)} %get-tuple-element.26, f32[]{:T(128)} %bitcast.99), kind=kLoop, calls=%fused_computation.12 | loop fusion | flops 2097152 | bytes 6291460 | tf_op jit(solution)/shard_map/convert_element_type | solution.py:185
  (194 shorter events, 148.8 us)
Async XLA Ops:
  1.5 12.5 %collective-permute-start = (bf16[1,8,4096]{2,1,0:T(8,128)(2,1)S(1)}, bf16[1,8,4096]{2,1,0:T(8,128)(2,1)S(1)}, u32[]{:S(2)}, u32[]{:S(2)}) collective-permute-start(bf16[1,8,4096]{2,1,0:T(8,128)(2,1)S(1)} %get-tuple-element.18), channel_id=1, source_target_pairs={{0,24},{1,25},{2,26},{3,27},{4,28},{5,29},{6,30},{7,31},{8,16},{9,... | collective-permute-start | bytes 196616 | tf_op jit(solution)/shard_map/ppermute | solution.py:101
  6.5 9.5 %collective-permute-start.5 = (bf16[1,8,4096]{2,1,0:T(8,128)(2,1)S(1)}, bf16[1,8,4096]{2,1,0:T(8,128)(2,1)S(1)}, u32[]{:S(2)}, u32[]{:S(2)}) collective-permute-start(bf16[1,8,4096]{2,1,0:T(8,128)(2,1)S(1)} %get-tuple-element.19), channel_id=1, source_target_pairs={{0,6},{1,7},{2,4},{3,5},{4,2},{5,3},{6,0},{7,1},{8,14},{9,15},{10,... | collective-permute-start | bytes 196616 | tf_op jit(solution)/shard_map/ppermute | solution.py:101
  21.0 9.5 %collective-permute-start.2 = (bf16[4,8,4096]{2,1,0:T(8,128)(2,1)S(1)}, bf16[4,8,4096]{2,1,0:T(8,128)(2,1)S(1)}, u32[]{:S(2)}, u32[]{:S(2)}) collective-permute-start(bf16[4,8,4096]{2,1,0:T(8,128)(2,1)S(1)} %bitcast.206), channel_id=1, source_target_pairs={{0,6},{1,7},{2,4},{3,5},{4,2},{5,3},{6,0},{7,1},{8,14},{9,15},{10,... | collective-permute-start | bytes 786440 | tf_op jit(solution)/shard_map/ppermute | solution.py:101
  23.8 9.5 %collective-permute-start.7 = (bf16[4,8,4096]{2,1,0:T(8,128)(2,1)S(1)}, bf16[4,8,4096]{2,1,0:T(8,128)(2,1)S(1)}, u32[]{:S(2)}, u32[]{:S(2)}) collective-permute-start(bf16[4,8,4096]{2,1,0:T(8,128)(2,1)S(1)} %bitcast.210), channel_id=1, source_target_pairs={{0,24},{1,25},{2,26},{3,27},{4,28},{5,29},{6,30},{7,31},{8,16},{9,... | collective-permute-start | bytes 786440 | tf_op jit(solution)/shard_map/ppermute | solution.py:101
  30.6 11.1 %collective-permute-start.3 = (bf16[8,8,4096]{2,1,0:T(8,128)(2,1)S(1)}, bf16[8,8,4096]{2,1,0:T(8,128)(2,1)S(1)}, u32[]{:S(2)}, u32[]{:S(2)}) collective-permute-start(bf16[8,8,4096]{2,1,0:T(8,128)(2,1)S(1)} %bitcast.196), channel_id=1, source_target_pairs={{0,2},{1,3},{2,0},{3,1},{4,6},{5,7},{6,4},{7,5},{8,10},{9,11},{10,... | collective-permute-start | bytes 1572872 | tf_op jit(solution)/shard_map/ppermute | solution.py:101
  33.4 12.3 %collective-permute-start.8 = (bf16[8,8,4096]{2,1,0:T(8,128)(2,1)S(1)}, bf16[8,8,4096]{2,1,0:T(8,128)(2,1)S(1)}, u32[]{:S(2)}, u32[]{:S(2)}) collective-permute-start(bf16[8,8,4096]{2,1,0:T(8,128)(2,1)S(1)} %bitcast.198), channel_id=1, source_target_pairs={{0,8},{1,9},{2,10},{3,11},{4,12},{5,13},{6,14},{7,15},{8,0},{9,1},... | collective-permute-start | bytes 1572872 | tf_op jit(solution)/shard_map/ppermute | solution.py:101
  63.4 15.9 %collective-permute-start.11 = (bf16[8,8,4096]{2,1,0:T(8,128)(2,1)S(1)}, bf16[8,8,4096]{2,1,0:T(8,128)(2,1)S(1)}, u32[]{:S(2)}, u32[]{:S(2)}) collective-permute-start(bf16[8,8,4096]{2,1,0:T(8,128)(2,1)S(1)} %fusion.11), channel_id=1, source_target_pairs={{0,2},{1,3},{2,0},{3,1},{4,6},{5,7},{6,4},{7,5},{8,10},{9,11},{10,... | collective-permute-start | bytes 1572872 | tf_op jit(solution)/shard_map/ppermute | solution.py:92
  65.7 16.8 %collective-permute-start.16 = (bf16[8,8,4096]{2,1,0:T(8,128)(2,1)S(1)}, bf16[8,8,4096]{2,1,0:T(8,128)(2,1)S(1)}, u32[]{:S(2)}, u32[]{:S(2)}) collective-permute-start(bf16[8,8,4096]{2,1,0:T(8,128)(2,1)S(1)} %fusion.12), channel_id=1, source_target_pairs={{0,8},{1,9},{2,10},{3,11},{4,12},{5,13},{6,14},{7,15},{8,0},{9,1},... | collective-permute-start | bytes 1572872 | tf_op jit(solution)/shard_map/ppermute | solution.py:92
  79.4 10.6 %collective-permute-start.12 = (bf16[4,8,4096]{2,1,0:T(8,128)(2,1)S(1)}, bf16[4,8,4096]{2,1,0:T(8,128)(2,1)S(1)}, u32[]{:S(2)}, u32[]{:S(2)}) collective-permute-start(bf16[4,8,4096]{2,1,0:T(8,128)(2,1)S(1)} %fusion.13), channel_id=1, source_target_pairs={{0,6},{1,7},{2,4},{3,5},{4,2},{5,3},{6,0},{7,1},{8,14},{9,15},{10,... | collective-permute-start | bytes 786440 | tf_op jit(solution)/shard_map/ppermute | solution.py:92
  82.7 10.6 %collective-permute-start.17 = (bf16[4,8,4096]{2,1,0:T(8,128)(2,1)S(1)}, bf16[4,8,4096]{2,1,0:T(8,128)(2,1)S(1)}, u32[]{:S(2)}, u32[]{:S(2)}) collective-permute-start(bf16[4,8,4096]{2,1,0:T(8,128)(2,1)S(1)} %fusion.14), channel_id=1, source_target_pairs={{0,24},{1,25},{2,26},{3,27},{4,28},{5,29},{6,30},{7,31},{8,16},{9,... | collective-permute-start | bytes 786440 | tf_op jit(solution)/shard_map/ppermute | solution.py:92
  108.6 10.1 %collective-permute-start.20 = (bf16[8,8192]{1,0:T(8,128)(2,1)S(1)}, bf16[8,8192]{1,0:T(8,128)(2,1)S(1)}, u32[]{:S(2)}, u32[]{:S(2)}) collective-permute-start(bf16[8,8192]{1,0:T(8,128)(2,1)S(1)} %pad_maximum_fusion.19), channel_id=1, source_target_pairs={{0,32},{32,0},{64,96},{96,64},{128,160},{160,128},{192,224},{224,1... | collective-permute-start | bytes 393224 | tf_op jit(solution)/shard_map/ppermute | solution.py:28
  110.7 10.9 %collective-permute-start.21 = (bf16[8,8192]{1,0:T(8,128)(2,1)S(1)}, bf16[8,8192]{1,0:T(8,128)(2,1)S(1)}, u32[]{:S(2)}, u32[]{:S(2)}) collective-permute-start(bf16[8,8192]{1,0:T(8,128)(2,1)S(1)} %pad_maximum_fusion.19), channel_id=1, source_target_pairs={{0,64},{32,96},{64,0},{96,32},{128,192},{160,224},{192,128},{224,1... | collective-permute-start | bytes 393224 | tf_op jit(solution)/shard_map/ppermute | solution.py:28
  124.7 21.1 %collective-permute-start.23 = (bf16[8,8192]{1,0:T(8,128)(2,1)S(1)}, bf16[8,8192]{1,0:T(8,128)(2,1)S(1)}, u32[]{:S(2)}, u32[]{:S(2)}) collective-permute-start(bf16[8,8192]{1,0:T(8,128)(2,1)S(1)} %add_convert_fusion), channel_id=1, source_target_pairs={{0,128},{32,160},{64,192},{96,224},{128,0},{160,32},{192,64},{224,... | collective-permute-start | bytes 393224 | tf_op jit(solution)/shard_map/ppermute | solution.py:28
  135.2 23.2 %collective-permute-start.24 = (bf16[8,8192]{1,0:T(8,128)(2,1)S(1)}, bf16[8,8192]{1,0:T(8,128)(2,1)S(1)}, u32[]{:S(2)}, u32[]{:S(2)}) collective-permute-start(bf16[8,8192]{1,0:T(8,128)(2,1)S(1)} %add_convert_fusion), channel_id=1, source_target_pairs={{0,384},{32,416},{64,448},{96,480},{128,256},{160,288},{192,320},{... | collective-permute-start | bytes 393224 | tf_op jit(solution)/shard_map/ppermute | solution.py:28
  140.3 18.2 %collective-permute-start.25 = (bf16[8,8192]{1,0:T(8,128)(2,1)S(1)}, bf16[8,8192]{1,0:T(8,128)(2,1)S(1)}, u32[]{:S(2)}, u32[]{:S(2)}) collective-permute-start(bf16[8,8192]{1,0:T(8,128)(2,1)S(1)} %add_convert_fusion), channel_id=1, source_target_pairs={{0,256},{32,288},{64,320},{96,352},{128,384},{160,416},{192,448},{... | collective-permute-start | bytes 393224 | tf_op jit(solution)/shard_map/ppermute | solution.py:28
  175.2 9.5 %collective-permute-start.28 = (bf16[4,8,4096]{2,1,0:T(8,128)(2,1)S(1)}, bf16[4,8,4096]{2,1,0:T(8,128)(2,1)S(1)}, u32[]{:S(2)}, u32[]{:S(2)}) collective-permute-start(bf16[4,8,4096]{2,1,0:T(8,128)(2,1)S(1)} %bitcast.204), channel_id=1, source_target_pairs={{0,6},{1,7},{2,4},{3,5},{4,2},{5,3},{6,0},{7,1},{8,14},{9,15},{10,... | collective-permute-start | bytes 786440 | tf_op jit(solution)/shard_map/ppermute | solution.py:101
  181.5 9.5 %collective-permute-start.33 = (bf16[4,8,4096]{2,1,0:T(8,128)(2,1)S(1)}, bf16[4,8,4096]{2,1,0:T(8,128)(2,1)S(1)}, u32[]{:S(2)}, u32[]{:S(2)}) collective-permute-start(bf16[4,8,4096]{2,1,0:T(8,128)(2,1)S(1)} %bitcast.208), channel_id=1, source_target_pairs={{0,24},{1,25},{2,26},{3,27},{4,28},{5,29},{6,30},{7,31},{8,16},{9,... | collective-permute-start | bytes 786440 | tf_op jit(solution)/shard_map/ppermute | solution.py:101
  184.9 11.1 %collective-permute-start.29 = (bf16[8,8,4096]{2,1,0:T(8,128)(2,1)S(1)}, bf16[8,8,4096]{2,1,0:T(8,128)(2,1)S(1)}, u32[]{:S(2)}, u32[]{:S(2)}) collective-permute-start(bf16[8,8,4096]{2,1,0:T(8,128)(2,1)S(1)} %bitcast.192), channel_id=1, source_target_pairs={{0,2},{1,3},{2,0},{3,1},{4,6},{5,7},{6,4},{7,5},{8,10},{9,11},{10,... | collective-permute-start | bytes 1572872 | tf_op jit(solution)/shard_map/ppermute | solution.py:101
  191.1 11.1 %collective-permute-start.34 = (bf16[8,8,4096]{2,1,0:T(8,128)(2,1)S(1)}, bf16[8,8,4096]{2,1,0:T(8,128)(2,1)S(1)}, u32[]{:S(2)}, u32[]{:S(2)}) collective-permute-start(bf16[8,8,4096]{2,1,0:T(8,128)(2,1)S(1)} %bitcast.194), channel_id=1, source_target_pairs={{0,8},{1,9},{2,10},{3,11},{4,12},{5,13},{6,14},{7,15},{8,0},{9,1},... | collective-permute-start | bytes 1572872 | tf_op jit(solution)/shard_map/ppermute | solution.py:101
  232.8 10.5 %collective-permute-start.39 = (f32[1,128]{1,0:T(1,128)S(1)}, f32[1,128]{1,0:T(1,128)S(1)}, u32[]{:S(2)}, u32[]{:S(2)}) collective-permute-start(f32[1,128]{1,0:T(1,128)S(1)} %add_add_fusion.3), channel_id=1, source_target_pairs={{0,6},{1,7},{2,4},{3,5},{4,2},{5,3},{6,0},{7,1},{8,14},{9,15},{10,... | collective-permute-start | bytes 1544 | tf_op jit(solution)/shard_map/ppermute | solution.py:28
  251.4 10.1 %collective-permute-start.43 = (f32[1,128]{1,0:T(1,128)S(1)}, f32[1,128]{1,0:T(1,128)S(1)}, u32[]{:S(2)}, u32[]{:S(2)}) collective-permute-start(f32[1,128]{1,0:T(1,128)S(1)} %add.316), channel_id=1, source_target_pairs={{0,32},{32,0},{64,96},{96,64},{128,160},{160,128},{192,224},{224,1... | collective-permute-start | bytes 1544 | tf_op jit(solution)/shard_map/ppermute | solution.py:28
  263.9 17.0 %collective-permute-start.46 = (f32[1,128]{1,0:T(1,128)S(1)}, f32[1,128]{1,0:T(1,128)S(1)}, u32[]{:S(2)}, u32[]{:S(2)}) collective-permute-start(f32[1,128]{1,0:T(1,128)S(1)} %add_add_fusion.1), channel_id=1, source_target_pairs={{0,128},{32,160},{64,192},{96,224},{128,0},{160,32},{192,64},{224,... | collective-permute-start | bytes 1544 | tf_op jit(solution)/shard_map/ppermute | solution.py:28
  271.0 9.9 %collective-permute-start.47 = (f32[1,128]{1,0:T(1,128)S(1)}, f32[1,128]{1,0:T(1,128)S(1)}, u32[]{:S(2)}, u32[]{:S(2)}) collective-permute-start(f32[1,128]{1,0:T(1,128)S(1)} %add_add_fusion.1), channel_id=1, source_target_pairs={{0,384},{32,416},{64,448},{96,480},{128,256},{160,288},{192,320},{... | collective-permute-start | bytes 1544 | tf_op jit(solution)/shard_map/ppermute | solution.py:28
  277.0 14.1 %collective-permute-start.48 = (f32[1,128]{1,0:T(1,128)S(1)}, f32[1,128]{1,0:T(1,128)S(1)}, u32[]{:S(2)}, u32[]{:S(2)}) collective-permute-start(f32[1,128]{1,0:T(1,128)S(1)} %add_add_fusion.1), channel_id=1, source_target_pairs={{0,256},{32,288},{64,320},{96,352},{128,384},{160,416},{192,448},{... | collective-permute-start | bytes 1544 | tf_op jit(solution)/shard_map/ppermute | solution.py:28
  (39 other events, 282.1 us)

commit v8 on v6

--- a/solution.py
+++ b/solution.py
@@ -57,8 +57,7 @@
 def lat_rank_of(p, masks):
     r = 0
     for j, m in enumerate(masks):
-        if (p >> (4 - j)) & 1:
-            r ^= m
+        r = r ^ (((p >> (4 - j)) & 1) * m)
     return r
 
 
@@ -66,40 +65,29 @@
     return [(i, i ^ mask) for i in range(n)]
 
 
-def halving_scatter(x, rank, n, masks):
-    me = logical_rank(rank, masks)
+def halving_scatter(x, n, masks):
     acc = x
-    for j, mask in enumerate(masks):
-        bit = (me >> (4 - j)) & 1
+    for mask in masks:
         acc = acc.reshape((2, acc.shape[0] // 2) + acc.shape[1:])
-        kept = lax.dynamic_index_in_dim(acc, bit, 0, keepdims=False)
-        sent = lax.dynamic_index_in_dim(acc, 1 - bit, 0, keepdims=False).astype(jnp.bfloat16)
-        acc = kept.astype(jnp.float32) + lax.ppermute(sent, "lat", masked_pairs(n, mask)).astype(jnp.float32)
+        sent = acc[1].astype(jnp.bfloat16)
+        acc = acc[0].astype(jnp.float32) + lax.ppermute(sent, "lat", masked_pairs(n, mask)).astype(jnp.float32)
     return acc[0]
 
 
-def doubling_gather(x, rank, n, masks):
-    me = logical_rank(rank, masks)
+def doubling_gather(x, n, masks):
     acc = x[None]
-    for j in reversed(range(len(masks))):
-        bit = (me >> (4 - j)) & 1
-        got = lax.ppermute(acc, "lat", masked_pairs(n, masks[j]))
-        pair = jnp.stack([acc, got])
-        acc = jnp.where(bit == 0, pair, pair[::-1]).reshape((2 * acc.shape[0],) + acc.shape[1:])
+    for mask in reversed(masks):
+        acc = jnp.concatenate([acc, lax.ppermute(acc, "lat", masked_pairs(n, mask))], axis=0)
     return acc
 
 
-def column_halves(x, rank, n):
+def column_halves(x, n):
     cols = x.shape[1] // 2
-    return [doubling_gather(x[:, k * cols:(k + 1) * cols], rank, n, masks) for k, masks in enumerate(ORDERS)]
-
-
-def block_perm(src_masks, dst_masks, n):
-    return np.array([logical_rank(lat_rank_of(p, dst_masks), src_masks) for p in range(n)], dtype=np.int32)
+    return [doubling_gather(x[:, k * cols:(k + 1) * cols], n, masks) for k, masks in enumerate(ORDERS)]
 
 
 def take_blocks(x, perm, rows):
-    return jnp.take(x.reshape((len(perm), rows) + x.shape[1:]), perm, axis=0).reshape(x.shape)
+    return jnp.take(x.reshape((perm.shape[0], rows) + x.shape[1:]), perm, axis=0).reshape(x.shape)
 
 
 def body(stream, batch_index, weight, enc_bias, dec_bias):
@@ -110,14 +98,16 @@
     n_tok = batch_index.shape[0]
     cols = weight.shape[0] // 2
     order_a, order_b = ORDERS
-    token_of_row = np.array(
-        [lat_rank_of(i // own_rows, order_a) * own_rows + i % own_rows for i in range(n_tok)], dtype=np.int32
-    )
+    me_a = logical_rank(rank_lat, order_a)
+    me_b = logical_rank(rank_lat, order_b)
+    blk = jnp.arange(n_lat, dtype=jnp.int32)
+    row = jnp.arange(n_tok, dtype=jnp.int32)
+    token_of_row = lat_rank_of(row // own_rows ^ me_a, order_a) * own_rows + row % own_rows
     src = jnp.take(batch_index, token_of_row)
-    stream_halves = column_halves(stream, rank_lat, n_lat)
+    stream_halves = column_halves(stream, n_lat)
     batch_halves = []
-    for masks, rows in zip(ORDERS, stream_halves):
-        place = logical_rank(src // own_rows, masks) * own_rows + src % own_rows
+    for masks, me, rows in zip(ORDERS, (me_a, me_b), stream_halves):
+        place = (logical_rank(src // own_rows, masks) ^ me) * own_rows + src % own_rows
         onehot = (place[:, None] == lax.broadcasted_iota(jnp.int32, (n_tok, n_tok), 1)).astype(rows.dtype)
         batch_halves.append(
             jnp.dot(onehot, rows.reshape(n_tok, cols), preferred_element_type=jnp.float32).astype(jnp.bfloat16)
@@ -126,23 +116,24 @@
     centered = (batch.astype(jnp.float32) - dec_bias).astype(jnp.bfloat16)
     preact = jnp.dot(centered, weight, preferred_element_type=jnp.float32) + enc_bias
     active = (jax.nn.softplus(sharpness * preact) / sharpness).astype(jnp.bfloat16)
-    own_block = logical_rank(rank_lat, order_a)
-    own_batch = lax.dynamic_slice_in_dim(batch, own_block * own_rows, own_rows, 0)
-    active_b = take_blocks(active, block_perm(order_a, order_b, n_lat), own_rows)
+    own_batch = batch[:own_rows]
+    a_of_b = logical_rank(lat_rank_of(blk ^ me_b, order_b), order_a) ^ me_a
+    b_of_a = logical_rank(lat_rank_of(blk ^ me_a, order_a), order_b) ^ me_b
+    active_b = take_blocks(active, a_of_b, own_rows)
     halves = []
     for k, (masks, rows) in enumerate(zip(ORDERS, (active, active_b))):
         part = lax.dot_general(
             rows, weight[k * cols:(k + 1) * cols], (((1,), (1,)), ((), ())), preferred_element_type=jnp.float32
         ).astype(jnp.bfloat16)
-        halves.append(halving_scatter(part.reshape(n_lat, own_rows, cols), rank_lat, n_lat, masks))
+        halves.append(halving_scatter(part.reshape(n_lat, own_rows, cols), n_lat, masks))
     block_recon = jnp.concatenate(halves, axis=1)
     recon = butterfly_sum(block_recon.astype(jnp.float32), "grp", n_grp, jnp.bfloat16, GRP_MASKS)
     error_own = recon + dec_bias - own_batch.astype(jnp.float32)
     grad_own = (2.0 * error_own).astype(jnp.bfloat16)
-    grad_a, grad_b = [g.reshape(n_tok, cols) for g in column_halves(grad_own, rank_lat, n_lat)]
+    grad_a, grad_b = [g.reshape(n_tok, cols) for g in column_halves(grad_own, n_lat)]
     active_part_b = jnp.dot(grad_b, weight[cols:], preferred_element_type=jnp.float32)
     grad_active = jnp.dot(grad_a, weight[:cols], preferred_element_type=jnp.float32) + take_blocks(
-        active_part_b, block_perm(order_b, order_a, n_lat), own_rows
+        active_part_b, b_of_a, own_rows
     )
     decoder_grad = jnp.concatenate(
         [

time: 281 us -> 287 us (1.021)
  waiting for transfers between devices: 94.9 us -> 79.5 us
  starting transfers between devices: 140 us -> 153 us
  local copies, waits for them, and re-layouts: 10.4 us -> 18.9 us
  other arithmetic: 14.4 us -> 9.39 us
  matrix products: 16.6 us -> 20.9 us
    ppermute x8, starting transfers between devices: 42.9 us -> 49.9 us  [butterfly_sum(): lax.ppermute(sent, axis, masked_pairs(n, mask)).astype(jnp.float32)]
    ppermute x20, waiting for transfers between devices: 29.1 us -> 23.5 us  [doubling_gather(): lax.ppermute(acc, 'lat', masked_pairs(n, mask))]
    ppermute x8, waiting for transfers between devices: 31.6 us -> 26.8 us  [butterfly_sum(): lax.ppermute(sent, axis, masked_pairs(n, mask)).astype(jnp.float32)]
    concatenate x0 -> x8, local copies, waits for them, and re-layouts: none -> 4.65 us  [doubling_gather(): jnp.concatenate([acc, lax.ppermute(acc, 'lat', masked_pairs(n, mask))], a...]
    unnamed x30 -> x40, local copies, waits for them, and re-layouts: 4.84 us -> 9.47 us
    ppermute x5, waiting for transfers between devices: 15.3 us -> 10.9 us  [body(): squares = squares + lax.ppermute(squares, 'lat', masked_pairs(n_lat, mask))]
    ppermute x5, starting transfers between devices: 11.8 us -> 16.2 us  [body(): squares = squares + lax.ppermute(squares, 'lat', masked_pairs(n_lat, mask))]
    select_n x16 -> x3, other arithmetic: 4.47 us -> 0.07 us  [the longest x2 0.05 us: take_blocks(): jnp.take(x.reshape((perm.shape[0], rows) + x.shape[1:]), perm, axis=0)]
  transfers between devices with their start and end apart: 43 -> 43, of which waited for: 32 -> 27; matrix products, arithmetic and copies ran while one was open for 4% -> 8% of each run, Pallas kernels for 0% -> 0%
where the time goes in v8:
time: 287 us; the launch traced here: 285 us
  starting transfers between devices  153 us (53%)
  waiting for transfers between devices  79.5 us (28%)
  matrix products  20.9 us (7%)
  local copies, waits for them, and re-layouts  18.9 us (7%)
  other arithmetic  9.39 us (3%)
  between operations  2.97 us (1%)
    ppermute x20, starting transfers between devices, doubling_gather(): lax.ppermute(acc, 'lat', masked_pairs(n, mask))  56 us
    ppermute x8, starting transfers between devices, butterfly_sum(): lax.ppermute(sent, axis, masked_pairs(n, mask)).astype(jnp.float32)  49.9 us
    ppermute x10, starting transfers between devices, halving_scatter(): lax.ppermute(sent, 'lat', masked_pairs(n, mask)).astype(jnp.float32)  30.8 us
    ppermute x8, waiting for transfers between devices, butterfly_sum(): lax.ppermute(sent, axis, masked_pairs(n, mask)).astype(jnp.float32)  26.8 us
    ppermute x20, waiting for transfers between devices, doubling_gather(): lax.ppermute(acc, 'lat', masked_pairs(n, mask))  23.5 us
    ppermute x10, waiting for transfers between devices, halving_scatter(): lax.ppermute(sent, 'lat', masked_pairs(n, mask)).astype(jnp.float32)  18.4 us
    ppermute x5, starting transfers between devices, body(): squares = squares + lax.ppermute(squares, 'lat', masked_pairs(n_lat, mask))  16.2 us
    ppermute x5, waiting for transfers between devices, body(): squares = squares + lax.ppermute(squares, 'lat', masked_pairs(n_lat, mask))  10.9 us
  transfers between devices with their start and end apart: 43, of which 27 were waited for; matrix products, arithmetic and copies ran while one was open for 8% of the time, Pallas kernels for 0%

profile of v8, /device:TPU:6, one launch (start us, length us, event | category | flops | bytes accessed | tf_op | source)
XLA Modules:
  0.0 284.6 jit_solution(8387280799032922518)
XLA Ops:
  1.5 4.9 %collective-permute-start = (bf16[1,8,4096]{2,1,0:T(8,128)(2,1)S(1)}, bf16[1,8,4096]{2,1,0:T(8,128)(2,1)S(1)}, u32[]{:S(2)}, u32[]{:S(2)}) collective-permute-start(bf16[1,8,4096]{2,1,0:T(8,128)(2,1)S(1)} %get-tuple-element.40), channel_id=1, source_target_pairs={{0,24},{1,25},{2,26},{3,27},{4,28},{5,29},{6,30},{7,31},{8,16},{9,... | collective-permute-start | bytes 196616 | tf_op jit(solution)/shard_map/ppermute | solution.py:80
  6.5 4.8 %collective-permute-start.5 = (bf16[1,8,4096]{2,1,0:T(8,128)(2,1)S(1)}, bf16[1,8,4096]{2,1,0:T(8,128)(2,1)S(1)}, u32[]{:S(2)}, u32[]{:S(2)}) collective-permute-start(bf16[1,8,4096]{2,1,0:T(8,128)(2,1)S(1)} %get-tuple-element.41), channel_id=1, source_target_pairs={{0,6},{1,7},{2,4},{3,5},{4,2},{5,3},{6,0},{7,1},{8,14},{9,15},{10,... | collective-permute-start | bytes 196616 | tf_op jit(solution)/shard_map/ppermute | solution.py:80
  24.1 4.8 %collective-permute-start.7 = (bf16[4,8,4096]{2,1,0:T(8,128)(2,1)S(1)}, bf16[4,8,4096]{2,1,0:T(8,128)(2,1)S(1)}, u32[]{:S(2)}, u32[]{:S(2)}) collective-permute-start(bf16[4,8,4096]{2,1,0:T(8,128)(2,1)S(1)} %pad_maximum_fusion.6), channel_id=1, source_target_pairs={{0,24},{1,25},{2,26},{3,27},{4,28},{5,29},{6,30},{7,31},{8,16},{9,... | collective-permute-start | bytes 786440 | tf_op jit(solution)/shard_map/ppermute | solution.py:80
  37.4 5.0 %collective-permute-done.3 = bf16[8,8,4096]{2,1,0:T(8,128)(2,1)S(1)} collective-permute-done((bf16[8,8,4096]{2,1,0:T(8,128)(2,1)S(1)}, bf16[8,8,4096]{2,1,0:T(8,128)(2,1)S(1)}, u32[]{:S(2)}, u32[]{:S(2)}) %collective-permute-start.3) | collective-permute-done | bytes 524320 | tf_op jit(solution)/shard_map/ppermute | solution.py:80
  74.0 10.4 %collective-permute-done.11 = bf16[8,8,4096]{2,1,0:T(8,128)(2,1)S(1)} collective-permute-done((bf16[8,8,4096]{2,1,0:T(8,128)(2,1)S(1)}, bf16[8,8,4096]{2,1,0:T(8,128)(2,1)S(1)}, u32[]{:S(2)}, u32[]{:S(2)}) %collective-permute-start.11) | collective-permute-done | bytes 524320 | tf_op jit(solution)/shard_map/ppermute | solution.py:73
  88.6 4.3 %collective-permute-start.17 = (bf16[4,8,4096]{2,1,0:T(8,128)(2,1)S(1)}, bf16[4,8,4096]{2,1,0:T(8,128)(2,1)S(1)}, u32[]{:S(2)}, u32[]{:S(2)}) collective-permute-start(bf16[4,8,4096]{2,1,0:T(8,128)(2,1)S(1)} %slice.242), channel_id=1, source_target_pairs={{0,24},{1,25},{2,26},{3,27},{4,28},{5,29},{6,30},{7,31},{8,16},{9,... | collective-permute-start | bytes 786440 | tf_op jit(solution)/shard_map/ppermute | solution.py:73
  102.3 4.6 %collective-permute-start.14 = (bf16[1,8,4096]{2,1,0:T(8,128)(2,1)S(1)}, bf16[1,8,4096]{2,1,0:T(8,128)(2,1)S(1)}, u32[]{:S(2)}, u32[]{:S(2)}) collective-permute-start(bf16[1,8,4096]{2,1,0:T(8,128)(2,1)S(1)} %slice.247), channel_id=1, source_target_pairs={{0,24},{1,25},{2,26},{3,27},{4,28},{5,29},{6,30},{7,31},{8,16},{9,... | collective-permute-start | bytes 196616 | tf_op jit(solution)/shard_map/ppermute | solution.py:73
  106.9 3.9 %collective-permute-start.19 = (bf16[1,8,4096]{2,1,0:T(8,128)(2,1)S(1)}, bf16[1,8,4096]{2,1,0:T(8,128)(2,1)S(1)}, u32[]{:S(2)}, u32[]{:S(2)}) collective-permute-start(bf16[1,8,4096]{2,1,0:T(8,128)(2,1)S(1)} %slice.246), channel_id=1, source_target_pairs={{0,6},{1,7},{2,4},{3,5},{4,2},{5,3},{6,0},{7,1},{8,14},{9,15},{10,... | collective-permute-start | bytes 196616 | tf_op jit(solution)/shard_map/ppermute | solution.py:73
  116.8 4.4 %collective-permute-done.20 = bf16[8,8192]{1,0:T(8,128)(2,1)S(1)} collective-permute-done((bf16[8,8192]{1,0:T(8,128)(2,1)S(1)}, bf16[8,8192]{1,0:T(8,128)(2,1)S(1)}, u32[]{:S(2)}, u32[]{:S(2)}) %collective-permute-start.20) | collective-permute-done | bytes 131104 | tf_op jit(solution)/shard_map/ppermute | solution.py:16
  121.2 4.7 %collective-permute-start.21 = (bf16[8,8192]{1,0:T(8,128)(2,1)S(1)}, bf16[8,8192]{1,0:T(8,128)(2,1)S(1)}, u32[]{:S(2)}, u32[]{:S(2)}) collective-permute-start(bf16[8,8192]{1,0:T(8,128)(2,1)S(1)} %add_convert_fusion.2), channel_id=1, source_target_pairs={{0,64},{32,96},{64,0},{96,32},{128,192},{160,224},{192,128},{224,1... | collective-permute-start | bytes 393224 | tf_op jit(solution)/shard_map/ppermute | solution.py:16
  125.9 4.5 %collective-permute-done.21 = bf16[8,8192]{1,0:T(8,128)(2,1)S(1)} collective-permute-done((bf16[8,8192]{1,0:T(8,128)(2,1)S(1)}, bf16[8,8192]{1,0:T(8,128)(2,1)S(1)}, u32[]{:S(2)}, u32[]{:S(2)}) %collective-permute-start.21) | collective-permute-done | bytes 131104 | tf_op jit(solution)/shard_map/ppermute | solution.py:16
  130.4 11.7 %collective-permute-start.22 = (bf16[8,8192]{1,0:T(8,128)(2,1)S(1)}, bf16[8,8192]{1,0:T(8,128)(2,1)S(1)}, u32[]{:S(2)}, u32[]{:S(2)}) collective-permute-start(bf16[8,8192]{1,0:T(8,128)(2,1)S(1)} %add_convert_fusion.1), channel_id=1, source_target_pairs={{0,128},{32,160},{64,192},{96,224},{128,0},{160,32},{192,64},{224,... | collective-permute-start | bytes 393224 | tf_op jit(solution)/shard_map/ppermute | solution.py:16
  142.1 4.8 %collective-permute-done.22 = bf16[8,8192]{1,0:T(8,128)(2,1)S(1)} collective-permute-done((bf16[8,8192]{1,0:T(8,128)(2,1)S(1)}, bf16[8,8192]{1,0:T(8,128)(2,1)S(1)}, u32[]{:S(2)}, u32[]{:S(2)}) %collective-permute-start.22) | collective-permute-done | bytes 131104 | tf_op jit(solution)/shard_map/ppermute | solution.py:16
  146.9 6.8 %collective-permute-start.23 = (bf16[8,8192]{1,0:T(8,128)(2,1)S(1)}, bf16[8,8192]{1,0:T(8,128)(2,1)S(1)}, u32[]{:S(2)}, u32[]{:S(2)}) collective-permute-start(bf16[8,8192]{1,0:T(8,128)(2,1)S(1)} %add_convert_fusion), channel_id=1, source_target_pairs={{0,384},{32,416},{64,448},{96,480},{128,256},{160,288},{192,320},{... | collective-permute-start | bytes 393224 | tf_op jit(solution)/shard_map/ppermute | solution.py:16
  153.9 5.1 %collective-permute-done.23 = bf16[8,8192]{1,0:T(8,128)(2,1)S(1)} collective-permute-done((bf16[8,8192]{1,0:T(8,128)(2,1)S(1)}, bf16[8,8192]{1,0:T(8,128)(2,1)S(1)}, u32[]{:S(2)}, u32[]{:S(2)}) %collective-permute-start.23) | collective-permute-done | bytes 131104 | tf_op jit(solution)/shard_map/ppermute | solution.py:16
  177.6 4.4 %collective-permute-start.31 = (bf16[4,8,4096]{2,1,0:T(8,128)(2,1)S(1)}, bf16[4,8,4096]{2,1,0:T(8,128)(2,1)S(1)}, u32[]{:S(2)}, u32[]{:S(2)}) collective-permute-start(bf16[4,8,4096]{2,1,0:T(8,128)(2,1)S(1)} %pad_maximum_fusion.8), channel_id=1, source_target_pairs={{0,24},{1,25},{2,26},{3,27},{4,28},{5,29},{6,30},{7,31},{8,16},{9,... | collective-permute-start | bytes 786440 | tf_op jit(solution)/shard_map/ppermute | solution.py:80
  182.1 5.0 %collective-permute-done.31 = bf16[4,8,4096]{2,1,0:T(8,128)(2,1)S(1)} collective-permute-done((bf16[4,8,4096]{2,1,0:T(8,128)(2,1)S(1)}, bf16[4,8,4096]{2,1,0:T(8,128)(2,1)S(1)}, u32[]{:S(2)}, u32[]{:S(2)}) %collective-permute-start.31) | collective-permute-done | bytes 262176 | tf_op jit(solution)/shard_map/ppermute | solution.py:80
  191.9 6.4 %collective-permute-done.32 = bf16[8,8,4096]{2,1,0:T(8,128)(2,1)S(1)} collective-permute-done((bf16[8,8,4096]{2,1,0:T(8,128)(2,1)S(1)}, bf16[8,8,4096]{2,1,0:T(8,128)(2,1)S(1)}, u32[]{:S(2)}, u32[]{:S(2)}) %collective-permute-start.32) | collective-permute-done | bytes 524320 | tf_op jit(solution)/shard_map/ppermute | solution.py:80
  213.8 5.6 %multiply_reduce_fusion = (f32[]{:T(128)}, f32[8192,128]{1,0:T(8,128)}) fusion(f32[4096,128]{1,0:T(8,128)} %convolution_bitcast_fusion, f32[4096,128]{1,0:T(8,128)S(1)} %copy-done.6, bf16[256,128]{1,0:T(8,128)(2,1)S(1)} %get-tuple-element.57, bf16[256,4096]{1,0:T(8,128)(2,1)S(1)} %copy-done.2, bf16[256,4096]{1,0:T(8,128)(2,1)S(1)} %convolution_convert_fusion.3, ...), kind=kOutput, calls=%fused_computation.14 | convolution fusion | flops 553648128 | bytes 12681220 | tf_op jit(solution)/shard_map/dot_general | solution.py:146
  229.2 4.4 %collective-permute-start.36 = (f32[1,128]{1,0:T(1,128)S(1)}, f32[1,128]{1,0:T(1,128)S(1)}, u32[]{:S(2)}, u32[]{:S(2)}) collective-permute-start(f32[1,128]{1,0:T(1,128)S(1)} %fusion.61), channel_id=1, source_target_pairs={{0,6},{1,7},{2,4},{3,5},{4,2},{5,3},{6,0},{7,1},{8,14},{9,15},{10,... | collective-permute-start | bytes 1544 | tf_op jit(solution)/shard_map/ppermute | solution.py:157
  241.2 4.4 %collective-permute-start.38 = (f32[1,128]{1,0:T(1,128)S(1)}, f32[1,128]{1,0:T(1,128)S(1)}, u32[]{:S(2)}, u32[]{:S(2)}) collective-permute-start(f32[1,128]{1,0:T(1,128)S(1)} %add.315), channel_id=1, source_target_pairs={{0,24},{1,25},{2,26},{3,27},{4,28},{5,29},{6,30},{7,31},{8,16},{9,... | collective-permute-start | bytes 1544 | tf_op jit(solution)/shard_map/ppermute | solution.py:157
  253.3 5.4 %collective-permute-start.40 = (f32[1,128]{1,0:T(1,128)S(1)}, f32[1,128]{1,0:T(1,128)S(1)}, u32[]{:S(2)}, u32[]{:S(2)}) collective-permute-start(f32[1,128]{1,0:T(1,128)S(1)} %add.317), channel_id=1, source_target_pairs={{0,64},{32,96},{64,0},{96,32},{128,192},{160,224},{192,128},{224,1... | collective-permute-start | bytes 1544 | tf_op jit(solution)/shard_map/ppermute | solution.py:16
  260.2 8.0 %collective-permute-start.41 = (f32[1,128]{1,0:T(1,128)S(1)}, f32[1,128]{1,0:T(1,128)S(1)}, u32[]{:S(2)}, u32[]{:S(2)}) collective-permute-start(f32[1,128]{1,0:T(1,128)S(1)} %add.318), channel_id=1, source_target_pairs={{0,128},{32,160},{64,192},{96,224},{128,0},{160,32},{192,64},{224,... | collective-permute-start | bytes 1544 | tf_op jit(solution)/shard_map/ppermute | solution.py:16
  269.8 9.0 %collective-permute-start.42 = (f32[1,128]{1,0:T(1,128)S(1)}, f32[1,128]{1,0:T(1,128)S(1)}, u32[]{:S(2)}, u32[]{:S(2)}) collective-permute-start(f32[1,128]{1,0:T(1,128)S(1)} %add.319), channel_id=1, source_target_pairs={{0,384},{32,416},{64,448},{96,480},{128,256},{160,288},{192,320},{... | collective-permute-start | bytes 1544 | tf_op jit(solution)/shard_map/ppermute | solution.py:16
  (189 shorter events, 144.5 us)
Async XLA Ops:
  1.5 13.3 %collective-permute-start = (bf16[1,8,4096]{2,1,0:T(8,128)(2,1)S(1)}, bf16[1,8,4096]{2,1,0:T(8,128)(2,1)S(1)}, u32[]{:S(2)}, u32[]{:S(2)}) collective-permute-start(bf16[1,8,4096]{2,1,0:T(8,128)(2,1)S(1)} %get-tuple-element.40), channel_id=1, source_target_pairs={{0,24},{1,25},{2,26},{3,27},{4,28},{5,29},{6,30},{7,31},{8,16},{9,... | collective-permute-start | bytes 196616 | tf_op jit(solution)/shard_map/ppermute | solution.py:80
  6.5 10.4 %collective-permute-start.5 = (bf16[1,8,4096]{2,1,0:T(8,128)(2,1)S(1)}, bf16[1,8,4096]{2,1,0:T(8,128)(2,1)S(1)}, u32[]{:S(2)}, u32[]{:S(2)}) collective-permute-start(bf16[1,8,4096]{2,1,0:T(8,128)(2,1)S(1)} %get-tuple-element.41), channel_id=1, source_target_pairs={{0,6},{1,7},{2,4},{3,5},{4,2},{5,3},{6,0},{7,1},{8,14},{9,15},{10,... | collective-permute-start | bytes 196616 | tf_op jit(solution)/shard_map/ppermute | solution.py:80
  21.8 9.5 %collective-permute-start.2 = (bf16[4,8,4096]{2,1,0:T(8,128)(2,1)S(1)}, bf16[4,8,4096]{2,1,0:T(8,128)(2,1)S(1)}, u32[]{:S(2)}, u32[]{:S(2)}) collective-permute-start(bf16[4,8,4096]{2,1,0:T(8,128)(2,1)S(1)} %pad_maximum_fusion.5), channel_id=1, source_target_pairs={{0,6},{1,7},{2,4},{3,5},{4,2},{5,3},{6,0},{7,1},{8,14},{9,15},{10,... | collective-permute-start | bytes 786440 | tf_op jit(solution)/shard_map/ppermute | solution.py:80
  24.1 9.5 %collective-permute-start.7 = (bf16[4,8,4096]{2,1,0:T(8,128)(2,1)S(1)}, bf16[4,8,4096]{2,1,0:T(8,128)(2,1)S(1)}, u32[]{:S(2)}, u32[]{:S(2)}) collective-permute-start(bf16[4,8,4096]{2,1,0:T(8,128)(2,1)S(1)} %pad_maximum_fusion.6), channel_id=1, source_target_pairs={{0,24},{1,25},{2,26},{3,27},{4,28},{5,29},{6,30},{7,31},{8,16},{9,... | collective-permute-start | bytes 786440 | tf_op jit(solution)/shard_map/ppermute | solution.py:80
  31.3 11.1 %collective-permute-start.3 = (bf16[8,8,4096]{2,1,0:T(8,128)(2,1)S(1)}, bf16[8,8,4096]{2,1,0:T(8,128)(2,1)S(1)}, u32[]{:S(2)}, u32[]{:S(2)}) collective-permute-start(bf16[8,8,4096]{2,1,0:T(8,128)(2,1)S(1)} %pad_maximum_fusion.1), channel_id=1, source_target_pairs={{0,2},{1,3},{2,0},{3,1},{4,6},{5,7},{6,4},{7,5},{8,10},{9,11},{10,... | collective-permute-start | bytes 1572872 | tf_op jit(solution)/shard_map/ppermute | solution.py:80
  33.7 12.7 %collective-permute-start.8 = (bf16[8,8,4096]{2,1,0:T(8,128)(2,1)S(1)}, bf16[8,8,4096]{2,1,0:T(8,128)(2,1)S(1)}, u32[]{:S(2)}, u32[]{:S(2)}) collective-permute-start(bf16[8,8,4096]{2,1,0:T(8,128)(2,1)S(1)} %pad_maximum_fusion.2), channel_id=1, source_target_pairs={{0,8},{1,9},{2,10},{3,11},{4,12},{5,13},{6,14},{7,15},{8,0},{9,1},... | collective-permute-start | bytes 1572872 | tf_op jit(solution)/shard_map/ppermute | solution.py:80
  68.4 16.0 %collective-permute-start.11 = (bf16[8,8,4096]{2,1,0:T(8,128)(2,1)S(1)}, bf16[8,8,4096]{2,1,0:T(8,128)(2,1)S(1)}, u32[]{:S(2)}, u32[]{:S(2)}) collective-permute-start(bf16[8,8,4096]{2,1,0:T(8,128)(2,1)S(1)} %slice.241), channel_id=1, source_target_pairs={{0,2},{1,3},{2,0},{3,1},{4,6},{5,7},{6,4},{7,5},{8,10},{9,11},{10,... | collective-permute-start | bytes 1572872 | tf_op jit(solution)/shard_map/ppermute | solution.py:73
  71.3 17.2 %collective-permute-start.16 = (bf16[8,8,4096]{2,1,0:T(8,128)(2,1)S(1)}, bf16[8,8,4096]{2,1,0:T(8,128)(2,1)S(1)}, u32[]{:S(2)}, u32[]{:S(2)}) collective-permute-start(bf16[8,8,4096]{2,1,0:T(8,128)(2,1)S(1)} %slice.240), channel_id=1, source_target_pairs={{0,8},{1,9},{2,10},{3,11},{4,12},{5,13},{6,14},{7,15},{8,0},{9,1},... | collective-permute-start | bytes 1572872 | tf_op jit(solution)/shard_map/ppermute | solution.py:73
  84.5 10.8 %collective-permute-start.12 = (bf16[4,8,4096]{2,1,0:T(8,128)(2,1)S(1)}, bf16[4,8,4096]{2,1,0:T(8,128)(2,1)S(1)}, u32[]{:S(2)}, u32[]{:S(2)}) collective-permute-start(bf16[4,8,4096]{2,1,0:T(8,128)(2,1)S(1)} %slice.243), channel_id=1, source_target_pairs={{0,6},{1,7},{2,4},{3,5},{4,2},{5,3},{6,0},{7,1},{8,14},{9,15},{10,... | collective-permute-start | bytes 786440 | tf_op jit(solution)/shard_map/ppermute | solution.py:73
  88.6 10.2 %collective-permute-start.17 = (bf16[4,8,4096]{2,1,0:T(8,128)(2,1)S(1)}, bf16[4,8,4096]{2,1,0:T(8,128)(2,1)S(1)}, u32[]{:S(2)}, u32[]{:S(2)}) collective-permute-start(bf16[4,8,4096]{2,1,0:T(8,128)(2,1)S(1)} %slice.242), channel_id=1, source_target_pairs={{0,24},{1,25},{2,26},{3,27},{4,28},{5,29},{6,30},{7,31},{8,16},{9,... | collective-permute-start | bytes 786440 | tf_op jit(solution)/shard_map/ppermute | solution.py:73
  98.9 7.9 %collective-permute-start.18 = (bf16[2,8,4096]{2,1,0:T(8,128)(2,1)S(1)}, bf16[2,8,4096]{2,1,0:T(8,128)(2,1)S(1)}, u32[]{:S(2)}, u32[]{:S(2)}) collective-permute-start(bf16[2,8,4096]{2,1,0:T(8,128)(2,1)S(1)} %slice.244), channel_id=1, source_target_pairs={{0,2},{1,3},{2,0},{3,1},{4,6},{5,7},{6,4},{7,5},{8,10},{9,11},{10,... | collective-permute-start | bytes 393224 | tf_op jit(solution)/shard_map/ppermute | solution.py:73
  102.3 8.6 %collective-permute-start.14 = (bf16[1,8,4096]{2,1,0:T(8,128)(2,1)S(1)}, bf16[1,8,4096]{2,1,0:T(8,128)(2,1)S(1)}, u32[]{:S(2)}, u32[]{:S(2)}) collective-permute-start(bf16[1,8,4096]{2,1,0:T(8,128)(2,1)S(1)} %slice.247), channel_id=1, source_target_pairs={{0,24},{1,25},{2,26},{3,27},{4,28},{5,29},{6,30},{7,31},{8,16},{9,... | collective-permute-start | bytes 196616 | tf_op jit(solution)/shard_map/ppermute | solution.py:73
  106.9 7.4 %collective-permute-start.19 = (bf16[1,8,4096]{2,1,0:T(8,128)(2,1)S(1)}, bf16[1,8,4096]{2,1,0:T(8,128)(2,1)S(1)}, u32[]{:S(2)}, u32[]{:S(2)}) collective-permute-start(bf16[1,8,4096]{2,1,0:T(8,128)(2,1)S(1)} %slice.246), channel_id=1, source_target_pairs={{0,6},{1,7},{2,4},{3,5},{4,2},{5,3},{6,0},{7,1},{8,14},{9,15},{10,... | collective-permute-start | bytes 196616 | tf_op jit(solution)/shard_map/ppermute | solution.py:73
  121.2 9.2 %collective-permute-start.21 = (bf16[8,8192]{1,0:T(8,128)(2,1)S(1)}, bf16[8,8192]{1,0:T(8,128)(2,1)S(1)}, u32[]{:S(2)}, u32[]{:S(2)}) collective-permute-start(bf16[8,8192]{1,0:T(8,128)(2,1)S(1)} %add_convert_fusion.2), channel_id=1, source_target_pairs={{0,64},{32,96},{64,0},{96,32},{128,192},{160,224},{192,128},{224,1... | collective-permute-start | bytes 393224 | tf_op jit(solution)/shard_map/ppermute | solution.py:16
  130.4 16.5 %collective-permute-start.22 = (bf16[8,8192]{1,0:T(8,128)(2,1)S(1)}, bf16[8,8192]{1,0:T(8,128)(2,1)S(1)}, u32[]{:S(2)}, u32[]{:S(2)}) collective-permute-start(bf16[8,8192]{1,0:T(8,128)(2,1)S(1)} %add_convert_fusion.1), channel_id=1, source_target_pairs={{0,128},{32,160},{64,192},{96,224},{128,0},{160,32},{192,64},{224,... | collective-permute-start | bytes 393224 | tf_op jit(solution)/shard_map/ppermute | solution.py:16
  146.9 12.1 %collective-permute-start.23 = (bf16[8,8192]{1,0:T(8,128)(2,1)S(1)}, bf16[8,8192]{1,0:T(8,128)(2,1)S(1)}, u32[]{:S(2)}, u32[]{:S(2)}) collective-permute-start(bf16[8,8192]{1,0:T(8,128)(2,1)S(1)} %add_convert_fusion), channel_id=1, source_target_pairs={{0,384},{32,416},{64,448},{96,480},{128,256},{160,288},{192,320},{... | collective-permute-start | bytes 393224 | tf_op jit(solution)/shard_map/ppermute | solution.py:16
  160.7 7.4 %collective-permute-start.24 = (bf16[1,8,4096]{2,1,0:T(8,128)(2,1)S(1)}, bf16[1,8,4096]{2,1,0:T(8,128)(2,1)S(1)}, u32[]{:S(2)}, u32[]{:S(2)}) collective-permute-start(bf16[1,8,4096]{2,1,0:T(8,128)(2,1)S(1)} %get-tuple-element.30), channel_id=1, source_target_pairs={{0,24},{1,25},{2,26},{3,27},{4,28},{5,29},{6,30},{7,31},{8,16},{9,... | collective-permute-start | bytes 196616 | tf_op jit(solution)/shard_map/ppermute | solution.py:80
  162.6 8.1 %collective-permute-start.29 = (bf16[1,8,4096]{2,1,0:T(8,128)(2,1)S(1)}, bf16[1,8,4096]{2,1,0:T(8,128)(2,1)S(1)}, u32[]{:S(2)}, u32[]{:S(2)}) collective-permute-start(bf16[1,8,4096]{2,1,0:T(8,128)(2,1)S(1)} %get-tuple-element.31), channel_id=1, source_target_pairs={{0,6},{1,7},{2,4},{3,5},{4,2},{5,3},{6,0},{7,1},{8,14},{9,15},{10,... | collective-permute-start | bytes 196616 | tf_op jit(solution)/shard_map/ppermute | solution.py:80
  175.0 14.2 %collective-permute-start.26 = (bf16[4,8,4096]{2,1,0:T(8,128)(2,1)S(1)}, bf16[4,8,4096]{2,1,0:T(8,128)(2,1)S(1)}, u32[]{:S(2)}, u32[]{:S(2)}) collective-permute-start(bf16[4,8,4096]{2,1,0:T(8,128)(2,1)S(1)} %pad_maximum_fusion.7), channel_id=1, source_target_pairs={{0,6},{1,7},{2,4},{3,5},{4,2},{5,3},{6,0},{7,1},{8,14},{9,15},{10,... | collective-permute-start | bytes 786440 | tf_op jit(solution)/shard_map/ppermute | solution.py:80
  177.6 9.5 %collective-permute-start.31 = (bf16[4,8,4096]{2,1,0:T(8,128)(2,1)S(1)}, bf16[4,8,4096]{2,1,0:T(8,128)(2,1)S(1)}, u32[]{:S(2)}, u32[]{:S(2)}) collective-permute-start(bf16[4,8,4096]{2,1,0:T(8,128)(2,1)S(1)} %pad_maximum_fusion.8), channel_id=1, source_target_pairs={{0,24},{1,25},{2,26},{3,27},{4,28},{5,29},{6,30},{7,31},{8,16},{9,... | collective-permute-start | bytes 786440 | tf_op jit(solution)/shard_map/ppermute | solution.py:80
  187.2 11.1 %collective-permute-start.32 = (bf16[8,8,4096]{2,1,0:T(8,128)(2,1)S(1)}, bf16[8,8,4096]{2,1,0:T(8,128)(2,1)S(1)}, u32[]{:S(2)}, u32[]{:S(2)}) collective-permute-start(bf16[8,8,4096]{2,1,0:T(8,128)(2,1)S(1)} %pad_maximum_fusion.4), channel_id=1, source_target_pairs={{0,8},{1,9},{2,10},{3,11},{4,12},{5,13},{6,14},{7,15},{8,0},{9,1},... | collective-permute-start | bytes 1572872 | tf_op jit(solution)/shard_map/ppermute | solution.py:80
  189.3 11.1 %collective-permute-start.27 = (bf16[8,8,4096]{2,1,0:T(8,128)(2,1)S(1)}, bf16[8,8,4096]{2,1,0:T(8,128)(2,1)S(1)}, u32[]{:S(2)}, u32[]{:S(2)}) collective-permute-start(bf16[8,8,4096]{2,1,0:T(8,128)(2,1)S(1)} %pad_maximum_fusion.3), channel_id=1, source_target_pairs={{0,2},{1,3},{2,0},{3,1},{4,6},{5,7},{6,4},{7,5},{8,10},{9,11},{10,... | collective-permute-start | bytes 1572872 | tf_op jit(solution)/shard_map/ppermute | solution.py:80
  260.2 9.5 %collective-permute-start.41 = (f32[1,128]{1,0:T(1,128)S(1)}, f32[1,128]{1,0:T(1,128)S(1)}, u32[]{:S(2)}, u32[]{:S(2)}) collective-permute-start(f32[1,128]{1,0:T(1,128)S(1)} %add.318), channel_id=1, source_target_pairs={{0,128},{32,160},{64,192},{96,224},{128,0},{160,32},{192,64},{224,... | collective-permute-start | bytes 1544 | tf_op jit(solution)/shard_map/ppermute | solution.py:16
  269.8 10.5 %collective-permute-start.42 = (f32[1,128]{1,0:T(1,128)S(1)}, f32[1,128]{1,0:T(1,128)S(1)}, u32[]{:S(2)}, u32[]{:S(2)}) collective-permute-start(f32[1,128]{1,0:T(1,128)S(1)} %add.319), channel_id=1, source_target_pairs={{0,384},{32,416},{64,448},{96,480},{128,256},{160,288},{192,320},{... | collective-permute-start | bytes 1544 | tf_op jit(solution)/shard_map/ppermute | solution.py:16
  (32 other events, 157.3 us)

commit v9 on v6

--- a/solution.py
+++ b/solution.py
@@ -20,7 +20,7 @@
 CORE, X1, X3, Y1, Y3 = 1, 2, 6, 8, 24
 LAT_MASKS = (CORE, X1, X3, Y1, Y3)
 ORDER_X_FIRST = (CORE, X1, X3, Y1, Y3)
-ORDER_Y_FIRST = (CORE, Y1, Y3, X1, X3)
+ORDER_Y_FIRST = (CORE, X3, X1, Y1, Y3)
 ORDERS = (ORDER_X_FIRST, ORDER_Y_FIRST)
 GRP_MASKS = (1, 2, 4, 12)
 
@@ -66,32 +66,47 @@
     return [(i, i ^ mask) for i in range(n)]
 
 
-def halving_scatter(x, rank, n, masks):
-    me = logical_rank(rank, masks)
-    acc = x
-    for j, mask in enumerate(masks):
-        bit = (me >> (4 - j)) & 1
-        acc = acc.reshape((2, acc.shape[0] // 2) + acc.shape[1:])
-        kept = lax.dynamic_index_in_dim(acc, bit, 0, keepdims=False)
-        sent = lax.dynamic_index_in_dim(acc, 1 - bit, 0, keepdims=False).astype(jnp.bfloat16)
-        acc = kept.astype(jnp.float32) + lax.ppermute(sent, "lat", masked_pairs(n, mask)).astype(jnp.float32)
-    return acc[0]
-
-
-def doubling_gather(x, rank, n, masks):
-    me = logical_rank(rank, masks)
-    acc = x[None]
-    for j in reversed(range(len(masks))):
-        bit = (me >> (4 - j)) & 1
-        got = lax.ppermute(acc, "lat", masked_pairs(n, masks[j]))
-        pair = jnp.stack([acc, got])
-        acc = jnp.where(bit == 0, pair, pair[::-1]).reshape((2 * acc.shape[0],) + acc.shape[1:])
-    return acc
+def halving_rounds(parts, rank, n, orders):
+    mes = [logical_rank(rank, masks) for masks in orders]
+    accs = list(parts)
+    for j in range(len(orders[0])):
+        accs = [a.reshape((2, a.shape[0] // 2) + a.shape[1:]) for a in accs]
+        bits = [(me >> (4 - j)) & 1 for me in mes]
+        kept = [lax.dynamic_index_in_dim(a, b, 0, keepdims=False) for a, b in zip(accs, bits)]
+        sent = [lax.dynamic_index_in_dim(a, 1 - b, 0, keepdims=False).astype(jnp.bfloat16) for a, b in zip(accs, bits)]
+        masks = [o[j] for o in orders]
+        if all(m == masks[0] for m in masks):
+            widths = [t.shape[-1] for t in sent]
+            got = lax.ppermute(jnp.concatenate(sent, axis=-1), "lat", masked_pairs(n, masks[0]))
+            got = jnp.split(got, np.cumsum(widths)[:-1], axis=-1)
+        else:
+            got = [lax.ppermute(t, "lat", masked_pairs(n, m)) for t, m in zip(sent, masks)]
+        accs = [k.astype(jnp.float32) + g.astype(jnp.float32) for k, g in zip(kept, got)]
+    return [a[0] for a in accs]
+
+
+def doubling_rounds(x, rank, n, orders):
+    mes = [logical_rank(rank, masks) for masks in orders]
+    width = x.shape[1] // len(orders)
+    accs = [x[None, :, k * width:(k + 1) * width] for k in range(len(orders))]
+    for j in reversed(range(len(orders[0]))):
+        masks = [o[j] for o in orders]
+        if all(m == masks[0] for m in masks):
+            got = lax.ppermute(jnp.concatenate(accs, axis=-1), "lat", masked_pairs(n, masks[0]))
+            got = jnp.split(got, len(accs), axis=-1)
+        else:
+            got = [lax.ppermute(a, "lat", masked_pairs(n, m)) for a, m in zip(accs, masks)]
+        new = []
+        for a, g, me in zip(accs, got, mes):
+            bit = (me >> (4 - j)) & 1
+            pair = jnp.stack([a, g])
+            new.append(jnp.where(bit == 0, pair, pair[::-1]).reshape((2 * a.shape[0],) + a.shape[1:]))
+        accs = new
+    return accs
 
 
 def column_halves(x, rank, n):
-    cols = x.shape[1] // 2
-    return [doubling_gather(x[:, k * cols:(k + 1) * cols], rank, n, masks) for k, masks in enumerate(ORDERS)]
+    return doubling_rounds(x, rank, n, ORDERS)
 
 
 def block_perm(src_masks, dst_masks, n):
@@ -129,13 +144,15 @@
     own_block = logical_rank(rank_lat, order_a)
     own_batch = lax.dynamic_slice_in_dim(batch, own_block * own_rows, own_rows, 0)
     active_b = take_blocks(active, block_perm(order_a, order_b, n_lat), own_rows)
-    halves = []
-    for k, (masks, rows) in enumerate(zip(ORDERS, (active, active_b))):
-        part = lax.dot_general(
+    parts = [
+        lax.dot_general(
             rows, weight[k * cols:(k + 1) * cols], (((1,), (1,)), ((), ())), preferred_element_type=jnp.float32
-        ).astype(jnp.bfloat16)
-        halves.append(halving_scatter(part.reshape(n_lat, own_rows, cols), rank_lat, n_lat, masks))
-    block_recon = jnp.concatenate(halves, axis=1)
+        )
+        .astype(jnp.bfloat16)
+        .reshape(n_lat, own_rows, cols)
+        for k, rows in enumerate((active, active_b))
+    ]
+    block_recon = jnp.concatenate(halving_rounds(parts, rank_lat, n_lat, ORDERS), axis=1)
     recon = butterfly_sum(block_recon.astype(jnp.float32), "grp", n_grp, jnp.bfloat16, GRP_MASKS)
     error_own = recon + dec_bias - own_batch.astype(jnp.float32)
     grad_own = (2.0 * error_own).astype(jnp.bfloat16)

time: 281 us -> 314 us (1.12)
  waiting for transfers between devices: 94.9 us -> 136 us
  starting transfers between devices: 140 us -> 114 us
  other arithmetic: 14.4 us -> 24.7 us
  local copies, waits for them, and re-layouts: 10.4 us -> 14.5 us
    ppermute x30 -> x21, waiting for transfers between devices: 48 us -> 93.7 us  [the longest x8 30.9 us: doubling_rounds(): lax.ppermute(a, 'lat', masked_pairs(n, m))]
    ppermute x30 -> x21, starting transfers between devices: 85.1 us -> 57 us  [the longest x8 24.2 us: doubling_rounds(): lax.ppermute(a, 'lat', masked_pairs(n, m))]
    add x8 -> x6, other arithmetic: 0.85 us -> 6.97 us  [halving_rounds(): k.astype(jnp.float32) + g.astype(jnp.float32)]
    concatenate x1 -> x10, other arithmetic: 0.01 us -> 3.99 us  [the longest x3 2.27 us: halving_rounds(): jnp.concatenate(sent, axis=-1)]
    ppermute x5, waiting for transfers between devices: 15.3 us -> 11.9 us  [body(): squares = squares + lax.ppermute(squares, 'lat', masked_pairs(n_lat, mask))]
    ppermute x5, starting transfers between devices: 11.8 us -> 15.1 us  [body(): squares = squares + lax.ppermute(squares, 'lat', masked_pairs(n_lat, mask))]
    unnamed x30 -> x42, local copies, waits for them, and re-layouts: 4.84 us -> 6.83 us
  transfers between devices with their start and end apart: 43 -> 34, of which waited for: 32 -> 33; matrix products, arithmetic and copies ran while one was open for 4% -> 2% of each run, Pallas kernels for 0% -> 0%
where the time goes in v9:
time: 314 us; the launch traced here: 310 us
  waiting for transfers between devices  136 us (43%)
  starting transfers between devices  114 us (36%)
  other arithmetic  24.7 us (8%)
  matrix products  18.6 us (6%)
  local copies, waits for them, and re-layouts  14.5 us (5%)
    ppermute x8, starting transfers between devices, butterfly_sum(): lax.ppermute(sent, axis, masked_pairs(n, mask)).astype(jnp.float32)  41.5 us
    ppermute x8, waiting for transfers between devices, doubling_rounds(): lax.ppermute(a, 'lat', masked_pairs(n, m))  30.9 us
    ppermute x8, waiting for transfers between devices, butterfly_sum(): lax.ppermute(sent, axis, masked_pairs(n, mask)).astype(jnp.float32)  29.9 us
    ppermute x6, waiting for transfers between devices, doubling_rounds(): lax.ppermute(jnp.concatenate(accs, axis=-1), 'lat', masked_pairs(n, masks...  26.4 us
    ppermute x8, starting transfers between devices, doubling_rounds(): lax.ppermute(a, 'lat', masked_pairs(n, m))  24.2 us
    ppermute x4, waiting for transfers between devices, halving_rounds(): lax.ppermute(t, 'lat', masked_pairs(n, m))  19 us
    ppermute x6, starting transfers between devices, doubling_rounds(): lax.ppermute(jnp.concatenate(accs, axis=-1), 'lat', masked_pairs(n, masks...  17.7 us
    ppermute x3, waiting for transfers between devices, halving_rounds(): lax.ppermute(jnp.concatenate(sent, axis=-1), 'lat', masked_pairs(n, masks...  17.4 us
  transfers between devices with their start and end apart: 34, of which 33 were waited for; matrix products, arithmetic and copies ran while one was open for 2% of the time, Pallas kernels for 0%

profile of v9, /device:TPU:6, one launch (start us, length us, event | category | flops | bytes accessed | tf_op | source)
XLA Modules:
  0.0 310.1 jit_solution(13567406774974250840)
XLA Ops:
  1.6 4.9 %collective-permute-start = (bf16[1,8,8192]{2,1,0:T(8,128)(2,1)S(1)}, bf16[1,8,8192]{2,1,0:T(8,128)(2,1)S(1)}, u32[]{:S(2)}, u32[]{:S(2)}) collective-permute-start(bf16[1,8,8192]{2,1,0:T(8,128)(2,1)S(1)} %pad_maximum_fusion.23), channel_id=1, source_target_pairs={{0,24},{1,25},{2,26},{3,27},{4,28},{5,29},{6,30},{7,31},{8,16},{9,... | collective-permute-start | bytes 393224 | tf_op jit(solution)/shard_map/ppermute | solution.py:95
  12.4 6.9 %collective-permute-done.1 = bf16[2,8,8192]{2,1,0:T(8,128)(2,1)S(1)} collective-permute-done((bf16[2,8,8192]{2,1,0:T(8,128)(2,1)S(1)}, bf16[2,8,8192]{2,1,0:T(8,128)(2,1)S(1)}, u32[]{:S(2)}, u32[]{:S(2)}) %collective-permute-start.1) | collective-permute-done | bytes 262176 | tf_op jit(solution)/shard_map/ppermute | solution.py:95
  19.4 6.5 %collective-permute-start.2 = (bf16[4,8,4096]{2,1,0:T(8,128)(2,1)S(1)}, bf16[4,8,4096]{2,1,0:T(8,128)(2,1)S(1)}, u32[]{:S(2)}, u32[]{:S(2)}) collective-permute-start(bf16[4,8,4096]{2,1,0:T(8,128)(2,1)S(1)} %bitcast.228), channel_id=1, source_target_pairs={{0,6},{1,7},{2,4},{3,5},{4,2},{5,3},{6,0},{7,1},{8,14},{9,15},{10,... | collective-permute-start | bytes 786440 | tf_op jit(solution)/shard_map/ppermute | solution.py:98
  32.3 4.7 %collective-permute-done.4 = bf16[4,8,4096]{2,1,0:T(8,128)(2,1)S(1)} collective-permute-done((bf16[4,8,4096]{2,1,0:T(8,128)(2,1)S(1)}, bf16[4,8,4096]{2,1,0:T(8,128)(2,1)S(1)}, u32[]{:S(2)}, u32[]{:S(2)}) %collective-permute-start.4) | collective-permute-done | bytes 262176 | tf_op jit(solution)/shard_map/ppermute | solution.py:98
  39.2 5.3 %collective-permute-done.3 = bf16[8,8,4096]{2,1,0:T(8,128)(2,1)S(1)} collective-permute-done((bf16[8,8,4096]{2,1,0:T(8,128)(2,1)S(1)}, bf16[8,8,4096]{2,1,0:T(8,128)(2,1)S(1)}, u32[]{:S(2)}, u32[]{:S(2)}) %collective-permute-start.3) | collective-permute-done | bytes 524320 | tf_op jit(solution)/shard_map/ppermute | solution.py:98
  44.8 4.7 %collective-permute-done.5 = bf16[8,8,4096]{2,1,0:T(8,128)(2,1)S(1)} collective-permute-done((bf16[8,8,4096]{2,1,0:T(8,128)(2,1)S(1)}, bf16[8,8,4096]{2,1,0:T(8,128)(2,1)S(1)}, u32[]{:S(2)}, u32[]{:S(2)}) %collective-permute-start.5) | collective-permute-done | bytes 524320 | tf_op jit(solution)/shard_map/ppermute | solution.py:98
  74.9 4.3 %collective-permute-done.7 = bf16[16,8,8192]{2,1,0:T(8,128)(2,1)} collective-permute-done((bf16[16,8,8192]{2,1,0:T(8,128)(2,1)}, bf16[16,8,8192]{2,1,0:T(8,128)(2,1)}, u32[]{:S(2)}, u32[]{:S(2)}) %collective-permute-start.7) | collective-permute-done | bytes 2097184 | tf_op jit(solution)/shard_map/ppermute | solution.py:80
  79.2 4.3 %convert_add_fusion.1 = (f32[16,8,4096]{2,1,0:T(8,128)}, f32[16,8,4096]{2,1,0:T(8,128)S(1)}) fusion(bf16[16,8,8192]{2,1,0:T(8,128)(2,1)} %collective-permute-done.7, bf16[2,16,8,4096]{3,2,1,0:T(8,128)(2,1)} %bitcast.196, s32[]{:T(128)S(6)} %select_n.270, bf16[2,16,8,4096]{3,2,1,0:T(8,128)(2,1)} %bitcast.199, s32[]{:T(128)S(6)} %select_n.281), kind=kLoop, calls=%fused_computation.27 | loop fusion | flops 3145728 | bytes 8388616 | tf_op jit(solution)/shard_map/add | solution.py:84
  90.2 11.9 %collective-permute-done.10 = bf16[8,8,4096]{2,1,0:T(8,128)(2,1)} collective-permute-done((bf16[8,8,4096]{2,1,0:T(8,128)(2,1)S(1)}, bf16[8,8,4096]{2,1,0:T(8,128)(2,1)}, u32[]{:S(2)}, u32[]{:S(2)}) %collective-permute-start.10) | collective-permute-done | bytes 524320 | tf_op jit(solution)/shard_map/ppermute | solution.py:83
  119.0 6.9 %collective-permute-done.12 = bf16[2,8,8192]{2,1,0:T(8,128)(2,1)} collective-permute-done((bf16[2,8,8192]{2,1,0:T(8,128)(2,1)}, bf16[2,8,8192]{2,1,0:T(8,128)(2,1)}, u32[]{:S(2)}, u32[]{:S(2)}) %collective-permute-start.12) | collective-permute-done | bytes 262176 | tf_op jit(solution)/shard_map/ppermute | solution.py:80
  129.6 6.1 %collective-permute-done.13 = bf16[1,8,8192]{2,1,0:T(8,128)(2,1)S(1)} collective-permute-done((bf16[1,8,8192]{2,1,0:T(8,128)(2,1)S(1)}, bf16[1,8,8192]{2,1,0:T(8,128)(2,1)S(1)}, u32[]{:S(2)}, u32[]{:S(2)}) %collective-permute-start.13) | collective-permute-done | bytes 131104 | tf_op jit(solution)/shard_map/ppermute | solution.py:80
  138.6 4.9 %collective-permute-done.14 = bf16[8,8192]{1,0:T(8,128)(2,1)S(1)} collective-permute-done((bf16[8,8192]{1,0:T(8,128)(2,1)S(1)}, bf16[8,8192]{1,0:T(8,128)(2,1)S(1)}, u32[]{:S(2)}, u32[]{:S(2)}) %collective-permute-start.14) | collective-permute-done | bytes 131104 | tf_op jit(solution)/shard_map/ppermute | solution.py:16
  145.5 6.7 %collective-permute-done.15 = bf16[8,8192]{1,0:T(8,128)(2,1)S(1)} collective-permute-done((bf16[8,8192]{1,0:T(8,128)(2,1)S(1)}, bf16[8,8192]{1,0:T(8,128)(2,1)S(1)}, u32[]{:S(2)}, u32[]{:S(2)}) %collective-permute-start.15) | collective-permute-done | bytes 131104 | tf_op jit(solution)/shard_map/ppermute | solution.py:16
  152.2 8.3 %collective-permute-start.16 = (bf16[8,8192]{1,0:T(8,128)(2,1)S(1)}, bf16[8,8192]{1,0:T(8,128)(2,1)S(1)}, u32[]{:S(2)}, u32[]{:S(2)}) collective-permute-start(bf16[8,8192]{1,0:T(8,128)(2,1)S(1)} %add_convert_fusion.1), channel_id=1, source_target_pairs={{0,128},{32,160},{64,192},{96,224},{128,0},{160,32},{192,64},{224,... | collective-permute-start | bytes 393224 | tf_op jit(solution)/shard_map/ppermute | solution.py:16
  160.5 5.4 %collective-permute-done.16 = bf16[8,8192]{1,0:T(8,128)(2,1)S(1)} collective-permute-done((bf16[8,8192]{1,0:T(8,128)(2,1)S(1)}, bf16[8,8192]{1,0:T(8,128)(2,1)S(1)}, u32[]{:S(2)}, u32[]{:S(2)}) %collective-permute-start.16) | collective-permute-done | bytes 131104 | tf_op jit(solution)/shard_map/ppermute | solution.py:16
  165.9 6.8 %collective-permute-start.17 = (bf16[8,8192]{1,0:T(8,128)(2,1)S(1)}, bf16[8,8192]{1,0:T(8,128)(2,1)S(1)}, u32[]{:S(2)}, u32[]{:S(2)}) collective-permute-start(bf16[8,8192]{1,0:T(8,128)(2,1)S(1)} %add_convert_fusion), channel_id=1, source_target_pairs={{0,384},{32,416},{64,448},{96,480},{128,256},{160,288},{192,320},{... | collective-permute-start | bytes 393224 | tf_op jit(solution)/shard_map/ppermute | solution.py:16
  178.6 4.8 %collective-permute-start.18 = (bf16[1,8,8192]{2,1,0:T(8,128)(2,1)S(1)}, bf16[1,8,8192]{2,1,0:T(8,128)(2,1)S(1)}, u32[]{:S(2)}, u32[]{:S(2)}) collective-permute-start(bf16[1,8,8192]{2,1,0:T(8,128)(2,1)S(1)} %pad_maximum_fusion.28), channel_id=1, source_target_pairs={{0,24},{1,25},{2,26},{3,27},{4,28},{5,29},{6,30},{7,31},{8,16},{9,... | collective-permute-start | bytes 393224 | tf_op jit(solution)/shard_map/ppermute | solution.py:95
  188.7 6.3 %collective-permute-done.19 = bf16[2,8,8192]{2,1,0:T(8,128)(2,1)S(1)} collective-permute-done((bf16[2,8,8192]{2,1,0:T(8,128)(2,1)S(1)}, bf16[2,8,8192]{2,1,0:T(8,128)(2,1)S(1)}, u32[]{:S(2)}, u32[]{:S(2)}) %collective-permute-start.19) | collective-permute-done | bytes 262176 | tf_op jit(solution)/shard_map/ppermute | solution.py:95
  216.4 5.2 %collective-permute-done.23 = bf16[8,8,4096]{2,1,0:T(8,128)(2,1)S(1)} collective-permute-done((bf16[8,8,4096]{2,1,0:T(8,128)(2,1)S(1)}, bf16[8,8,4096]{2,1,0:T(8,128)(2,1)S(1)}, u32[]{:S(2)}, u32[]{:S(2)}) %collective-permute-start.23) | collective-permute-done | bytes 524320 | tf_op jit(solution)/shard_map/ppermute | solution.py:98
  239.5 6.4 %multiply_reduce_fusion = (f32[]{:T(128)}, f32[8192,128]{1,0:T(8,128)}) fusion(f32[4096,128]{1,0:T(8,128)S(1)} %fusion.33, f32[4096,128]{1,0:T(8,128)S(1)} %fusion.41, bf16[256,128]{1,0:T(8,128)(2,1)S(1)} %get-tuple-element.46, bf16[256,4096]{1,0:T(8,128)(2,1)S(1)} %copy-done.6, bf16[256,4096]{1,0:T(8,128)(2,1)S(1)} %copy-done.4, f32[8192]{0:T(1024)S(1)} %copy-done.16), kind=kOutput, calls=%fused_computation.13 | convolution fusion | flops 553648128 | bytes 12681220 | tf_op jit(solution)/shard_map/dot_general | solution.py:172
  267.7 4.8 %collective-permute-start.29 = (f32[1,128]{1,0:T(1,128)S(1)}, f32[1,128]{1,0:T(1,128)S(1)}, u32[]{:S(2)}, u32[]{:S(2)}) collective-permute-start(f32[1,128]{1,0:T(1,128)S(1)} %add.293), channel_id=1, source_target_pairs={{0,24},{1,25},{2,26},{3,27},{4,28},{5,29},{6,30},{7,31},{8,16},{9,... | collective-permute-start | bytes 1544 | tf_op jit(solution)/shard_map/ppermute | solution.py:183
  279.7 5.3 %collective-permute-start.31 = (f32[1,128]{1,0:T(1,128)S(1)}, f32[1,128]{1,0:T(1,128)S(1)}, u32[]{:S(2)}, u32[]{:S(2)}) collective-permute-start(f32[1,128]{1,0:T(1,128)S(1)} %add.295), channel_id=1, source_target_pairs={{0,64},{32,96},{64,0},{96,32},{128,192},{160,224},{192,128},{224,1... | collective-permute-start | bytes 1544 | tf_op jit(solution)/shard_map/ppermute | solution.py:16
  286.5 8.4 %collective-permute-start.32 = (f32[1,128]{1,0:T(1,128)S(1)}, f32[1,128]{1,0:T(1,128)S(1)}, u32[]{:S(2)}, u32[]{:S(2)}) collective-permute-start(f32[1,128]{1,0:T(1,128)S(1)} %add.296), channel_id=1, source_target_pairs={{0,128},{32,160},{64,192},{96,224},{128,0},{160,32},{192,64},{224,... | collective-permute-start | bytes 1544 | tf_op jit(solution)/shard_map/ppermute | solution.py:16
  296.4 7.0 %collective-permute-start.33 = (f32[1,128]{1,0:T(1,128)S(1)}, f32[1,128]{1,0:T(1,128)S(1)}, u32[]{:S(2)}, u32[]{:S(2)}) collective-permute-start(f32[1,128]{1,0:T(1,128)S(1)} %add.297), channel_id=1, source_target_pairs={{0,384},{32,416},{64,448},{96,480},{128,256},{160,288},{192,320},{... | collective-permute-start | bytes 1544 | tf_op jit(solution)/shard_map/ppermute | solution.py:16
  (195 shorter events, 160.0 us)
Async XLA Ops:
  1.6 8.4 %collective-permute-start = (bf16[1,8,8192]{2,1,0:T(8,128)(2,1)S(1)}, bf16[1,8,8192]{2,1,0:T(8,128)(2,1)S(1)}, u32[]{:S(2)}, u32[]{:S(2)}) collective-permute-start(bf16[1,8,8192]{2,1,0:T(8,128)(2,1)S(1)} %pad_maximum_fusion.23), channel_id=1, source_target_pairs={{0,24},{1,25},{2,26},{3,27},{4,28},{5,29},{6,30},{7,31},{8,16},{9,... | collective-permute-start | bytes 393224 | tf_op jit(solution)/shard_map/ppermute | solution.py:95
  10.1 9.1 %collective-permute-start.1 = (bf16[2,8,8192]{2,1,0:T(8,128)(2,1)S(1)}, bf16[2,8,8192]{2,1,0:T(8,128)(2,1)S(1)}, u32[]{:S(2)}, u32[]{:S(2)}) collective-permute-start(bf16[2,8,8192]{2,1,0:T(8,128)(2,1)S(1)} %pad_maximum_fusion.16), channel_id=1, source_target_pairs={{0,8},{1,9},{2,10},{3,11},{4,12},{5,13},{6,14},{7,15},{8,0},{9,1},... | collective-permute-start | bytes 786440 | tf_op jit(solution)/shard_map/ppermute | solution.py:95
  19.4 10.9 %collective-permute-start.2 = (bf16[4,8,4096]{2,1,0:T(8,128)(2,1)S(1)}, bf16[4,8,4096]{2,1,0:T(8,128)(2,1)S(1)}, u32[]{:S(2)}, u32[]{:S(2)}) collective-permute-start(bf16[4,8,4096]{2,1,0:T(8,128)(2,1)S(1)} %bitcast.228), channel_id=1, source_target_pairs={{0,6},{1,7},{2,4},{3,5},{4,2},{5,3},{6,0},{7,1},{8,14},{9,15},{10,... | collective-permute-start | bytes 786440 | tf_op jit(solution)/shard_map/ppermute | solution.py:98
  26.0 11.1 %collective-permute-start.4 = (bf16[4,8,4096]{2,1,0:T(8,128)(2,1)S(1)}, bf16[4,8,4096]{2,1,0:T(8,128)(2,1)S(1)}, u32[]{:S(2)}, u32[]{:S(2)}) collective-permute-start(bf16[4,8,4096]{2,1,0:T(8,128)(2,1)S(1)} %bitcast.226), channel_id=1, source_target_pairs={{0,2},{1,3},{2,0},{3,1},{4,6},{5,7},{6,4},{7,5},{8,10},{9,11},{10,... | collective-permute-start | bytes 786440 | tf_op jit(solution)/shard_map/ppermute | solution.py:98
  30.4 14.1 %collective-permute-start.3 = (bf16[8,8,4096]{2,1,0:T(8,128)(2,1)S(1)}, bf16[8,8,4096]{2,1,0:T(8,128)(2,1)S(1)}, u32[]{:S(2)}, u32[]{:S(2)}) collective-permute-start(bf16[8,8,4096]{2,1,0:T(8,128)(2,1)S(1)} %bitcast.212), channel_id=1, source_target_pairs={{0,2},{1,3},{2,0},{3,1},{4,6},{5,7},{6,4},{7,5},{8,10},{9,11},{10,... | collective-permute-start | bytes 1572872 | tf_op jit(solution)/shard_map/ppermute | solution.py:98
  37.2 12.3 %collective-permute-start.5 = (bf16[8,8,4096]{2,1,0:T(8,128)(2,1)S(1)}, bf16[8,8,4096]{2,1,0:T(8,128)(2,1)S(1)}, u32[]{:S(2)}, u32[]{:S(2)}) collective-permute-start(bf16[8,8,4096]{2,1,0:T(8,128)(2,1)S(1)} %bitcast.216), channel_id=1, source_target_pairs={{0,6},{1,7},{2,4},{3,5},{4,2},{5,3},{6,0},{7,1},{8,14},{9,15},{10,... | collective-permute-start | bytes 1572872 | tf_op jit(solution)/shard_map/ppermute | solution.py:98
  84.9 17.2 %collective-permute-start.10 = (bf16[8,8,4096]{2,1,0:T(8,128)(2,1)S(1)}, bf16[8,8,4096]{2,1,0:T(8,128)(2,1)}, u32[]{:S(2)}, u32[]{:S(2)}) collective-permute-start(bf16[8,8,4096]{2,1,0:T(8,128)(2,1)S(1)} %fusion.12), channel_id=1, source_target_pairs={{0,6},{1,7},{2,4},{3,5},{4,2},{5,3},{6,0},{7,1},{8,14},{9,15},{10,... | collective-permute-start | bytes 1572872 | tf_op jit(solution)/shard_map/ppermute | solution.py:83
  88.2 17.3 %collective-permute-start.8 = (bf16[8,8,4096]{2,1,0:T(8,128)(2,1)S(1)}, bf16[8,8,4096]{2,1,0:T(8,128)(2,1)S(1)}, u32[]{:S(2)}, u32[]{:S(2)}) collective-permute-start(bf16[8,8,4096]{2,1,0:T(8,128)(2,1)S(1)} %fusion.11), channel_id=1, source_target_pairs={{0,2},{1,3},{2,0},{3,1},{4,6},{5,7},{6,4},{7,5},{8,10},{9,11},{10,... | collective-permute-start | bytes 1572872 | tf_op jit(solution)/shard_map/ppermute | solution.py:83
  103.6 9.4 %collective-permute-start.11 = (bf16[4,8,4096]{2,1,0:T(8,128)(2,1)S(1)}, bf16[4,8,4096]{2,1,0:T(8,128)(2,1)S(1)}, u32[]{:S(2)}, u32[]{:S(2)}) collective-permute-start(bf16[4,8,4096]{2,1,0:T(8,128)(2,1)S(1)} %fusion.14), channel_id=1, source_target_pairs={{0,2},{1,3},{2,0},{3,1},{4,6},{5,7},{6,4},{7,5},{8,10},{9,11},{10,... | collective-permute-start | bytes 786440 | tf_op jit(solution)/shard_map/ppermute | solution.py:83
  105.7 10.6 %collective-permute-start.9 = (bf16[4,8,4096]{2,1,0:T(8,128)(2,1)S(1)}, bf16[4,8,4096]{2,1,0:T(8,128)(2,1)S(1)}, u32[]{:S(2)}, u32[]{:S(2)}) collective-permute-start(bf16[4,8,4096]{2,1,0:T(8,128)(2,1)S(1)} %fusion.13), channel_id=1, source_target_pairs={{0,6},{1,7},{2,4},{3,5},{4,2},{5,3},{6,0},{7,1},{8,14},{9,15},{10,... | collective-permute-start | bytes 786440 | tf_op jit(solution)/shard_map/ppermute | solution.py:83
  117.1 8.8 %collective-permute-start.12 = (bf16[2,8,8192]{2,1,0:T(8,128)(2,1)}, bf16[2,8,8192]{2,1,0:T(8,128)(2,1)}, u32[]{:S(2)}, u32[]{:S(2)}) collective-permute-start(bf16[2,8,8192]{2,1,0:T(8,128)(2,1)} %pad_maximum_fusion.19), channel_id=1, source_target_pairs={{0,8},{1,9},{2,10},{3,11},{4,12},{5,13},{6,14},{7,15},{8,0},{9,1},... | collective-permute-start | bytes 786440 | tf_op jit(solution)/shard_map/ppermute | solution.py:80
  127.7 8.1 %collective-permute-start.13 = (bf16[1,8,8192]{2,1,0:T(8,128)(2,1)S(1)}, bf16[1,8,8192]{2,1,0:T(8,128)(2,1)S(1)}, u32[]{:S(2)}, u32[]{:S(2)}) collective-permute-start(bf16[1,8,8192]{2,1,0:T(8,128)(2,1)S(1)} %pad_maximum_fusion.26), channel_id=1, source_target_pairs={{0,24},{1,25},{2,26},{3,27},{4,28},{5,29},{6,30},{7,31},{8,16},{9,... | collective-permute-start | bytes 393224 | tf_op jit(solution)/shard_map/ppermute | solution.py:80
  136.7 6.9 %collective-permute-start.14 = (bf16[8,8192]{1,0:T(8,128)(2,1)S(1)}, bf16[8,8192]{1,0:T(8,128)(2,1)S(1)}, u32[]{:S(2)}, u32[]{:S(2)}) collective-permute-start(bf16[8,8192]{1,0:T(8,128)(2,1)S(1)} %pad_maximum_fusion.27), channel_id=1, source_target_pairs={{0,32},{32,0},{64,96},{96,64},{128,160},{160,128},{192,224},{224,1... | collective-permute-start | bytes 393224 | tf_op jit(solution)/shard_map/ppermute | solution.py:16
  143.6 8.6 %collective-permute-start.15 = (bf16[8,8192]{1,0:T(8,128)(2,1)S(1)}, bf16[8,8192]{1,0:T(8,128)(2,1)S(1)}, u32[]{:S(2)}, u32[]{:S(2)}) collective-permute-start(bf16[8,8192]{1,0:T(8,128)(2,1)S(1)} %add_convert_fusion.2), channel_id=1, source_target_pairs={{0,64},{32,96},{64,0},{96,32},{128,192},{160,224},{192,128},{224,1... | collective-permute-start | bytes 393224 | tf_op jit(solution)/shard_map/ppermute | solution.py:16
  152.2 13.7 %collective-permute-start.16 = (bf16[8,8192]{1,0:T(8,128)(2,1)S(1)}, bf16[8,8192]{1,0:T(8,128)(2,1)S(1)}, u32[]{:S(2)}, u32[]{:S(2)}) collective-permute-start(bf16[8,8192]{1,0:T(8,128)(2,1)S(1)} %add_convert_fusion.1), channel_id=1, source_target_pairs={{0,128},{32,160},{64,192},{96,224},{128,0},{160,32},{192,64},{224,... | collective-permute-start | bytes 393224 | tf_op jit(solution)/shard_map/ppermute | solution.py:16
  165.9 10.9 %collective-permute-start.17 = (bf16[8,8192]{1,0:T(8,128)(2,1)S(1)}, bf16[8,8192]{1,0:T(8,128)(2,1)S(1)}, u32[]{:S(2)}, u32[]{:S(2)}) collective-permute-start(bf16[8,8192]{1,0:T(8,128)(2,1)S(1)} %add_convert_fusion), channel_id=1, source_target_pairs={{0,384},{32,416},{64,448},{96,480},{128,256},{160,288},{192,320},{... | collective-permute-start | bytes 393224 | tf_op jit(solution)/shard_map/ppermute | solution.py:16
  178.6 8.1 %collective-permute-start.18 = (bf16[1,8,8192]{2,1,0:T(8,128)(2,1)S(1)}, bf16[1,8,8192]{2,1,0:T(8,128)(2,1)S(1)}, u32[]{:S(2)}, u32[]{:S(2)}) collective-permute-start(bf16[1,8,8192]{2,1,0:T(8,128)(2,1)S(1)} %pad_maximum_fusion.28), channel_id=1, source_target_pairs={{0,24},{1,25},{2,26},{3,27},{4,28},{5,29},{6,30},{7,31},{8,16},{9,... | collective-permute-start | bytes 393224 | tf_op jit(solution)/shard_map/ppermute | solution.py:95
  186.8 8.3 %collective-permute-start.19 = (bf16[2,8,8192]{2,1,0:T(8,128)(2,1)S(1)}, bf16[2,8,8192]{2,1,0:T(8,128)(2,1)S(1)}, u32[]{:S(2)}, u32[]{:S(2)}) collective-permute-start(bf16[2,8,8192]{2,1,0:T(8,128)(2,1)S(1)} %pad_maximum_fusion.20), channel_id=1, source_target_pairs={{0,8},{1,9},{2,10},{3,11},{4,12},{5,13},{6,14},{7,15},{8,0},{9,1},... | collective-permute-start | bytes 786440 | tf_op jit(solution)/shard_map/ppermute | solution.py:95
  195.2 9.5 %collective-permute-start.20 = (bf16[4,8,4096]{2,1,0:T(8,128)(2,1)S(1)}, bf16[4,8,4096]{2,1,0:T(8,128)(2,1)S(1)}, u32[]{:S(2)}, u32[]{:S(2)}) collective-permute-start(bf16[4,8,4096]{2,1,0:T(8,128)(2,1)S(1)} %bitcast.224), channel_id=1, source_target_pairs={{0,6},{1,7},{2,4},{3,5},{4,2},{5,3},{6,0},{7,1},{8,14},{9,15},{10,... | collective-permute-start | bytes 786440 | tf_op jit(solution)/shard_map/ppermute | solution.py:98
  199.0 10.2 %collective-permute-start.22 = (bf16[4,8,4096]{2,1,0:T(8,128)(2,1)S(1)}, bf16[4,8,4096]{2,1,0:T(8,128)(2,1)S(1)}, u32[]{:S(2)}, u32[]{:S(2)}) collective-permute-start(bf16[4,8,4096]{2,1,0:T(8,128)(2,1)S(1)} %bitcast.222), channel_id=1, source_target_pairs={{0,2},{1,3},{2,0},{3,1},{4,6},{5,7},{6,4},{7,5},{8,10},{9,11},{10,... | collective-permute-start | bytes 786440 | tf_op jit(solution)/shard_map/ppermute | solution.py:98
  204.8 11.3 %collective-permute-start.21 = (bf16[8,8,4096]{2,1,0:T(8,128)(2,1)S(1)}, bf16[8,8,4096]{2,1,0:T(8,128)(2,1)S(1)}, u32[]{:S(2)}, u32[]{:S(2)}) collective-permute-start(bf16[8,8,4096]{2,1,0:T(8,128)(2,1)S(1)} %bitcast.210), channel_id=1, source_target_pairs={{0,2},{1,3},{2,0},{3,1},{4,6},{5,7},{6,4},{7,5},{8,10},{9,11},{10,... | collective-permute-start | bytes 1572872 | tf_op jit(solution)/shard_map/ppermute | solution.py:98
  209.3 12.3 %collective-permute-start.23 = (bf16[8,8,4096]{2,1,0:T(8,128)(2,1)S(1)}, bf16[8,8,4096]{2,1,0:T(8,128)(2,1)S(1)}, u32[]{:S(2)}, u32[]{:S(2)}) collective-permute-start(bf16[8,8,4096]{2,1,0:T(8,128)(2,1)S(1)} %bitcast.214), channel_id=1, source_target_pairs={{0,6},{1,7},{2,4},{3,5},{4,2},{5,3},{6,0},{7,1},{8,14},{9,15},{10,... | collective-permute-start | bytes 1572872 | tf_op jit(solution)/shard_map/ppermute | solution.py:98
  286.5 9.9 %collective-permute-start.32 = (f32[1,128]{1,0:T(1,128)S(1)}, f32[1,128]{1,0:T(1,128)S(1)}, u32[]{:S(2)}, u32[]{:S(2)}) collective-permute-start(f32[1,128]{1,0:T(1,128)S(1)} %add.296), channel_id=1, source_target_pairs={{0,128},{32,160},{64,192},{96,224},{128,0},{160,32},{192,64},{224,... | collective-permute-start | bytes 1544 | tf_op jit(solution)/shard_map/ppermute | solution.py:16
  296.4 9.3 %collective-permute-start.33 = (f32[1,128]{1,0:T(1,128)S(1)}, f32[1,128]{1,0:T(1,128)S(1)}, u32[]{:S(2)}, u32[]{:S(2)}) collective-permute-start(f32[1,128]{1,0:T(1,128)S(1)} %add.297), channel_id=1, source_target_pairs={{0,384},{32,416},{64,448},{96,480},{128,256},{160,288},{192,320},{... | collective-permute-start | bytes 1544 | tf_op jit(solution)/shard_map/ppermute | solution.py:16
  (31 other events, 290.1 us)

commit v10 on v6

--- a/solution.py
+++ b/solution.py
@@ -87,6 +87,23 @@
         pair = jnp.stack([acc, got])
         acc = jnp.where(bit == 0, pair, pair[::-1]).reshape((2 * acc.shape[0],) + acc.shape[1:])
     return acc
+
+
+def gather_but_last(x, rank, n, masks):
+    me = logical_rank(rank, masks)
+    acc = x[None]
+    for j in reversed(range(1, len(masks))):
+        bit = (me >> (4 - j)) & 1
+        got = lax.ppermute(acc, "lat", masked_pairs(n, masks[j]))
+        pair = jnp.stack([acc, got])
+        acc = jnp.where(bit == 0, pair, pair[::-1]).reshape((2 * acc.shape[0],) + acc.shape[1:])
+    got = lax.ppermute(acc, "lat", masked_pairs(n, masks[0]))
+    return acc, got, (me >> 4) & 1
+
+
+def by_bit(bit, mine, got):
+    pair = jnp.stack([mine, got])
+    return jnp.where(bit == 0, pair, pair[::-1]).reshape((2 * mine.shape[0],) + mine.shape[1:])
 
 
 def column_halves(x, rank, n):
@@ -139,18 +156,29 @@
     recon = butterfly_sum(block_recon.astype(jnp.float32), "grp", n_grp, jnp.bfloat16, GRP_MASKS)
     error_own = recon + dec_bias - own_batch.astype(jnp.float32)
     grad_own = (2.0 * error_own).astype(jnp.bfloat16)
-    grad_a, grad_b = [g.reshape(n_tok, cols) for g in column_halves(grad_own, rank_lat, n_lat)]
-    active_part_b = jnp.dot(grad_b, weight[cols:], preferred_element_type=jnp.float32)
-    grad_active = jnp.dot(grad_a, weight[:cols], preferred_element_type=jnp.float32) + take_blocks(
-        active_part_b, block_perm(order_b, order_a, n_lat), own_rows
-    )
-    decoder_grad = jnp.concatenate(
-        [
-            lax.dot_general(g, a, (((0,), (0,)), ((), ())), preferred_element_type=jnp.float32)
-            for g, a in ((grad_a, active), (grad_b, active_b))
-        ],
-        axis=0,
-    )
+    half_rows = n_tok // 2
+    grad_active = None
+    decoder_parts = []
+    for k, (masks, rows) in enumerate(zip(ORDERS, (active, active_b))):
+        mine, got, bit = gather_but_last(grad_own[:, k * cols:(k + 1) * cols], rank_lat, n_lat, masks)
+        mine = mine.reshape(half_rows, cols)
+        got = got.reshape(half_rows, cols)
+        w = weight[k * cols:(k + 1) * cols]
+        part = by_bit(
+            bit,
+            jnp.dot(mine, w, preferred_element_type=jnp.float32),
+            jnp.dot(got, w, preferred_element_type=jnp.float32),
+        )
+        if k == 1:
+            part = take_blocks(part, block_perm(order_b, order_a, n_lat), own_rows)
+        grad_active = part if grad_active is None else grad_active + part
+        own_active = lax.dynamic_slice_in_dim(rows, bit * half_rows, half_rows, 0)
+        other_active = lax.dynamic_slice_in_dim(rows, (1 - bit) * half_rows, half_rows, 0)
+        decoder_parts.append(
+            lax.dot_general(mine, own_active, (((0,), (0,)), ((), ())), preferred_element_type=jnp.float32)
+            + lax.dot_general(got, other_active, (((0,), (0,)), ((), ())), preferred_element_type=jnp.float32)
+        )
+    decoder_grad = jnp.concatenate(decoder_parts, axis=0)
     grad_pre = (grad_active + penalty) * jax.nn.sigmoid(sharpness * preact)
     encoder_grad = lax.dot_general(
         centered,

time: 281 us -> 283 us (level)
  matrix products: 16.6 us -> 20.7 us
    ppermute x0 -> x10, starting transfers between devices: none -> 27 us  [the longest x8 23.1 us: gather_but_last(): got = lax.ppermute(acc, 'lat', masked_pairs(n, masks[j]))]
    ppermute x20 -> x10, starting transfers between devices: 55.7 us -> 28.9 us  [doubling_gather(): got = lax.ppermute(acc, 'lat', masked_pairs(n, masks[j]))]
    ppermute x20 -> x10, waiting for transfers between devices: 29.1 us -> 14.7 us  [doubling_gather(): got = lax.ppermute(acc, 'lat', masked_pairs(n, masks[j]))]
    ppermute x0 -> x10, waiting for transfers between devices: none -> 13.8 us  [the longest x8 13.8 us: gather_but_last(): got = lax.ppermute(acc, 'lat', masked_pairs(n, masks[j]))]
    dot_general x4 -> x8, matrix products: 4.53 us -> 8.01 us  [the longest x2 3.64 us: body(): lax.dot_general(mine, own_active, (((0,), (0,)), ((), ())), preferred_ele...]
    select_n x16 -> x8, other arithmetic: 4.47 us -> 1.57 us  [doubling_gather(): jnp.where(bit == 0, pair, pair[::-1])]
  transfers between devices with their start and end apart: 43 -> 43, of which waited for: 32 -> 31; matrix products, arithmetic and copies ran while one was open for 4% -> 5% of each run, Pallas kernels for 0% -> 0%
where the time goes in v10:
time: 283 us; the launch traced here: 282 us
  starting transfers between devices  140 us (49%)
  waiting for transfers between devices  94.3 us (33%)
  matrix products  20.7 us (7%)
  other arithmetic  12.9 us (5%)
  local copies, waits for them, and re-layouts  10.2 us (4%)
  between operations  3.14 us (1%)
    ppermute x8, starting transfers between devices, butterfly_sum(): lax.ppermute(sent, axis, masked_pairs(n, mask)).astype(jnp.float32)  42.9 us
    ppermute x8, waiting for transfers between devices, butterfly_sum(): lax.ppermute(sent, axis, masked_pairs(n, mask)).astype(jnp.float32)  31.7 us
    ppermute x10, starting transfers between devices, halving_scatter(): lax.ppermute(sent, 'lat', masked_pairs(n, mask)).astype(jnp.float32)  29.5 us
    ppermute x10, starting transfers between devices, doubling_gather(): got = lax.ppermute(acc, 'lat', masked_pairs(n, masks[j]))  28.9 us
    ppermute x8, starting transfers between devices, gather_but_last(): got = lax.ppermute(acc, 'lat', masked_pairs(n, masks[j]))  23.1 us
    ppermute x10, waiting for transfers between devices, halving_scatter(): lax.ppermute(sent, 'lat', masked_pairs(n, mask)).astype(jnp.float32)  18.8 us
    ppermute x5, waiting for transfers between devices, body(): squares = squares + lax.ppermute(squares, 'lat', masked_pairs(n_lat, mask))  15.2 us
    ppermute x10, waiting for transfers between devices, doubling_gather(): got = lax.ppermute(acc, 'lat', masked_pairs(n, masks[j]))  14.7 us
  transfers between devices with their start and end apart: 43, of which 31 were waited for; matrix products, arithmetic and copies ran while one was open for 5% of the time, Pallas kernels for 0%

profile of v10, /device:TPU:6, one launch (start us, length us, event | category | flops | bytes accessed | tf_op | source)
XLA Modules:
  0.0 281.6 jit_solution(16602254990361415223)
XLA Ops:
  1.5 4.9 %collective-permute-start = (bf16[1,8,4096]{2,1,0:T(8,128)(2,1)S(1)}, bf16[1,8,4096]{2,1,0:T(8,128)(2,1)S(1)}, u32[]{:S(2)}, u32[]{:S(2)}) collective-permute-start(bf16[1,8,4096]{2,1,0:T(8,128)(2,1)S(1)} %get-tuple-element.20), channel_id=1, source_target_pairs={{0,24},{1,25},{2,26},{3,27},{4,28},{5,29},{6,30},{7,31},{8,16},{9,... | collective-permute-start | bytes 196616 | tf_op jit(solution)/shard_map/ppermute | solution.py:86
  6.5 4.8 %collective-permute-start.5 = (bf16[1,8,4096]{2,1,0:T(8,128)(2,1)S(1)}, bf16[1,8,4096]{2,1,0:T(8,128)(2,1)S(1)}, u32[]{:S(2)}, u32[]{:S(2)}) collective-permute-start(bf16[1,8,4096]{2,1,0:T(8,128)(2,1)S(1)} %get-tuple-element.21), channel_id=1, source_target_pairs={{0,6},{1,7},{2,4},{3,5},{4,2},{5,3},{6,0},{7,1},{8,14},{9,15},{10,... | collective-permute-start | bytes 196616 | tf_op jit(solution)/shard_map/ppermute | solution.py:86
  23.8 4.4 %collective-permute-start.7 = (bf16[4,8,4096]{2,1,0:T(8,128)(2,1)S(1)}, bf16[4,8,4096]{2,1,0:T(8,128)(2,1)S(1)}, u32[]{:S(2)}, u32[]{:S(2)}) collective-permute-start(bf16[4,8,4096]{2,1,0:T(8,128)(2,1)S(1)} %bitcast.224), channel_id=1, source_target_pairs={{0,24},{1,25},{2,26},{3,27},{4,28},{5,29},{6,30},{7,31},{8,16},{9,... | collective-permute-start | bytes 786440 | tf_op jit(solution)/shard_map/ppermute | solution.py:86
  36.0 5.7 %collective-permute-done.3 = bf16[8,8,4096]{2,1,0:T(8,128)(2,1)S(1)} collective-permute-done((bf16[8,8,4096]{2,1,0:T(8,128)(2,1)S(1)}, bf16[8,8,4096]{2,1,0:T(8,128)(2,1)S(1)}, u32[]{:S(2)}, u32[]{:S(2)}) %collective-permute-start.3) | collective-permute-done | bytes 524320 | tf_op jit(solution)/shard_map/ppermute | solution.py:86
  69.9 11.4 %collective-permute-done.11 = bf16[8,8,4096]{2,1,0:T(8,128)(2,1)S(1)} collective-permute-done((bf16[8,8,4096]{2,1,0:T(8,128)(2,1)S(1)}, bf16[8,8,4096]{2,1,0:T(8,128)(2,1)S(1)}, u32[]{:S(2)}, u32[]{:S(2)}) %collective-permute-start.11) | collective-permute-done | bytes 524320 | tf_op jit(solution)/shard_map/ppermute | solution.py:77
  84.7 5.1 %collective-permute-start.17 = (bf16[4,8,4096]{2,1,0:T(8,128)(2,1)S(1)}, bf16[4,8,4096]{2,1,0:T(8,128)(2,1)S(1)}, u32[]{:S(2)}, u32[]{:S(2)}) collective-permute-start(bf16[4,8,4096]{2,1,0:T(8,128)(2,1)S(1)} %fusion.16), channel_id=1, source_target_pairs={{0,24},{1,25},{2,26},{3,27},{4,28},{5,29},{6,30},{7,31},{8,16},{9,... | collective-permute-start | bytes 786440 | tf_op jit(solution)/shard_map/ppermute | solution.py:77
  99.1 3.9 %collective-permute-start.14 = (bf16[1,8,4096]{2,1,0:T(8,128)(2,1)S(1)}, bf16[1,8,4096]{2,1,0:T(8,128)(2,1)S(1)}, u32[]{:S(2)}, u32[]{:S(2)}) collective-permute-start(bf16[1,8,4096]{2,1,0:T(8,128)(2,1)S(1)} %dynamic-slice_convert_fusion.7), channel_id=1, source_target_pairs={{0,24},{1,25},{2,26},{3,27},{4,28},{5,29},{6,30},{7,31},{8,16},{9,... | collective-permute-start | bytes 196616 | tf_op jit(solution)/shard_map/ppermute | solution.py:77
  103.1 4.3 %collective-permute-start.19 = (bf16[1,8,4096]{2,1,0:T(8,128)(2,1)S(1)}, bf16[1,8,4096]{2,1,0:T(8,128)(2,1)S(1)}, u32[]{:S(2)}, u32[]{:S(2)}) collective-permute-start(bf16[1,8,4096]{2,1,0:T(8,128)(2,1)S(1)} %dynamic-slice_convert_fusion.6), channel_id=1, source_target_pairs={{0,6},{1,7},{2,4},{3,5},{4,2},{5,3},{6,0},{7,1},{8,14},{9,15},{10,... | collective-permute-start | bytes 196616 | tf_op jit(solution)/shard_map/ppermute | solution.py:77
  112.8 4.6 %collective-permute-done.20 = bf16[8,8192]{1,0:T(8,128)(2,1)S(1)} collective-permute-done((bf16[8,8192]{1,0:T(8,128)(2,1)S(1)}, bf16[8,8192]{1,0:T(8,128)(2,1)S(1)}, u32[]{:S(2)}, u32[]{:S(2)}) %collective-permute-start.20) | collective-permute-done | bytes 131104 | tf_op jit(solution)/shard_map/ppermute | solution.py:16
  117.4 3.9 %collective-permute-start.21 = (bf16[8,8192]{1,0:T(8,128)(2,1)S(1)}, bf16[8,8192]{1,0:T(8,128)(2,1)S(1)}, u32[]{:S(2)}, u32[]{:S(2)}) collective-permute-start(bf16[8,8192]{1,0:T(8,128)(2,1)S(1)} %add_convert_fusion.2), channel_id=1, source_target_pairs={{0,64},{32,96},{64,0},{96,32},{128,192},{160,224},{192,128},{224,1... | collective-permute-start | bytes 393224 | tf_op jit(solution)/shard_map/ppermute | solution.py:16
  121.3 5.3 %collective-permute-done.21 = bf16[8,8192]{1,0:T(8,128)(2,1)S(1)} collective-permute-done((bf16[8,8192]{1,0:T(8,128)(2,1)S(1)}, bf16[8,8192]{1,0:T(8,128)(2,1)S(1)}, u32[]{:S(2)}, u32[]{:S(2)}) %collective-permute-start.21) | collective-permute-done | bytes 131104 | tf_op jit(solution)/shard_map/ppermute | solution.py:16
  126.6 8.5 %collective-permute-start.22 = (bf16[8,8192]{1,0:T(8,128)(2,1)S(1)}, bf16[8,8192]{1,0:T(8,128)(2,1)S(1)}, u32[]{:S(2)}, u32[]{:S(2)}) collective-permute-start(bf16[8,8192]{1,0:T(8,128)(2,1)S(1)} %add_convert_fusion.1), channel_id=1, source_target_pairs={{0,128},{32,160},{64,192},{96,224},{128,0},{160,32},{192,64},{224,... | collective-permute-start | bytes 393224 | tf_op jit(solution)/shard_map/ppermute | solution.py:16
  135.1 7.1 %collective-permute-done.22 = bf16[8,8192]{1,0:T(8,128)(2,1)S(1)} collective-permute-done((bf16[8,8192]{1,0:T(8,128)(2,1)S(1)}, bf16[8,8192]{1,0:T(8,128)(2,1)S(1)}, u32[]{:S(2)}, u32[]{:S(2)}) %collective-permute-start.22) | collective-permute-done | bytes 131104 | tf_op jit(solution)/shard_map/ppermute | solution.py:16
  142.3 6.5 %collective-permute-start.23 = (bf16[8,8192]{1,0:T(8,128)(2,1)S(1)}, bf16[8,8192]{1,0:T(8,128)(2,1)S(1)}, u32[]{:S(2)}, u32[]{:S(2)}) collective-permute-start(bf16[8,8192]{1,0:T(8,128)(2,1)S(1)} %add_convert_fusion), channel_id=1, source_target_pairs={{0,384},{32,416},{64,448},{96,480},{128,256},{160,288},{192,320},{... | collective-permute-start | bytes 393224 | tf_op jit(solution)/shard_map/ppermute | solution.py:16
  148.8 4.4 %collective-permute-done.23 = bf16[8,8192]{1,0:T(8,128)(2,1)S(1)} collective-permute-done((bf16[8,8192]{1,0:T(8,128)(2,1)S(1)}, bf16[8,8192]{1,0:T(8,128)(2,1)S(1)}, u32[]{:S(2)}, u32[]{:S(2)}) %collective-permute-start.23) | collective-permute-done | bytes 131104 | tf_op jit(solution)/shard_map/ppermute | solution.py:16
  154.9 4.7 %collective-permute-start.24 = (bf16[1,8,4096]{2,1,0:T(8,128)(2,1)S(1)}, bf16[1,8,4096]{2,1,0:T(8,128)(2,1)S(1)}, u32[]{:S(2)}, u32[]{:S(2)}) collective-permute-start(bf16[1,8,4096]{2,1,0:T(8,128)(2,1)S(1)} %get-tuple-element.12), channel_id=1, source_target_pairs={{0,24},{1,25},{2,26},{3,27},{4,28},{5,29},{6,30},{7,31},{8,16},{9,... | collective-permute-start | bytes 196616 | tf_op jit(solution)/shard_map/ppermute | solution.py:97
  169.5 4.2 %collective-permute-start.26 = (bf16[4,8,4096]{2,1,0:T(8,128)(2,1)S(1)}, bf16[4,8,4096]{2,1,0:T(8,128)(2,1)S(1)}, u32[]{:S(2)}, u32[]{:S(2)}) collective-permute-start(bf16[4,8,4096]{2,1,0:T(8,128)(2,1)S(1)} %bitcast.218), channel_id=1, source_target_pairs={{0,6},{1,7},{2,4},{3,5},{4,2},{5,3},{6,0},{7,1},{8,14},{9,15},{10,... | collective-permute-start | bytes 786440 | tf_op jit(solution)/shard_map/ppermute | solution.py:97
  185.5 4.7 %collective-permute-done.27 = bf16[8,8,4096]{2,1,0:T(8,128)(2,1)S(1)} collective-permute-done((bf16[8,8,4096]{2,1,0:T(8,128)(2,1)S(1)}, bf16[8,8,4096]{2,1,0:T(8,128)(2,1)S(1)}, u32[]{:S(2)}, u32[]{:S(2)}) %collective-permute-start.27) | collective-permute-done | bytes 524320 | tf_op jit(solution)/shard_map/ppermute | solution.py:97
  210.0 6.4 %multiply_reduce_fusion = (f32[]{:T(128)}, f32[8192,128]{1,0:T(8,128)}) fusion(f32[4096,128]{1,0:T(8,128)S(1)} %convolution_add_fusion.1, f32[4096,128]{1,0:T(8,128)S(1)} %convolution_add_fusion.2, bf16[256,128]{1,0:T(8,128)(2,1)S(1)} %get-tuple-element.6, bf16[256,4096]{1,0:T(8,128)(2,1)S(1)} %copy-done.3, ...), kind=kOutput, calls=%fused_computation.15 | convolution fusion | flops 553648128 | bytes 12681220 | tf_op jit(solution)/shard_map/dot_general | solution.py:183
  229.3 3.8 %collective-permute-done.36 = f32[1,128]{1,0:T(1,128)S(1)} collective-permute-done((f32[1,128]{1,0:T(1,128)S(1)}, f32[1,128]{1,0:T(1,128)S(1)}, u32[]{:S(2)}, u32[]{:S(2)}) %collective-permute-start.36) | collective-permute-done | bytes 544 | tf_op jit(solution)/shard_map/ppermute | solution.py:194
  250.5 6.5 %collective-permute-start.40 = (f32[1,128]{1,0:T(1,128)S(1)}, f32[1,128]{1,0:T(1,128)S(1)}, u32[]{:S(2)}, u32[]{:S(2)}) collective-permute-start(f32[1,128]{1,0:T(1,128)S(1)} %add.319), channel_id=1, source_target_pairs={{0,64},{32,96},{64,0},{96,32},{128,192},{160,224},{192,128},{224,1... | collective-permute-start | bytes 1544 | tf_op jit(solution)/shard_map/ppermute | solution.py:16
  258.6 5.6 %collective-permute-start.41 = (f32[1,128]{1,0:T(1,128)S(1)}, f32[1,128]{1,0:T(1,128)S(1)}, u32[]{:S(2)}, u32[]{:S(2)}) collective-permute-start(f32[1,128]{1,0:T(1,128)S(1)} %add.320), channel_id=1, source_target_pairs={{0,128},{32,160},{64,192},{96,224},{128,0},{160,32},{192,64},{224,... | collective-permute-start | bytes 1544 | tf_op jit(solution)/shard_map/ppermute | solution.py:16
  267.9 7.7 %collective-permute-start.42 = (f32[1,128]{1,0:T(1,128)S(1)}, f32[1,128]{1,0:T(1,128)S(1)}, u32[]{:S(2)}, u32[]{:S(2)}) collective-permute-start(f32[1,128]{1,0:T(1,128)S(1)} %add.321), channel_id=1, source_target_pairs={{0,384},{32,416},{64,448},{96,480},{128,256},{160,288},{192,320},{... | collective-permute-start | bytes 1544 | tf_op jit(solution)/shard_map/ppermute | solution.py:16
  277.8 3.7 %multiply_convert_fusion = bf16[8192,128]{1,0:T(8,128)(2,1)} fusion(f32[8192,128]{1,0:T(8,128)} %get-tuple-element.28, f32[]{:T(128)} %bitcast.101), kind=kLoop, calls=%fused_computation.14 | loop fusion | flops 2097152 | bytes 6291460 | tf_op jit(solution)/shard_map/convert_element_type | solution.py:199
  (195 shorter events, 146.3 us)
Async XLA Ops:
  1.5 12.4 %collective-permute-start = (bf16[1,8,4096]{2,1,0:T(8,128)(2,1)S(1)}, bf16[1,8,4096]{2,1,0:T(8,128)(2,1)S(1)}, u32[]{:S(2)}, u32[]{:S(2)}) collective-permute-start(bf16[1,8,4096]{2,1,0:T(8,128)(2,1)S(1)} %get-tuple-element.20), channel_id=1, source_target_pairs={{0,24},{1,25},{2,26},{3,27},{4,28},{5,29},{6,30},{7,31},{8,16},{9,... | collective-permute-start | bytes 196616 | tf_op jit(solution)/shard_map/ppermute | solution.py:86
  6.5 9.5 %collective-permute-start.5 = (bf16[1,8,4096]{2,1,0:T(8,128)(2,1)S(1)}, bf16[1,8,4096]{2,1,0:T(8,128)(2,1)S(1)}, u32[]{:S(2)}, u32[]{:S(2)}) collective-permute-start(bf16[1,8,4096]{2,1,0:T(8,128)(2,1)S(1)} %get-tuple-element.21), channel_id=1, source_target_pairs={{0,6},{1,7},{2,4},{3,5},{4,2},{5,3},{6,0},{7,1},{8,14},{9,15},{10,... | collective-permute-start | bytes 196616 | tf_op jit(solution)/shard_map/ppermute | solution.py:86
  16.1 7.6 %collective-permute-start.6 = (bf16[2,8,4096]{2,1,0:T(8,128)(2,1)S(1)}, bf16[2,8,4096]{2,1,0:T(8,128)(2,1)S(1)}, u32[]{:S(2)}, u32[]{:S(2)}) collective-permute-start(bf16[2,8,4096]{2,1,0:T(8,128)(2,1)S(1)} %get-tuple-element.24), channel_id=1, source_target_pairs={{0,2},{1,3},{2,0},{3,1},{4,6},{5,7},{6,4},{7,5},{8,10},{9,11},{10,... | collective-permute-start | bytes 393224 | tf_op jit(solution)/shard_map/ppermute | solution.py:86
  21.0 9.5 %collective-permute-start.2 = (bf16[4,8,4096]{2,1,0:T(8,128)(2,1)S(1)}, bf16[4,8,4096]{2,1,0:T(8,128)(2,1)S(1)}, u32[]{:S(2)}, u32[]{:S(2)}) collective-permute-start(bf16[4,8,4096]{2,1,0:T(8,128)(2,1)S(1)} %bitcast.220), channel_id=1, source_target_pairs={{0,6},{1,7},{2,4},{3,5},{4,2},{5,3},{6,0},{7,1},{8,14},{9,15},{10,... | collective-permute-start | bytes 786440 | tf_op jit(solution)/shard_map/ppermute | solution.py:86
  23.8 9.5 %collective-permute-start.7 = (bf16[4,8,4096]{2,1,0:T(8,128)(2,1)S(1)}, bf16[4,8,4096]{2,1,0:T(8,128)(2,1)S(1)}, u32[]{:S(2)}, u32[]{:S(2)}) collective-permute-start(bf16[4,8,4096]{2,1,0:T(8,128)(2,1)S(1)} %bitcast.224), channel_id=1, source_target_pairs={{0,24},{1,25},{2,26},{3,27},{4,28},{5,29},{6,30},{7,31},{8,16},{9,... | collective-permute-start | bytes 786440 | tf_op jit(solution)/shard_map/ppermute | solution.py:86
  30.6 11.1 %collective-permute-start.3 = (bf16[8,8,4096]{2,1,0:T(8,128)(2,1)S(1)}, bf16[8,8,4096]{2,1,0:T(8,128)(2,1)S(1)}, u32[]{:S(2)}, u32[]{:S(2)}) collective-permute-start(bf16[8,8,4096]{2,1,0:T(8,128)(2,1)S(1)} %bitcast.210), channel_id=1, source_target_pairs={{0,2},{1,3},{2,0},{3,1},{4,6},{5,7},{6,4},{7,5},{8,10},{9,11},{10,... | collective-permute-start | bytes 1572872 | tf_op jit(solution)/shard_map/ppermute | solution.py:86
  33.4 12.3 %collective-permute-start.8 = (bf16[8,8,4096]{2,1,0:T(8,128)(2,1)S(1)}, bf16[8,8,4096]{2,1,0:T(8,128)(2,1)S(1)}, u32[]{:S(2)}, u32[]{:S(2)}) collective-permute-start(bf16[8,8,4096]{2,1,0:T(8,128)(2,1)S(1)} %bitcast.212), channel_id=1, source_target_pairs={{0,8},{1,9},{2,10},{3,11},{4,12},{5,13},{6,14},{7,15},{8,0},{9,1},... | collective-permute-start | bytes 1572872 | tf_op jit(solution)/shard_map/ppermute | solution.py:86
  65.5 15.9 %collective-permute-start.11 = (bf16[8,8,4096]{2,1,0:T(8,128)(2,1)S(1)}, bf16[8,8,4096]{2,1,0:T(8,128)(2,1)S(1)}, u32[]{:S(2)}, u32[]{:S(2)}) collective-permute-start(bf16[8,8,4096]{2,1,0:T(8,128)(2,1)S(1)} %fusion.13), channel_id=1, source_target_pairs={{0,2},{1,3},{2,0},{3,1},{4,6},{5,7},{6,4},{7,5},{8,10},{9,11},{10,... | collective-permute-start | bytes 1572872 | tf_op jit(solution)/shard_map/ppermute | solution.py:77
  67.8 16.8 %collective-permute-start.16 = (bf16[8,8,4096]{2,1,0:T(8,128)(2,1)S(1)}, bf16[8,8,4096]{2,1,0:T(8,128)(2,1)S(1)}, u32[]{:S(2)}, u32[]{:S(2)}) collective-permute-start(bf16[8,8,4096]{2,1,0:T(8,128)(2,1)S(1)} %fusion.14), channel_id=1, source_target_pairs={{0,8},{1,9},{2,10},{3,11},{4,12},{5,13},{6,14},{7,15},{8,0},{9,1},... | collective-permute-start | bytes 1572872 | tf_op jit(solution)/shard_map/ppermute | solution.py:77
  81.5 10.6 %collective-permute-start.12 = (bf16[4,8,4096]{2,1,0:T(8,128)(2,1)S(1)}, bf16[4,8,4096]{2,1,0:T(8,128)(2,1)S(1)}, u32[]{:S(2)}, u32[]{:S(2)}) collective-permute-start(bf16[4,8,4096]{2,1,0:T(8,128)(2,1)S(1)} %fusion.15), channel_id=1, source_target_pairs={{0,6},{1,7},{2,4},{3,5},{4,2},{5,3},{6,0},{7,1},{8,14},{9,15},{10,... | collective-permute-start | bytes 786440 | tf_op jit(solution)/shard_map/ppermute | solution.py:77
  84.7 10.6 %collective-permute-start.17 = (bf16[4,8,4096]{2,1,0:T(8,128)(2,1)S(1)}, bf16[4,8,4096]{2,1,0:T(8,128)(2,1)S(1)}, u32[]{:S(2)}, u32[]{:S(2)}) collective-permute-start(bf16[4,8,4096]{2,1,0:T(8,128)(2,1)S(1)} %fusion.16), channel_id=1, source_target_pairs={{0,24},{1,25},{2,26},{3,27},{4,28},{5,29},{6,30},{7,31},{8,16},{9,... | collective-permute-start | bytes 786440 | tf_op jit(solution)/shard_map/ppermute | solution.py:77
  99.1 8.3 %collective-permute-start.14 = (bf16[1,8,4096]{2,1,0:T(8,128)(2,1)S(1)}, bf16[1,8,4096]{2,1,0:T(8,128)(2,1)S(1)}, u32[]{:S(2)}, u32[]{:S(2)}) collective-permute-start(bf16[1,8,4096]{2,1,0:T(8,128)(2,1)S(1)} %dynamic-slice_convert_fusion.7), channel_id=1, source_target_pairs={{0,24},{1,25},{2,26},{3,27},{4,28},{5,29},{6,30},{7,31},{8,16},{9,... | collective-permute-start | bytes 196616 | tf_op jit(solution)/shard_map/ppermute | solution.py:77
  117.4 9.2 %collective-permute-start.21 = (bf16[8,8192]{1,0:T(8,128)(2,1)S(1)}, bf16[8,8192]{1,0:T(8,128)(2,1)S(1)}, u32[]{:S(2)}, u32[]{:S(2)}) collective-permute-start(bf16[8,8192]{1,0:T(8,128)(2,1)S(1)} %add_convert_fusion.2), channel_id=1, source_target_pairs={{0,64},{32,96},{64,0},{96,32},{128,192},{160,224},{192,128},{224,1... | collective-permute-start | bytes 393224 | tf_op jit(solution)/shard_map/ppermute | solution.py:16
  126.6 15.6 %collective-permute-start.22 = (bf16[8,8192]{1,0:T(8,128)(2,1)S(1)}, bf16[8,8192]{1,0:T(8,128)(2,1)S(1)}, u32[]{:S(2)}, u32[]{:S(2)}) collective-permute-start(bf16[8,8192]{1,0:T(8,128)(2,1)S(1)} %add_convert_fusion.1), channel_id=1, source_target_pairs={{0,128},{32,160},{64,192},{96,224},{128,0},{160,32},{192,64},{224,... | collective-permute-start | bytes 393224 | tf_op jit(solution)/shard_map/ppermute | solution.py:16
  142.3 10.9 %collective-permute-start.23 = (bf16[8,8192]{1,0:T(8,128)(2,1)S(1)}, bf16[8,8192]{1,0:T(8,128)(2,1)S(1)}, u32[]{:S(2)}, u32[]{:S(2)}) collective-permute-start(bf16[8,8192]{1,0:T(8,128)(2,1)S(1)} %add_convert_fusion), channel_id=1, source_target_pairs={{0,384},{32,416},{64,448},{96,480},{128,256},{160,288},{192,320},{... | collective-permute-start | bytes 393224 | tf_op jit(solution)/shard_map/ppermute | solution.py:16
  154.9 7.6 %collective-permute-start.24 = (bf16[1,8,4096]{2,1,0:T(8,128)(2,1)S(1)}, bf16[1,8,4096]{2,1,0:T(8,128)(2,1)S(1)}, u32[]{:S(2)}, u32[]{:S(2)}) collective-permute-start(bf16[1,8,4096]{2,1,0:T(8,128)(2,1)S(1)} %get-tuple-element.12), channel_id=1, source_target_pairs={{0,24},{1,25},{2,26},{3,27},{4,28},{5,29},{6,30},{7,31},{8,16},{9,... | collective-permute-start | bytes 196616 | tf_op jit(solution)/shard_map/ppermute | solution.py:97
  169.5 9.5 %collective-permute-start.26 = (bf16[4,8,4096]{2,1,0:T(8,128)(2,1)S(1)}, bf16[4,8,4096]{2,1,0:T(8,128)(2,1)S(1)}, u32[]{:S(2)}, u32[]{:S(2)}) collective-permute-start(bf16[4,8,4096]{2,1,0:T(8,128)(2,1)S(1)} %bitcast.218), channel_id=1, source_target_pairs={{0,6},{1,7},{2,4},{3,5},{4,2},{5,3},{6,0},{7,1},{8,14},{9,15},{10,... | collective-permute-start | bytes 786440 | tf_op jit(solution)/shard_map/ppermute | solution.py:97
  173.9 9.5 %collective-permute-start.31 = (bf16[4,8,4096]{2,1,0:T(8,128)(2,1)S(1)}, bf16[4,8,4096]{2,1,0:T(8,128)(2,1)S(1)}, u32[]{:S(2)}, u32[]{:S(2)}) collective-permute-start(bf16[4,8,4096]{2,1,0:T(8,128)(2,1)S(1)} %bitcast.222), channel_id=1, source_target_pairs={{0,24},{1,25},{2,26},{3,27},{4,28},{5,29},{6,30},{7,31},{8,16},{9,... | collective-permute-start | bytes 786440 | tf_op jit(solution)/shard_map/ppermute | solution.py:97
  179.1 11.1 %collective-permute-start.27 = (bf16[8,8,4096]{2,1,0:T(8,128)(2,1)S(1)}, bf16[8,8,4096]{2,1,0:T(8,128)(2,1)S(1)}, u32[]{:S(2)}, u32[]{:S(2)}) collective-permute-start(bf16[8,8,4096]{2,1,0:T(8,128)(2,1)S(1)} %bitcast.206), channel_id=1, source_target_pairs={{0,2},{1,3},{2,0},{3,1},{4,6},{5,7},{6,4},{7,5},{8,10},{9,11},{10,... | collective-permute-start | bytes 1572872 | tf_op jit(solution)/shard_map/ppermute | solution.py:97
  183.6 11.1 %collective-permute-start.32 = (bf16[8,8,4096]{2,1,0:T(8,128)(2,1)S(1)}, bf16[8,8,4096]{2,1,0:T(8,128)(2,1)S(1)}, u32[]{:S(2)}, u32[]{:S(2)}) collective-permute-start(bf16[8,8,4096]{2,1,0:T(8,128)(2,1)S(1)} %bitcast.208), channel_id=1, source_target_pairs={{0,8},{1,9},{2,10},{3,11},{4,12},{5,13},{6,14},{7,15},{8,0},{9,1},... | collective-permute-start | bytes 1572872 | tf_op jit(solution)/shard_map/ppermute | solution.py:97
  190.5 11.0 %collective-permute-start.28 = (bf16[16,8,4096]{2,1,0:T(8,128)(2,1)S(1)}, bf16[16,8,4096]{2,1,0:T(8,128)(2,1)S(1)}, u32[]{:S(2)}, u32[]{:S(2)}) collective-permute-start(bf16[16,8,4096]{2,1,0:T(8,128)(2,1)S(1)} %bitcast.192), channel_id=1, source_target_pairs={{0,1},{1,0},{2,3},{3,2},{4,5},{5,4},{6,7},{7,6},{8,9},{9,8},{10,11... | collective-permute-start | bytes 3145736 | tf_op jit(solution)/shard_map/ppermute | solution.py:100
  250.5 8.0 %collective-permute-start.40 = (f32[1,128]{1,0:T(1,128)S(1)}, f32[1,128]{1,0:T(1,128)S(1)}, u32[]{:S(2)}, u32[]{:S(2)}) collective-permute-start(f32[1,128]{1,0:T(1,128)S(1)} %add.319), channel_id=1, source_target_pairs={{0,64},{32,96},{64,0},{96,32},{128,192},{160,224},{192,128},{224,1... | collective-permute-start | bytes 1544 | tf_op jit(solution)/shard_map/ppermute | solution.py:16
  258.6 9.3 %collective-permute-start.41 = (f32[1,128]{1,0:T(1,128)S(1)}, f32[1,128]{1,0:T(1,128)S(1)}, u32[]{:S(2)}, u32[]{:S(2)}) collective-permute-start(f32[1,128]{1,0:T(1,128)S(1)} %add.320), channel_id=1, source_target_pairs={{0,128},{32,160},{64,192},{96,224},{128,0},{160,32},{192,64},{224,... | collective-permute-start | bytes 1544 | tf_op jit(solution)/shard_map/ppermute | solution.py:16
  267.9 9.3 %collective-permute-start.42 = (f32[1,128]{1,0:T(1,128)S(1)}, f32[1,128]{1,0:T(1,128)S(1)}, u32[]{:S(2)}, u32[]{:S(2)}) collective-permute-start(f32[1,128]{1,0:T(1,128)S(1)} %add.321), channel_id=1, source_target_pairs={{0,384},{32,416},{64,448},{96,480},{128,256},{160,288},{192,320},{... | collective-permute-start | bytes 1544 | tf_op jit(solution)/shard_map/ppermute | solution.py:16
  (34 other events, 162.8 us)

commit v11 on v6

--- a/solution.py
+++ b/solution.py
@@ -158,7 +158,7 @@
         (((0,), (0,)), ((), ())),
         preferred_element_type=jnp.float32,
     )
-    grad_raw = encoder_grad + decoder_grad
+    grad_raw = lax.optimization_barrier(encoder_grad + decoder_grad)
     bias_raw = jnp.sum(grad_pre, axis=0)
     local_squares = jnp.sum(grad_raw * grad_raw) + jnp.sum(bias_raw * bias_raw)
     squares = jnp.broadcast_to(local_squares, (1, 128))

time: 281 us -> 279 us (level)
  matrix products: 16.6 us -> 11.8 us
    dot_general x1, matrix products: 6.4 us -> 1.53 us  [body(): lax.dot_general(centered, grad_pre.astype(jnp.bfloat16), (((0,), (0,)), (...]
where the time goes in v11:
time: 279 us; the launch traced here: 277 us
  starting transfers between devices  140 us (50%)
  waiting for transfers between devices  95 us (34%)
  other arithmetic  16.2 us (6%)
  matrix products  11.8 us (4%)
  local copies, waits for them, and re-layouts  11.1 us (4%)
  between operations  3.17 us (1%)
    ppermute x20, starting transfers between devices, doubling_gather(): got = lax.ppermute(acc, 'lat', masked_pairs(n, masks[j]))  55.7 us
    ppermute x8, starting transfers between devices, butterfly_sum(): lax.ppermute(sent, axis, masked_pairs(n, mask)).astype(jnp.float32)  42.9 us
    ppermute x8, waiting for transfers between devices, butterfly_sum(): lax.ppermute(sent, axis, masked_pairs(n, mask)).astype(jnp.float32)  31.6 us
    ppermute x10, starting transfers between devices, halving_scatter(): lax.ppermute(sent, 'lat', masked_pairs(n, mask)).astype(jnp.float32)  29.4 us
    ppermute x20, waiting for transfers between devices, doubling_gather(): got = lax.ppermute(acc, 'lat', masked_pairs(n, masks[j]))  29.1 us
    ppermute x10, waiting for transfers between devices, halving_scatter(): lax.ppermute(sent, 'lat', masked_pairs(n, mask)).astype(jnp.float32)  18.9 us
    ppermute x5, waiting for transfers between devices, body(): squares = squares + lax.ppermute(squares, 'lat', masked_pairs(n_lat, mask))  15.4 us
    ppermute x5, starting transfers between devices, body(): squares = squares + lax.ppermute(squares, 'lat', masked_pairs(n_lat, mask))  11.7 us
  transfers between devices with their start and end apart: 43, of which 32 were waited for; matrix products, arithmetic and copies ran while one was open for 4% of the time, Pallas kernels for 0%

profile of v11, /device:TPU:6, one launch (start us, length us, event | category | flops | bytes accessed | tf_op | source)
XLA Modules:
  0.0 277.0 jit_solution(15455822215964568785)
XLA Ops:
  1.5 4.9 %collective-permute-start = (bf16[1,8,4096]{2,1,0:T(8,128)(2,1)S(1)}, bf16[1,8,4096]{2,1,0:T(8,128)(2,1)S(1)}, u32[]{:S(2)}, u32[]{:S(2)}) collective-permute-start(bf16[1,8,4096]{2,1,0:T(8,128)(2,1)S(1)} %get-tuple-element.18), channel_id=1, source_target_pairs={{0,24},{1,25},{2,26},{3,27},{4,28},{5,29},{6,30},{7,31},{8,16},{9,... | collective-permute-start | bytes 196616 | tf_op jit(solution)/shard_map/ppermute | solution.py:86
  6.5 4.8 %collective-permute-start.5 = (bf16[1,8,4096]{2,1,0:T(8,128)(2,1)S(1)}, bf16[1,8,4096]{2,1,0:T(8,128)(2,1)S(1)}, u32[]{:S(2)}, u32[]{:S(2)}) collective-permute-start(bf16[1,8,4096]{2,1,0:T(8,128)(2,1)S(1)} %get-tuple-element.19), channel_id=1, source_target_pairs={{0,6},{1,7},{2,4},{3,5},{4,2},{5,3},{6,0},{7,1},{8,14},{9,15},{10,... | collective-permute-start | bytes 196616 | tf_op jit(solution)/shard_map/ppermute | solution.py:86
  23.8 4.4 %collective-permute-start.7 = (bf16[4,8,4096]{2,1,0:T(8,128)(2,1)S(1)}, bf16[4,8,4096]{2,1,0:T(8,128)(2,1)S(1)}, u32[]{:S(2)}, u32[]{:S(2)}) collective-permute-start(bf16[4,8,4096]{2,1,0:T(8,128)(2,1)S(1)} %bitcast.210), channel_id=1, source_target_pairs={{0,24},{1,25},{2,26},{3,27},{4,28},{5,29},{6,30},{7,31},{8,16},{9,... | collective-permute-start | bytes 786440 | tf_op jit(solution)/shard_map/ppermute | solution.py:86
  36.0 5.7 %collective-permute-done.3 = bf16[8,8,4096]{2,1,0:T(8,128)(2,1)S(1)} collective-permute-done((bf16[8,8,4096]{2,1,0:T(8,128)(2,1)S(1)}, bf16[8,8,4096]{2,1,0:T(8,128)(2,1)S(1)}, u32[]{:S(2)}, u32[]{:S(2)}) %collective-permute-start.3) | collective-permute-done | bytes 524320 | tf_op jit(solution)/shard_map/ppermute | solution.py:86
  69.4 11.4 %collective-permute-done.11 = bf16[8,8,4096]{2,1,0:T(8,128)(2,1)S(1)} collective-permute-done((bf16[8,8,4096]{2,1,0:T(8,128)(2,1)S(1)}, bf16[8,8,4096]{2,1,0:T(8,128)(2,1)S(1)}, u32[]{:S(2)}, u32[]{:S(2)}) %collective-permute-start.11) | collective-permute-done | bytes 524320 | tf_op jit(solution)/shard_map/ppermute | solution.py:77
  84.2 5.1 %collective-permute-start.17 = (bf16[4,8,4096]{2,1,0:T(8,128)(2,1)S(1)}, bf16[4,8,4096]{2,1,0:T(8,128)(2,1)S(1)}, u32[]{:S(2)}, u32[]{:S(2)}) collective-permute-start(bf16[4,8,4096]{2,1,0:T(8,128)(2,1)S(1)} %fusion.14), channel_id=1, source_target_pairs={{0,24},{1,25},{2,26},{3,27},{4,28},{5,29},{6,30},{7,31},{8,16},{9,... | collective-permute-start | bytes 786440 | tf_op jit(solution)/shard_map/ppermute | solution.py:77
  98.5 3.9 %collective-permute-start.14 = (bf16[1,8,4096]{2,1,0:T(8,128)(2,1)S(1)}, bf16[1,8,4096]{2,1,0:T(8,128)(2,1)S(1)}, u32[]{:S(2)}, u32[]{:S(2)}) collective-permute-start(bf16[1,8,4096]{2,1,0:T(8,128)(2,1)S(1)} %dynamic-slice_convert_fusion.7), channel_id=1, source_target_pairs={{0,24},{1,25},{2,26},{3,27},{4,28},{5,29},{6,30},{7,31},{8,16},{9,... | collective-permute-start | bytes 196616 | tf_op jit(solution)/shard_map/ppermute | solution.py:77
  102.6 4.3 %collective-permute-start.19 = (bf16[1,8,4096]{2,1,0:T(8,128)(2,1)S(1)}, bf16[1,8,4096]{2,1,0:T(8,128)(2,1)S(1)}, u32[]{:S(2)}, u32[]{:S(2)}) collective-permute-start(bf16[1,8,4096]{2,1,0:T(8,128)(2,1)S(1)} %dynamic-slice_convert_fusion.6), channel_id=1, source_target_pairs={{0,6},{1,7},{2,4},{3,5},{4,2},{5,3},{6,0},{7,1},{8,14},{9,15},{10,... | collective-permute-start | bytes 196616 | tf_op jit(solution)/shard_map/ppermute | solution.py:77
  112.2 4.6 %collective-permute-done.20 = bf16[8,8192]{1,0:T(8,128)(2,1)S(1)} collective-permute-done((bf16[8,8192]{1,0:T(8,128)(2,1)S(1)}, bf16[8,8192]{1,0:T(8,128)(2,1)S(1)}, u32[]{:S(2)}, u32[]{:S(2)}) %collective-permute-start.20) | collective-permute-done | bytes 131104 | tf_op jit(solution)/shard_map/ppermute | solution.py:16
  116.9 3.8 %collective-permute-start.21 = (bf16[8,8192]{1,0:T(8,128)(2,1)S(1)}, bf16[8,8192]{1,0:T(8,128)(2,1)S(1)}, u32[]{:S(2)}, u32[]{:S(2)}) collective-permute-start(bf16[8,8192]{1,0:T(8,128)(2,1)S(1)} %add_convert_fusion.2), channel_id=1, source_target_pairs={{0,64},{32,96},{64,0},{96,32},{128,192},{160,224},{192,128},{224,1... | collective-permute-start | bytes 393224 | tf_op jit(solution)/shard_map/ppermute | solution.py:16
  120.7 5.3 %collective-permute-done.21 = bf16[8,8192]{1,0:T(8,128)(2,1)S(1)} collective-permute-done((bf16[8,8192]{1,0:T(8,128)(2,1)S(1)}, bf16[8,8192]{1,0:T(8,128)(2,1)S(1)}, u32[]{:S(2)}, u32[]{:S(2)}) %collective-permute-start.21) | collective-permute-done | bytes 131104 | tf_op jit(solution)/shard_map/ppermute | solution.py:16
  126.1 8.5 %collective-permute-start.22 = (bf16[8,8192]{1,0:T(8,128)(2,1)S(1)}, bf16[8,8192]{1,0:T(8,128)(2,1)S(1)}, u32[]{:S(2)}, u32[]{:S(2)}) collective-permute-start(bf16[8,8192]{1,0:T(8,128)(2,1)S(1)} %add_convert_fusion.1), channel_id=1, source_target_pairs={{0,128},{32,160},{64,192},{96,224},{128,0},{160,32},{192,64},{224,... | collective-permute-start | bytes 393224 | tf_op jit(solution)/shard_map/ppermute | solution.py:16
  134.6 7.1 %collective-permute-done.22 = bf16[8,8192]{1,0:T(8,128)(2,1)S(1)} collective-permute-done((bf16[8,8192]{1,0:T(8,128)(2,1)S(1)}, bf16[8,8192]{1,0:T(8,128)(2,1)S(1)}, u32[]{:S(2)}, u32[]{:S(2)}) %collective-permute-start.22) | collective-permute-done | bytes 131104 | tf_op jit(solution)/shard_map/ppermute | solution.py:16
  141.8 6.4 %collective-permute-start.23 = (bf16[8,8192]{1,0:T(8,128)(2,1)S(1)}, bf16[8,8192]{1,0:T(8,128)(2,1)S(1)}, u32[]{:S(2)}, u32[]{:S(2)}) collective-permute-start(bf16[8,8192]{1,0:T(8,128)(2,1)S(1)} %add_convert_fusion), channel_id=1, source_target_pairs={{0,384},{32,416},{64,448},{96,480},{128,256},{160,288},{192,320},{... | collective-permute-start | bytes 393224 | tf_op jit(solution)/shard_map/ppermute | solution.py:16
  148.2 4.5 %collective-permute-done.23 = bf16[8,8192]{1,0:T(8,128)(2,1)S(1)} collective-permute-done((bf16[8,8192]{1,0:T(8,128)(2,1)S(1)}, bf16[8,8192]{1,0:T(8,128)(2,1)S(1)}, u32[]{:S(2)}, u32[]{:S(2)}) %collective-permute-start.23) | collective-permute-done | bytes 131104 | tf_op jit(solution)/shard_map/ppermute | solution.py:16
  154.4 4.6 %collective-permute-start.24 = (bf16[1,8,4096]{2,1,0:T(8,128)(2,1)S(1)}, bf16[1,8,4096]{2,1,0:T(8,128)(2,1)S(1)}, u32[]{:S(2)}, u32[]{:S(2)}) collective-permute-start(bf16[1,8,4096]{2,1,0:T(8,128)(2,1)S(1)} %get-tuple-element.10), channel_id=1, source_target_pairs={{0,24},{1,25},{2,26},{3,27},{4,28},{5,29},{6,30},{7,31},{8,16},{9,... | collective-permute-start | bytes 196616 | tf_op jit(solution)/shard_map/ppermute | solution.py:86
  168.9 4.2 %collective-permute-start.26 = (bf16[4,8,4096]{2,1,0:T(8,128)(2,1)S(1)}, bf16[4,8,4096]{2,1,0:T(8,128)(2,1)S(1)}, u32[]{:S(2)}, u32[]{:S(2)}) collective-permute-start(bf16[4,8,4096]{2,1,0:T(8,128)(2,1)S(1)} %bitcast.204), channel_id=1, source_target_pairs={{0,6},{1,7},{2,4},{3,5},{4,2},{5,3},{6,0},{7,1},{8,14},{9,15},{10,... | collective-permute-start | bytes 786440 | tf_op jit(solution)/shard_map/ppermute | solution.py:86
  184.9 4.7 %collective-permute-done.27 = bf16[8,8,4096]{2,1,0:T(8,128)(2,1)S(1)} collective-permute-done((bf16[8,8,4096]{2,1,0:T(8,128)(2,1)S(1)}, bf16[8,8,4096]{2,1,0:T(8,128)(2,1)S(1)}, u32[]{:S(2)}, u32[]{:S(2)}) %collective-permute-start.27) | collective-permute-done | bytes 524320 | tf_op jit(solution)/shard_map/ppermute | solution.py:86
  224.8 3.7 %collective-permute-done.36 = f32[1,128]{1,0:T(1,128)S(1)} collective-permute-done((f32[1,128]{1,0:T(1,128)S(1)}, f32[1,128]{1,0:T(1,128)S(1)}, u32[]{:S(2)}, u32[]{:S(2)}) %collective-permute-start.36) | collective-permute-done | bytes 544 | tf_op jit(solution)/shard_map/ppermute | solution.py:166
  237.0 3.6 %collective-permute-done.38 = f32[1,128]{1,0:T(1,128)S(1)} collective-permute-done((f32[1,128]{1,0:T(1,128)S(1)}, f32[1,128]{1,0:T(1,128)S(1)}, u32[]{:S(2)}, u32[]{:S(2)}) %collective-permute-start.38) | collective-permute-done | bytes 544 | tf_op jit(solution)/shard_map/ppermute | solution.py:166
  246.1 6.4 %collective-permute-start.40 = (f32[1,128]{1,0:T(1,128)S(1)}, f32[1,128]{1,0:T(1,128)S(1)}, u32[]{:S(2)}, u32[]{:S(2)}) collective-permute-start(f32[1,128]{1,0:T(1,128)S(1)} %add.295), channel_id=1, source_target_pairs={{0,64},{32,96},{64,0},{96,32},{128,192},{160,224},{192,128},{224,1... | collective-permute-start | bytes 1544 | tf_op jit(solution)/shard_map/ppermute | solution.py:16
  254.0 5.7 %collective-permute-start.41 = (f32[1,128]{1,0:T(1,128)S(1)}, f32[1,128]{1,0:T(1,128)S(1)}, u32[]{:S(2)}, u32[]{:S(2)}) collective-permute-start(f32[1,128]{1,0:T(1,128)S(1)} %add.296), channel_id=1, source_target_pairs={{0,128},{32,160},{64,192},{96,224},{128,0},{160,32},{192,64},{224,... | collective-permute-start | bytes 1544 | tf_op jit(solution)/shard_map/ppermute | solution.py:16
  263.3 7.8 %collective-permute-start.42 = (f32[1,128]{1,0:T(1,128)S(1)}, f32[1,128]{1,0:T(1,128)S(1)}, u32[]{:S(2)}, u32[]{:S(2)}) collective-permute-start(f32[1,128]{1,0:T(1,128)S(1)} %add.297), channel_id=1, source_target_pairs={{0,384},{32,416},{64,448},{96,480},{128,256},{160,288},{192,320},{... | collective-permute-start | bytes 1544 | tf_op jit(solution)/shard_map/ppermute | solution.py:16
  273.3 3.7 %multiply_convert_fusion = bf16[8192,128]{1,0:T(8,128)(2,1)} fusion(f32[8192,128]{1,0:T(8,128)} %copy-done.3, f32[]{:T(128)} %bitcast.99), kind=kLoop, calls=%fused_computation.12 | loop fusion | flops 2097152 | bytes 6291460 | tf_op jit(solution)/shard_map/convert_element_type | solution.py:171
  (193 shorter events, 144.4 us)
Async XLA Ops:
  1.5 12.5 %collective-permute-start = (bf16[1,8,4096]{2,1,0:T(8,128)(2,1)S(1)}, bf16[1,8,4096]{2,1,0:T(8,128)(2,1)S(1)}, u32[]{:S(2)}, u32[]{:S(2)}) collective-permute-start(bf16[1,8,4096]{2,1,0:T(8,128)(2,1)S(1)} %get-tuple-element.18), channel_id=1, source_target_pairs={{0,24},{1,25},{2,26},{3,27},{4,28},{5,29},{6,30},{7,31},{8,16},{9,... | collective-permute-start | bytes 196616 | tf_op jit(solution)/shard_map/ppermute | solution.py:86
  6.5 9.5 %collective-permute-start.5 = (bf16[1,8,4096]{2,1,0:T(8,128)(2,1)S(1)}, bf16[1,8,4096]{2,1,0:T(8,128)(2,1)S(1)}, u32[]{:S(2)}, u32[]{:S(2)}) collective-permute-start(bf16[1,8,4096]{2,1,0:T(8,128)(2,1)S(1)} %get-tuple-element.19), channel_id=1, source_target_pairs={{0,6},{1,7},{2,4},{3,5},{4,2},{5,3},{6,0},{7,1},{8,14},{9,15},{10,... | collective-permute-start | bytes 196616 | tf_op jit(solution)/shard_map/ppermute | solution.py:86
  16.1 7.6 %collective-permute-start.6 = (bf16[2,8,4096]{2,1,0:T(8,128)(2,1)S(1)}, bf16[2,8,4096]{2,1,0:T(8,128)(2,1)S(1)}, u32[]{:S(2)}, u32[]{:S(2)}) collective-permute-start(bf16[2,8,4096]{2,1,0:T(8,128)(2,1)S(1)} %get-tuple-element.22), channel_id=1, source_target_pairs={{0,2},{1,3},{2,0},{3,1},{4,6},{5,7},{6,4},{7,5},{8,10},{9,11},{10,... | collective-permute-start | bytes 393224 | tf_op jit(solution)/shard_map/ppermute | solution.py:86
  21.0 9.5 %collective-permute-start.2 = (bf16[4,8,4096]{2,1,0:T(8,128)(2,1)S(1)}, bf16[4,8,4096]{2,1,0:T(8,128)(2,1)S(1)}, u32[]{:S(2)}, u32[]{:S(2)}) collective-permute-start(bf16[4,8,4096]{2,1,0:T(8,128)(2,1)S(1)} %bitcast.206), channel_id=1, source_target_pairs={{0,6},{1,7},{2,4},{3,5},{4,2},{5,3},{6,0},{7,1},{8,14},{9,15},{10,... | collective-permute-start | bytes 786440 | tf_op jit(solution)/shard_map/ppermute | solution.py:86
  23.8 9.5 %collective-permute-start.7 = (bf16[4,8,4096]{2,1,0:T(8,128)(2,1)S(1)}, bf16[4,8,4096]{2,1,0:T(8,128)(2,1)S(1)}, u32[]{:S(2)}, u32[]{:S(2)}) collective-permute-start(bf16[4,8,4096]{2,1,0:T(8,128)(2,1)S(1)} %bitcast.210), channel_id=1, source_target_pairs={{0,24},{1,25},{2,26},{3,27},{4,28},{5,29},{6,30},{7,31},{8,16},{9,... | collective-permute-start | bytes 786440 | tf_op jit(solution)/shard_map/ppermute | solution.py:86
  30.6 11.1 %collective-permute-start.3 = (bf16[8,8,4096]{2,1,0:T(8,128)(2,1)S(1)}, bf16[8,8,4096]{2,1,0:T(8,128)(2,1)S(1)}, u32[]{:S(2)}, u32[]{:S(2)}) collective-permute-start(bf16[8,8,4096]{2,1,0:T(8,128)(2,1)S(1)} %bitcast.196), channel_id=1, source_target_pairs={{0,2},{1,3},{2,0},{3,1},{4,6},{5,7},{6,4},{7,5},{8,10},{9,11},{10,... | collective-permute-start | bytes 1572872 | tf_op jit(solution)/shard_map/ppermute | solution.py:86
  33.4 12.3 %collective-permute-start.8 = (bf16[8,8,4096]{2,1,0:T(8,128)(2,1)S(1)}, bf16[8,8,4096]{2,1,0:T(8,128)(2,1)S(1)}, u32[]{:S(2)}, u32[]{:S(2)}) collective-permute-start(bf16[8,8,4096]{2,1,0:T(8,128)(2,1)S(1)} %bitcast.198), channel_id=1, source_target_pairs={{0,8},{1,9},{2,10},{3,11},{4,12},{5,13},{6,14},{7,15},{8,0},{9,1},... | collective-permute-start | bytes 1572872 | tf_op jit(solution)/shard_map/ppermute | solution.py:86
  64.9 15.9 %collective-permute-start.11 = (bf16[8,8,4096]{2,1,0:T(8,128)(2,1)S(1)}, bf16[8,8,4096]{2,1,0:T(8,128)(2,1)S(1)}, u32[]{:S(2)}, u32[]{:S(2)}) collective-permute-start(bf16[8,8,4096]{2,1,0:T(8,128)(2,1)S(1)} %fusion.11), channel_id=1, source_target_pairs={{0,2},{1,3},{2,0},{3,1},{4,6},{5,7},{6,4},{7,5},{8,10},{9,11},{10,... | collective-permute-start | bytes 1572872 | tf_op jit(solution)/shard_map/ppermute | solution.py:77
  67.2 16.8 %collective-permute-start.16 = (bf16[8,8,4096]{2,1,0:T(8,128)(2,1)S(1)}, bf16[8,8,4096]{2,1,0:T(8,128)(2,1)S(1)}, u32[]{:S(2)}, u32[]{:S(2)}) collective-permute-start(bf16[8,8,4096]{2,1,0:T(8,128)(2,1)S(1)} %fusion.12), channel_id=1, source_target_pairs={{0,8},{1,9},{2,10},{3,11},{4,12},{5,13},{6,14},{7,15},{8,0},{9,1},... | collective-permute-start | bytes 1572872 | tf_op jit(solution)/shard_map/ppermute | solution.py:77
  80.9 10.6 %collective-permute-start.12 = (bf16[4,8,4096]{2,1,0:T(8,128)(2,1)S(1)}, bf16[4,8,4096]{2,1,0:T(8,128)(2,1)S(1)}, u32[]{:S(2)}, u32[]{:S(2)}) collective-permute-start(bf16[4,8,4096]{2,1,0:T(8,128)(2,1)S(1)} %fusion.13), channel_id=1, source_target_pairs={{0,6},{1,7},{2,4},{3,5},{4,2},{5,3},{6,0},{7,1},{8,14},{9,15},{10,... | collective-permute-start | bytes 786440 | tf_op jit(solution)/shard_map/ppermute | solution.py:77
  84.2 10.6 %collective-permute-start.17 = (bf16[4,8,4096]{2,1,0:T(8,128)(2,1)S(1)}, bf16[4,8,4096]{2,1,0:T(8,128)(2,1)S(1)}, u32[]{:S(2)}, u32[]{:S(2)}) collective-permute-start(bf16[4,8,4096]{2,1,0:T(8,128)(2,1)S(1)} %fusion.14), channel_id=1, source_target_pairs={{0,24},{1,25},{2,26},{3,27},{4,28},{5,29},{6,30},{7,31},{8,16},{9,... | collective-permute-start | bytes 786440 | tf_op jit(solution)/shard_map/ppermute | solution.py:77
  94.9 7.6 %collective-permute-start.18 = (bf16[2,8,4096]{2,1,0:T(8,128)(2,1)S(1)}, bf16[2,8,4096]{2,1,0:T(8,128)(2,1)S(1)}, u32[]{:S(2)}, u32[]{:S(2)}) collective-permute-start(bf16[2,8,4096]{2,1,0:T(8,128)(2,1)S(1)} %fusion.18), channel_id=1, source_target_pairs={{0,2},{1,3},{2,0},{3,1},{4,6},{5,7},{6,4},{7,5},{8,10},{9,11},{10,... | collective-permute-start | bytes 393224 | tf_op jit(solution)/shard_map/ppermute | solution.py:77
  98.5 8.3 %collective-permute-start.14 = (bf16[1,8,4096]{2,1,0:T(8,128)(2,1)S(1)}, bf16[1,8,4096]{2,1,0:T(8,128)(2,1)S(1)}, u32[]{:S(2)}, u32[]{:S(2)}) collective-permute-start(bf16[1,8,4096]{2,1,0:T(8,128)(2,1)S(1)} %dynamic-slice_convert_fusion.7), channel_id=1, source_target_pairs={{0,24},{1,25},{2,26},{3,27},{4,28},{5,29},{6,30},{7,31},{8,16},{9,... | collective-permute-start | bytes 196616 | tf_op jit(solution)/shard_map/ppermute | solution.py:77
  116.9 9.2 %collective-permute-start.21 = (bf16[8,8192]{1,0:T(8,128)(2,1)S(1)}, bf16[8,8192]{1,0:T(8,128)(2,1)S(1)}, u32[]{:S(2)}, u32[]{:S(2)}) collective-permute-start(bf16[8,8192]{1,0:T(8,128)(2,1)S(1)} %add_convert_fusion.2), channel_id=1, source_target_pairs={{0,64},{32,96},{64,0},{96,32},{128,192},{160,224},{192,128},{224,1... | collective-permute-start | bytes 393224 | tf_op jit(solution)/shard_map/ppermute | solution.py:16
  126.1 15.7 %collective-permute-start.22 = (bf16[8,8192]{1,0:T(8,128)(2,1)S(1)}, bf16[8,8192]{1,0:T(8,128)(2,1)S(1)}, u32[]{:S(2)}, u32[]{:S(2)}) collective-permute-start(bf16[8,8192]{1,0:T(8,128)(2,1)S(1)} %add_convert_fusion.1), channel_id=1, source_target_pairs={{0,128},{32,160},{64,192},{96,224},{128,0},{160,32},{192,64},{224,... | collective-permute-start | bytes 393224 | tf_op jit(solution)/shard_map/ppermute | solution.py:16
  141.8 10.9 %collective-permute-start.23 = (bf16[8,8192]{1,0:T(8,128)(2,1)S(1)}, bf16[8,8192]{1,0:T(8,128)(2,1)S(1)}, u32[]{:S(2)}, u32[]{:S(2)}) collective-permute-start(bf16[8,8192]{1,0:T(8,128)(2,1)S(1)} %add_convert_fusion), channel_id=1, source_target_pairs={{0,384},{32,416},{64,448},{96,480},{128,256},{160,288},{192,320},{... | collective-permute-start | bytes 393224 | tf_op jit(solution)/shard_map/ppermute | solution.py:16
  154.4 7.5 %collective-permute-start.24 = (bf16[1,8,4096]{2,1,0:T(8,128)(2,1)S(1)}, bf16[1,8,4096]{2,1,0:T(8,128)(2,1)S(1)}, u32[]{:S(2)}, u32[]{:S(2)}) collective-permute-start(bf16[1,8,4096]{2,1,0:T(8,128)(2,1)S(1)} %get-tuple-element.10), channel_id=1, source_target_pairs={{0,24},{1,25},{2,26},{3,27},{4,28},{5,29},{6,30},{7,31},{8,16},{9,... | collective-permute-start | bytes 196616 | tf_op jit(solution)/shard_map/ppermute | solution.py:86
  168.9 9.5 %collective-permute-start.26 = (bf16[4,8,4096]{2,1,0:T(8,128)(2,1)S(1)}, bf16[4,8,4096]{2,1,0:T(8,128)(2,1)S(1)}, u32[]{:S(2)}, u32[]{:S(2)}) collective-permute-start(bf16[4,8,4096]{2,1,0:T(8,128)(2,1)S(1)} %bitcast.204), channel_id=1, source_target_pairs={{0,6},{1,7},{2,4},{3,5},{4,2},{5,3},{6,0},{7,1},{8,14},{9,15},{10,... | collective-permute-start | bytes 786440 | tf_op jit(solution)/shard_map/ppermute | solution.py:86
  173.3 9.5 %collective-permute-start.31 = (bf16[4,8,4096]{2,1,0:T(8,128)(2,1)S(1)}, bf16[4,8,4096]{2,1,0:T(8,128)(2,1)S(1)}, u32[]{:S(2)}, u32[]{:S(2)}) collective-permute-start(bf16[4,8,4096]{2,1,0:T(8,128)(2,1)S(1)} %bitcast.208), channel_id=1, source_target_pairs={{0,24},{1,25},{2,26},{3,27},{4,28},{5,29},{6,30},{7,31},{8,16},{9,... | collective-permute-start | bytes 786440 | tf_op jit(solution)/shard_map/ppermute | solution.py:86
  178.5 11.1 %collective-permute-start.27 = (bf16[8,8,4096]{2,1,0:T(8,128)(2,1)S(1)}, bf16[8,8,4096]{2,1,0:T(8,128)(2,1)S(1)}, u32[]{:S(2)}, u32[]{:S(2)}) collective-permute-start(bf16[8,8,4096]{2,1,0:T(8,128)(2,1)S(1)} %bitcast.192), channel_id=1, source_target_pairs={{0,2},{1,3},{2,0},{3,1},{4,6},{5,7},{6,4},{7,5},{8,10},{9,11},{10,... | collective-permute-start | bytes 1572872 | tf_op jit(solution)/shard_map/ppermute | solution.py:86
  183.0 11.1 %collective-permute-start.32 = (bf16[8,8,4096]{2,1,0:T(8,128)(2,1)S(1)}, bf16[8,8,4096]{2,1,0:T(8,128)(2,1)S(1)}, u32[]{:S(2)}, u32[]{:S(2)}) collective-permute-start(bf16[8,8,4096]{2,1,0:T(8,128)(2,1)S(1)} %bitcast.194), channel_id=1, source_target_pairs={{0,8},{1,9},{2,10},{3,11},{4,12},{5,13},{6,14},{7,15},{8,0},{9,1},... | collective-permute-start | bytes 1572872 | tf_op jit(solution)/shard_map/ppermute | solution.py:86
  246.1 7.9 %collective-permute-start.40 = (f32[1,128]{1,0:T(1,128)S(1)}, f32[1,128]{1,0:T(1,128)S(1)}, u32[]{:S(2)}, u32[]{:S(2)}) collective-permute-start(f32[1,128]{1,0:T(1,128)S(1)} %add.295), channel_id=1, source_target_pairs={{0,64},{32,96},{64,0},{96,32},{128,192},{160,224},{192,128},{224,1... | collective-permute-start | bytes 1544 | tf_op jit(solution)/shard_map/ppermute | solution.py:16
  254.0 9.3 %collective-permute-start.41 = (f32[1,128]{1,0:T(1,128)S(1)}, f32[1,128]{1,0:T(1,128)S(1)}, u32[]{:S(2)}, u32[]{:S(2)}) collective-permute-start(f32[1,128]{1,0:T(1,128)S(1)} %add.296), channel_id=1, source_target_pairs={{0,128},{32,160},{64,192},{96,224},{128,0},{160,32},{192,64},{224,... | collective-permute-start | bytes 1544 | tf_op jit(solution)/shard_map/ppermute | solution.py:16
  263.3 9.3 %collective-permute-start.42 = (f32[1,128]{1,0:T(1,128)S(1)}, f32[1,128]{1,0:T(1,128)S(1)}, u32[]{:S(2)}, u32[]{:S(2)}) collective-permute-start(f32[1,128]{1,0:T(1,128)S(1)} %add.297), channel_id=1, source_target_pairs={{0,384},{32,416},{64,448},{96,480},{128,256},{160,288},{192,320},{... | collective-permute-start | bytes 1544 | tf_op jit(solution)/shard_map/ppermute | solution.py:16
  (35 other events, 264.0 us)

commit v12 on v11

--- a/solution.py
+++ b/solution.py
@@ -128,6 +128,7 @@
     active = (jax.nn.softplus(sharpness * preact) / sharpness).astype(jnp.bfloat16)
     own_block = logical_rank(rank_lat, order_a)
     own_batch = lax.dynamic_slice_in_dim(batch, own_block * own_rows, own_rows, 0)
+    own_offset = lax.optimization_barrier(dec_bias - own_batch.astype(jnp.float32))
     active_b = take_blocks(active, block_perm(order_a, order_b, n_lat), own_rows)
     halves = []
     for k, (masks, rows) in enumerate(zip(ORDERS, (active, active_b))):
@@ -137,7 +138,7 @@
         halves.append(halving_scatter(part.reshape(n_lat, own_rows, cols), rank_lat, n_lat, masks))
     block_recon = jnp.concatenate(halves, axis=1)
     recon = butterfly_sum(block_recon.astype(jnp.float32), "grp", n_grp, jnp.bfloat16, GRP_MASKS)
-    error_own = recon + dec_bias - own_batch.astype(jnp.float32)
+    error_own = recon + own_offset
     grad_own = (2.0 * error_own).astype(jnp.bfloat16)
     grad_a, grad_b = [g.reshape(n_tok, cols) for g in column_halves(grad_own, rank_lat, n_lat)]
     active_part_b = jnp.dot(grad_b, weight[cols:], preferred_element_type=jnp.float32)

time: 279 us -> 278 us (level)
  transfers between devices with their start and end apart: 43 -> 43, of which waited for: 32 -> 32; matrix products, arithmetic and copies ran while one was open for 4% -> 5% of each run, Pallas kernels for 0% -> 0%
where the time goes in v12:
time: 278 us; the launch traced here: 276 us
  starting transfers between devices  140 us (50%)
  waiting for transfers between devices  94 us (34%)
  other arithmetic  16.2 us (6%)
  matrix products  11.7 us (4%)
  local copies, waits for them, and re-layouts  11.1 us (4%)
  between operations  3.18 us (1%)
    ppermute x20, starting transfers between devices, doubling_gather(): got = lax.ppermute(acc, 'lat', masked_pairs(n, masks[j]))  55.7 us
    ppermute x8, starting transfers between devices, butterfly_sum(): lax.ppermute(sent, axis, masked_pairs(n, mask)).astype(jnp.float32)  43 us
    ppermute x8, waiting for transfers between devices, butterfly_sum(): lax.ppermute(sent, axis, masked_pairs(n, mask)).astype(jnp.float32)  30.7 us
    ppermute x10, starting transfers between devices, halving_scatter(): lax.ppermute(sent, 'lat', masked_pairs(n, mask)).astype(jnp.float32)  29.5 us
    ppermute x20, waiting for transfers between devices, doubling_gather(): got = lax.ppermute(acc, 'lat', masked_pairs(n, masks[j]))  29.1 us
    ppermute x10, waiting for transfers between devices, halving_scatter(): lax.ppermute(sent, 'lat', masked_pairs(n, mask)).astype(jnp.float32)  18.9 us
    ppermute x5, waiting for transfers between devices, body(): squares = squares + lax.ppermute(squares, 'lat', masked_pairs(n_lat, mask))  15.3 us
    ppermute x5, starting transfers between devices, body(): squares = squares + lax.ppermute(squares, 'lat', masked_pairs(n_lat, mask))  11.8 us
  transfers between devices with their start and end apart: 43, of which 32 were waited for; matrix products, arithmetic and copies ran while one was open for 5% of the time, Pallas kernels for 0%

profile of v12, /device:TPU:6, one launch (start us, length us, event | category | flops | bytes accessed | tf_op | source)
XLA Modules:
  0.0 276.1 jit_solution(13074745796538884896)
XLA Ops:
  1.5 4.9 %collective-permute-start = (bf16[1,8,4096]{2,1,0:T(8,128)(2,1)S(1)}, bf16[1,8,4096]{2,1,0:T(8,128)(2,1)S(1)}, u32[]{:S(2)}, u32[]{:S(2)}) collective-permute-start(bf16[1,8,4096]{2,1,0:T(8,128)(2,1)S(1)} %get-tuple-element.18), channel_id=1, source_target_pairs={{0,24},{1,25},{2,26},{3,27},{4,28},{5,29},{6,30},{7,31},{8,16},{9,... | collective-permute-start | bytes 196616 | tf_op jit(solution)/shard_map/ppermute | solution.py:86
  6.5 4.8 %collective-permute-start.5 = (bf16[1,8,4096]{2,1,0:T(8,128)(2,1)S(1)}, bf16[1,8,4096]{2,1,0:T(8,128)(2,1)S(1)}, u32[]{:S(2)}, u32[]{:S(2)}) collective-permute-start(bf16[1,8,4096]{2,1,0:T(8,128)(2,1)S(1)} %get-tuple-element.19), channel_id=1, source_target_pairs={{0,6},{1,7},{2,4},{3,5},{4,2},{5,3},{6,0},{7,1},{8,14},{9,15},{10,... | collective-permute-start | bytes 196616 | tf_op jit(solution)/shard_map/ppermute | solution.py:86
  23.8 4.4 %collective-permute-start.7 = (bf16[4,8,4096]{2,1,0:T(8,128)(2,1)S(1)}, bf16[4,8,4096]{2,1,0:T(8,128)(2,1)S(1)}, u32[]{:S(2)}, u32[]{:S(2)}) collective-permute-start(bf16[4,8,4096]{2,1,0:T(8,128)(2,1)S(1)} %bitcast.210), channel_id=1, source_target_pairs={{0,24},{1,25},{2,26},{3,27},{4,28},{5,29},{6,30},{7,31},{8,16},{9,... | collective-permute-start | bytes 786440 | tf_op jit(solution)/shard_map/ppermute | solution.py:86
  36.0 5.7 %collective-permute-done.3 = bf16[8,8,4096]{2,1,0:T(8,128)(2,1)S(1)} collective-permute-done((bf16[8,8,4096]{2,1,0:T(8,128)(2,1)S(1)}, bf16[8,8,4096]{2,1,0:T(8,128)(2,1)S(1)}, u32[]{:S(2)}, u32[]{:S(2)}) %collective-permute-start.3) | collective-permute-done | bytes 524320 | tf_op jit(solution)/shard_map/ppermute | solution.py:86
  69.4 11.4 %collective-permute-done.11 = bf16[8,8,4096]{2,1,0:T(8,128)(2,1)S(1)} collective-permute-done((bf16[8,8,4096]{2,1,0:T(8,128)(2,1)S(1)}, bf16[8,8,4096]{2,1,0:T(8,128)(2,1)S(1)}, u32[]{:S(2)}, u32[]{:S(2)}) %collective-permute-start.11) | collective-permute-done | bytes 524320 | tf_op jit(solution)/shard_map/ppermute | solution.py:77
  84.2 5.1 %collective-permute-start.17 = (bf16[4,8,4096]{2,1,0:T(8,128)(2,1)S(1)}, bf16[4,8,4096]{2,1,0:T(8,128)(2,1)S(1)}, u32[]{:S(2)}, u32[]{:S(2)}) collective-permute-start(bf16[4,8,4096]{2,1,0:T(8,128)(2,1)S(1)} %fusion.14), channel_id=1, source_target_pairs={{0,24},{1,25},{2,26},{3,27},{4,28},{5,29},{6,30},{7,31},{8,16},{9,... | collective-permute-start | bytes 786440 | tf_op jit(solution)/shard_map/ppermute | solution.py:77
  98.6 4.0 %collective-permute-start.14 = (bf16[1,8,4096]{2,1,0:T(8,128)(2,1)S(1)}, bf16[1,8,4096]{2,1,0:T(8,128)(2,1)S(1)}, u32[]{:S(2)}, u32[]{:S(2)}) collective-permute-start(bf16[1,8,4096]{2,1,0:T(8,128)(2,1)S(1)} %dynamic-slice_convert_fusion.7), channel_id=1, source_target_pairs={{0,24},{1,25},{2,26},{3,27},{4,28},{5,29},{6,30},{7,31},{8,16},{9,... | collective-permute-start | bytes 196616 | tf_op jit(solution)/shard_map/ppermute | solution.py:77
  102.6 4.3 %collective-permute-start.19 = (bf16[1,8,4096]{2,1,0:T(8,128)(2,1)S(1)}, bf16[1,8,4096]{2,1,0:T(8,128)(2,1)S(1)}, u32[]{:S(2)}, u32[]{:S(2)}) collective-permute-start(bf16[1,8,4096]{2,1,0:T(8,128)(2,1)S(1)} %dynamic-slice_convert_fusion.6), channel_id=1, source_target_pairs={{0,6},{1,7},{2,4},{3,5},{4,2},{5,3},{6,0},{7,1},{8,14},{9,15},{10,... | collective-permute-start | bytes 196616 | tf_op jit(solution)/shard_map/ppermute | solution.py:77
  112.3 4.6 %collective-permute-done.20 = bf16[8,8192]{1,0:T(8,128)(2,1)S(1)} collective-permute-done((bf16[8,8192]{1,0:T(8,128)(2,1)S(1)}, bf16[8,8192]{1,0:T(8,128)(2,1)S(1)}, u32[]{:S(2)}, u32[]{:S(2)}) %collective-permute-start.20) | collective-permute-done | bytes 131104 | tf_op jit(solution)/shard_map/ppermute | solution.py:16
  116.9 3.8 %collective-permute-start.21 = (bf16[8,8192]{1,0:T(8,128)(2,1)S(1)}, bf16[8,8192]{1,0:T(8,128)(2,1)S(1)}, u32[]{:S(2)}, u32[]{:S(2)}) collective-permute-start(bf16[8,8192]{1,0:T(8,128)(2,1)S(1)} %add_convert_fusion.2), channel_id=1, source_target_pairs={{0,64},{32,96},{64,0},{96,32},{128,192},{160,224},{192,128},{224,1... | collective-permute-start | bytes 393224 | tf_op jit(solution)/shard_map/ppermute | solution.py:16
  120.7 5.3 %collective-permute-done.21 = bf16[8,8192]{1,0:T(8,128)(2,1)S(1)} collective-permute-done((bf16[8,8192]{1,0:T(8,128)(2,1)S(1)}, bf16[8,8192]{1,0:T(8,128)(2,1)S(1)}, u32[]{:S(2)}, u32[]{:S(2)}) %collective-permute-start.21) | collective-permute-done | bytes 131104 | tf_op jit(solution)/shard_map/ppermute | solution.py:16
  126.1 8.5 %collective-permute-start.22 = (bf16[8,8192]{1,0:T(8,128)(2,1)S(1)}, bf16[8,8192]{1,0:T(8,128)(2,1)S(1)}, u32[]{:S(2)}, u32[]{:S(2)}) collective-permute-start(bf16[8,8192]{1,0:T(8,128)(2,1)S(1)} %add_convert_fusion.1), channel_id=1, source_target_pairs={{0,128},{32,160},{64,192},{96,224},{128,0},{160,32},{192,64},{224,... | collective-permute-start | bytes 393224 | tf_op jit(solution)/shard_map/ppermute | solution.py:16
  134.6 7.1 %collective-permute-done.22 = bf16[8,8192]{1,0:T(8,128)(2,1)S(1)} collective-permute-done((bf16[8,8192]{1,0:T(8,128)(2,1)S(1)}, bf16[8,8192]{1,0:T(8,128)(2,1)S(1)}, u32[]{:S(2)}, u32[]{:S(2)}) %collective-permute-start.22) | collective-permute-done | bytes 131104 | tf_op jit(solution)/shard_map/ppermute | solution.py:16
  141.8 6.4 %collective-permute-start.23 = (bf16[8,8192]{1,0:T(8,128)(2,1)S(1)}, bf16[8,8192]{1,0:T(8,128)(2,1)S(1)}, u32[]{:S(2)}, u32[]{:S(2)}) collective-permute-start(bf16[8,8192]{1,0:T(8,128)(2,1)S(1)} %add_convert_fusion), channel_id=1, source_target_pairs={{0,384},{32,416},{64,448},{96,480},{128,256},{160,288},{192,320},{... | collective-permute-start | bytes 393224 | tf_op jit(solution)/shard_map/ppermute | solution.py:16
  149.1 3.6 %collective-permute-done.23 = bf16[8,8192]{1,0:T(8,128)(2,1)S(1)} collective-permute-done((bf16[8,8192]{1,0:T(8,128)(2,1)S(1)}, bf16[8,8192]{1,0:T(8,128)(2,1)S(1)}, u32[]{:S(2)}, u32[]{:S(2)}) %collective-permute-start.23) | collective-permute-done | bytes 131104 | tf_op jit(solution)/shard_map/ppermute | solution.py:16
  153.5 4.6 %collective-permute-start.24 = (bf16[1,8,4096]{2,1,0:T(8,128)(2,1)S(1)}, bf16[1,8,4096]{2,1,0:T(8,128)(2,1)S(1)}, u32[]{:S(2)}, u32[]{:S(2)}) collective-permute-start(bf16[1,8,4096]{2,1,0:T(8,128)(2,1)S(1)} %get-tuple-element.10), channel_id=1, source_target_pairs={{0,24},{1,25},{2,26},{3,27},{4,28},{5,29},{6,30},{7,31},{8,16},{9,... | collective-permute-start | bytes 196616 | tf_op jit(solution)/shard_map/ppermute | solution.py:86
  168.0 4.2 %collective-permute-start.26 = (bf16[4,8,4096]{2,1,0:T(8,128)(2,1)S(1)}, bf16[4,8,4096]{2,1,0:T(8,128)(2,1)S(1)}, u32[]{:S(2)}, u32[]{:S(2)}) collective-permute-start(bf16[4,8,4096]{2,1,0:T(8,128)(2,1)S(1)} %bitcast.204), channel_id=1, source_target_pairs={{0,6},{1,7},{2,4},{3,5},{4,2},{5,3},{6,0},{7,1},{8,14},{9,15},{10,... | collective-permute-start | bytes 786440 | tf_op jit(solution)/shard_map/ppermute | solution.py:86
  184.0 4.7 %collective-permute-done.27 = bf16[8,8,4096]{2,1,0:T(8,128)(2,1)S(1)} collective-permute-done((bf16[8,8,4096]{2,1,0:T(8,128)(2,1)S(1)}, bf16[8,8,4096]{2,1,0:T(8,128)(2,1)S(1)}, u32[]{:S(2)}, u32[]{:S(2)}) %collective-permute-start.27) | collective-permute-done | bytes 524320 | tf_op jit(solution)/shard_map/ppermute | solution.py:86
  223.9 3.7 %collective-permute-done.36 = f32[1,128]{1,0:T(1,128)S(1)} collective-permute-done((f32[1,128]{1,0:T(1,128)S(1)}, f32[1,128]{1,0:T(1,128)S(1)}, u32[]{:S(2)}, u32[]{:S(2)}) %collective-permute-start.36) | collective-permute-done | bytes 544 | tf_op jit(solution)/shard_map/ppermute | solution.py:167
  236.1 3.6 %collective-permute-done.38 = f32[1,128]{1,0:T(1,128)S(1)} collective-permute-done((f32[1,128]{1,0:T(1,128)S(1)}, f32[1,128]{1,0:T(1,128)S(1)}, u32[]{:S(2)}, u32[]{:S(2)}) %collective-permute-start.38) | collective-permute-done | bytes 544 | tf_op jit(solution)/shard_map/ppermute | solution.py:167
  245.2 6.4 %collective-permute-start.40 = (f32[1,128]{1,0:T(1,128)S(1)}, f32[1,128]{1,0:T(1,128)S(1)}, u32[]{:S(2)}, u32[]{:S(2)}) collective-permute-start(f32[1,128]{1,0:T(1,128)S(1)} %add.289), channel_id=1, source_target_pairs={{0,64},{32,96},{64,0},{96,32},{128,192},{160,224},{192,128},{224,1... | collective-permute-start | bytes 1544 | tf_op jit(solution)/shard_map/ppermute | solution.py:16
  253.1 5.7 %collective-permute-start.41 = (f32[1,128]{1,0:T(1,128)S(1)}, f32[1,128]{1,0:T(1,128)S(1)}, u32[]{:S(2)}, u32[]{:S(2)}) collective-permute-start(f32[1,128]{1,0:T(1,128)S(1)} %add.290), channel_id=1, source_target_pairs={{0,128},{32,160},{64,192},{96,224},{128,0},{160,32},{192,64},{224,... | collective-permute-start | bytes 1544 | tf_op jit(solution)/shard_map/ppermute | solution.py:16
  262.4 7.8 %collective-permute-start.42 = (f32[1,128]{1,0:T(1,128)S(1)}, f32[1,128]{1,0:T(1,128)S(1)}, u32[]{:S(2)}, u32[]{:S(2)}) collective-permute-start(f32[1,128]{1,0:T(1,128)S(1)} %add.291), channel_id=1, source_target_pairs={{0,384},{32,416},{64,448},{96,480},{128,256},{160,288},{192,320},{... | collective-permute-start | bytes 1544 | tf_op jit(solution)/shard_map/ppermute | solution.py:16
  272.4 3.7 %multiply_convert_fusion = bf16[8192,128]{1,0:T(8,128)(2,1)} fusion(f32[8192,128]{1,0:T(8,128)} %copy-done.3, f32[]{:T(128)} %bitcast.99), kind=kLoop, calls=%fused_computation.12 | loop fusion | flops 2097152 | bytes 6291460 | tf_op jit(solution)/shard_map/convert_element_type | solution.py:172
  (193 shorter events, 144.4 us)
Async XLA Ops:
  1.5 12.5 %collective-permute-start = (bf16[1,8,4096]{2,1,0:T(8,128)(2,1)S(1)}, bf16[1,8,4096]{2,1,0:T(8,128)(2,1)S(1)}, u32[]{:S(2)}, u32[]{:S(2)}) collective-permute-start(bf16[1,8,4096]{2,1,0:T(8,128)(2,1)S(1)} %get-tuple-element.18), channel_id=1, source_target_pairs={{0,24},{1,25},{2,26},{3,27},{4,28},{5,29},{6,30},{7,31},{8,16},{9,... | collective-permute-start | bytes 196616 | tf_op jit(solution)/shard_map/ppermute | solution.py:86
  6.5 9.5 %collective-permute-start.5 = (bf16[1,8,4096]{2,1,0:T(8,128)(2,1)S(1)}, bf16[1,8,4096]{2,1,0:T(8,128)(2,1)S(1)}, u32[]{:S(2)}, u32[]{:S(2)}) collective-permute-start(bf16[1,8,4096]{2,1,0:T(8,128)(2,1)S(1)} %get-tuple-element.19), channel_id=1, source_target_pairs={{0,6},{1,7},{2,4},{3,5},{4,2},{5,3},{6,0},{7,1},{8,14},{9,15},{10,... | collective-permute-start | bytes 196616 | tf_op jit(solution)/shard_map/ppermute | solution.py:86
  16.1 7.6 %collective-permute-start.6 = (bf16[2,8,4096]{2,1,0:T(8,128)(2,1)S(1)}, bf16[2,8,4096]{2,1,0:T(8,128)(2,1)S(1)}, u32[]{:S(2)}, u32[]{:S(2)}) collective-permute-start(bf16[2,8,4096]{2,1,0:T(8,128)(2,1)S(1)} %get-tuple-element.22), channel_id=1, source_target_pairs={{0,2},{1,3},{2,0},{3,1},{4,6},{5,7},{6,4},{7,5},{8,10},{9,11},{10,... | collective-permute-start | bytes 393224 | tf_op jit(solution)/shard_map/ppermute | solution.py:86
  21.0 9.5 %collective-permute-start.2 = (bf16[4,8,4096]{2,1,0:T(8,128)(2,1)S(1)}, bf16[4,8,4096]{2,1,0:T(8,128)(2,1)S(1)}, u32[]{:S(2)}, u32[]{:S(2)}) collective-permute-start(bf16[4,8,4096]{2,1,0:T(8,128)(2,1)S(1)} %bitcast.206), channel_id=1, source_target_pairs={{0,6},{1,7},{2,4},{3,5},{4,2},{5,3},{6,0},{7,1},{8,14},{9,15},{10,... | collective-permute-start | bytes 786440 | tf_op jit(solution)/shard_map/ppermute | solution.py:86
  23.8 9.5 %collective-permute-start.7 = (bf16[4,8,4096]{2,1,0:T(8,128)(2,1)S(1)}, bf16[4,8,4096]{2,1,0:T(8,128)(2,1)S(1)}, u32[]{:S(2)}, u32[]{:S(2)}) collective-permute-start(bf16[4,8,4096]{2,1,0:T(8,128)(2,1)S(1)} %bitcast.210), channel_id=1, source_target_pairs={{0,24},{1,25},{2,26},{3,27},{4,28},{5,29},{6,30},{7,31},{8,16},{9,... | collective-permute-start | bytes 786440 | tf_op jit(solution)/shard_map/ppermute | solution.py:86
  30.6 11.1 %collective-permute-start.3 = (bf16[8,8,4096]{2,1,0:T(8,128)(2,1)S(1)}, bf16[8,8,4096]{2,1,0:T(8,128)(2,1)S(1)}, u32[]{:S(2)}, u32[]{:S(2)}) collective-permute-start(bf16[8,8,4096]{2,1,0:T(8,128)(2,1)S(1)} %bitcast.196), channel_id=1, source_target_pairs={{0,2},{1,3},{2,0},{3,1},{4,6},{5,7},{6,4},{7,5},{8,10},{9,11},{10,... | collective-permute-start | bytes 1572872 | tf_op jit(solution)/shard_map/ppermute | solution.py:86
  33.4 12.3 %collective-permute-start.8 = (bf16[8,8,4096]{2,1,0:T(8,128)(2,1)S(1)}, bf16[8,8,4096]{2,1,0:T(8,128)(2,1)S(1)}, u32[]{:S(2)}, u32[]{:S(2)}) collective-permute-start(bf16[8,8,4096]{2,1,0:T(8,128)(2,1)S(1)} %bitcast.198), channel_id=1, source_target_pairs={{0,8},{1,9},{2,10},{3,11},{4,12},{5,13},{6,14},{7,15},{8,0},{9,1},... | collective-permute-start | bytes 1572872 | tf_op jit(solution)/shard_map/ppermute | solution.py:86
  64.9 15.9 %collective-permute-start.11 = (bf16[8,8,4096]{2,1,0:T(8,128)(2,1)S(1)}, bf16[8,8,4096]{2,1,0:T(8,128)(2,1)S(1)}, u32[]{:S(2)}, u32[]{:S(2)}) collective-permute-start(bf16[8,8,4096]{2,1,0:T(8,128)(2,1)S(1)} %fusion.11), channel_id=1, source_target_pairs={{0,2},{1,3},{2,0},{3,1},{4,6},{5,7},{6,4},{7,5},{8,10},{9,11},{10,... | collective-permute-start | bytes 1572872 | tf_op jit(solution)/shard_map/ppermute | solution.py:77
  67.3 16.8 %collective-permute-start.16 = (bf16[8,8,4096]{2,1,0:T(8,128)(2,1)S(1)}, bf16[8,8,4096]{2,1,0:T(8,128)(2,1)S(1)}, u32[]{:S(2)}, u32[]{:S(2)}) collective-permute-start(bf16[8,8,4096]{2,1,0:T(8,128)(2,1)S(1)} %fusion.12), channel_id=1, source_target_pairs={{0,8},{1,9},{2,10},{3,11},{4,12},{5,13},{6,14},{7,15},{8,0},{9,1},... | collective-permute-start | bytes 1572872 | tf_op jit(solution)/shard_map/ppermute | solution.py:77
  80.9 10.6 %collective-permute-start.12 = (bf16[4,8,4096]{2,1,0:T(8,128)(2,1)S(1)}, bf16[4,8,4096]{2,1,0:T(8,128)(2,1)S(1)}, u32[]{:S(2)}, u32[]{:S(2)}) collective-permute-start(bf16[4,8,4096]{2,1,0:T(8,128)(2,1)S(1)} %fusion.13), channel_id=1, source_target_pairs={{0,6},{1,7},{2,4},{3,5},{4,2},{5,3},{6,0},{7,1},{8,14},{9,15},{10,... | collective-permute-start | bytes 786440 | tf_op jit(solution)/shard_map/ppermute | solution.py:77
  84.2 10.6 %collective-permute-start.17 = (bf16[4,8,4096]{2,1,0:T(8,128)(2,1)S(1)}, bf16[4,8,4096]{2,1,0:T(8,128)(2,1)S(1)}, u32[]{:S(2)}, u32[]{:S(2)}) collective-permute-start(bf16[4,8,4096]{2,1,0:T(8,128)(2,1)S(1)} %fusion.14), channel_id=1, source_target_pairs={{0,24},{1,25},{2,26},{3,27},{4,28},{5,29},{6,30},{7,31},{8,16},{9,... | collective-permute-start | bytes 786440 | tf_op jit(solution)/shard_map/ppermute | solution.py:77
  94.9 7.6 %collective-permute-start.18 = (bf16[2,8,4096]{2,1,0:T(8,128)(2,1)S(1)}, bf16[2,8,4096]{2,1,0:T(8,128)(2,1)S(1)}, u32[]{:S(2)}, u32[]{:S(2)}) collective-permute-start(bf16[2,8,4096]{2,1,0:T(8,128)(2,1)S(1)} %fusion.17), channel_id=1, source_target_pairs={{0,2},{1,3},{2,0},{3,1},{4,6},{5,7},{6,4},{7,5},{8,10},{9,11},{10,... | collective-permute-start | bytes 393224 | tf_op jit(solution)/shard_map/ppermute | solution.py:77
  98.6 8.3 %collective-permute-start.14 = (bf16[1,8,4096]{2,1,0:T(8,128)(2,1)S(1)}, bf16[1,8,4096]{2,1,0:T(8,128)(2,1)S(1)}, u32[]{:S(2)}, u32[]{:S(2)}) collective-permute-start(bf16[1,8,4096]{2,1,0:T(8,128)(2,1)S(1)} %dynamic-slice_convert_fusion.7), channel_id=1, source_target_pairs={{0,24},{1,25},{2,26},{3,27},{4,28},{5,29},{6,30},{7,31},{8,16},{9,... | collective-permute-start | bytes 196616 | tf_op jit(solution)/shard_map/ppermute | solution.py:77
  116.9 9.2 %collective-permute-start.21 = (bf16[8,8192]{1,0:T(8,128)(2,1)S(1)}, bf16[8,8192]{1,0:T(8,128)(2,1)S(1)}, u32[]{:S(2)}, u32[]{:S(2)}) collective-permute-start(bf16[8,8192]{1,0:T(8,128)(2,1)S(1)} %add_convert_fusion.2), channel_id=1, source_target_pairs={{0,64},{32,96},{64,0},{96,32},{128,192},{160,224},{192,128},{224,1... | collective-permute-start | bytes 393224 | tf_op jit(solution)/shard_map/ppermute | solution.py:16
  126.1 15.7 %collective-permute-start.22 = (bf16[8,8192]{1,0:T(8,128)(2,1)S(1)}, bf16[8,8192]{1,0:T(8,128)(2,1)S(1)}, u32[]{:S(2)}, u32[]{:S(2)}) collective-permute-start(bf16[8,8192]{1,0:T(8,128)(2,1)S(1)} %add_convert_fusion.1), channel_id=1, source_target_pairs={{0,128},{32,160},{64,192},{96,224},{128,0},{160,32},{192,64},{224,... | collective-permute-start | bytes 393224 | tf_op jit(solution)/shard_map/ppermute | solution.py:16
  141.8 10.9 %collective-permute-start.23 = (bf16[8,8192]{1,0:T(8,128)(2,1)S(1)}, bf16[8,8192]{1,0:T(8,128)(2,1)S(1)}, u32[]{:S(2)}, u32[]{:S(2)}) collective-permute-start(bf16[8,8192]{1,0:T(8,128)(2,1)S(1)} %add_convert_fusion), channel_id=1, source_target_pairs={{0,384},{32,416},{64,448},{96,480},{128,256},{160,288},{192,320},{... | collective-permute-start | bytes 393224 | tf_op jit(solution)/shard_map/ppermute | solution.py:16
  153.5 7.5 %collective-permute-start.24 = (bf16[1,8,4096]{2,1,0:T(8,128)(2,1)S(1)}, bf16[1,8,4096]{2,1,0:T(8,128)(2,1)S(1)}, u32[]{:S(2)}, u32[]{:S(2)}) collective-permute-start(bf16[1,8,4096]{2,1,0:T(8,128)(2,1)S(1)} %get-tuple-element.10), channel_id=1, source_target_pairs={{0,24},{1,25},{2,26},{3,27},{4,28},{5,29},{6,30},{7,31},{8,16},{9,... | collective-permute-start | bytes 196616 | tf_op jit(solution)/shard_map/ppermute | solution.py:86
  168.0 9.5 %collective-permute-start.26 = (bf16[4,8,4096]{2,1,0:T(8,128)(2,1)S(1)}, bf16[4,8,4096]{2,1,0:T(8,128)(2,1)S(1)}, u32[]{:S(2)}, u32[]{:S(2)}) collective-permute-start(bf16[4,8,4096]{2,1,0:T(8,128)(2,1)S(1)} %bitcast.204), channel_id=1, source_target_pairs={{0,6},{1,7},{2,4},{3,5},{4,2},{5,3},{6,0},{7,1},{8,14},{9,15},{10,... | collective-permute-start | bytes 786440 | tf_op jit(solution)/shard_map/ppermute | solution.py:86
  172.5 9.5 %collective-permute-start.31 = (bf16[4,8,4096]{2,1,0:T(8,128)(2,1)S(1)}, bf16[4,8,4096]{2,1,0:T(8,128)(2,1)S(1)}, u32[]{:S(2)}, u32[]{:S(2)}) collective-permute-start(bf16[4,8,4096]{2,1,0:T(8,128)(2,1)S(1)} %bitcast.208), channel_id=1, source_target_pairs={{0,24},{1,25},{2,26},{3,27},{4,28},{5,29},{6,30},{7,31},{8,16},{9,... | collective-permute-start | bytes 786440 | tf_op jit(solution)/shard_map/ppermute | solution.py:86
  177.6 11.1 %collective-permute-start.27 = (bf16[8,8,4096]{2,1,0:T(8,128)(2,1)S(1)}, bf16[8,8,4096]{2,1,0:T(8,128)(2,1)S(1)}, u32[]{:S(2)}, u32[]{:S(2)}) collective-permute-start(bf16[8,8,4096]{2,1,0:T(8,128)(2,1)S(1)} %bitcast.192), channel_id=1, source_target_pairs={{0,2},{1,3},{2,0},{3,1},{4,6},{5,7},{6,4},{7,5},{8,10},{9,11},{10,... | collective-permute-start | bytes 1572872 | tf_op jit(solution)/shard_map/ppermute | solution.py:86
  182.1 11.1 %collective-permute-start.32 = (bf16[8,8,4096]{2,1,0:T(8,128)(2,1)S(1)}, bf16[8,8,4096]{2,1,0:T(8,128)(2,1)S(1)}, u32[]{:S(2)}, u32[]{:S(2)}) collective-permute-start(bf16[8,8,4096]{2,1,0:T(8,128)(2,1)S(1)} %bitcast.194), channel_id=1, source_target_pairs={{0,8},{1,9},{2,10},{3,11},{4,12},{5,13},{6,14},{7,15},{8,0},{9,1},... | collective-permute-start | bytes 1572872 | tf_op jit(solution)/shard_map/ppermute | solution.py:86
  245.2 7.9 %collective-permute-start.40 = (f32[1,128]{1,0:T(1,128)S(1)}, f32[1,128]{1,0:T(1,128)S(1)}, u32[]{:S(2)}, u32[]{:S(2)}) collective-permute-start(f32[1,128]{1,0:T(1,128)S(1)} %add.289), channel_id=1, source_target_pairs={{0,64},{32,96},{64,0},{96,32},{128,192},{160,224},{192,128},{224,1... | collective-permute-start | bytes 1544 | tf_op jit(solution)/shard_map/ppermute | solution.py:16
  253.1 9.3 %collective-permute-start.41 = (f32[1,128]{1,0:T(1,128)S(1)}, f32[1,128]{1,0:T(1,128)S(1)}, u32[]{:S(2)}, u32[]{:S(2)}) collective-permute-start(f32[1,128]{1,0:T(1,128)S(1)} %add.290), channel_id=1, source_target_pairs={{0,128},{32,160},{64,192},{96,224},{128,0},{160,32},{192,64},{224,... | collective-permute-start | bytes 1544 | tf_op jit(solution)/shard_map/ppermute | solution.py:16
  262.4 9.3 %collective-permute-start.42 = (f32[1,128]{1,0:T(1,128)S(1)}, f32[1,128]{1,0:T(1,128)S(1)}, u32[]{:S(2)}, u32[]{:S(2)}) collective-permute-start(f32[1,128]{1,0:T(1,128)S(1)} %add.291), channel_id=1, source_target_pairs={{0,384},{32,416},{64,448},{96,480},{128,256},{160,288},{192,320},{... | collective-permute-start | bytes 1544 | tf_op jit(solution)/shard_map/ppermute | solution.py:16
  (35 other events, 259.6 us)

commit v13 on v12

--- a/solution.py
+++ b/solution.py
@@ -129,6 +129,7 @@
     own_block = logical_rank(rank_lat, order_a)
     own_batch = lax.dynamic_slice_in_dim(batch, own_block * own_rows, own_rows, 0)
     own_offset = lax.optimization_barrier(dec_bias - own_batch.astype(jnp.float32))
+    gate = lax.optimization_barrier(jax.nn.sigmoid(sharpness * preact))
     active_b = take_blocks(active, block_perm(order_a, order_b, n_lat), own_rows)
     halves = []
     for k, (masks, rows) in enumerate(zip(ORDERS, (active, active_b))):
@@ -152,7 +153,7 @@
         ],
         axis=0,
     )
-    grad_pre = (grad_active + penalty) * jax.nn.sigmoid(sharpness * preact)
+    grad_pre = (grad_active + penalty) * gate
     encoder_grad = lax.dot_general(
         centered,
         grad_pre.astype(jnp.bfloat16),

time: 278 us -> 278 us (level)
  no operation moved by 1% of the time
where the time goes in v13:
time: 278 us; the launch traced here: 276 us
  starting transfers between devices  140 us (50%)
  waiting for transfers between devices  94 us (34%)
  other arithmetic  16.2 us (6%)
  matrix products  11.8 us (4%)
  local copies, waits for them, and re-layouts  11.4 us (4%)
  between operations  3.18 us (1%)
    ppermute x20, starting transfers between devices, doubling_gather(): got = lax.ppermute(acc, 'lat', masked_pairs(n, masks[j]))  55.8 us
    ppermute x8, starting transfers between devices, butterfly_sum(): lax.ppermute(sent, axis, masked_pairs(n, mask)).astype(jnp.float32)  43 us
    ppermute x8, waiting for transfers between devices, butterfly_sum(): lax.ppermute(sent, axis, masked_pairs(n, mask)).astype(jnp.float32)  30.7 us
    ppermute x10, starting transfers between devices, halving_scatter(): lax.ppermute(sent, 'lat', masked_pairs(n, mask)).astype(jnp.float32)  29.5 us
    ppermute x20, waiting for transfers between devices, doubling_gather(): got = lax.ppermute(acc, 'lat', masked_pairs(n, masks[j]))  29 us
    ppermute x10, waiting for transfers between devices, halving_scatter(): lax.ppermute(sent, 'lat', masked_pairs(n, mask)).astype(jnp.float32)  18.8 us
    ppermute x5, waiting for transfers between devices, body(): squares = squares + lax.ppermute(squares, 'lat', masked_pairs(n_lat, mask))  15.4 us
    ppermute x5, starting transfers between devices, body(): squares = squares + lax.ppermute(squares, 'lat', masked_pairs(n_lat, mask))  11.7 us
  transfers between devices with their start and end apart: 43, of which 32 were waited for; matrix products, arithmetic and copies ran while one was open for 5% of the time, Pallas kernels for 0%

profile of v13, /device:TPU:6, one launch (start us, length us, event | category | flops | bytes accessed | tf_op | source)
XLA Modules:
  0.0 276.5 jit_solution(10902592787711707725)
XLA Ops:
  1.5 4.9 %collective-permute-start = (bf16[1,8,4096]{2,1,0:T(8,128)(2,1)S(1)}, bf16[1,8,4096]{2,1,0:T(8,128)(2,1)S(1)}, u32[]{:S(2)}, u32[]{:S(2)}) collective-permute-start(bf16[1,8,4096]{2,1,0:T(8,128)(2,1)S(1)} %get-tuple-element.20), channel_id=1, source_target_pairs={{0,24},{1,25},{2,26},{3,27},{4,28},{5,29},{6,30},{7,31},{8,16},{9,... | collective-permute-start | bytes 196616 | tf_op jit(solution)/shard_map/ppermute | solution.py:86
  6.5 4.8 %collective-permute-start.5 = (bf16[1,8,4096]{2,1,0:T(8,128)(2,1)S(1)}, bf16[1,8,4096]{2,1,0:T(8,128)(2,1)S(1)}, u32[]{:S(2)}, u32[]{:S(2)}) collective-permute-start(bf16[1,8,4096]{2,1,0:T(8,128)(2,1)S(1)} %get-tuple-element.21), channel_id=1, source_target_pairs={{0,6},{1,7},{2,4},{3,5},{4,2},{5,3},{6,0},{7,1},{8,14},{9,15},{10,... | collective-permute-start | bytes 196616 | tf_op jit(solution)/shard_map/ppermute | solution.py:86
  23.8 4.4 %collective-permute-start.7 = (bf16[4,8,4096]{2,1,0:T(8,128)(2,1)S(1)}, bf16[4,8,4096]{2,1,0:T(8,128)(2,1)S(1)}, u32[]{:S(2)}, u32[]{:S(2)}) collective-permute-start(bf16[4,8,4096]{2,1,0:T(8,128)(2,1)S(1)} %bitcast.210), channel_id=1, source_target_pairs={{0,24},{1,25},{2,26},{3,27},{4,28},{5,29},{6,30},{7,31},{8,16},{9,... | collective-permute-start | bytes 786440 | tf_op jit(solution)/shard_map/ppermute | solution.py:86
  36.0 5.7 %collective-permute-done.3 = bf16[8,8,4096]{2,1,0:T(8,128)(2,1)S(1)} collective-permute-done((bf16[8,8,4096]{2,1,0:T(8,128)(2,1)S(1)}, bf16[8,8,4096]{2,1,0:T(8,128)(2,1)S(1)}, u32[]{:S(2)}, u32[]{:S(2)}) %collective-permute-start.3) | collective-permute-done | bytes 524320 | tf_op jit(solution)/shard_map/ppermute | solution.py:86
  69.4 11.4 %collective-permute-done.11 = bf16[8,8,4096]{2,1,0:T(8,128)(2,1)S(1)} collective-permute-done((bf16[8,8,4096]{2,1,0:T(8,128)(2,1)S(1)}, bf16[8,8,4096]{2,1,0:T(8,128)(2,1)S(1)}, u32[]{:S(2)}, u32[]{:S(2)}) %collective-permute-start.11) | collective-permute-done | bytes 524320 | tf_op jit(solution)/shard_map/ppermute | solution.py:77
  84.2 5.1 %collective-permute-start.17 = (bf16[4,8,4096]{2,1,0:T(8,128)(2,1)S(1)}, bf16[4,8,4096]{2,1,0:T(8,128)(2,1)S(1)}, u32[]{:S(2)}, u32[]{:S(2)}) collective-permute-start(bf16[4,8,4096]{2,1,0:T(8,128)(2,1)S(1)} %fusion.14), channel_id=1, source_target_pairs={{0,24},{1,25},{2,26},{3,27},{4,28},{5,29},{6,30},{7,31},{8,16},{9,... | collective-permute-start | bytes 786440 | tf_op jit(solution)/shard_map/ppermute | solution.py:77
  98.6 3.9 %collective-permute-start.14 = (bf16[1,8,4096]{2,1,0:T(8,128)(2,1)S(1)}, bf16[1,8,4096]{2,1,0:T(8,128)(2,1)S(1)}, u32[]{:S(2)}, u32[]{:S(2)}) collective-permute-start(bf16[1,8,4096]{2,1,0:T(8,128)(2,1)S(1)} %dynamic-slice_convert_fusion.7), channel_id=1, source_target_pairs={{0,24},{1,25},{2,26},{3,27},{4,28},{5,29},{6,30},{7,31},{8,16},{9,... | collective-permute-start | bytes 196616 | tf_op jit(solution)/shard_map/ppermute | solution.py:77
  102.6 4.3 %collective-permute-start.19 = (bf16[1,8,4096]{2,1,0:T(8,128)(2,1)S(1)}, bf16[1,8,4096]{2,1,0:T(8,128)(2,1)S(1)}, u32[]{:S(2)}, u32[]{:S(2)}) collective-permute-start(bf16[1,8,4096]{2,1,0:T(8,128)(2,1)S(1)} %dynamic-slice_convert_fusion.6), channel_id=1, source_target_pairs={{0,6},{1,7},{2,4},{3,5},{4,2},{5,3},{6,0},{7,1},{8,14},{9,15},{10,... | collective-permute-start | bytes 196616 | tf_op jit(solution)/shard_map/ppermute | solution.py:77
  112.3 4.6 %collective-permute-done.20 = bf16[8,8192]{1,0:T(8,128)(2,1)S(1)} collective-permute-done((bf16[8,8192]{1,0:T(8,128)(2,1)S(1)}, bf16[8,8192]{1,0:T(8,128)(2,1)S(1)}, u32[]{:S(2)}, u32[]{:S(2)}) %collective-permute-start.20) | collective-permute-done | bytes 131104 | tf_op jit(solution)/shard_map/ppermute | solution.py:16
  116.9 3.9 %collective-permute-start.21 = (bf16[8,8192]{1,0:T(8,128)(2,1)S(1)}, bf16[8,8192]{1,0:T(8,128)(2,1)S(1)}, u32[]{:S(2)}, u32[]{:S(2)}) collective-permute-start(bf16[8,8192]{1,0:T(8,128)(2,1)S(1)} %add_convert_fusion.2), channel_id=1, source_target_pairs={{0,64},{32,96},{64,0},{96,32},{128,192},{160,224},{192,128},{224,1... | collective-permute-start | bytes 393224 | tf_op jit(solution)/shard_map/ppermute | solution.py:16
  120.8 5.3 %collective-permute-done.21 = bf16[8,8192]{1,0:T(8,128)(2,1)S(1)} collective-permute-done((bf16[8,8192]{1,0:T(8,128)(2,1)S(1)}, bf16[8,8192]{1,0:T(8,128)(2,1)S(1)}, u32[]{:S(2)}, u32[]{:S(2)}) %collective-permute-start.21) | collective-permute-done | bytes 131104 | tf_op jit(solution)/shard_map/ppermute | solution.py:16
  126.1 8.5 %collective-permute-start.22 = (bf16[8,8192]{1,0:T(8,128)(2,1)S(1)}, bf16[8,8192]{1,0:T(8,128)(2,1)S(1)}, u32[]{:S(2)}, u32[]{:S(2)}) collective-permute-start(bf16[8,8192]{1,0:T(8,128)(2,1)S(1)} %add_convert_fusion.1), channel_id=1, source_target_pairs={{0,128},{32,160},{64,192},{96,224},{128,0},{160,32},{192,64},{224,... | collective-permute-start | bytes 393224 | tf_op jit(solution)/shard_map/ppermute | solution.py:16
  134.6 7.1 %collective-permute-done.22 = bf16[8,8192]{1,0:T(8,128)(2,1)S(1)} collective-permute-done((bf16[8,8192]{1,0:T(8,128)(2,1)S(1)}, bf16[8,8192]{1,0:T(8,128)(2,1)S(1)}, u32[]{:S(2)}, u32[]{:S(2)}) %collective-permute-start.22) | collective-permute-done | bytes 131104 | tf_op jit(solution)/shard_map/ppermute | solution.py:16
  141.8 6.4 %collective-permute-start.23 = (bf16[8,8192]{1,0:T(8,128)(2,1)S(1)}, bf16[8,8192]{1,0:T(8,128)(2,1)S(1)}, u32[]{:S(2)}, u32[]{:S(2)}) collective-permute-start(bf16[8,8192]{1,0:T(8,128)(2,1)S(1)} %add_convert_fusion), channel_id=1, source_target_pairs={{0,384},{32,416},{64,448},{96,480},{128,256},{160,288},{192,320},{... | collective-permute-start | bytes 393224 | tf_op jit(solution)/shard_map/ppermute | solution.py:16
  149.1 3.6 %collective-permute-done.23 = bf16[8,8192]{1,0:T(8,128)(2,1)S(1)} collective-permute-done((bf16[8,8192]{1,0:T(8,128)(2,1)S(1)}, bf16[8,8192]{1,0:T(8,128)(2,1)S(1)}, u32[]{:S(2)}, u32[]{:S(2)}) %collective-permute-start.23) | collective-permute-done | bytes 131104 | tf_op jit(solution)/shard_map/ppermute | solution.py:16
  153.4 4.7 %collective-permute-start.24 = (bf16[1,8,4096]{2,1,0:T(8,128)(2,1)S(1)}, bf16[1,8,4096]{2,1,0:T(8,128)(2,1)S(1)}, u32[]{:S(2)}, u32[]{:S(2)}) collective-permute-start(bf16[1,8,4096]{2,1,0:T(8,128)(2,1)S(1)} %get-tuple-element.12), channel_id=1, source_target_pairs={{0,24},{1,25},{2,26},{3,27},{4,28},{5,29},{6,30},{7,31},{8,16},{9,... | collective-permute-start | bytes 196616 | tf_op jit(solution)/shard_map/ppermute | solution.py:86
  168.0 4.2 %collective-permute-start.26 = (bf16[4,8,4096]{2,1,0:T(8,128)(2,1)S(1)}, bf16[4,8,4096]{2,1,0:T(8,128)(2,1)S(1)}, u32[]{:S(2)}, u32[]{:S(2)}) collective-permute-start(bf16[4,8,4096]{2,1,0:T(8,128)(2,1)S(1)} %bitcast.204), channel_id=1, source_target_pairs={{0,6},{1,7},{2,4},{3,5},{4,2},{5,3},{6,0},{7,1},{8,14},{9,15},{10,... | collective-permute-start | bytes 786440 | tf_op jit(solution)/shard_map/ppermute | solution.py:86
  184.0 4.7 %collective-permute-done.27 = bf16[8,8,4096]{2,1,0:T(8,128)(2,1)S(1)} collective-permute-done((bf16[8,8,4096]{2,1,0:T(8,128)(2,1)S(1)}, bf16[8,8,4096]{2,1,0:T(8,128)(2,1)S(1)}, u32[]{:S(2)}, u32[]{:S(2)}) %collective-permute-start.27) | collective-permute-done | bytes 524320 | tf_op jit(solution)/shard_map/ppermute | solution.py:86
  224.2 3.8 %collective-permute-done.36 = f32[1,128]{1,0:T(1,128)S(1)} collective-permute-done((f32[1,128]{1,0:T(1,128)S(1)}, f32[1,128]{1,0:T(1,128)S(1)}, u32[]{:S(2)}, u32[]{:S(2)}) %collective-permute-start.36) | collective-permute-done | bytes 544 | tf_op jit(solution)/shard_map/ppermute | solution.py:168
  236.4 3.7 %collective-permute-done.38 = f32[1,128]{1,0:T(1,128)S(1)} collective-permute-done((f32[1,128]{1,0:T(1,128)S(1)}, f32[1,128]{1,0:T(1,128)S(1)}, u32[]{:S(2)}, u32[]{:S(2)}) %collective-permute-start.38) | collective-permute-done | bytes 544 | tf_op jit(solution)/shard_map/ppermute | solution.py:168
  245.5 6.5 %collective-permute-start.40 = (f32[1,128]{1,0:T(1,128)S(1)}, f32[1,128]{1,0:T(1,128)S(1)}, u32[]{:S(2)}, u32[]{:S(2)}) collective-permute-start(f32[1,128]{1,0:T(1,128)S(1)} %add.289), channel_id=1, source_target_pairs={{0,64},{32,96},{64,0},{96,32},{128,192},{160,224},{192,128},{224,1... | collective-permute-start | bytes 1544 | tf_op jit(solution)/shard_map/ppermute | solution.py:16
  253.5 5.7 %collective-permute-start.41 = (f32[1,128]{1,0:T(1,128)S(1)}, f32[1,128]{1,0:T(1,128)S(1)}, u32[]{:S(2)}, u32[]{:S(2)}) collective-permute-start(f32[1,128]{1,0:T(1,128)S(1)} %add.290), channel_id=1, source_target_pairs={{0,128},{32,160},{64,192},{96,224},{128,0},{160,32},{192,64},{224,... | collective-permute-start | bytes 1544 | tf_op jit(solution)/shard_map/ppermute | solution.py:16
  262.8 7.8 %collective-permute-start.42 = (f32[1,128]{1,0:T(1,128)S(1)}, f32[1,128]{1,0:T(1,128)S(1)}, u32[]{:S(2)}, u32[]{:S(2)}) collective-permute-start(f32[1,128]{1,0:T(1,128)S(1)} %add.291), channel_id=1, source_target_pairs={{0,384},{32,416},{64,448},{96,480},{128,256},{160,288},{192,320},{... | collective-permute-start | bytes 1544 | tf_op jit(solution)/shard_map/ppermute | solution.py:16
  272.8 3.7 %multiply_convert_fusion = bf16[8192,128]{1,0:T(8,128)(2,1)} fusion(f32[8192,128]{1,0:T(8,128)} %copy-done.3, f32[]{:T(128)} %bitcast.99), kind=kLoop, calls=%fused_computation.12 | loop fusion | flops 2097152 | bytes 6291460 | tf_op jit(solution)/shard_map/convert_element_type | solution.py:173
  (193 shorter events, 144.7 us)
Async XLA Ops:
  1.5 12.5 %collective-permute-start = (bf16[1,8,4096]{2,1,0:T(8,128)(2,1)S(1)}, bf16[1,8,4096]{2,1,0:T(8,128)(2,1)S(1)}, u32[]{:S(2)}, u32[]{:S(2)}) collective-permute-start(bf16[1,8,4096]{2,1,0:T(8,128)(2,1)S(1)} %get-tuple-element.20), channel_id=1, source_target_pairs={{0,24},{1,25},{2,26},{3,27},{4,28},{5,29},{6,30},{7,31},{8,16},{9,... | collective-permute-start | bytes 196616 | tf_op jit(solution)/shard_map/ppermute | solution.py:86
  6.5 9.5 %collective-permute-start.5 = (bf16[1,8,4096]{2,1,0:T(8,128)(2,1)S(1)}, bf16[1,8,4096]{2,1,0:T(8,128)(2,1)S(1)}, u32[]{:S(2)}, u32[]{:S(2)}) collective-permute-start(bf16[1,8,4096]{2,1,0:T(8,128)(2,1)S(1)} %get-tuple-element.21), channel_id=1, source_target_pairs={{0,6},{1,7},{2,4},{3,5},{4,2},{5,3},{6,0},{7,1},{8,14},{9,15},{10,... | collective-permute-start | bytes 196616 | tf_op jit(solution)/shard_map/ppermute | solution.py:86
  16.1 7.6 %collective-permute-start.6 = (bf16[2,8,4096]{2,1,0:T(8,128)(2,1)S(1)}, bf16[2,8,4096]{2,1,0:T(8,128)(2,1)S(1)}, u32[]{:S(2)}, u32[]{:S(2)}) collective-permute-start(bf16[2,8,4096]{2,1,0:T(8,128)(2,1)S(1)} %get-tuple-element.24), channel_id=1, source_target_pairs={{0,2},{1,3},{2,0},{3,1},{4,6},{5,7},{6,4},{7,5},{8,10},{9,11},{10,... | collective-permute-start | bytes 393224 | tf_op jit(solution)/shard_map/ppermute | solution.py:86
  21.0 9.5 %collective-permute-start.2 = (bf16[4,8,4096]{2,1,0:T(8,128)(2,1)S(1)}, bf16[4,8,4096]{2,1,0:T(8,128)(2,1)S(1)}, u32[]{:S(2)}, u32[]{:S(2)}) collective-permute-start(bf16[4,8,4096]{2,1,0:T(8,128)(2,1)S(1)} %bitcast.206), channel_id=1, source_target_pairs={{0,6},{1,7},{2,4},{3,5},{4,2},{5,3},{6,0},{7,1},{8,14},{9,15},{10,... | collective-permute-start | bytes 786440 | tf_op jit(solution)/shard_map/ppermute | solution.py:86
  23.8 9.5 %collective-permute-start.7 = (bf16[4,8,4096]{2,1,0:T(8,128)(2,1)S(1)}, bf16[4,8,4096]{2,1,0:T(8,128)(2,1)S(1)}, u32[]{:S(2)}, u32[]{:S(2)}) collective-permute-start(bf16[4,8,4096]{2,1,0:T(8,128)(2,1)S(1)} %bitcast.210), channel_id=1, source_target_pairs={{0,24},{1,25},{2,26},{3,27},{4,28},{5,29},{6,30},{7,31},{8,16},{9,... | collective-permute-start | bytes 786440 | tf_op jit(solution)/shard_map/ppermute | solution.py:86
  30.6 11.1 %collective-permute-start.3 = (bf16[8,8,4096]{2,1,0:T(8,128)(2,1)S(1)}, bf16[8,8,4096]{2,1,0:T(8,128)(2,1)S(1)}, u32[]{:S(2)}, u32[]{:S(2)}) collective-permute-start(bf16[8,8,4096]{2,1,0:T(8,128)(2,1)S(1)} %bitcast.196), channel_id=1, source_target_pairs={{0,2},{1,3},{2,0},{3,1},{4,6},{5,7},{6,4},{7,5},{8,10},{9,11},{10,... | collective-permute-start | bytes 1572872 | tf_op jit(solution)/shard_map/ppermute | solution.py:86
  33.4 12.3 %collective-permute-start.8 = (bf16[8,8,4096]{2,1,0:T(8,128)(2,1)S(1)}, bf16[8,8,4096]{2,1,0:T(8,128)(2,1)S(1)}, u32[]{:S(2)}, u32[]{:S(2)}) collective-permute-start(bf16[8,8,4096]{2,1,0:T(8,128)(2,1)S(1)} %bitcast.198), channel_id=1, source_target_pairs={{0,8},{1,9},{2,10},{3,11},{4,12},{5,13},{6,14},{7,15},{8,0},{9,1},... | collective-permute-start | bytes 1572872 | tf_op jit(solution)/shard_map/ppermute | solution.py:86
  64.9 15.9 %collective-permute-start.11 = (bf16[8,8,4096]{2,1,0:T(8,128)(2,1)S(1)}, bf16[8,8,4096]{2,1,0:T(8,128)(2,1)S(1)}, u32[]{:S(2)}, u32[]{:S(2)}) collective-permute-start(bf16[8,8,4096]{2,1,0:T(8,128)(2,1)S(1)} %fusion.11), channel_id=1, source_target_pairs={{0,2},{1,3},{2,0},{3,1},{4,6},{5,7},{6,4},{7,5},{8,10},{9,11},{10,... | collective-permute-start | bytes 1572872 | tf_op jit(solution)/shard_map/ppermute | solution.py:77
  67.3 16.8 %collective-permute-start.16 = (bf16[8,8,4096]{2,1,0:T(8,128)(2,1)S(1)}, bf16[8,8,4096]{2,1,0:T(8,128)(2,1)S(1)}, u32[]{:S(2)}, u32[]{:S(2)}) collective-permute-start(bf16[8,8,4096]{2,1,0:T(8,128)(2,1)S(1)} %fusion.12), channel_id=1, source_target_pairs={{0,8},{1,9},{2,10},{3,11},{4,12},{5,13},{6,14},{7,15},{8,0},{9,1},... | collective-permute-start | bytes 1572872 | tf_op jit(solution)/shard_map/ppermute | solution.py:77
  81.0 10.6 %collective-permute-start.12 = (bf16[4,8,4096]{2,1,0:T(8,128)(2,1)S(1)}, bf16[4,8,4096]{2,1,0:T(8,128)(2,1)S(1)}, u32[]{:S(2)}, u32[]{:S(2)}) collective-permute-start(bf16[4,8,4096]{2,1,0:T(8,128)(2,1)S(1)} %fusion.13), channel_id=1, source_target_pairs={{0,6},{1,7},{2,4},{3,5},{4,2},{5,3},{6,0},{7,1},{8,14},{9,15},{10,... | collective-permute-start | bytes 786440 | tf_op jit(solution)/shard_map/ppermute | solution.py:77
  84.2 10.6 %collective-permute-start.17 = (bf16[4,8,4096]{2,1,0:T(8,128)(2,1)S(1)}, bf16[4,8,4096]{2,1,0:T(8,128)(2,1)S(1)}, u32[]{:S(2)}, u32[]{:S(2)}) collective-permute-start(bf16[4,8,4096]{2,1,0:T(8,128)(2,1)S(1)} %fusion.14), channel_id=1, source_target_pairs={{0,24},{1,25},{2,26},{3,27},{4,28},{5,29},{6,30},{7,31},{8,16},{9,... | collective-permute-start | bytes 786440 | tf_op jit(solution)/shard_map/ppermute | solution.py:77
  94.9 7.6 %collective-permute-start.18 = (bf16[2,8,4096]{2,1,0:T(8,128)(2,1)S(1)}, bf16[2,8,4096]{2,1,0:T(8,128)(2,1)S(1)}, u32[]{:S(2)}, u32[]{:S(2)}) collective-permute-start(bf16[2,8,4096]{2,1,0:T(8,128)(2,1)S(1)} %fusion.17), channel_id=1, source_target_pairs={{0,2},{1,3},{2,0},{3,1},{4,6},{5,7},{6,4},{7,5},{8,10},{9,11},{10,... | collective-permute-start | bytes 393224 | tf_op jit(solution)/shard_map/ppermute | solution.py:77
  98.6 8.3 %collective-permute-start.14 = (bf16[1,8,4096]{2,1,0:T(8,128)(2,1)S(1)}, bf16[1,8,4096]{2,1,0:T(8,128)(2,1)S(1)}, u32[]{:S(2)}, u32[]{:S(2)}) collective-permute-start(bf16[1,8,4096]{2,1,0:T(8,128)(2,1)S(1)} %dynamic-slice_convert_fusion.7), channel_id=1, source_target_pairs={{0,24},{1,25},{2,26},{3,27},{4,28},{5,29},{6,30},{7,31},{8,16},{9,... | collective-permute-start | bytes 196616 | tf_op jit(solution)/shard_map/ppermute | solution.py:77
  116.9 9.2 %collective-permute-start.21 = (bf16[8,8192]{1,0:T(8,128)(2,1)S(1)}, bf16[8,8192]{1,0:T(8,128)(2,1)S(1)}, u32[]{:S(2)}, u32[]{:S(2)}) collective-permute-start(bf16[8,8192]{1,0:T(8,128)(2,1)S(1)} %add_convert_fusion.2), channel_id=1, source_target_pairs={{0,64},{32,96},{64,0},{96,32},{128,192},{160,224},{192,128},{224,1... | collective-permute-start | bytes 393224 | tf_op jit(solution)/shard_map/ppermute | solution.py:16
  126.1 15.6 %collective-permute-start.22 = (bf16[8,8192]{1,0:T(8,128)(2,1)S(1)}, bf16[8,8192]{1,0:T(8,128)(2,1)S(1)}, u32[]{:S(2)}, u32[]{:S(2)}) collective-permute-start(bf16[8,8192]{1,0:T(8,128)(2,1)S(1)} %add_convert_fusion.1), channel_id=1, source_target_pairs={{0,128},{32,160},{64,192},{96,224},{128,0},{160,32},{192,64},{224,... | collective-permute-start | bytes 393224 | tf_op jit(solution)/shard_map/ppermute | solution.py:16
  141.8 10.9 %collective-permute-start.23 = (bf16[8,8192]{1,0:T(8,128)(2,1)S(1)}, bf16[8,8192]{1,0:T(8,128)(2,1)S(1)}, u32[]{:S(2)}, u32[]{:S(2)}) collective-permute-start(bf16[8,8192]{1,0:T(8,128)(2,1)S(1)} %add_convert_fusion), channel_id=1, source_target_pairs={{0,384},{32,416},{64,448},{96,480},{128,256},{160,288},{192,320},{... | collective-permute-start | bytes 393224 | tf_op jit(solution)/shard_map/ppermute | solution.py:16
  153.4 7.6 %collective-permute-start.24 = (bf16[1,8,4096]{2,1,0:T(8,128)(2,1)S(1)}, bf16[1,8,4096]{2,1,0:T(8,128)(2,1)S(1)}, u32[]{:S(2)}, u32[]{:S(2)}) collective-permute-start(bf16[1,8,4096]{2,1,0:T(8,128)(2,1)S(1)} %get-tuple-element.12), channel_id=1, source_target_pairs={{0,24},{1,25},{2,26},{3,27},{4,28},{5,29},{6,30},{7,31},{8,16},{9,... | collective-permute-start | bytes 196616 | tf_op jit(solution)/shard_map/ppermute | solution.py:86
  168.0 9.5 %collective-permute-start.26 = (bf16[4,8,4096]{2,1,0:T(8,128)(2,1)S(1)}, bf16[4,8,4096]{2,1,0:T(8,128)(2,1)S(1)}, u32[]{:S(2)}, u32[]{:S(2)}) collective-permute-start(bf16[4,8,4096]{2,1,0:T(8,128)(2,1)S(1)} %bitcast.204), channel_id=1, source_target_pairs={{0,6},{1,7},{2,4},{3,5},{4,2},{5,3},{6,0},{7,1},{8,14},{9,15},{10,... | collective-permute-start | bytes 786440 | tf_op jit(solution)/shard_map/ppermute | solution.py:86
  172.5 9.5 %collective-permute-start.31 = (bf16[4,8,4096]{2,1,0:T(8,128)(2,1)S(1)}, bf16[4,8,4096]{2,1,0:T(8,128)(2,1)S(1)}, u32[]{:S(2)}, u32[]{:S(2)}) collective-permute-start(bf16[4,8,4096]{2,1,0:T(8,128)(2,1)S(1)} %bitcast.208), channel_id=1, source_target_pairs={{0,24},{1,25},{2,26},{3,27},{4,28},{5,29},{6,30},{7,31},{8,16},{9,... | collective-permute-start | bytes 786440 | tf_op jit(solution)/shard_map/ppermute | solution.py:86
  177.6 11.1 %collective-permute-start.27 = (bf16[8,8,4096]{2,1,0:T(8,128)(2,1)S(1)}, bf16[8,8,4096]{2,1,0:T(8,128)(2,1)S(1)}, u32[]{:S(2)}, u32[]{:S(2)}) collective-permute-start(bf16[8,8,4096]{2,1,0:T(8,128)(2,1)S(1)} %bitcast.192), channel_id=1, source_target_pairs={{0,2},{1,3},{2,0},{3,1},{4,6},{5,7},{6,4},{7,5},{8,10},{9,11},{10,... | collective-permute-start | bytes 1572872 | tf_op jit(solution)/shard_map/ppermute | solution.py:86
  182.1 11.1 %collective-permute-start.32 = (bf16[8,8,4096]{2,1,0:T(8,128)(2,1)S(1)}, bf16[8,8,4096]{2,1,0:T(8,128)(2,1)S(1)}, u32[]{:S(2)}, u32[]{:S(2)}) collective-permute-start(bf16[8,8,4096]{2,1,0:T(8,128)(2,1)S(1)} %bitcast.194), channel_id=1, source_target_pairs={{0,8},{1,9},{2,10},{3,11},{4,12},{5,13},{6,14},{7,15},{8,0},{9,1},... | collective-permute-start | bytes 1572872 | tf_op jit(solution)/shard_map/ppermute | solution.py:86
  245.5 8.0 %collective-permute-start.40 = (f32[1,128]{1,0:T(1,128)S(1)}, f32[1,128]{1,0:T(1,128)S(1)}, u32[]{:S(2)}, u32[]{:S(2)}) collective-permute-start(f32[1,128]{1,0:T(1,128)S(1)} %add.289), channel_id=1, source_target_pairs={{0,64},{32,96},{64,0},{96,32},{128,192},{160,224},{192,128},{224,1... | collective-permute-start | bytes 1544 | tf_op jit(solution)/shard_map/ppermute | solution.py:16
  253.5 9.3 %collective-permute-start.41 = (f32[1,128]{1,0:T(1,128)S(1)}, f32[1,128]{1,0:T(1,128)S(1)}, u32[]{:S(2)}, u32[]{:S(2)}) collective-permute-start(f32[1,128]{1,0:T(1,128)S(1)} %add.290), channel_id=1, source_target_pairs={{0,128},{32,160},{64,192},{96,224},{128,0},{160,32},{192,64},{224,... | collective-permute-start | bytes 1544 | tf_op jit(solution)/shard_map/ppermute | solution.py:16
  262.8 9.3 %collective-permute-start.42 = (f32[1,128]{1,0:T(1,128)S(1)}, f32[1,128]{1,0:T(1,128)S(1)}, u32[]{:S(2)}, u32[]{:S(2)}) collective-permute-start(f32[1,128]{1,0:T(1,128)S(1)} %add.291), channel_id=1, source_target_pairs={{0,384},{32,416},{64,448},{96,480},{128,256},{160,288},{192,320},{... | collective-permute-start | bytes 1544 | tf_op jit(solution)/shard_map/ppermute | solution.py:16
  (35 other events, 258.5 us)
